TPU v7x, 512 devices: a whole 4x4x16 slice. The times are simulated.
512 devices in a mesh: patch: 128 (over z, y, core), mp: 4 (over x).
Axes of the slice: x: 4, y: 4, z: 16, core: 2. Of those that a mesh axis runs over, the one named last changes fastest.
Arguments:
- features: bfloat16 [65536, 1024], P('patch'), may hold values from -16 to 16
- gain_attn: float32 [1024], replicated, may hold values from 0.1 to 1.9
- w_qkv: bfloat16 [3, 1024, 1024], P(None, None, 'mp'), as said below
- w_out: bfloat16 [1024, 1024], P('mp'), may hold values from -0.1875 to 0.1875
- gain_mlp: float32 [1024], replicated, may hold values from 0.1 to 1.9
- w_up: bfloat16 [1024, 2048], P(None, 'mp'), may hold values from -0.1875 to 0.1875
- w_down: bfloat16 [2048, 1024], P('mp'), may hold values from -0.125 to 0.125
- neighbours: int32 [512, 8], replicated, may hold values from 0 to 511, as said below
Outputs:
- layer_out: bfloat16 [65536, 1024], P('patch', 'mp')
Inputs may be any that keep to these rules, and one draw needn't show every extreme that they name: `neighbours`: row p lists 8 different patches; the first is p itself. Patch q belongs to device q // 4 of the patch axis, and every listed patch belongs to a device whose index differs from that of p's device by at most 2 around the patch axis (the lining closes into a cycle). `w_qkv`: projection weights of mean zero.
All inputs are finite; a program needn't handle non-finite values.
Results may differ from a plain program's by a relative error of at most 0.012.
Values may be sent and summed in bfloat16 or wider, within the bound.
No kernel may reach another device: no remote copies, remote signals or barrier semaphores. Data moves between devices by JAX's collectives and lax.ppermute only.
A program may use at most 64 MiB of HBM per device.

v0:
```python
import jax
import jax.numpy as jnp
from jax import lax
from jax.sharding import PartitionSpec as P

D = 1024
HD = 64
PN = 128
K_NB = 8
REACH = 2


def from_behind(array, axis, by):
    length = lax.axis_size(axis)
    return lax.ppermute(array, axis, [(i, (i + by) % length) for i in range(length)])


def normalize(rows, gain):
    rows32 = rows.astype(jnp.float32)
    mean_sq = jnp.mean(rows32 * rows32, axis=-1, keepdims=True)
    return (rows32 * lax.rsqrt(mean_sq + 1e-05) * gain).astype(jnp.bfloat16)


def per_device(features, gain_attn, w_qkv, w_out, gain_mlp, w_up, w_down, neighbours):
    row_count = features.shape[0]
    patches_here = row_count // PN
    heads_here = w_qkv.shape[2] // HD
    normed = normalize(features, gain_attn)
    queries = jnp.dot(normed, w_qkv[0], preferred_element_type=jnp.float32).astype(jnp.bfloat16)
    own_keys = (
        jnp.dot(normed, w_qkv[1], preferred_element_type=jnp.float32)
        .astype(jnp.bfloat16)
        .reshape(patches_here, PN, -1)
    )
    own_vals = (
        jnp.dot(normed, w_qkv[2], preferred_element_type=jnp.float32)
        .astype(jnp.bfloat16)
        .reshape(patches_here, PN, -1)
    )
    window = {0: (own_keys, own_vals)}
    for offset in range(-REACH, REACH + 1):
        if offset != 0:
            window[offset] = from_behind((own_keys, own_vals), "patch", -offset)
    keys_win = jnp.concatenate([window[offset][0] for offset in range(-REACH, REACH + 1)], axis=0)
    vals_win = jnp.concatenate([window[offset][1] for offset in range(-REACH, REACH + 1)], axis=0)
    device = lax.axis_index("patch")
    n_dev = lax.axis_size("patch")
    listed = lax.dynamic_slice_in_dim(neighbours, device * patches_here, patches_here, 0)
    owner_dev = listed // patches_here
    offset_dev = jnp.mod(owner_dev - device + n_dev // 2, n_dev) - n_dev // 2
    slot_index = (offset_dev + REACH) * patches_here + jnp.mod(listed, patches_here)
    keys_nb = keys_win[slot_index].reshape(patches_here, K_NB * PN, heads_here, HD)
    vals_nb = vals_win[slot_index].reshape(patches_here, K_NB * PN, heads_here, HD)
    query_blk = queries.reshape(patches_here, PN, heads_here, HD)
    scores = jnp.einsum(
        "pqhd,pkhd->phqk", query_blk, keys_nb, preferred_element_type=jnp.float32
    ) * (1.0 / HD**0.5)
    probs = jax.nn.softmax(scores, axis=-1).astype(jnp.bfloat16)
    mixed_rows = jnp.einsum("phqk,pkhd->pqhd", probs, vals_nb, preferred_element_type=jnp.float32)
    attended = mixed_rows.astype(jnp.bfloat16).reshape(row_count, heads_here * HD)
    partial_value = jnp.dot(attended, w_out, preferred_element_type=jnp.float32)
    col_share = lax.psum_scatter(
        partial_value.astype(jnp.bfloat16), "mp", scatter_dimension=1, tiled=True
    ).astype(jnp.float32)
    col_width = col_share.shape[1]
    col_begin = lax.axis_index("mp") * col_width
    residual_cols = (
        lax.dynamic_slice_in_dim(features, col_begin, col_width, 1).astype(jnp.float32) + col_share
    )
    gain_cols = lax.dynamic_slice_in_dim(gain_mlp, col_begin, col_width, 0)
    square_sum = lax.psum(jnp.sum(residual_cols * residual_cols, axis=1), "mp")
    inverse_rms = lax.rsqrt(square_sum / D + 1e-05)
    normed_cols = (residual_cols * inverse_rms[:, None] * gain_cols).astype(jnp.bfloat16)
    normed2 = lax.all_gather(normed_cols, "mp", axis=1, tiled=True)
    hidden = jax.nn.gelu(
        jnp.dot(normed2, w_up, preferred_element_type=jnp.float32), approximate=True
    ).astype(jnp.bfloat16)
    down_term = jnp.dot(hidden, w_down, preferred_element_type=jnp.float32)
    down_cols = lax.psum_scatter(
        down_term.astype(jnp.bfloat16), "mp", scatter_dimension=1, tiled=True
    ).astype(jnp.float32)
    return (residual_cols + down_cols).astype(jnp.bfloat16)


def solution(mesh):
    return jax.shard_map(
        per_device,
        mesh=mesh,
        in_specs=(
            P("patch", None),
            P(),
            P(None, None, "mp"),
            P("mp", None),
            P(),
            P(None, "mp"),
            P("mp", None),
            P(),
        ),
        out_specs=P("patch", "mp"),
        check_vma=False,
    )
```

profile of v0, /device:TPU:8, one launch (start us, length us, event | category | flops | bytes accessed | tf_op | source)
XLA Modules:
  0.0 209.8 jit_solution(8594160232992480794)
XLA Ops:
  6.6 1.7 fusion.9
  8.2 1.9 convolution_convert_fusion.2
  10.1 3.5 %collective-permute-start.4 = (bf16[4,128,256]{2,1,0:T(8,128)(2,1)S(1)}, bf16[4,128,256]{2,1,0:T(8,128)(2,1)}, u32[]{:S(2)}, u32[]{:S(2)}) collective-permute-start(bf16[4,128,256]{2,1,0:T(8,128)(2,1)S(1)} %bitcast.30), channel_id=1, source_target_pairs={{0,8},{4,12},{8,16},{12,20},{16,24},{20,28},{24,32},{28,36},{32,40... | collective-permute-start | bytes 786440 | tf_op jit(solution)/shard_map/ppermute | solution.py:15
  13.6 1.9 collective-permute-start.5
  15.5 3.6 %collective-permute-start.6 = (bf16[4,128,256]{2,1,0:T(8,128)(2,1)S(1)}, bf16[4,128,256]{2,1,0:T(8,128)(2,1)S(1)}, u32[]{:S(2)}, u32[]{:S(2)}) collective-permute-start(bf16[4,128,256]{2,1,0:T(8,128)(2,1)S(1)} %bitcast.32), channel_id=1, source_target_pairs={{0,508},{4,0},{8,4},{12,8},{16,12},{20,16},{24,20},{28,24},{32,28}... | collective-permute-start | bytes 786440 | tf_op jit(solution)/shard_map/ppermute | solution.py:15
  19.2 10.4 %collective-permute-start.7 = (bf16[4,128,256]{2,1,0:T(8,128)(2,1)S(1)}, bf16[4,128,256]{2,1,0:T(8,128)(2,1)S(1)}, u32[]{:S(2)}, u32[]{:S(2)}) collective-permute-start(bf16[4,128,256]{2,1,0:T(8,128)(2,1)S(1)} %bitcast.33), channel_id=1, source_target_pairs={{0,504},{4,508},{8,0},{12,4},{16,8},{20,12},{24,16},{28,20},{32,24... | collective-permute-start | bytes 786440 | tf_op jit(solution)/shard_map/ppermute | solution.py:15
  29.7 0.5 convolution_convert_fusion.4
  30.1 1.9 collective-permute-start
  32.1 0.5 convolution_convert_fusion.3
  32.6 0.8 compare_select_fusion
  33.4 0.1 copy.17
  33.5 0.1 reshape.39
  33.5 1.0 reshape.60
  34.6 1.9 collective-permute-start.1
  36.5 1.7 constant_dynamic-update-slice_fusion.9
  38.2 3.6 %collective-permute-start.2 = (bf16[4,128,256]{2,1,0:T(8,128)(2,1)S(1)}, bf16[4,128,256]{2,1,0:T(8,128)(2,1)}, u32[]{:S(2)}, u32[]{:S(2)}) collective-permute-start(bf16[4,128,256]{2,1,0:T(8,128)(2,1)S(1)} %bitcast.27), channel_id=1, source_target_pairs={{0,508},{4,0},{8,4},{12,8},{16,12},{20,16},{24,20},{28,24},{32,28}... | collective-permute-start | bytes 786440 | tf_op jit(solution)/shard_map/ppermute | solution.py:15
  41.8 1.7 constant_dynamic-update-slice_fusion.8
  43.5 0.7 constant_dynamic-update-slice_fusion.7
  44.2 7.5 %collective-permute-start.3 = (bf16[4,128,256]{2,1,0:T(8,128)(2,1)S(1)}, bf16[4,128,256]{2,1,0:T(8,128)(2,1)}, u32[]{:S(2)}, u32[]{:S(2)}) collective-permute-start(bf16[4,128,256]{2,1,0:T(8,128)(2,1)S(1)} %bitcast.28), channel_id=1, source_target_pairs={{0,504},{4,508},{8,0},{12,4},{16,8},{20,12},{24,16},{28,20},{32,24... | collective-permute-start | bytes 786440 | tf_op jit(solution)/shard_map/ppermute | solution.py:15
  51.7 0.7 constant_dynamic-update-slice_fusion.6
  52.5 0.7 constant_dynamic-update-slice_fusion.5
  53.2 2.0 gather_fusion.1
  55.2 3.2 %reshape.61 = bf16[4,1024,4,64]{3,2,1,0:T(4,128)(2,1)} reshape(bf16[32,128,256]{2,1,0:T(8,128)(2,1)S(1)} %gather_fusion.1) | data formatting | bytes 4194304 | tf_op jit(solution)/shard_map/reshape | solution.py:52
  58.4 3.6 %fusion.4 = f32[4,4,128,1024]{3,2,1,0:T(8,128)S(1)} fusion(bf16[4,1024,4,64]{3,2,1,0:T(4,128)(2,1)} %reshape.61, bf16[4,128,4,64]{3,2,1,0:T(4,128)(2,1)} %reshape.60), kind=kOutput, calls=%fused_computation.7 | convolution fusion | flops 268435456 | bytes 10747904 | tf_op jit(solution)/shard_map/pqhd,pkhd->phqk/dot_general | solution.py:55
  62.1 2.2 %fusion.62 = f32[4,4,128]{2,1,0:T(4,128)S(1)} fusion(f32[4,4,128,1024]{3,2,1,0:T(8,128)S(1)} %fusion.4), kind=kOutput, calls=%fused_computation.87 | output fusion | flops 8389631 | bytes 8396800 | tf_op jit(solution)/shard_map/sub | solution.py:58
  64.2 1.0 copy-done.1
  65.3 1.7 constant_dynamic-update-slice_fusion.4
  67.0 1.7 constant_dynamic-update-slice_fusion.3
  68.6 0.7 constant_dynamic-update-slice_fusion.2
  69.4 1.7 constant_dynamic-update-slice_fusion.1
  71.1 1.7 constant_dynamic-update-slice_fusion
  72.7 2.0 gather_fusion
  74.7 3.3 %reshape.59 = bf16[4,1024,4,64]{3,2,1,0:T(4,128)(2,1)} reshape(bf16[32,128,256]{2,1,0:T(8,128)(2,1)S(1)} %gather_fusion) | data formatting | bytes 4194304 | tf_op jit(solution)/shard_map/reshape | solution.py:53
  78.0 12.1 %fusion.15 = bf16[4,128,4,64]{1,3,2,0:T(8,128)(2,1)S(1)} fusion(f32[4,4,128]{2,1,0:T(4,128)S(1)} %fusion.62, bf16[4,1024,4,64]{3,2,1,0:T(4,128)(2,1)} %reshape.59, f32[4,4,128,1024]{3,2,1,0:T(8,128)} %copy-done.1), kind=kOutput, calls=%fused_computation.24 | convolution fusion | flops 279055360 | bytes 10756096 | tf_op jit(solution)/shard_map/phqk,pkhd->pqhd/dot_general | solution.py:59
  90.2 0.2 copy.24
  90.4 1.4 convolution_convert_fusion
  91.8 0.0 reduce-scatter.3.cloned.1.call-update
  91.8 0.0 all-gather.2.cloned.1.call-start
  91.9 0.8 dynamic_slice.11
  92.7 28.3 %reduce-scatter.3.cloned.1.call-done = bf16[512,256]{1,0:T(8,128)(2,1)} async-done(((bf16[512,1024]{1,0:T(8,128)(2,1)}), bf16[512,256]{1,0:T(8,128)(2,1)}) %reduce-scatter.3.cloned.1.call-update) | async-done | bytes 262160 | tf_op jit(solution)/shard_map/reduce_scatter | solution.py:62
  121.1 1.1 multiply_reduce_fusion.1
  122.2 8.4 %psum.7 = f32[512]{0:T(512)S(1)} all-reduce(f32[512]{0:T(512)S(1)} %multiply_reduce_fusion.1), channel_id=1, replica_groups=mesh['patch'=128,'mp'=4] {'mp'}, use_global_device_ids=true, to_apply=%region_5.6 | all-reduce | flops 512 | bytes 4096 | tf_op jit(solution)/shard_map/psum | solution.py:71
  130.6 1.8 multiply_convert_fusion
  132.4 0.0 reduce-scatter.5.cloned.1.call-start
  132.4 32.9 %all-gather.2.cloned.1.call-done = bf16[512,1024]{1,0:T(8,128)(2,1)} async-done(((bf16[512,256]{1,0:T(8,128)(2,1)}), bf16[512,1024]{1,0:T(8,128)(2,1)}) %all-gather.2.cloned.1.call-update) | async-done | bytes 1048592 | tf_op jit(solution)/shard_map/all_gather | solution.py:74
  165.3 3.6 %convolution_convert_fusion.1 = bf16[512,1024]{1,0:T(8,128)(2,1)} fusion(bf16[512,1024]{1,0:T(8,128)(2,1)S(1)} %copy-done, bf16[512,1024]{1,0:T(8,128)(2,1)} %all-gather.2.cloned.1.call-done, bf16[1024,512]{1,0:T(8,128)(2,1)S(1)} %copy-done.7), kind=kOutput, calls=%fused_computation.19 | convolution fusion | flops 1076625408 | bytes 4194304 | tf_op jit(solution)/shard_map/dot_general | solution.py:78
  168.9 32.6 %reduce-scatter.5.cloned.1.call-done = bf16[512,256]{1,0:T(8,128)(2,1)} async-done(((bf16[512,1024]{1,0:T(8,128)(2,1)}), bf16[512,256]{1,0:T(8,128)(2,1)}) %reduce-scatter.5.cloned.1.call-update) | async-done | bytes 262160 | tf_op jit(solution)/shard_map/reduce_scatter | solution.py:79
  201.5 1.8 add_convert_fusion
  (31 shorter events, 0.1 us)
Async XLA Ops:
  6.5 158.8 %copy-start = (bf16[512,1024]{1,0:T(8,128)(2,1)S(1)}, bf16[512,1024]{1,0:T(8,128)(2,1)}, u32[]{:S(2)}) copy-start(bf16[512,1024]{1,0:T(8,128)(2,1)} %param.14) | copy-start | bytes 3145732
  6.5 23.1 %copy-start.2 = (bf16[512,1024]{1,0:T(8,128)(2,1)S(1)}, bf16[512,1024]{1,0:T(8,128)(2,1)}, u32[]{:S(2)}) copy-start(bf16[512,1024]{1,0:T(8,128)(2,1)} %param.8) | copy-start | bytes 3145732
  6.5 23.1 %copy-start.8 = (f32[1024]{0:T(1024)S(1)}, f32[1024]{0:T(1024)}, u32[]{:S(2)}) copy-start(f32[1024]{0:T(1024)} %param.9) | copy-start | bytes 12292
  6.5 114.5 %reduce-scatter.3.cloned.1.call-start = ((), (), s32[]{:S(2)}) async-start(), calls=%async_computation.2 | async-start | bytes 1310720 | tf_op jit(solution)/shard_map/reduce_scatter | solution.py:62
  6.5 23.1 %copy-start.6 = (bf16[3,1024,256]{2,1,0:T(8,128)(2,1)S(1)}, bf16[3,1024,256]{2,1,0:T(8,128)(2,1)}, u32[]{:S(2)}) copy-start(bf16[3,1024,256]{2,1,0:T(8,128)(2,1)} %param.10) | copy-start | bytes 4718596
  10.1 24.5 %collective-permute-start.4 = (bf16[4,128,256]{2,1,0:T(8,128)(2,1)S(1)}, bf16[4,128,256]{2,1,0:T(8,128)(2,1)}, u32[]{:S(2)}, u32[]{:S(2)}) collective-permute-start(bf16[4,128,256]{2,1,0:T(8,128)(2,1)S(1)} %bitcast.30), channel_id=1, source_target_pairs={{0,8},{4,12},{8,16},{12,20},{16,24},{20,28},{24,32},{28,36},{32,40... | collective-permute-start | bytes 786440 | tf_op jit(solution)/shard_map/ppermute | solution.py:15
  13.6 24.6 %collective-permute-start.5 = (bf16[4,128,256]{2,1,0:T(8,128)(2,1)S(1)}, bf16[4,128,256]{2,1,0:T(8,128)(2,1)}, u32[]{:S(2)}, u32[]{:S(2)}) collective-permute-start(bf16[4,128,256]{2,1,0:T(8,128)(2,1)S(1)} %bitcast.31), channel_id=1, source_target_pairs={{0,4},{4,8},{8,12},{12,16},{16,20},{20,24},{24,28},{28,32},{32,36}... | collective-permute-start | bytes 786440 | tf_op jit(solution)/shard_map/ppermute | solution.py:15
  15.5 28.7 %collective-permute-start.6 = (bf16[4,128,256]{2,1,0:T(8,128)(2,1)S(1)}, bf16[4,128,256]{2,1,0:T(8,128)(2,1)S(1)}, u32[]{:S(2)}, u32[]{:S(2)}) collective-permute-start(bf16[4,128,256]{2,1,0:T(8,128)(2,1)S(1)} %bitcast.32), channel_id=1, source_target_pairs={{0,508},{4,0},{8,4},{12,8},{16,12},{20,16},{24,20},{28,24},{32,28}... | collective-permute-start | bytes 786440 | tf_op jit(solution)/shard_map/ppermute | solution.py:15
  19.2 33.3 %collective-permute-start.7 = (bf16[4,128,256]{2,1,0:T(8,128)(2,1)S(1)}, bf16[4,128,256]{2,1,0:T(8,128)(2,1)S(1)}, u32[]{:S(2)}, u32[]{:S(2)}) collective-permute-start(bf16[4,128,256]{2,1,0:T(8,128)(2,1)S(1)} %bitcast.33), channel_id=1, source_target_pairs={{0,504},{4,508},{8,0},{12,4},{16,8},{20,12},{24,16},{28,20},{32,24... | collective-permute-start | bytes 786440 | tf_op jit(solution)/shard_map/ppermute | solution.py:15
  30.1 35.1 %collective-permute-start = (bf16[4,128,256]{2,1,0:T(8,128)(2,1)S(1)}, bf16[4,128,256]{2,1,0:T(8,128)(2,1)}, u32[]{:S(2)}, u32[]{:S(2)}) collective-permute-start(bf16[4,128,256]{2,1,0:T(8,128)(2,1)S(1)} %bitcast.25), channel_id=1, source_target_pairs={{0,8},{4,12},{8,16},{12,20},{16,24},{20,28},{24,32},{28,36},{32,40... | collective-permute-start | bytes 786440 | tf_op jit(solution)/shard_map/ppermute | solution.py:15
  34.6 32.4 %collective-permute-start.1 = (bf16[4,128,256]{2,1,0:T(8,128)(2,1)S(1)}, bf16[4,128,256]{2,1,0:T(8,128)(2,1)}, u32[]{:S(2)}, u32[]{:S(2)}) collective-permute-start(bf16[4,128,256]{2,1,0:T(8,128)(2,1)S(1)} %bitcast.26), channel_id=1, source_target_pairs={{0,4},{4,8},{8,12},{12,16},{16,20},{20,24},{24,28},{28,32},{32,36}... | collective-permute-start | bytes 786440 | tf_op jit(solution)/shard_map/ppermute | solution.py:15
  38.2 31.2 %collective-permute-start.2 = (bf16[4,128,256]{2,1,0:T(8,128)(2,1)S(1)}, bf16[4,128,256]{2,1,0:T(8,128)(2,1)}, u32[]{:S(2)}, u32[]{:S(2)}) collective-permute-start(bf16[4,128,256]{2,1,0:T(8,128)(2,1)S(1)} %bitcast.27), channel_id=1, source_target_pairs={{0,508},{4,0},{8,4},{12,8},{16,12},{20,16},{24,20},{28,24},{32,28}... | collective-permute-start | bytes 786440 | tf_op jit(solution)/shard_map/ppermute | solution.py:15
  44.2 26.9 %collective-permute-start.3 = (bf16[4,128,256]{2,1,0:T(8,128)(2,1)S(1)}, bf16[4,128,256]{2,1,0:T(8,128)(2,1)}, u32[]{:S(2)}, u32[]{:S(2)}) collective-permute-start(bf16[4,128,256]{2,1,0:T(8,128)(2,1)S(1)} %bitcast.28), channel_id=1, source_target_pairs={{0,504},{4,508},{8,0},{12,4},{16,8},{20,12},{24,16},{28,20},{32,24... | collective-permute-start | bytes 786440 | tf_op jit(solution)/shard_map/ppermute | solution.py:15
  62.0 3.2 %copy-start.1 = (f32[4,4,128,1024]{3,2,1,0:T(8,128)}, f32[4,4,128,1024]{3,2,1,0:T(8,128)S(1)}, u32[]{:S(2)}) copy-start(f32[4,4,128,1024]{3,2,1,0:T(8,128)S(1)} %fusion.4) | copy-start | bytes 25165828
  78.0 12.4 %copy-start.5 = (bf16[256,1024]{1,0:T(8,128)(2,1)S(1)}, bf16[256,1024]{1,0:T(8,128)(2,1)}, u32[]{:S(2)}) copy-start(bf16[256,1024]{1,0:T(8,128)(2,1)} %param.11) | copy-start | bytes 1572868
  90.1 30.9 %copy-start.3 = (bf16[512,1024]{1,0:T(8,128)(2,1)S(1)}, bf16[512,1024]{1,0:T(8,128)(2,1)}, u32[]{:S(2)}) copy-start(bf16[512,1024]{1,0:T(8,128)(2,1)} %param.8) | copy-start | bytes 3145732
  91.8 73.5 %copy-start.7 = (bf16[1024,512]{1,0:T(8,128)(2,1)S(1)}, bf16[1024,512]{1,0:T(8,128)(2,1)}, u32[]{:S(2)}) copy-start(bf16[1024,512]{1,0:T(8,128)(2,1)} %param.13) | copy-start | bytes 3145732
  91.8 73.5 %all-gather.2.cloned.1.call-start = ((), (), s32[]{:S(2)}) async-start(), calls=%async_computation.3 | async-start | bytes 1310720 | tf_op jit(solution)/shard_map/all_gather | solution.py:74
  132.4 69.1 %copy-start.4 = (bf16[512,256]{1,0:T(8,128)(2,1)S(1)}, bf16[512,256]{1,0:T(8,128)(2,1)}, u32[]{:S(2)}) copy-start(bf16[512,256]{1,0:T(8,128)(2,1)} %reduce-scatter.3.cloned.1.call-done) | copy-start | bytes 786436
  132.4 69.1 %reduce-scatter.5.cloned.1.call-start = ((), (), s32[]{:S(2)}) async-start(), calls=%async_computation.4 | async-start | bytes 1310720 | tf_op jit(solution)/shard_map/reduce_scatter | solution.py:79
Sparse Core Ops, SparseCore 0:
  92.0 29.0 reduce-scatter.2
  132.5 32.8 all-gather.1
  169.1 32.3 reduce-scatter.4
where the time goes:
time: 211 us; the launch traced here: 210 us
  waiting for transfers between devices  93.9 us (45%)
  starting transfers between devices  34.6 us (16%)
  local copies, waits for them, and re-layouts  26.8 us (13%)
  matrix products  23.6 us (11%)
  between operations  13.3 us (6%)
  other arithmetic  9.3 us (4%)
  blocking collectives  8.37 us (4%)
    ppermute x8, starting transfers between devices, from_behind(): lax.ppermute(array, axis, [(i, (i + by) % length) for i in range(length)])  34.5 us
    all_gather x1, waiting for transfers between devices, per_device(): normed2 = lax.all_gather(normed_cols, 'mp', axis=1, tiled=True)  32.9 us
    reduce_scatter x1, waiting for transfers between devices, per_device(): lax.psum_scatter(down_term.astype(jnp.bfloat16), 'mp', scatter_dimension=...  32.6 us
    reduce_scatter x1, waiting for transfers between devices, per_device(): lax.psum_scatter(partial_value.astype(jnp.bfloat16), 'mp', scatter_dimens...  28.3 us
    dot_general x1, matrix products, per_device(): jnp.einsum('phqk,pkhd->pqhd', probs, vals_nb, preferred_element_type=jnp....  12.1 us
    unnamed x26, local copies, waits for them, and re-layouts  11.6 us
    psum x1, blocking collectives, per_device(): square_sum = lax.psum(jnp.sum(residual_cols * residual_cols, axis=1), 'mp')  8.37 us
  transfers between devices with their start and end apart: 11, of which 3 were waited for; matrix products, arithmetic and copies ran while one was open for 12% of the time, Pallas kernels for 0%

commit v1 on v0

--- a/solution.py
+++ b/solution.py
@@ -13,6 +13,29 @@
 def from_behind(array, axis, by):
     length = lax.axis_size(axis)
     return lax.ppermute(array, axis, [(i, (i + by) % length) for i in range(length)])
+
+
+def scatter_sum(parts, n_mp):
+    rows, cols = parts.shape
+    got = lax.all_to_all(parts.reshape(rows, n_mp, cols // n_mp), "mp", 1, 1)
+    total = got[:, 0].astype(jnp.float32)
+    for which in range(1, n_mp):
+        total = total + got[:, which].astype(jnp.float32)
+    return total
+
+
+def gather_sum(vector, n_mp):
+    got = lax.all_to_all(jnp.broadcast_to(vector[None], (n_mp,) + vector.shape), "mp", 0, 0)
+    total = got[0]
+    for which in range(1, n_mp):
+        total = total + got[which]
+    return total
+
+
+def gather_cols(block, n_mp):
+    rows, cols = block.shape
+    spread = jnp.broadcast_to(block[:, None], (rows, n_mp, cols))
+    return lax.all_to_all(spread, "mp", 1, 1).reshape(rows, n_mp * cols)
 
 
 def normalize(rows, gain):
@@ -58,27 +81,24 @@
     probs = jax.nn.softmax(scores, axis=-1).astype(jnp.bfloat16)
     mixed_rows = jnp.einsum("phqk,pkhd->pqhd", probs, vals_nb, preferred_element_type=jnp.float32)
     attended = mixed_rows.astype(jnp.bfloat16).reshape(row_count, heads_here * HD)
+    n_mp = lax.axis_size("mp")
     partial_value = jnp.dot(attended, w_out, preferred_element_type=jnp.float32)
-    col_share = lax.psum_scatter(
-        partial_value.astype(jnp.bfloat16), "mp", scatter_dimension=1, tiled=True
-    ).astype(jnp.float32)
+    col_share = scatter_sum(partial_value.astype(jnp.bfloat16), n_mp)
     col_width = col_share.shape[1]
     col_begin = lax.axis_index("mp") * col_width
     residual_cols = (
         lax.dynamic_slice_in_dim(features, col_begin, col_width, 1).astype(jnp.float32) + col_share
     )
     gain_cols = lax.dynamic_slice_in_dim(gain_mlp, col_begin, col_width, 0)
-    square_sum = lax.psum(jnp.sum(residual_cols * residual_cols, axis=1), "mp")
+    square_sum = gather_sum(jnp.sum(residual_cols * residual_cols, axis=1), n_mp)
     inverse_rms = lax.rsqrt(square_sum / D + 1e-05)
     normed_cols = (residual_cols * inverse_rms[:, None] * gain_cols).astype(jnp.bfloat16)
-    normed2 = lax.all_gather(normed_cols, "mp", axis=1, tiled=True)
+    normed2 = gather_cols(normed_cols, n_mp)
     hidden = jax.nn.gelu(
         jnp.dot(normed2, w_up, preferred_element_type=jnp.float32), approximate=True
     ).astype(jnp.bfloat16)
     down_term = jnp.dot(hidden, w_down, preferred_element_type=jnp.float32)
-    down_cols = lax.psum_scatter(
-        down_term.astype(jnp.bfloat16), "mp", scatter_dimension=1, tiled=True
-    ).astype(jnp.float32)
+    down_cols = scatter_sum(down_term.astype(jnp.bfloat16), n_mp)
     return (residual_cols + down_cols).astype(jnp.bfloat16)
 
 

time: 211 us -> 146 us (0.69)
  the two profiles are of different devices: /device:TPU:8 before, /device:TPU:2 now
where the time goes in v1:
time: 146 us; the launch traced here: 145 us
  starting transfers between devices  45.6 us (31%)
  local copies, waits for them, and re-layouts  27.9 us (19%)
  blocking collectives  27.5 us (19%)
  matrix products  22 us (15%)
  waiting for transfers between devices  15.4 us (11%)
  other arithmetic  6.84 us (5%)
    ppermute x8, starting transfers between devices, from_behind(): lax.ppermute(array, axis, [(i, (i + by) % length) for i in range(length)])  36 us
    all_to_all x1, blocking collectives, gather_cols(): return lax.all_to_all(spread, 'mp', 1, 1).reshape(rows, n_mp * cols)  14.2 us
    all_to_all x1, blocking collectives, scatter_sum(): got = lax.all_to_all(parts.reshape(rows, n_mp, cols // n_mp), 'mp', 1, 1)  13.3 us
    all_to_all x1, waiting for transfers between devices, scatter_sum(): got = lax.all_to_all(parts.reshape(rows, n_mp, cols // n_mp), 'mp', 1, 1)  12.3 us
    dot_general x1, matrix products, per_device(): jnp.einsum('phqk,pkhd->pqhd', probs, vals_nb, preferred_element_type=jnp....  12.1 us
    unnamed x20, local copies, waits for them, and re-layouts  9.7 us
    all_to_all x1, starting transfers between devices, scatter_sum(): got = lax.all_to_all(parts.reshape(rows, n_mp, cols // n_mp), 'mp', 1, 1)  4.83 us
    all_to_all x1, starting transfers between devices, gather_sum(): lax.all_to_all(jnp.broadcast_to(vector[None], (n_mp,) + vector.shape), 'm...  4.68 us
  transfers between devices with their start and end apart: 10, of which 2 were waited for; matrix products, arithmetic and copies ran while one was open for 17% of the time, Pallas kernels for 0%

profile of v1, /device:TPU:2, one launch (start us, length us, event | category | flops | bytes accessed | tf_op | source)
XLA Modules:
  0.0 145.4 jit_solution(13814441974721888056)
XLA Ops:
  0.0 1.7 %fusion.9 = f32[512]{0:T(512)S(1)} fusion(bf16[512,1024]{1,0:T(8,128)(2,1)} %param.8), kind=kLoop, calls=%fused_computation.14 | loop fusion | flops 1572352 | bytes 1050624 | tf_op jit(solution)/shard_map/reduce_sum | solution.py:43
  1.7 1.9 %convolution_convert_fusion.2 = bf16[512,256]{1,0:T(8,128)(2,1)S(1)} fusion(bf16[3,1024,256]{2,1,0:T(8,128)(2,1)} %param.10, bf16[512,1024]{1,0:T(8,128)(2,1)} %param.8, f32[1024]{0:T(1024)} %param.9, f32[512]{0:T(512)S(1)} %add_rsqrt_fusion.1), kind=kOutput, calls=%fused_computation.20 | convolution fusion | flops 270663680 | bytes 1841152 | tf_op jit(solution)/shard_map/dot_general | solution.py:54
  3.6 3.5 %collective-permute-start.4 = (bf16[4,128,256]{2,1,0:T(8,128)(2,1)S(1)}, bf16[4,128,256]{2,1,0:T(8,128)(2,1)S(1)}, u32[]{:S(2)}, u32[]{:S(2)}) collective-permute-start(bf16[4,128,256]{2,1,0:T(8,128)(2,1)S(1)} %bitcast.52), channel_id=1, source_target_pairs={{0,8},{4,12},{8,16},{12,20},{16,24},{20,28},{24,32},{28,36},{32,40... | collective-permute-start | bytes 786440 | tf_op jit(solution)/shard_map/ppermute | solution.py:15
  7.1 1.9 %collective-permute-start.5 = (bf16[4,128,256]{2,1,0:T(8,128)(2,1)S(1)}, bf16[4,128,256]{2,1,0:T(8,128)(2,1)S(1)}, u32[]{:S(2)}, u32[]{:S(2)}) collective-permute-start(bf16[4,128,256]{2,1,0:T(8,128)(2,1)S(1)} %bitcast.53), channel_id=1, source_target_pairs={{0,4},{4,8},{8,12},{12,16},{16,20},{20,24},{24,28},{28,32},{32,36}... | collective-permute-start | bytes 786440 | tf_op jit(solution)/shard_map/ppermute | solution.py:15
  9.0 11.7 %collective-permute-start.6 = (bf16[4,128,256]{2,1,0:T(8,128)(2,1)S(1)}, bf16[4,128,256]{2,1,0:T(8,128)(2,1)S(1)}, u32[]{:S(2)}, u32[]{:S(2)}) collective-permute-start(bf16[4,128,256]{2,1,0:T(8,128)(2,1)S(1)} %bitcast.54), channel_id=1, source_target_pairs={{0,508},{4,0},{8,4},{12,8},{16,12},{20,16},{24,20},{28,24},{32,28}... | collective-permute-start | bytes 786440 | tf_op jit(solution)/shard_map/ppermute | solution.py:15
  20.7 4.2 %collective-permute-start.7 = (bf16[4,128,256]{2,1,0:T(8,128)(2,1)S(1)}, bf16[4,128,256]{2,1,0:T(8,128)(2,1)S(1)}, u32[]{:S(2)}, u32[]{:S(2)}) collective-permute-start(bf16[4,128,256]{2,1,0:T(8,128)(2,1)S(1)} %bitcast.55), channel_id=1, source_target_pairs={{0,504},{4,508},{8,0},{12,4},{16,8},{20,12},{24,16},{28,20},{32,24... | collective-permute-start | bytes 786440 | tf_op jit(solution)/shard_map/ppermute | solution.py:15
  25.0 0.5 convolution_convert_fusion.4
  25.5 1.9 %collective-permute-start = (bf16[4,128,256]{2,1,0:T(8,128)(2,1)S(1)}, bf16[4,128,256]{2,1,0:T(8,128)(2,1)}, u32[]{:S(2)}, u32[]{:S(2)}) collective-permute-start(bf16[4,128,256]{2,1,0:T(8,128)(2,1)S(1)} %bitcast.47), channel_id=1, source_target_pairs={{0,8},{4,12},{8,16},{12,20},{16,24},{20,28},{24,32},{28,36},{32,40... | collective-permute-start | bytes 786440 | tf_op jit(solution)/shard_map/ppermute | solution.py:15
  27.4 0.5 convolution_convert_fusion.3
  27.9 0.8 compare_select_fusion
  28.9 1.1 reshape.130
  29.9 1.9 %collective-permute-start.1 = (bf16[4,128,256]{2,1,0:T(8,128)(2,1)S(1)}, bf16[4,128,256]{2,1,0:T(8,128)(2,1)}, u32[]{:S(2)}, u32[]{:S(2)}) collective-permute-start(bf16[4,128,256]{2,1,0:T(8,128)(2,1)S(1)} %bitcast.48), channel_id=1, source_target_pairs={{0,4},{4,8},{8,12},{12,16},{16,20},{20,24},{24,28},{28,32},{32,36}... | collective-permute-start | bytes 786440 | tf_op jit(solution)/shard_map/ppermute | solution.py:15
  31.9 0.7 constant_dynamic-update-slice_fusion.9
  32.6 7.0 %collective-permute-start.2 = (bf16[4,128,256]{2,1,0:T(8,128)(2,1)S(1)}, bf16[4,128,256]{2,1,0:T(8,128)(2,1)}, u32[]{:S(2)}, u32[]{:S(2)}) collective-permute-start(bf16[4,128,256]{2,1,0:T(8,128)(2,1)S(1)} %bitcast.49), channel_id=1, source_target_pairs={{0,508},{4,0},{8,4},{12,8},{16,12},{20,16},{24,20},{28,24},{32,28}... | collective-permute-start | bytes 786440 | tf_op jit(solution)/shard_map/ppermute | solution.py:15
  39.5 0.7 constant_dynamic-update-slice_fusion.8
  40.3 0.7 constant_dynamic-update-slice_fusion.7
  41.0 3.9 %collective-permute-start.3 = (bf16[4,128,256]{2,1,0:T(8,128)(2,1)S(1)}, bf16[4,128,256]{2,1,0:T(8,128)(2,1)}, u32[]{:S(2)}, u32[]{:S(2)}) collective-permute-start(bf16[4,128,256]{2,1,0:T(8,128)(2,1)S(1)} %bitcast.50), channel_id=1, source_target_pairs={{0,504},{4,508},{8,0},{12,4},{16,8},{20,12},{24,16},{28,20},{32,24... | collective-permute-start | bytes 786440 | tf_op jit(solution)/shard_map/ppermute | solution.py:15
  44.9 0.7 constant_dynamic-update-slice_fusion.6
  45.6 0.7 constant_dynamic-update-slice_fusion.5
  46.3 2.0 %gather_fusion.1 = bf16[32,128,256]{2,1,0:T(8,128)(2,1)S(1)} fusion(bf16[20,128,256]{2,1,0:T(8,128)(2,1)} %constant_dynamic-update-slice_fusion.5, s32[1024]{0:T(1024)S(1)} %pad_clamp_fusion), kind=kCustom, calls=%fused_computation.1 | custom fusion | bytes 4194432 | tf_op jit(solution)/shard_map/gather | solution.py:75
  48.3 3.2 %reshape.131 = bf16[4,1024,4,64]{3,2,1,0:T(4,128)(2,1)} reshape(bf16[32,128,256]{2,1,0:T(8,128)(2,1)S(1)} %gather_fusion.1) | data formatting | bytes 4194304 | tf_op jit(solution)/shard_map/reshape | solution.py:75
  51.6 3.6 %fusion.4 = f32[4,4,128,1024]{3,2,1,0:T(8,128)S(1)} fusion(bf16[4,1024,4,64]{3,2,1,0:T(4,128)(2,1)} %reshape.131, bf16[4,128,4,64]{3,2,1,0:T(4,128)(2,1)} %reshape.130), kind=kOutput, calls=%fused_computation.7 | convolution fusion | flops 268435456 | bytes 10747904 | tf_op jit(solution)/shard_map/pqhd,pkhd->phqk/dot_general | solution.py:78
  55.2 2.2 %fusion.64 = f32[4,4,128]{2,1,0:T(4,128)S(1)} fusion(f32[4,4,128,1024]{3,2,1,0:T(8,128)S(1)} %fusion.4), kind=kOutput, calls=%fused_computation.94 | output fusion | flops 8389631 | bytes 8396800 | tf_op jit(solution)/shard_map/sub | solution.py:81
  57.4 1.0 copy-done.1
  58.4 1.7 %constant_dynamic-update-slice_fusion.4 = bf16[20,128,256]{2,1,0:T(8,128)(2,1)} fusion(bf16[4,128,256]{2,1,0:T(8,128)(2,1)} %collective-permute-done), kind=kLoop, calls=%fused_computation.57 | loop fusion | bytes 524288
  60.1 1.7 %constant_dynamic-update-slice_fusion.3 = bf16[20,128,256]{2,1,0:T(8,128)(2,1)} fusion(bf16[20,128,256]{2,1,0:T(8,128)(2,1)} %constant_dynamic-update-slice_fusion.4, bf16[4,128,256]{2,1,0:T(8,128)(2,1)} %collective-permute-done.1), kind=kLoop, calls=%fused_computation.56 | loop fusion | bytes 524288
  61.8 0.7 constant_dynamic-update-slice_fusion.2
  62.5 1.7 %constant_dynamic-update-slice_fusion.1 = bf16[20,128,256]{2,1,0:T(8,128)(2,1)} fusion(bf16[20,128,256]{2,1,0:T(8,128)(2,1)} %constant_dynamic-update-slice_fusion.2, bf16[4,128,256]{2,1,0:T(8,128)(2,1)} %collective-permute-done.2), kind=kLoop, calls=%fused_computation.54 | loop fusion | bytes 524288
  64.2 1.7 %constant_dynamic-update-slice_fusion = bf16[20,128,256]{2,1,0:T(8,128)(2,1)} fusion(bf16[20,128,256]{2,1,0:T(8,128)(2,1)} %constant_dynamic-update-slice_fusion.1, bf16[4,128,256]{2,1,0:T(8,128)(2,1)} %collective-permute-done.3), kind=kLoop, calls=%fused_computation.53 | loop fusion | bytes 524288 | tf_op jit(solution)/shard_map/concatenate | solution.py:68
  65.9 2.0 %gather_fusion = bf16[32,128,256]{2,1,0:T(8,128)(2,1)S(1)} fusion(bf16[20,128,256]{2,1,0:T(8,128)(2,1)} %constant_dynamic-update-slice_fusion, s32[1024]{0:T(1024)S(1)} %pad_clamp_fusion), kind=kCustom, calls=%fused_computation | custom fusion | bytes 4194432 | tf_op jit(solution)/shard_map/gather | solution.py:76
  67.9 3.3 %reshape.129 = bf16[4,1024,4,64]{3,2,1,0:T(4,128)(2,1)} reshape(bf16[32,128,256]{2,1,0:T(8,128)(2,1)S(1)} %gather_fusion) | data formatting | bytes 4194304 | tf_op jit(solution)/shard_map/reshape | solution.py:76
  71.2 12.1 %fusion.15 = bf16[4,128,4,64]{1,3,2,0:T(8,128)(2,1)S(1)} fusion(f32[4,4,128]{2,1,0:T(4,128)S(1)} %fusion.64, bf16[4,1024,4,64]{3,2,1,0:T(4,128)(2,1)} %reshape.129, f32[4,4,128,1024]{3,2,1,0:T(8,128)} %copy-done.1), kind=kOutput, calls=%fused_computation.24 | convolution fusion | flops 279055360 | bytes 10756096 | tf_op jit(solution)/shard_map/phqk,pkhd->pqhd/dot_general | solution.py:82
  83.3 0.2 copy.48
  83.5 0.5 convolution_convert_fusion
  84.0 1.0 copy.78
  85.0 4.8 %all-to-all-start = ((bf16[512,4,256]{2,0,1:T(8,128)(2,1)}), bf16[512,4,256]{2,0,1:T(8,128)(2,1)S(1)}, u32[]{:S(2)}, u32[]{:S(2)}) async-start(bf16[512,4,256]{2,0,1:T(8,128)(2,1)} %bitcast.42), calls=%async_computation | async-start | bytes 2097152 | tf_op jit(solution)/shard_map/all_to_all | solution.py:20
  89.8 12.3 %all-to-all-done = bf16[512,4,256]{2,0,1:T(8,128)(2,1)S(1)} async-done(((bf16[512,4,256]{2,0,1:T(8,128)(2,1)}), bf16[512,4,256]{2,0,1:T(8,128)(2,1)S(1)}, u32[]{:S(2)}, u32[]{:S(2)}) %all-to-all-start) | async-done | bytes 1048608 | tf_op jit(solution)/shard_map/all_to_all | solution.py:20
  102.1 1.2 multiply_reduce_fusion.1
  103.3 0.6 broadcast_in_dim.7
  104.0 4.7 %all-to-all-start.1 = ((f32[4,1,512]{2,1,0:T(1,128)}), f32[4,1,512]{2,1,0:T(1,128)S(1)}, u32[]{:S(2)}, u32[]{:S(2)}) async-start(f32[4,1,512]{2,1,0:T(1,128)} %broadcast_in_dim.7), calls=%async_computation.1 | async-start | bytes 16384 | tf_op jit(solution)/shard_map/all_to_all | solution.py:28
  108.6 0.8 dynamic_slice.11
  109.4 3.1 %all-to-all-done.1 = f32[4,1,512]{2,1,0:T(1,128)S(1)} async-done(((f32[4,1,512]{2,1,0:T(1,128)}), f32[4,1,512]{2,1,0:T(1,128)S(1)}, u32[]{:S(2)}, u32[]{:S(2)}) %all-to-all-start.1) | async-done | bytes 8224 | tf_op jit(solution)/shard_map/all_to_all | solution.py:28
  112.5 0.1 multiply_convert_fusion
  112.7 14.2 %all_to_all.21 = bf16[512,4,256]{2,0,1:T(8,128)(2,1)S(1)} all-to-all(bf16[512,4,256]{2,0,1:T(8,128)(2,1)S(1)} %broadcast_in_dim.8), channel_id=1, replica_groups=mesh['patch'=128,'mp'=4] {'mp'}, dimensions={1} | all-to-all | bytes 2097152 | tf_op jit(solution)/shard_map/all_to_all | solution.py:38
  126.9 1.3 copy.50
  128.2 2.9 %convolution_convert_fusion.1 = bf16[512,1024]{1,0:T(8,128)(2,1)S(1)} fusion(bf16[512,1024]{1,0:T(8,128)(2,1)S(1)} %copy-done, bf16[512,1024]{0,1:T(8,128)(2,1)} %bitcast.45, bf16[1024,512]{1,0:T(8,128)(2,1)} %param.13), kind=kOutput, calls=%fused_computation.19 | convolution fusion | flops 1076625408 | bytes 4194304 | tf_op jit(solution)/shard_map/dot_general | solution.py:100
  131.2 13.3 %all_to_all.22 = bf16[512,4,256]{2,0,1:T(8,128)(2,1)S(1)} all-to-all(bf16[512,4,256]{2,0,1:T(8,128)(2,1)S(1)} %bitcast.43), channel_id=1, replica_groups=mesh['patch'=128,'mp'=4] {'mp'}, dimensions={1} | all-to-all | bytes 2097152 | tf_op jit(solution)/shard_map/all_to_all | solution.py:20
  144.6 0.8 fusion.27
  (26 shorter events, 0.4 us)
Async XLA Ops:
  0.0 128.2 %copy-start = (bf16[512,1024]{1,0:T(8,128)(2,1)S(1)}, bf16[512,1024]{1,0:T(8,128)(2,1)}, u32[]{:S(2)}) copy-start(bf16[512,1024]{1,0:T(8,128)(2,1)} %param.14) | copy-start | bytes 3145732
  0.0 24.9 %copy-start.2 = (bf16[512,1024]{1,0:T(8,128)(2,1)S(1)}, bf16[512,1024]{1,0:T(8,128)(2,1)}, u32[]{:S(2)}) copy-start(bf16[512,1024]{1,0:T(8,128)(2,1)} %param.8) | copy-start | bytes 3145732
  0.0 24.9 %copy-start.4 = (bf16[3,1024,256]{2,1,0:T(8,128)(2,1)S(1)}, bf16[3,1024,256]{2,1,0:T(8,128)(2,1)}, u32[]{:S(2)}) copy-start(bf16[3,1024,256]{2,1,0:T(8,128)(2,1)} %param.10) | copy-start | bytes 4718596
  0.0 24.9 %copy-start.5 = (f32[1024]{0:T(1024)S(1)}, f32[1024]{0:T(1024)}, u32[]{:S(2)}) copy-start(f32[1024]{0:T(1024)} %param.9) | copy-start | bytes 12292
  3.6 26.4 %collective-permute-start.4 = (bf16[4,128,256]{2,1,0:T(8,128)(2,1)S(1)}, bf16[4,128,256]{2,1,0:T(8,128)(2,1)S(1)}, u32[]{:S(2)}, u32[]{:S(2)}) collective-permute-start(bf16[4,128,256]{2,1,0:T(8,128)(2,1)S(1)} %bitcast.52), channel_id=1, source_target_pairs={{0,8},{4,12},{8,16},{12,20},{16,24},{20,28},{24,32},{28,36},{32,40... | collective-permute-start | bytes 786440 | tf_op jit(solution)/shard_map/ppermute | solution.py:15
  7.1 25.5 %collective-permute-start.5 = (bf16[4,128,256]{2,1,0:T(8,128)(2,1)S(1)}, bf16[4,128,256]{2,1,0:T(8,128)(2,1)S(1)}, u32[]{:S(2)}, u32[]{:S(2)}) collective-permute-start(bf16[4,128,256]{2,1,0:T(8,128)(2,1)S(1)} %bitcast.53), channel_id=1, source_target_pairs={{0,4},{4,8},{8,12},{12,16},{16,20},{20,24},{24,28},{28,32},{32,36}... | collective-permute-start | bytes 786440 | tf_op jit(solution)/shard_map/ppermute | solution.py:15
  9.0 32.0 %collective-permute-start.6 = (bf16[4,128,256]{2,1,0:T(8,128)(2,1)S(1)}, bf16[4,128,256]{2,1,0:T(8,128)(2,1)S(1)}, u32[]{:S(2)}, u32[]{:S(2)}) collective-permute-start(bf16[4,128,256]{2,1,0:T(8,128)(2,1)S(1)} %bitcast.54), channel_id=1, source_target_pairs={{0,508},{4,0},{8,4},{12,8},{16,12},{20,16},{24,20},{28,24},{32,28}... | collective-permute-start | bytes 786440 | tf_op jit(solution)/shard_map/ppermute | solution.py:15
  20.7 24.9 %collective-permute-start.7 = (bf16[4,128,256]{2,1,0:T(8,128)(2,1)S(1)}, bf16[4,128,256]{2,1,0:T(8,128)(2,1)S(1)}, u32[]{:S(2)}, u32[]{:S(2)}) collective-permute-start(bf16[4,128,256]{2,1,0:T(8,128)(2,1)S(1)} %bitcast.55), channel_id=1, source_target_pairs={{0,504},{4,508},{8,0},{12,4},{16,8},{20,12},{24,16},{28,20},{32,24... | collective-permute-start | bytes 786440 | tf_op jit(solution)/shard_map/ppermute | solution.py:15
  25.5 33.0 %collective-permute-start = (bf16[4,128,256]{2,1,0:T(8,128)(2,1)S(1)}, bf16[4,128,256]{2,1,0:T(8,128)(2,1)}, u32[]{:S(2)}, u32[]{:S(2)}) collective-permute-start(bf16[4,128,256]{2,1,0:T(8,128)(2,1)S(1)} %bitcast.47), channel_id=1, source_target_pairs={{0,8},{4,12},{8,16},{12,20},{16,24},{20,28},{24,32},{28,36},{32,40... | collective-permute-start | bytes 786440 | tf_op jit(solution)/shard_map/ppermute | solution.py:15
  29.9 30.2 %collective-permute-start.1 = (bf16[4,128,256]{2,1,0:T(8,128)(2,1)S(1)}, bf16[4,128,256]{2,1,0:T(8,128)(2,1)}, u32[]{:S(2)}, u32[]{:S(2)}) collective-permute-start(bf16[4,128,256]{2,1,0:T(8,128)(2,1)S(1)} %bitcast.48), channel_id=1, source_target_pairs={{0,4},{4,8},{8,12},{12,16},{16,20},{20,24},{24,28},{28,32},{32,36}... | collective-permute-start | bytes 786440 | tf_op jit(solution)/shard_map/ppermute | solution.py:15
  32.6 30.0 %collective-permute-start.2 = (bf16[4,128,256]{2,1,0:T(8,128)(2,1)S(1)}, bf16[4,128,256]{2,1,0:T(8,128)(2,1)}, u32[]{:S(2)}, u32[]{:S(2)}) collective-permute-start(bf16[4,128,256]{2,1,0:T(8,128)(2,1)S(1)} %bitcast.49), channel_id=1, source_target_pairs={{0,508},{4,0},{8,4},{12,8},{16,12},{20,16},{24,20},{28,24},{32,28}... | collective-permute-start | bytes 786440 | tf_op jit(solution)/shard_map/ppermute | solution.py:15
  41.0 23.2 %collective-permute-start.3 = (bf16[4,128,256]{2,1,0:T(8,128)(2,1)S(1)}, bf16[4,128,256]{2,1,0:T(8,128)(2,1)}, u32[]{:S(2)}, u32[]{:S(2)}) collective-permute-start(bf16[4,128,256]{2,1,0:T(8,128)(2,1)S(1)} %bitcast.50), channel_id=1, source_target_pairs={{0,504},{4,508},{8,0},{12,4},{16,8},{20,12},{24,16},{28,20},{32,24... | collective-permute-start | bytes 786440 | tf_op jit(solution)/shard_map/ppermute | solution.py:15
  55.2 3.2 %copy-start.1 = (f32[4,4,128,1024]{3,2,1,0:T(8,128)}, f32[4,4,128,1024]{3,2,1,0:T(8,128)S(1)}, u32[]{:S(2)}) copy-start(f32[4,4,128,1024]{3,2,1,0:T(8,128)S(1)} %fusion.4) | copy-start | bytes 25165828
  71.1 12.3 %copy-start.3 = (bf16[256,1024]{1,0:T(8,128)(2,1)S(1)}, bf16[256,1024]{1,0:T(8,128)(2,1)}, u32[]{:S(2)}) copy-start(bf16[256,1024]{1,0:T(8,128)(2,1)} %param.11) | copy-start | bytes 1572868
  85.0 17.1 %all-to-all-start = ((bf16[512,4,256]{2,0,1:T(8,128)(2,1)}), bf16[512,4,256]{2,0,1:T(8,128)(2,1)S(1)}, u32[]{:S(2)}, u32[]{:S(2)}) async-start(bf16[512,4,256]{2,0,1:T(8,128)(2,1)} %bitcast.42), calls=%async_computation | async-start | bytes 2097152 | tf_op jit(solution)/shard_map/all_to_all | solution.py:20
  104.0 8.5 %all-to-all-start.1 = ((f32[4,1,512]{2,1,0:T(1,128)}), f32[4,1,512]{2,1,0:T(1,128)S(1)}, u32[]{:S(2)}, u32[]{:S(2)}) async-start(f32[4,1,512]{2,1,0:T(1,128)} %broadcast_in_dim.7), calls=%async_computation.1 | async-start | bytes 16384 | tf_op jit(solution)/shard_map/all_to_all | solution.py:28

commit v2 on v1

--- a/solution.py
+++ b/solution.py
@@ -1,6 +1,9 @@
+import functools
+
 import jax
 import jax.numpy as jnp
 from jax import lax
+from jax.experimental import pallas as pl
 from jax.sharding import PartitionSpec as P
 
 D = 1024
@@ -13,6 +16,12 @@
 def from_behind(array, axis, by):
     length = lax.axis_size(axis)
     return lax.ppermute(array, axis, [(i, (i + by) % length) for i in range(length)])
+
+
+def normalize(rows, gain):
+    rows32 = rows.astype(jnp.float32)
+    mean_sq = jnp.mean(rows32 * rows32, axis=-1, keepdims=True)
+    return (rows32 * lax.rsqrt(mean_sq + 1e-05) * gain).astype(jnp.bfloat16)
 
 
 def scatter_sum(parts, n_mp):
@@ -38,49 +47,82 @@
     return lax.all_to_all(spread, "mp", 1, 1).reshape(rows, n_mp * cols)
 
 
-def normalize(rows, gain):
-    rows32 = rows.astype(jnp.float32)
-    mean_sq = jnp.mean(rows32 * rows32, axis=-1, keepdims=True)
-    return (rows32 * lax.rsqrt(mean_sq + 1e-05) * gain).astype(jnp.bfloat16)
+def window_attention(query_ref, bias_ref, *refs, n_heads, n_win):
+    kv_refs, out_ref = refs[:n_win], refs[n_win]
+    width = n_heads * HD
+    win_rows = kv_refs[0].shape[0]
+    bias = bias_ref[0]
+    lane = lax.broadcasted_iota(jnp.int32, (PN, 2 * HD), 1)
+    for pair in range(n_heads // 2):
+        cols = slice(pair * 2 * HD, (pair + 1) * 2 * HD)
+        q_pair = query_ref[:, cols]
+        mixed = []
+        for half in range(2):
+            keep = (lane >= half * HD) & (lane < (half + 1) * HD)
+            q_head = jnp.where(keep, q_pair, jnp.zeros_like(q_pair))
+            scores = []
+            for w in range(n_win):
+                s = lax.dot_general(
+                    q_head, kv_refs[w][:, cols], (((1,), (1,)), ((), ())),
+                    preferred_element_type=jnp.float32,
+                )
+                scores.append(s * (1.0 / HD**0.5) + bias[:, w * win_rows:(w + 1) * win_rows])
+            top = scores[0].max(axis=1, keepdims=True)
+            for s in scores[1:]:
+                top = jnp.maximum(top, s.max(axis=1, keepdims=True))
+            exps = [jnp.exp(s - top) for s in scores]
+            total = exps[0].sum(axis=1, keepdims=True)
+            for e in exps[1:]:
+                total = total + e.sum(axis=1, keepdims=True)
+            acc = None
+            for w in range(n_win):
+                probs = (exps[w] / total).astype(jnp.bfloat16)
+                v_cols = slice(width + pair * 2 * HD, width + (pair + 1) * 2 * HD)
+                term = jnp.dot(probs, kv_refs[w][:, v_cols], preferred_element_type=jnp.float32)
+                acc = term if acc is None else acc + term
+            mixed.append(acc)
+        out = jnp.where(lane < HD, mixed[0], mixed[1])
+        out_ref[:, cols] = out.astype(out_ref.dtype)
 
 
 def per_device(features, gain_attn, w_qkv, w_out, gain_mlp, w_up, w_down, neighbours):
     row_count = features.shape[0]
     patches_here = row_count // PN
-    heads_here = w_qkv.shape[2] // HD
+    width = w_qkv.shape[2]
+    heads_here = width // HD
+    n_win = 2 * REACH + 1
     normed = normalize(features, gain_attn)
-    queries = jnp.dot(normed, w_qkv[0], preferred_element_type=jnp.float32).astype(jnp.bfloat16)
-    own_keys = (
-        jnp.dot(normed, w_qkv[1], preferred_element_type=jnp.float32)
-        .astype(jnp.bfloat16)
-        .reshape(patches_here, PN, -1)
-    )
-    own_vals = (
-        jnp.dot(normed, w_qkv[2], preferred_element_type=jnp.float32)
-        .astype(jnp.bfloat16)
-        .reshape(patches_here, PN, -1)
-    )
-    window = {0: (own_keys, own_vals)}
+    w_all = jnp.concatenate([w_qkv[0], w_qkv[1], w_qkv[2]], axis=1)
+    qkv = jnp.dot(normed, w_all, preferred_element_type=jnp.float32).astype(jnp.bfloat16)
+    queries = qkv[:, :width]
+    own_kv = qkv[:, width:]
+    window = {0: own_kv}
     for offset in range(-REACH, REACH + 1):
         if offset != 0:
-            window[offset] = from_behind((own_keys, own_vals), "patch", -offset)
-    keys_win = jnp.concatenate([window[offset][0] for offset in range(-REACH, REACH + 1)], axis=0)
-    vals_win = jnp.concatenate([window[offset][1] for offset in range(-REACH, REACH + 1)], axis=0)
+            window[offset] = from_behind(own_kv, "patch", -offset)
     device = lax.axis_index("patch")
     n_dev = lax.axis_size("patch")
     listed = lax.dynamic_slice_in_dim(neighbours, device * patches_here, patches_here, 0)
     owner_dev = listed // patches_here
     offset_dev = jnp.mod(owner_dev - device + n_dev // 2, n_dev) - n_dev // 2
     slot_index = (offset_dev + REACH) * patches_here + jnp.mod(listed, patches_here)
-    keys_nb = keys_win[slot_index].reshape(patches_here, K_NB * PN, heads_here, HD)
-    vals_nb = vals_win[slot_index].reshape(patches_here, K_NB * PN, heads_here, HD)
-    query_blk = queries.reshape(patches_here, PN, heads_here, HD)
-    scores = jnp.einsum(
-        "pqhd,pkhd->phqk", query_blk, keys_nb, preferred_element_type=jnp.float32
-    ) * (1.0 / HD**0.5)
-    probs = jax.nn.softmax(scores, axis=-1).astype(jnp.bfloat16)
-    mixed_rows = jnp.einsum("phqk,pkhd->pqhd", probs, vals_nb, preferred_element_type=jnp.float32)
-    attended = mixed_rows.astype(jnp.bfloat16).reshape(row_count, heads_here * HD)
+    slots = jnp.arange(n_win * patches_here, dtype=jnp.int32)
+    chosen = jnp.any(slot_index[:, :, None] == slots[None, None, :], axis=1)
+    bias = jnp.where(chosen, 0.0, -jnp.inf).astype(jnp.float32)
+    bias = jnp.repeat(bias, PN, axis=1).reshape(patches_here, 1, n_win * patches_here * PN)
+    kv_list = [window[offset] for offset in range(-REACH, REACH + 1)]
+    kv_spec = pl.BlockSpec((row_count, 2 * width), lambda p: (0, 0))
+    attended = pl.pallas_call(
+        functools.partial(window_attention, n_heads=heads_here, n_win=n_win),
+        grid=(patches_here,),
+        in_specs=[
+            pl.BlockSpec((PN, width), lambda p: (p, 0)),
+            pl.BlockSpec((1, 1, n_win * row_count), lambda p: (p, 0, 0)),
+        ]
+        + [kv_spec] * n_win,
+        out_specs=pl.BlockSpec((PN, width), lambda p: (p, 0)),
+        out_shape=jax.ShapeDtypeStruct((row_count, width), jnp.bfloat16),
+    )(queries, bias, *kv_list)
     n_mp = lax.axis_size("mp")
     partial_value = jnp.dot(attended, w_out, preferred_element_type=jnp.float32)
     col_share = scatter_sum(partial_value.astype(jnp.bfloat16), n_mp)

time: 146 us -> 114 us (0.78)
  local copies, waits for them, and re-layouts: 27.9 us -> 7.24 us
  matrix products: 22 us -> 5.36 us
  Pallas kernels: 0 us -> 15.5 us
  starting transfers between devices: 45.6 us -> 30.8 us
  waiting for transfers between devices: 15.4 us -> 24.7 us
  other arithmetic: 6.84 us -> 3.37 us
    dot_general x5 -> x1, matrix products: 18.6 us -> 1.04 us  [per_device(): jnp.dot(normed, w_all, preferred_element_type=jnp.float32)]
    pallas_call x0 -> x1, Pallas kernels: none -> 15.5 us  [per_device(): pl.pallas_call(functools.partial(window_attention, n_heads=heads_here, n_...]
    ppermute x8 -> x4, starting transfers between devices: 36 us -> 21.3 us  [from_behind(): lax.ppermute(array, axis, [(i, (i + by) % length) for i in range(length)])]
    ppermute x8 -> x4, waiting for transfers between devices: 0.02 us -> 11.3 us  [from_behind(): lax.ppermute(array, axis, [(i, (i + by) % length) for i in range(length)])]
    unnamed x20 -> x14, local copies, waits for them, and re-layouts: 9.7 us -> 0.19 us
    reshape x3 -> x0, local copies, waits for them, and re-layouts: 7.58 us -> none  [the longest x1 3.27 us: per_device(): vals_win[slot_index].reshape(patches_here, K_NB * PN, heads_here, HD)]
    gather x2 -> x0, local copies, waits for them, and re-layouts: 3.99 us -> none  [the longest x1 2 us: per_device(): keys_win[slot_index].reshape(patches_here, K_NB * PN, heads_here, HD)]
    concatenate x2 -> x0, local copies, waits for them, and re-layouts: 2.38 us -> none  [the longest x1 1.66 us: per_device(): jnp.concatenate([window[offset][1] for offset in range(-REACH, REACH + 1)...]
  transfers between devices with their start and end apart: 10 -> 6, of which waited for: 2 -> 5; matrix products, arithmetic and copies ran while one was open for 17% -> 3% of each run, Pallas kernels for 0% -> 0%
where the time goes in v2:
time: 114 us
  starting transfers between devices  30.8 us (27%)
  blocking collectives  26.6 us (23%)
  waiting for transfers between devices  24.7 us (22%)
  Pallas kernels  15.5 us (14%)
  local copies, waits for them, and re-layouts  7.24 us (6%)
  matrix products  5.36 us (5%)
  other arithmetic  3.37 us (3%)
    ppermute x4, starting transfers between devices, from_behind(): lax.ppermute(array, axis, [(i, (i + by) % length) for i in range(length)])  21.3 us
    pallas_call x1, Pallas kernels, per_device(): pl.pallas_call(functools.partial(window_attention, n_heads=heads_here, n_...  15.5 us
    all_to_all x1, blocking collectives, gather_cols(): return lax.all_to_all(spread, 'mp', 1, 1).reshape(rows, n_mp * cols)  13.3 us
    all_to_all x1, blocking collectives, scatter_sum(): got = lax.all_to_all(parts.reshape(rows, n_mp, cols // n_mp), 'mp', 1, 1)  13.3 us
    ppermute x4, waiting for transfers between devices, from_behind(): lax.ppermute(array, axis, [(i, (i + by) % length) for i in range(length)])  11.3 us
    all_to_all x1, waiting for transfers between devices, scatter_sum(): got = lax.all_to_all(parts.reshape(rows, n_mp, cols // n_mp), 'mp', 1, 1)  10.3 us
    all_to_all x1, starting transfers between devices, scatter_sum(): got = lax.all_to_all(parts.reshape(rows, n_mp, cols // n_mp), 'mp', 1, 1)  4.82 us
    all_to_all x1, starting transfers between devices, gather_sum(): lax.all_to_all(jnp.broadcast_to(vector[None], (n_mp,) + vector.shape), 'm...  4.68 us
  transfers between devices with their start and end apart: 6, of which 5 were waited for; matrix products, arithmetic and copies ran while one was open for 3% of the time, Pallas kernels for 0%

profile of v2, /device:TPU:2, one launch (start us, length us, event | category | flops | bytes accessed | tf_op | source)
XLA Modules:
  0.0 113.8 jit_solution(4444758242800531931)
XLA Ops:
  0.0 0.0 copy-start
  0.0 0.0 copy-start.2
  0.0 0.0 copy-start.6
  0.0 1.6 %slice_bitcast_fusion.2 = (bf16[1024,256]{1,0:T(8,128)(2,1)S(1)}, bf16[1024,256]{1,0:T(8,128)(2,1)S(1)}, bf16[1024,256]{1,0:T(8,128)(2,1)S(1)}) fusion(bf16[3,1024,256]{2,1,0:T(8,128)(2,1)} %param.10), kind=kLoop, calls=%fused_computation.38 | loop fusion | bytes 3145728 | tf_op jit(solution)/shard_map/squeeze | solution.py:95
  1.6 0.2 copy-done.2
  1.8 0.3 fusion
  2.1 0.0 copy-done.6
  2.1 1.0 fusion.9
  3.2 0.0 copy-start.1
  3.2 3.5 %collective-permute-start = (bf16[512,512]{1,0:T(8,128)(2,1)S(1)}, bf16[512,512]{1,0:T(8,128)(2,1)S(1)}, u32[]{:S(2)}, u32[]{:S(2)}) collective-permute-start(bf16[512,512]{1,0:T(8,128)(2,1)S(1)} %slice.73.refs_2_), channel_id=1, source_target_pairs={{0,8},{4,12},{8,16},{12,20},{16,24},{20,28},{24,32},{28,36},{32,40... | collective-permute-start | bytes 1572872 | tf_op jit(solution)/shard_map/ppermute | solution.py:18
  6.7 1.9 %collective-permute-start.1 = (bf16[512,512]{1,0:T(8,128)(2,1)S(1)}, bf16[512,512]{1,0:T(8,128)(2,1)S(1)}, u32[]{:S(2)}, u32[]{:S(2)}) collective-permute-start(bf16[512,512]{1,0:T(8,128)(2,1)S(1)} %slice.73.refs_2_), channel_id=1, source_target_pairs={{0,4},{4,8},{8,12},{12,16},{16,20},{20,24},{24,28},{28,32},{32,36}... | collective-permute-start | bytes 1572872 | tf_op jit(solution)/shard_map/ppermute | solution.py:18
  8.6 11.7 %collective-permute-start.2 = (bf16[512,512]{1,0:T(8,128)(2,1)S(1)}, bf16[512,512]{1,0:T(8,128)(2,1)}, u32[]{:S(2)}, u32[]{:S(2)}) collective-permute-start(bf16[512,512]{1,0:T(8,128)(2,1)S(1)} %slice.73.refs_2_), channel_id=1, source_target_pairs={{0,508},{4,0},{8,4},{12,8},{16,12},{20,16},{24,20},{28,24},{32,28}... | collective-permute-start | bytes 1572872 | tf_op jit(solution)/shard_map/ppermute | solution.py:18
  20.3 4.2 %collective-permute-start.3 = (bf16[512,512]{1,0:T(8,128)(2,1)S(1)}, bf16[512,512]{1,0:T(8,128)(2,1)}, u32[]{:S(2)}, u32[]{:S(2)}) collective-permute-start(bf16[512,512]{1,0:T(8,128)(2,1)S(1)} %slice.73.refs_2_), channel_id=1, source_target_pairs={{0,504},{4,508},{8,0},{12,4},{16,8},{20,12},{24,16},{28,20},{32,24... | collective-permute-start | bytes 1572872 | tf_op jit(solution)/shard_map/ppermute | solution.py:18
  24.6 0.7 slice.72.query_ref
  25.3 0.8 fusion.35
  26.1 0.1 copy.25
  26.1 0.1 fusion.29
  26.2 0.1 broadcast_in_dim.16
  26.3 0.7 reshape_reshape.4.bias_ref
  27.0 0.0 copy-start.3
  27.0 2.8 %collective-permute-done.refs_0_ = bf16[512,512]{1,0:T(8,128)(2,1)S(1)} collective-permute-done((bf16[512,512]{1,0:T(8,128)(2,1)S(1)}, bf16[512,512]{1,0:T(8,128)(2,1)S(1)}, u32[]{:S(2)}, u32[]{:S(2)}) %collective-permute-start) | collective-permute-done | bytes 524320 | tf_op jit(solution)/shard_map/ppermute | solution.py:18
  29.8 0.0 copy-start.4
  29.8 4.8 %collective-permute-done.1.refs_1_ = bf16[512,512]{1,0:T(8,128)(2,1)S(1)} collective-permute-done((bf16[512,512]{1,0:T(8,128)(2,1)S(1)}, bf16[512,512]{1,0:T(8,128)(2,1)S(1)}, u32[]{:S(2)}, u32[]{:S(2)}) %collective-permute-start.1) | collective-permute-done | bytes 524320 | tf_op jit(solution)/shard_map/ppermute | solution.py:18
  34.6 0.0 collective-permute-done.2.refs_3_
  34.6 3.7 %collective-permute-done.3.refs_4_ = bf16[512,512]{1,0:T(8,128)(2,1)} collective-permute-done((bf16[512,512]{1,0:T(8,128)(2,1)S(1)}, bf16[512,512]{1,0:T(8,128)(2,1)}, u32[]{:S(2)}, u32[]{:S(2)}) %collective-permute-start.3) | collective-permute-done | bytes 524320 | tf_op jit(solution)/shard_map/ppermute | solution.py:18
  38.3 0.0 copy-done.1
  38.3 0.0 copy-done.4
  38.3 0.0 copy-done.5
  38.3 15.5 %shard_map.82 = bf16[512,256]{1,0:T(8,128)(2,1)} custom-call(bf16[512,256]{1,0:T(8,128)(2,1)} %slice.72.query_ref, f32[4,1,2560]{2,1,0:T(1,128)} %reshape_reshape.4.bias_ref, bf16[512,512]{1,0:T(8,128)(2,1)} %copy-done.4, bf16[512,512]{1,0:T(8,128)(2,1)} %copy-done.5, bf16[512,512]{1,0:T(8,128)(2,1)} %copy-done.1, ...), custom_call_target="tpu_custom_call" | custom-call | tf_op jit(solution)/shard_map/pallas_call | solution.py:115
  53.8 0.0 copy-done.3
  53.8 1.4 %convolution_convert_fusion = bf16[512,1024]{1,0:T(8,128)(2,1)S(1)} fusion(bf16[512,256]{1,0:T(8,128)(2,1)} %shard_map.82, bf16[256,1024]{1,0:T(8,128)(2,1)S(1)} %copy-done.3), kind=kOutput, calls=%fused_computation.12 | convolution fusion | flops 268959744 | bytes 1835008 | tf_op jit(solution)/shard_map/dot_general | solution.py:127
  55.2 1.0 copy.35
  56.2 4.8 %all-to-all-start = ((bf16[512,4,256]{2,0,1:T(8,128)(2,1)}), bf16[512,4,256]{2,0,1:T(8,128)(2,1)S(1)}, u32[]{:S(2)}, u32[]{:S(2)}) async-start(bf16[512,4,256]{2,0,1:T(8,128)(2,1)} %bitcast.29), calls=%async_computation | async-start | bytes 2097152 | tf_op jit(solution)/shard_map/all_to_all | solution.py:29
  61.1 10.3 %all-to-all-done = bf16[512,4,256]{2,0,1:T(8,128)(2,1)S(1)} async-done(((bf16[512,4,256]{2,0,1:T(8,128)(2,1)}), bf16[512,4,256]{2,0,1:T(8,128)(2,1)S(1)}, u32[]{:S(2)}, u32[]{:S(2)}) %all-to-all-start) | async-done | bytes 1048608 | tf_op jit(solution)/shard_map/all_to_all | solution.py:29
  71.4 1.2 %multiply_reduce_fusion = (f32[512]{0:T(512)S(1)}, f32[512,256]{1,0:T(8,128)S(1)}) fusion(bf16[512,4,256]{2,0,1:T(8,128)(2,1)S(1)} %all-to-all-done, bf16[512,1024]{1,0:T(8,128)(2,1)} %param.8, s32[]{:T(128)S(6)} %select_n.27), kind=kLoop, calls=%fused_computation.35 | loop fusion | flops 1441280 | bytes 1837060 | tf_op jit(solution)/shard_map/reduce_sum | solution.py:135
  72.6 0.6 broadcast_in_dim.17
  73.2 4.7 %all-to-all-start.1 = ((f32[4,1,512]{2,1,0:T(1,128)}), f32[4,1,512]{2,1,0:T(1,128)S(1)}, u32[]{:S(2)}, u32[]{:S(2)}) async-start(f32[4,1,512]{2,1,0:T(1,128)} %broadcast_in_dim.17), calls=%async_computation.1 | async-start | bytes 16384 | tf_op jit(solution)/shard_map/all_to_all | solution.py:37
  77.9 0.8 dynamic_slice.11
  78.6 3.1 %all-to-all-done.1 = f32[4,1,512]{2,1,0:T(1,128)S(1)} async-done(((f32[4,1,512]{2,1,0:T(1,128)}), f32[4,1,512]{2,1,0:T(1,128)S(1)}, u32[]{:S(2)}, u32[]{:S(2)}) %all-to-all-start.1) | async-done | bytes 8224 | tf_op jit(solution)/shard_map/all_to_all | solution.py:37
  81.7 0.1 multiply_convert_fusion
  81.9 0.1 broadcast_in_dim.18
  82.0 13.3 %all_to_all.21 = bf16[512,4,256]{2,0,1:T(8,128)(2,1)S(1)} all-to-all(bf16[512,4,256]{2,0,1:T(8,128)(2,1)S(1)} %broadcast_in_dim.18), channel_id=1, replica_groups=mesh['patch'=128,'mp'=4] {'mp'}, dimensions={1} | all-to-all | bytes 2097152 | tf_op jit(solution)/shard_map/all_to_all | solution.py:47
  95.3 1.3 %copy.28 = bf16[512,4,256]{0,2,1:T(8,128)(2,1)} copy(bf16[512,4,256]{2,0,1:T(8,128)(2,1)S(1)} %all_to_all.21) | data formatting | bytes 2097152 | tf_op jit(solution)/shard_map/all_to_all | solution.py:47
  96.6 0.0 copy-done
  96.6 2.9 %convolution_convert_fusion.1 = bf16[512,1024]{1,0:T(8,128)(2,1)S(1)} fusion(bf16[512,1024]{1,0:T(8,128)(2,1)S(1)} %copy-done, bf16[512,1024]{0,1:T(8,128)(2,1)} %bitcast.31, bf16[1024,512]{1,0:T(8,128)(2,1)} %param.13), kind=kOutput, calls=%fused_computation.13 | convolution fusion | flops 1076625408 | bytes 4194304 | tf_op jit(solution)/shard_map/dot_general | solution.py:142
  99.5 0.1 copy.34
  99.6 13.3 %all_to_all.22 = bf16[512,4,256]{2,0,1:T(8,128)(2,1)S(1)} all-to-all(bf16[512,4,256]{2,0,1:T(8,128)(2,1)S(1)} %bitcast.30), channel_id=1, replica_groups=mesh['patch'=128,'mp'=4] {'mp'}, dimensions={1} | all-to-all | bytes 2097152 | tf_op jit(solution)/shard_map/all_to_all | solution.py:29
  112.9 0.8 fusion.24
  (5 shorter events, 0.1 us)
Async XLA Ops:
  0.0 96.6 %copy-start = (bf16[512,1024]{1,0:T(8,128)(2,1)S(1)}, bf16[512,1024]{1,0:T(8,128)(2,1)}, u32[]{:S(2)}) copy-start(bf16[512,1024]{1,0:T(8,128)(2,1)} %param.14) | copy-start | bytes 3145732
  0.0 1.8 %copy-start.2 = (bf16[512,1024]{1,0:T(8,128)(2,1)S(1)}, bf16[512,1024]{1,0:T(8,128)(2,1)}, u32[]{:S(2)}) copy-start(bf16[512,1024]{1,0:T(8,128)(2,1)} %param.8) | copy-start | bytes 3145732
  0.0 2.1 %copy-start.6 = (f32[1024]{0:T(1024)S(1)}, f32[1024]{0:T(1024)}, u32[]{:S(2)}) copy-start(f32[1024]{0:T(1024)} %param.9) | copy-start | bytes 12292
  3.2 35.1 %copy-start.1 = (bf16[512,512]{1,0:T(8,128)(2,1)}, bf16[512,512]{1,0:T(8,128)(2,1)S(1)}, u32[]{:S(2)}) copy-start(bf16[512,512]{1,0:T(8,128)(2,1)S(1)} %slice.73.refs_2_) | copy-start | bytes 1572868
  3.2 26.6 %collective-permute-start = (bf16[512,512]{1,0:T(8,128)(2,1)S(1)}, bf16[512,512]{1,0:T(8,128)(2,1)S(1)}, u32[]{:S(2)}, u32[]{:S(2)}) collective-permute-start(bf16[512,512]{1,0:T(8,128)(2,1)S(1)} %slice.73.refs_2_), channel_id=1, source_target_pairs={{0,8},{4,12},{8,16},{12,20},{16,24},{20,28},{24,32},{28,36},{32,40... | collective-permute-start | bytes 1572872 | tf_op jit(solution)/shard_map/ppermute | solution.py:18
  6.7 27.9 %collective-permute-start.1 = (bf16[512,512]{1,0:T(8,128)(2,1)S(1)}, bf16[512,512]{1,0:T(8,128)(2,1)S(1)}, u32[]{:S(2)}, u32[]{:S(2)}) collective-permute-start(bf16[512,512]{1,0:T(8,128)(2,1)S(1)} %slice.73.refs_2_), channel_id=1, source_target_pairs={{0,4},{4,8},{8,12},{12,16},{16,20},{20,24},{24,28},{28,32},{32,36}... | collective-permute-start | bytes 1572872 | tf_op jit(solution)/shard_map/ppermute | solution.py:18
  8.6 26.0 %collective-permute-start.2 = (bf16[512,512]{1,0:T(8,128)(2,1)S(1)}, bf16[512,512]{1,0:T(8,128)(2,1)}, u32[]{:S(2)}, u32[]{:S(2)}) collective-permute-start(bf16[512,512]{1,0:T(8,128)(2,1)S(1)} %slice.73.refs_2_), channel_id=1, source_target_pairs={{0,508},{4,0},{8,4},{12,8},{16,12},{20,16},{24,20},{28,24},{32,28}... | collective-permute-start | bytes 1572872 | tf_op jit(solution)/shard_map/ppermute | solution.py:18
  20.3 17.9 %collective-permute-start.3 = (bf16[512,512]{1,0:T(8,128)(2,1)S(1)}, bf16[512,512]{1,0:T(8,128)(2,1)}, u32[]{:S(2)}, u32[]{:S(2)}) collective-permute-start(bf16[512,512]{1,0:T(8,128)(2,1)S(1)} %slice.73.refs_2_), channel_id=1, source_target_pairs={{0,504},{4,508},{8,0},{12,4},{16,8},{20,12},{24,16},{28,20},{32,24... | collective-permute-start | bytes 1572872 | tf_op jit(solution)/shard_map/ppermute | solution.py:18
  27.0 26.8 %copy-start.3 = (bf16[256,1024]{1,0:T(8,128)(2,1)S(1)}, bf16[256,1024]{1,0:T(8,128)(2,1)}, u32[]{:S(2)}) copy-start(bf16[256,1024]{1,0:T(8,128)(2,1)} %param.11) | copy-start | bytes 1572868
  29.8 8.5 %copy-start.4 = (bf16[512,512]{1,0:T(8,128)(2,1)}, bf16[512,512]{1,0:T(8,128)(2,1)S(1)}, u32[]{:S(2)}) copy-start(bf16[512,512]{1,0:T(8,128)(2,1)S(1)} %collective-permute-done.refs_0_) | copy-start | bytes 1572868
  34.6 3.7 %copy-start.5 = (bf16[512,512]{1,0:T(8,128)(2,1)}, bf16[512,512]{1,0:T(8,128)(2,1)S(1)}, u32[]{:S(2)}) copy-start(bf16[512,512]{1,0:T(8,128)(2,1)S(1)} %collective-permute-done.1.refs_1_) | copy-start | bytes 1572868
  56.2 15.1 %all-to-all-start = ((bf16[512,4,256]{2,0,1:T(8,128)(2,1)}), bf16[512,4,256]{2,0,1:T(8,128)(2,1)S(1)}, u32[]{:S(2)}, u32[]{:S(2)}) async-start(bf16[512,4,256]{2,0,1:T(8,128)(2,1)} %bitcast.29), calls=%async_computation | async-start | bytes 2097152 | tf_op jit(solution)/shard_map/all_to_all | solution.py:29
  73.2 8.5 %all-to-all-start.1 = ((f32[4,1,512]{2,1,0:T(1,128)}), f32[4,1,512]{2,1,0:T(1,128)S(1)}, u32[]{:S(2)}, u32[]{:S(2)}) async-start(f32[4,1,512]{2,1,0:T(1,128)} %broadcast_in_dim.17), calls=%async_computation.1 | async-start | bytes 16384 | tf_op jit(solution)/shard_map/all_to_all | solution.py:37

commit v3 on v2

--- a/solution.py
+++ b/solution.py
@@ -33,18 +33,27 @@
     return total
 
 
-def gather_sum(vector, n_mp):
-    got = lax.all_to_all(jnp.broadcast_to(vector[None], (n_mp,) + vector.shape), "mp", 0, 0)
-    total = got[0]
-    for which in range(1, n_mp):
-        total = total + got[which]
-    return total
-
-
-def gather_cols(block, n_mp):
+def gather_with_sums(block, vector, n_mp):
     rows, cols = block.shape
-    spread = jnp.broadcast_to(block[:, None], (rows, n_mp, cols))
-    return lax.all_to_all(spread, "mp", 1, 1).reshape(rows, n_mp * cols)
+    pieces = []
+    rest = vector
+    for _ in range(3):
+        piece = rest.astype(jnp.bfloat16)
+        rest = rest - piece.astype(jnp.float32)
+        pieces.append(piece.reshape(-1, cols))
+    extra = jnp.concatenate(pieces, axis=0)
+    pad = (-extra.shape[0]) % 8
+    extra = jnp.concatenate([extra, jnp.zeros((pad, cols), jnp.bfloat16)], axis=0)
+    packed = jnp.concatenate([block, extra], axis=0)
+    spread = jnp.broadcast_to(packed[:, None], (packed.shape[0], n_mp, cols))
+    got = lax.all_to_all(spread, "mp", 1, 1)
+    gathered = got[:rows].reshape(rows, n_mp * cols)
+    per_row = rows // cols
+    sums = []
+    for which in range(n_mp):
+        bits = got[rows:rows + 3 * per_row, which].astype(jnp.float32).reshape(3, rows)
+        sums.append((bits[0] + bits[1]) + bits[2])
+    return gathered, sums
 
 
 def window_attention(query_ref, bias_ref, *refs, n_heads, n_win):
@@ -132,10 +141,14 @@
         lax.dynamic_slice_in_dim(features, col_begin, col_width, 1).astype(jnp.float32) + col_share
     )
     gain_cols = lax.dynamic_slice_in_dim(gain_mlp, col_begin, col_width, 0)
-    square_sum = gather_sum(jnp.sum(residual_cols * residual_cols, axis=1), n_mp)
+    scaled_cols = (residual_cols * gain_cols).astype(jnp.bfloat16)
+    square_part = jnp.sum(residual_cols * residual_cols, axis=1)
+    scaled, square_parts = gather_with_sums(scaled_cols, square_part, n_mp)
+    square_sum = square_parts[0]
+    for which in range(1, n_mp):
+        square_sum = square_sum + square_parts[which]
     inverse_rms = lax.rsqrt(square_sum / D + 1e-05)
-    normed_cols = (residual_cols * inverse_rms[:, None] * gain_cols).astype(jnp.bfloat16)
-    normed2 = gather_cols(normed_cols, n_mp)
+    normed2 = (scaled.astype(jnp.float32) * inverse_rms[:, None]).astype(jnp.bfloat16)
     hidden = jax.nn.gelu(
         jnp.dot(normed2, w_up, preferred_element_type=jnp.float32), approximate=True
     ).astype(jnp.bfloat16)

time: 114 us -> 127 us (1.11)
  the two profiles are of different devices: /device:TPU:2 before, /device:TPU:1 now
where the time goes in v3:
time: 127 us; the launch traced here: 126 us
  blocking collectives  35.3 us (28%)
  waiting for transfers between devices  30.8 us (24%)
  starting transfers between devices  25.9 us (20%)
  Pallas kernels  15.5 us (12%)
  local copies, waits for them, and re-layouts  8.68 us (7%)
  matrix products  5.37 us (4%)
  other arithmetic  4.61 us (4%)
    ppermute x4, starting transfers between devices, from_behind(): lax.ppermute(array, axis, [(i, (i + by) % length) for i in range(length)])  21.9 us
    all_to_all x1, blocking collectives, gather_with_sums(): got = lax.all_to_all(spread, 'mp', 1, 1)  18.1 us
    ppermute x4, waiting for transfers between devices, from_behind(): lax.ppermute(array, axis, [(i, (i + by) % length) for i in range(length)])  17.4 us
    all_to_all x1, blocking collectives, scatter_sum(): got = lax.all_to_all(parts.reshape(rows, n_mp, cols // n_mp), 'mp', 1, 1)  17.2 us
    pallas_call x1, Pallas kernels, per_device(): pl.pallas_call(functools.partial(window_attention, n_heads=heads_here, n_...  15.5 us
    all_to_all x1, waiting for transfers between devices, scatter_sum(): got = lax.all_to_all(parts.reshape(rows, n_mp, cols // n_mp), 'mp', 1, 1)  13.4 us
    all_to_all x1, starting transfers between devices, scatter_sum(): got = lax.all_to_all(parts.reshape(rows, n_mp, cols // n_mp), 'mp', 1, 1)  4.04 us
    dot_general x1, matrix products, per_device(): down_term = jnp.dot(hidden, w_down, preferred_element_type=jnp.float32)  2.95 us
  transfers between devices with their start and end apart: 5, of which 5 were waited for; matrix products, arithmetic and copies ran while one was open for 3% of the time, Pallas kernels for 0%

profile of v3, /device:TPU:1, one launch (start us, length us, event | category | flops | bytes accessed | tf_op | source)
XLA Modules:
  0.0 126.4 jit_solution(3786949451215060012)
XLA Ops:
  0.0 0.0 copy-start
  0.0 1.6 %fusion = f32[512]{0:T(512)S(1)} fusion(bf16[512,1024]{1,0:T(8,128)(2,1)} %param.8), kind=kLoop, calls=%fused_computation.2 | loop fusion | flops 1572352 | bytes 1050624 | tf_op jit(solution)/shard_map/reduce_sum | solution.py:23
  1.6 0.0 copy-start.2
  1.6 0.0 copy-start.6
  1.6 1.5 %slice_bitcast_fusion.2 = (bf16[1024,256]{1,0:T(8,128)(2,1)S(1)}, bf16[1024,256]{1,0:T(8,128)(2,1)S(1)}, bf16[1024,256]{1,0:T(8,128)(2,1)S(1)}) fusion(bf16[3,1024,256]{2,1,0:T(8,128)(2,1)} %param.10), kind=kLoop, calls=%fused_computation.42 | loop fusion | bytes 3145728 | tf_op jit(solution)/shard_map/squeeze | solution.py:104
  3.2 0.1 copy-done.2
  3.3 0.0 copy-done.6
  3.3 1.0 fusion.10
  4.4 0.0 copy-start.1
  4.4 14.4 %collective-permute-start.3 = (bf16[512,512]{1,0:T(8,128)(2,1)S(1)}, bf16[512,512]{1,0:T(8,128)(2,1)S(1)}, u32[]{:S(2)}, u32[]{:S(2)}) collective-permute-start(bf16[512,512]{1,0:T(8,128)(2,1)S(1)} %slice.145.refs_2_), channel_id=1, source_target_pairs={{0,504},{4,508},{8,0},{12,4},{16,8},{20,12},{24,16},{28,20},{32,24... | collective-permute-start | bytes 1572872 | tf_op jit(solution)/shard_map/ppermute | solution.py:18
  18.8 2.9 %collective-permute-start.2 = (bf16[512,512]{1,0:T(8,128)(2,1)S(1)}, bf16[512,512]{1,0:T(8,128)(2,1)S(1)}, u32[]{:S(2)}, u32[]{:S(2)}) collective-permute-start(bf16[512,512]{1,0:T(8,128)(2,1)S(1)} %slice.145.refs_2_), channel_id=1, source_target_pairs={{0,508},{4,0},{8,4},{12,8},{16,12},{20,16},{24,20},{28,24},{32,28}... | collective-permute-start | bytes 1572872 | tf_op jit(solution)/shard_map/ppermute | solution.py:18
  21.7 2.7 %collective-permute-start.1 = (bf16[512,512]{1,0:T(8,128)(2,1)S(1)}, bf16[512,512]{1,0:T(8,128)(2,1)}, u32[]{:S(2)}, u32[]{:S(2)}) collective-permute-start(bf16[512,512]{1,0:T(8,128)(2,1)S(1)} %slice.145.refs_2_), channel_id=1, source_target_pairs={{0,4},{4,8},{8,12},{12,16},{16,20},{20,24},{24,28},{28,32},{32,36}... | collective-permute-start | bytes 1572872 | tf_op jit(solution)/shard_map/ppermute | solution.py:18
  24.4 1.9 %collective-permute-start = (bf16[512,512]{1,0:T(8,128)(2,1)S(1)}, bf16[512,512]{1,0:T(8,128)(2,1)}, u32[]{:S(2)}, u32[]{:S(2)}) collective-permute-start(bf16[512,512]{1,0:T(8,128)(2,1)S(1)} %slice.145.refs_2_), channel_id=1, source_target_pairs={{0,8},{4,12},{8,16},{12,20},{16,24},{20,28},{24,32},{28,36},{32,40... | collective-permute-start | bytes 1572872 | tf_op jit(solution)/shard_map/ppermute | solution.py:18
  26.3 0.7 slice.144.query_ref
  27.0 0.8 fusion.42
  27.8 0.1 copy.25
  27.9 0.1 fusion.36
  28.0 0.1 broadcast_in_dim.28
  28.1 0.7 reshape_reshape.4.bias_ref
  28.7 0.0 copy-start.3
  28.7 0.6 collective-permute-done.3.refs_4_
  29.4 0.0 copy-start.4
  29.4 0.3 collective-permute-done.2.refs_3_
  29.7 0.0 copy-start.5
  29.7 3.9 %collective-permute-done.1.refs_1_ = bf16[512,512]{1,0:T(8,128)(2,1)} collective-permute-done((bf16[512,512]{1,0:T(8,128)(2,1)S(1)}, bf16[512,512]{1,0:T(8,128)(2,1)}, u32[]{:S(2)}, u32[]{:S(2)}) %collective-permute-start.1) | collective-permute-done | bytes 524320 | tf_op jit(solution)/shard_map/ppermute | solution.py:18
  33.6 12.6 %collective-permute-done.refs_0_ = bf16[512,512]{1,0:T(8,128)(2,1)} collective-permute-done((bf16[512,512]{1,0:T(8,128)(2,1)S(1)}, bf16[512,512]{1,0:T(8,128)(2,1)}, u32[]{:S(2)}, u32[]{:S(2)}) %collective-permute-start) | collective-permute-done | bytes 524320 | tf_op jit(solution)/shard_map/ppermute | solution.py:18
  46.2 0.0 copy-done.1
  46.2 0.0 copy-done.4
  46.2 0.0 copy-done.5
  46.2 15.5 %shard_map.82 = bf16[512,256]{1,0:T(8,128)(2,1)} custom-call(bf16[512,256]{1,0:T(8,128)(2,1)} %slice.144.query_ref, f32[4,1,2560]{2,1,0:T(1,128)} %reshape_reshape.4.bias_ref, bf16[512,512]{1,0:T(8,128)(2,1)} %collective-permute-done.refs_0_, bf16[512,512]{1,0:T(8,128)(2,1)} %collective-permute-done.1.refs_1_, bf16[512,512]{1,0:T(8,128)(2,1)} %copy-done.1, ...), custom_call_target="tpu_custom_call" | custom-call | tf_op jit(solution)/shard_map/pallas_call | solution.py:124
  61.7 0.0 copy-done.3
  61.7 1.4 %convolution_convert_fusion = bf16[512,1024]{1,0:T(8,128)(2,1)S(1)} fusion(bf16[512,256]{1,0:T(8,128)(2,1)} %shard_map.82, bf16[256,1024]{1,0:T(8,128)(2,1)S(1)} %copy-done.3), kind=kOutput, calls=%fused_computation.14 | convolution fusion | flops 268959744 | bytes 1835008 | tf_op jit(solution)/shard_map/dot_general | solution.py:136
  63.1 1.0 copy.37
  64.1 4.0 %all-to-all-start = ((bf16[512,4,256]{2,0,1:T(8,128)(2,1)}), bf16[512,4,256]{2,0,1:T(8,128)(2,1)S(1)}, u32[]{:S(2)}, u32[]{:S(2)}) async-start(bf16[512,4,256]{2,0,1:T(8,128)(2,1)} %bitcast.32), calls=%async_computation | async-start | bytes 2097152 | tf_op jit(solution)/shard_map/all_to_all | solution.py:29
  68.2 0.8 dynamic_slice.11
  68.9 13.4 %all-to-all-done = bf16[512,4,256]{2,0,1:T(8,128)(2,1)S(1)} async-done(((bf16[512,4,256]{2,0,1:T(8,128)(2,1)}), bf16[512,4,256]{2,0,1:T(8,128)(2,1)S(1)}, u32[]{:S(2)}, u32[]{:S(2)}) %all-to-all-start) | async-done | bytes 1048608 | tf_op jit(solution)/shard_map/all_to_all | solution.py:29
  82.3 1.2 multiply_reduce_fusion
  83.6 0.1 concatenate.7
  83.7 0.1 broadcast_in_dim.30
  83.8 18.1 %all_to_all.15 = bf16[520,4,256]{2,0,1:T(8,128)(2,1)S(1)} all-to-all(bf16[520,4,256]{2,0,1:T(8,128)(2,1)S(1)} %broadcast_in_dim.30), channel_id=1, replica_groups=mesh['patch'=128,'mp'=4] {'mp'}, dimensions={1} | all-to-all | bytes 2129920 | tf_op jit(solution)/shard_map/all_to_all | solution.py:49
  101.9 1.0 slice.150
  103.0 2.3 %copy.30 = bf16[512,4,256]{0,2,1:T(8,128)(2,1)} copy(bf16[512,4,256]{2,0,1:T(8,128)(2,1)} %slice.150) | data formatting | bytes 2097152
  105.3 0.0 copy-done
  105.3 3.0 %convolution_convert_fusion.1 = bf16[512,1024]{1,0:T(8,128)(2,1)S(1)} fusion(bf16[512,1024]{1,0:T(8,128)(2,1)S(1)} %copy-done, bf16[1024,512]{1,0:T(8,128)(2,1)} %param.13, bf16[512,1024]{0,1:T(8,128)(2,1)} %bitcast.34, f32[512]{0:T(512)S(1)} %bitcast.36), kind=kOutput, calls=%fused_computation.15 | convolution fusion | flops 1078198272 | bytes 4196352 | tf_op jit(solution)/shard_map/dot_general | solution.py:155
  108.3 0.1 copy.36
  108.3 17.2 %all_to_all.16 = bf16[512,4,256]{2,0,1:T(8,128)(2,1)S(1)} all-to-all(bf16[512,4,256]{2,0,1:T(8,128)(2,1)S(1)} %bitcast.33), channel_id=1, replica_groups=mesh['patch'=128,'mp'=4] {'mp'}, dimensions={1} | all-to-all | bytes 2097152 | tf_op jit(solution)/shard_map/all_to_all | solution.py:29
  125.6 0.8 fusion.31
  (10 shorter events, 0.1 us)
Async XLA Ops:
  0.0 105.3 %copy-start = (bf16[512,1024]{1,0:T(8,128)(2,1)S(1)}, bf16[512,1024]{1,0:T(8,128)(2,1)}, u32[]{:S(2)}) copy-start(bf16[512,1024]{1,0:T(8,128)(2,1)} %param.14) | copy-start | bytes 3145732
  1.6 1.7 %copy-start.2 = (bf16[512,1024]{1,0:T(8,128)(2,1)S(1)}, bf16[512,1024]{1,0:T(8,128)(2,1)}, u32[]{:S(2)}) copy-start(bf16[512,1024]{1,0:T(8,128)(2,1)} %param.8) | copy-start | bytes 3145732
  1.6 1.7 %copy-start.6 = (f32[1024]{0:T(1024)S(1)}, f32[1024]{0:T(1024)}, u32[]{:S(2)}) copy-start(f32[1024]{0:T(1024)} %param.9) | copy-start | bytes 12292
  4.4 41.8 %copy-start.1 = (bf16[512,512]{1,0:T(8,128)(2,1)}, bf16[512,512]{1,0:T(8,128)(2,1)S(1)}, u32[]{:S(2)}) copy-start(bf16[512,512]{1,0:T(8,128)(2,1)S(1)} %slice.145.refs_2_) | copy-start | bytes 1572868
  4.4 25.0 %collective-permute-start.3 = (bf16[512,512]{1,0:T(8,128)(2,1)S(1)}, bf16[512,512]{1,0:T(8,128)(2,1)S(1)}, u32[]{:S(2)}, u32[]{:S(2)}) collective-permute-start(bf16[512,512]{1,0:T(8,128)(2,1)S(1)} %slice.145.refs_2_), channel_id=1, source_target_pairs={{0,504},{4,508},{8,0},{12,4},{16,8},{20,12},{24,16},{28,20},{32,24... | collective-permute-start | bytes 1572872 | tf_op jit(solution)/shard_map/ppermute | solution.py:18
  18.8 10.9 %collective-permute-start.2 = (bf16[512,512]{1,0:T(8,128)(2,1)S(1)}, bf16[512,512]{1,0:T(8,128)(2,1)S(1)}, u32[]{:S(2)}, u32[]{:S(2)}) collective-permute-start(bf16[512,512]{1,0:T(8,128)(2,1)S(1)} %slice.145.refs_2_), channel_id=1, source_target_pairs={{0,508},{4,0},{8,4},{12,8},{16,12},{20,16},{24,20},{28,24},{32,28}... | collective-permute-start | bytes 1572872 | tf_op jit(solution)/shard_map/ppermute | solution.py:18
  21.7 11.9 %collective-permute-start.1 = (bf16[512,512]{1,0:T(8,128)(2,1)S(1)}, bf16[512,512]{1,0:T(8,128)(2,1)}, u32[]{:S(2)}, u32[]{:S(2)}) collective-permute-start(bf16[512,512]{1,0:T(8,128)(2,1)S(1)} %slice.145.refs_2_), channel_id=1, source_target_pairs={{0,4},{4,8},{8,12},{12,16},{16,20},{20,24},{24,28},{28,32},{32,36}... | collective-permute-start | bytes 1572872 | tf_op jit(solution)/shard_map/ppermute | solution.py:18
  24.4 21.8 %collective-permute-start = (bf16[512,512]{1,0:T(8,128)(2,1)S(1)}, bf16[512,512]{1,0:T(8,128)(2,1)}, u32[]{:S(2)}, u32[]{:S(2)}) collective-permute-start(bf16[512,512]{1,0:T(8,128)(2,1)S(1)} %slice.145.refs_2_), channel_id=1, source_target_pairs={{0,8},{4,12},{8,16},{12,20},{16,24},{20,28},{24,32},{28,36},{32,40... | collective-permute-start | bytes 1572872 | tf_op jit(solution)/shard_map/ppermute | solution.py:18
  28.7 33.0 %copy-start.3 = (bf16[256,1024]{1,0:T(8,128)(2,1)S(1)}, bf16[256,1024]{1,0:T(8,128)(2,1)}, u32[]{:S(2)}) copy-start(bf16[256,1024]{1,0:T(8,128)(2,1)} %param.11) | copy-start | bytes 1572868
  29.4 16.8 %copy-start.4 = (bf16[512,512]{1,0:T(8,128)(2,1)}, bf16[512,512]{1,0:T(8,128)(2,1)S(1)}, u32[]{:S(2)}) copy-start(bf16[512,512]{1,0:T(8,128)(2,1)S(1)} %collective-permute-done.3.refs_4_) | copy-start | bytes 1572868
  29.7 16.5 %copy-start.5 = (bf16[512,512]{1,0:T(8,128)(2,1)}, bf16[512,512]{1,0:T(8,128)(2,1)S(1)}, u32[]{:S(2)}) copy-start(bf16[512,512]{1,0:T(8,128)(2,1)S(1)} %collective-permute-done.2.refs_3_) | copy-start | bytes 1572868
  64.1 18.2 %all-to-all-start = ((bf16[512,4,256]{2,0,1:T(8,128)(2,1)}), bf16[512,4,256]{2,0,1:T(8,128)(2,1)S(1)}, u32[]{:S(2)}, u32[]{:S(2)}) async-start(bf16[512,4,256]{2,0,1:T(8,128)(2,1)} %bitcast.32), calls=%async_computation | async-start | bytes 2097152 | tf_op jit(solution)/shard_map/all_to_all | solution.py:29

commit v4 on v2

--- a/solution.py
+++ b/solution.py
@@ -30,14 +30,6 @@
     total = got[:, 0].astype(jnp.float32)
     for which in range(1, n_mp):
         total = total + got[:, which].astype(jnp.float32)
-    return total
-
-
-def gather_sum(vector, n_mp):
-    got = lax.all_to_all(jnp.broadcast_to(vector[None], (n_mp,) + vector.shape), "mp", 0, 0)
-    total = got[0]
-    for which in range(1, n_mp):
-        total = total + got[which]
     return total
 
 
@@ -131,11 +123,10 @@
     residual_cols = (
         lax.dynamic_slice_in_dim(features, col_begin, col_width, 1).astype(jnp.float32) + col_share
     )
-    gain_cols = lax.dynamic_slice_in_dim(gain_mlp, col_begin, col_width, 0)
-    square_sum = gather_sum(jnp.sum(residual_cols * residual_cols, axis=1), n_mp)
+    rows_full = gather_cols(residual_cols.astype(jnp.bfloat16), n_mp).astype(jnp.float32)
+    square_sum = jnp.sum(rows_full * rows_full, axis=1, keepdims=True)
     inverse_rms = lax.rsqrt(square_sum / D + 1e-05)
-    normed_cols = (residual_cols * inverse_rms[:, None] * gain_cols).astype(jnp.bfloat16)
-    normed2 = gather_cols(normed_cols, n_mp)
+    normed2 = (rows_full * inverse_rms * gain_mlp).astype(jnp.bfloat16)
     hidden = jax.nn.gelu(
         jnp.dot(normed2, w_up, preferred_element_type=jnp.float32), approximate=True
     ).astype(jnp.bfloat16)

time: 114 us -> 129 us (1.13)
  the two profiles are of different devices: /device:TPU:2 before, /device:TPU:1 now
where the time goes in v4:
time: 129 us
  blocking collectives  35.9 us (28%)
  waiting for transfers between devices  31.6 us (24%)
  starting transfers between devices  25.9 us (20%)
  Pallas kernels  15.5 us (12%)
  local copies, waits for them, and re-layouts  7.17 us (6%)
  matrix products  6.37 us (5%)
  other arithmetic  6.15 us (5%)
    ppermute x4, starting transfers between devices, from_behind(): lax.ppermute(array, axis, [(i, (i + by) % length) for i in range(length)])  21.9 us
    all_to_all x1, blocking collectives, gather_cols(): return lax.all_to_all(spread, 'mp', 1, 1).reshape(rows, n_mp * cols)  18.7 us
    ppermute x4, waiting for transfers between devices, from_behind(): lax.ppermute(array, axis, [(i, (i + by) % length) for i in range(length)])  17.4 us
    all_to_all x1, blocking collectives, scatter_sum(): got = lax.all_to_all(parts.reshape(rows, n_mp, cols // n_mp), 'mp', 1, 1)  17.2 us
    pallas_call x1, Pallas kernels, per_device(): pl.pallas_call(functools.partial(window_attention, n_heads=heads_here, n_...  15.5 us
    all_to_all x1, waiting for transfers between devices, scatter_sum(): got = lax.all_to_all(parts.reshape(rows, n_mp, cols // n_mp), 'mp', 1, 1)  14.2 us
    all_to_all x1, starting transfers between devices, scatter_sum(): got = lax.all_to_all(parts.reshape(rows, n_mp, cols // n_mp), 'mp', 1, 1)  3.99 us
    dot_general x1, matrix products, per_device(): down_term = jnp.dot(hidden, w_down, preferred_element_type=jnp.float32)  3.95 us
  transfers between devices with their start and end apart: 5, of which 5 were waited for; matrix products, arithmetic and copies ran while one was open for 2% of the time, Pallas kernels for 0%

profile of v4, /device:TPU:1, one launch (start us, length us, event | category | flops | bytes accessed | tf_op | source)
XLA Modules:
  0.0 128.7 jit_solution(9862248097317524092)
XLA Ops:
  0.0 0.0 copy-start
  0.0 1.6 %fusion = f32[512]{0:T(512)S(1)} fusion(bf16[512,1024]{1,0:T(8,128)(2,1)} %param.8), kind=kLoop, calls=%fused_computation.2 | loop fusion | flops 1572352 | bytes 1050624 | tf_op jit(solution)/shard_map/reduce_sum | solution.py:23
  1.6 0.0 copy-start.1
  1.6 0.0 copy-start.5
  1.6 1.5 %slice_bitcast_fusion.2 = (bf16[1024,256]{1,0:T(8,128)(2,1)S(1)}, bf16[1024,256]{1,0:T(8,128)(2,1)S(1)}, bf16[1024,256]{1,0:T(8,128)(2,1)S(1)}) fusion(bf16[3,1024,256]{2,1,0:T(8,128)(2,1)} %param.10), kind=kLoop, calls=%fused_computation.40 | loop fusion | bytes 3145728 | tf_op jit(solution)/shard_map/squeeze | solution.py:87
  3.2 0.1 copy-done.1
  3.3 0.0 copy-done.5
  3.3 1.0 fusion.11
  4.4 0.0 copy-start.2
  4.4 14.4 %collective-permute-start.3 = (bf16[512,512]{1,0:T(8,128)(2,1)S(1)}, bf16[512,512]{1,0:T(8,128)(2,1)}, u32[]{:S(2)}, u32[]{:S(2)}) collective-permute-start(bf16[512,512]{1,0:T(8,128)(2,1)S(1)} %slice.53.refs_2_), channel_id=1, source_target_pairs={{0,504},{4,508},{8,0},{12,4},{16,8},{20,12},{24,16},{28,20},{32,24... | collective-permute-start | bytes 1572872 | tf_op jit(solution)/shard_map/ppermute | solution.py:18
  18.8 2.9 %collective-permute-start.2 = (bf16[512,512]{1,0:T(8,128)(2,1)S(1)}, bf16[512,512]{1,0:T(8,128)(2,1)}, u32[]{:S(2)}, u32[]{:S(2)}) collective-permute-start(bf16[512,512]{1,0:T(8,128)(2,1)S(1)} %slice.53.refs_2_), channel_id=1, source_target_pairs={{0,508},{4,0},{8,4},{12,8},{16,12},{20,16},{24,20},{28,24},{32,28}... | collective-permute-start | bytes 1572872 | tf_op jit(solution)/shard_map/ppermute | solution.py:18
  21.7 2.7 %collective-permute-start.1 = (bf16[512,512]{1,0:T(8,128)(2,1)S(1)}, bf16[512,512]{1,0:T(8,128)(2,1)}, u32[]{:S(2)}, u32[]{:S(2)}) collective-permute-start(bf16[512,512]{1,0:T(8,128)(2,1)S(1)} %slice.53.refs_2_), channel_id=1, source_target_pairs={{0,4},{4,8},{8,12},{12,16},{16,20},{20,24},{24,28},{28,32},{32,36}... | collective-permute-start | bytes 1572872 | tf_op jit(solution)/shard_map/ppermute | solution.py:18
  24.4 1.9 %collective-permute-start = (bf16[512,512]{1,0:T(8,128)(2,1)S(1)}, bf16[512,512]{1,0:T(8,128)(2,1)}, u32[]{:S(2)}, u32[]{:S(2)}) collective-permute-start(bf16[512,512]{1,0:T(8,128)(2,1)S(1)} %slice.53.refs_2_), channel_id=1, source_target_pairs={{0,8},{4,12},{8,16},{12,20},{16,24},{20,28},{24,32},{28,36},{32,40... | collective-permute-start | bytes 1572872 | tf_op jit(solution)/shard_map/ppermute | solution.py:18
  26.3 0.7 slice.52.query_ref
  27.0 0.8 fusion.37
  27.8 0.1 copy.25
  27.9 0.1 fusion.31
  28.0 0.1 broadcast_in_dim.14
  28.1 0.7 reshape_reshape.4.bias_ref
  28.7 0.0 copy-start.3
  28.7 0.6 collective-permute-done.3.refs_4_
  29.4 0.3 collective-permute-done.2.refs_3_
  29.7 3.9 %collective-permute-done.1.refs_1_ = bf16[512,512]{1,0:T(8,128)(2,1)} collective-permute-done((bf16[512,512]{1,0:T(8,128)(2,1)S(1)}, bf16[512,512]{1,0:T(8,128)(2,1)}, u32[]{:S(2)}, u32[]{:S(2)}) %collective-permute-start.1) | collective-permute-done | bytes 524320 | tf_op jit(solution)/shard_map/ppermute | solution.py:18
  33.6 12.6 %collective-permute-done.refs_0_ = bf16[512,512]{1,0:T(8,128)(2,1)} collective-permute-done((bf16[512,512]{1,0:T(8,128)(2,1)S(1)}, bf16[512,512]{1,0:T(8,128)(2,1)}, u32[]{:S(2)}, u32[]{:S(2)}) %collective-permute-start) | collective-permute-done | bytes 524320 | tf_op jit(solution)/shard_map/ppermute | solution.py:18
  46.2 0.0 copy-done.2
  46.2 15.5 %shard_map.82 = bf16[512,256]{1,0:T(8,128)(2,1)} custom-call(bf16[512,256]{1,0:T(8,128)(2,1)} %slice.52.query_ref, f32[4,1,2560]{2,1,0:T(1,128)} %reshape_reshape.4.bias_ref, bf16[512,512]{1,0:T(8,128)(2,1)} %collective-permute-done.refs_0_, bf16[512,512]{1,0:T(8,128)(2,1)} %collective-permute-done.1.refs_1_, bf16[512,512]{1,0:T(8,128)(2,1)} %copy-done.2, ...), custom_call_target="tpu_custom_call" | custom-call | tf_op jit(solution)/shard_map/pallas_call | solution.py:107
  61.7 0.0 copy-done.3
  61.7 1.4 %convolution_convert_fusion = bf16[512,1024]{1,0:T(8,128)(2,1)S(1)} fusion(bf16[512,256]{1,0:T(8,128)(2,1)} %shard_map.82, bf16[256,1024]{1,0:T(8,128)(2,1)S(1)} %copy-done.3), kind=kOutput, calls=%fused_computation.16 | convolution fusion | flops 268959744 | bytes 1835008 | tf_op jit(solution)/shard_map/dot_general | solution.py:119
  63.1 1.0 copy.35
  64.1 4.0 %all-to-all-start = ((bf16[512,4,256]{2,0,1:T(8,128)(2,1)}), bf16[512,4,256]{2,0,1:T(8,128)(2,1)S(1)}, u32[]{:S(2)}, u32[]{:S(2)}) async-start(bf16[512,4,256]{2,0,1:T(8,128)(2,1)} %bitcast.34), calls=%async_computation | async-start | bytes 2097152 | tf_op jit(solution)/shard_map/all_to_all | solution.py:29
  68.1 14.2 %all-to-all-done = bf16[512,4,256]{2,0,1:T(8,128)(2,1)S(1)} async-done(((bf16[512,4,256]{2,0,1:T(8,128)(2,1)}), bf16[512,4,256]{2,0,1:T(8,128)(2,1)S(1)}, u32[]{:S(2)}, u32[]{:S(2)}) %all-to-all-start) | async-done | bytes 1048608 | tf_op jit(solution)/shard_map/all_to_all | solution.py:29
  82.3 0.2 fusion.44
  82.5 0.1 broadcast_in_dim.26
  82.5 18.7 %all_to_all.15 = bf16[512,4,256]{2,0,1:T(8,128)(2,1)} all-to-all(bf16[512,4,256]{2,0,1:T(8,128)(2,1)S(1)} %broadcast_in_dim.26), channel_id=1, replica_groups=mesh['patch'=128,'mp'=4] {'mp'}, dimensions={1} | all-to-all | bytes 2097152 | tf_op jit(solution)/shard_map/all_to_all | solution.py:39
  101.2 0.0 copy-start.4
  101.2 1.5 %copy.28 = bf16[512,4,256]{0,2,1:T(8,128)(2,1)S(1)} copy(bf16[512,4,256]{2,0,1:T(8,128)(2,1)} %all_to_all.15) | data formatting | bytes 2097152 | tf_op jit(solution)/shard_map/all_to_all | solution.py:39
  102.7 0.3 multiply_reduce_fusion
  103.0 0.0 copy-done.4
  103.0 1.3 fusion.4
  104.3 0.0 copy-done
  104.3 4.0 %convolution_convert_fusion.1 = bf16[512,1024]{1,0:T(8,128)(2,1)} fusion(bf16[512,1024]{1,0:T(8,128)(2,1)S(1)} %copy-done, bf16[512,1024]{0,1:T(8,128)(2,1)} %fusion.4, bf16[1024,512]{1,0:T(8,128)(2,1)} %param.13), kind=kOutput, calls=%fused_computation.17 | convolution fusion | flops 1076625408 | bytes 4194304 | tf_op jit(solution)/shard_map/dot_general | solution.py:133
  108.3 1.3 %copy.34 = bf16[64,4,8,256]{3,2,0,1:T(8,128)(2,1)S(1)} copy(bf16[64,4,8,256]{3,2,1,0:T(8,128)(2,1)} %bitcast.37) | data formatting | bytes 2097152 | tf_op jit(solution)/shard_map/reshape | solution.py:29
  109.6 17.2 %all_to_all.16 = bf16[512,4,256]{2,0,1:T(8,128)(2,1)S(1)} all-to-all(bf16[512,4,256]{2,0,1:T(8,128)(2,1)S(1)} %bitcast.36), channel_id=1, replica_groups=mesh['patch'=128,'mp'=4] {'mp'}, dimensions={1} | all-to-all | bytes 2097152 | tf_op jit(solution)/shard_map/all_to_all | solution.py:29
  126.8 2.0 %fusion.26 = bf16[512,256]{1,0:T(8,128)(2,1)} fusion(bf16[512,4,256]{2,0,1:T(8,128)(2,1)S(1)} %all_to_all.16, bf16[512,4,256]{2,0,1:T(8,128)(2,1)S(1)} %all-to-all-done, bf16[512,1024]{1,0:T(8,128)(2,1)} %param.8, s32[]{:T(128)S(6)} %select_n.26), kind=kLoop, calls=%fused_computation.32 | loop fusion | flops 2359296 | bytes 2621444 | tf_op jit(solution)/shard_map/convert_element_type | solution.py:135
  (4 shorter events, 0.1 us)
Async XLA Ops:
  0.0 104.3 %copy-start = (bf16[512,1024]{1,0:T(8,128)(2,1)S(1)}, bf16[512,1024]{1,0:T(8,128)(2,1)}, u32[]{:S(2)}) copy-start(bf16[512,1024]{1,0:T(8,128)(2,1)} %param.14) | copy-start | bytes 3145732
  1.6 1.7 %copy-start.1 = (bf16[512,1024]{1,0:T(8,128)(2,1)S(1)}, bf16[512,1024]{1,0:T(8,128)(2,1)}, u32[]{:S(2)}) copy-start(bf16[512,1024]{1,0:T(8,128)(2,1)} %param.8) | copy-start | bytes 3145732
  1.6 1.7 %copy-start.5 = (f32[1024]{0:T(1024)S(1)}, f32[1024]{0:T(1024)}, u32[]{:S(2)}) copy-start(f32[1024]{0:T(1024)} %param.9) | copy-start | bytes 12292
  4.4 41.8 %copy-start.2 = (bf16[512,512]{1,0:T(8,128)(2,1)}, bf16[512,512]{1,0:T(8,128)(2,1)S(1)}, u32[]{:S(2)}) copy-start(bf16[512,512]{1,0:T(8,128)(2,1)S(1)} %slice.53.refs_2_) | copy-start | bytes 1572868
  4.4 25.0 %collective-permute-start.3 = (bf16[512,512]{1,0:T(8,128)(2,1)S(1)}, bf16[512,512]{1,0:T(8,128)(2,1)}, u32[]{:S(2)}, u32[]{:S(2)}) collective-permute-start(bf16[512,512]{1,0:T(8,128)(2,1)S(1)} %slice.53.refs_2_), channel_id=1, source_target_pairs={{0,504},{4,508},{8,0},{12,4},{16,8},{20,12},{24,16},{28,20},{32,24... | collective-permute-start | bytes 1572872 | tf_op jit(solution)/shard_map/ppermute | solution.py:18
  18.8 10.9 %collective-permute-start.2 = (bf16[512,512]{1,0:T(8,128)(2,1)S(1)}, bf16[512,512]{1,0:T(8,128)(2,1)}, u32[]{:S(2)}, u32[]{:S(2)}) collective-permute-start(bf16[512,512]{1,0:T(8,128)(2,1)S(1)} %slice.53.refs_2_), channel_id=1, source_target_pairs={{0,508},{4,0},{8,4},{12,8},{16,12},{20,16},{24,20},{28,24},{32,28}... | collective-permute-start | bytes 1572872 | tf_op jit(solution)/shard_map/ppermute | solution.py:18
  21.7 11.9 %collective-permute-start.1 = (bf16[512,512]{1,0:T(8,128)(2,1)S(1)}, bf16[512,512]{1,0:T(8,128)(2,1)}, u32[]{:S(2)}, u32[]{:S(2)}) collective-permute-start(bf16[512,512]{1,0:T(8,128)(2,1)S(1)} %slice.53.refs_2_), channel_id=1, source_target_pairs={{0,4},{4,8},{8,12},{12,16},{16,20},{20,24},{24,28},{28,32},{32,36}... | collective-permute-start | bytes 1572872 | tf_op jit(solution)/shard_map/ppermute | solution.py:18
  24.4 21.8 %collective-permute-start = (bf16[512,512]{1,0:T(8,128)(2,1)S(1)}, bf16[512,512]{1,0:T(8,128)(2,1)}, u32[]{:S(2)}, u32[]{:S(2)}) collective-permute-start(bf16[512,512]{1,0:T(8,128)(2,1)S(1)} %slice.53.refs_2_), channel_id=1, source_target_pairs={{0,8},{4,12},{8,16},{12,20},{16,24},{20,28},{24,32},{28,36},{32,40... | collective-permute-start | bytes 1572872 | tf_op jit(solution)/shard_map/ppermute | solution.py:18
  28.7 33.0 %copy-start.3 = (bf16[256,1024]{1,0:T(8,128)(2,1)S(1)}, bf16[256,1024]{1,0:T(8,128)(2,1)}, u32[]{:S(2)}) copy-start(bf16[256,1024]{1,0:T(8,128)(2,1)} %param.11) | copy-start | bytes 1572868
  64.1 18.2 %all-to-all-start = ((bf16[512,4,256]{2,0,1:T(8,128)(2,1)}), bf16[512,4,256]{2,0,1:T(8,128)(2,1)S(1)}, u32[]{:S(2)}, u32[]{:S(2)}) async-start(bf16[512,4,256]{2,0,1:T(8,128)(2,1)} %bitcast.34), calls=%async_computation | async-start | bytes 2097152 | tf_op jit(solution)/shard_map/all_to_all | solution.py:29
  101.2 1.8 %copy-start.4 = (f32[1024]{0:T(1024)S(1)}, f32[1024]{0:T(1024)}, u32[]{:S(2)}) copy-start(f32[1024]{0:T(1024)} %param.12) | copy-start | bytes 12292

commit v5 on v2

--- a/solution.py
+++ b/solution.py
@@ -4,6 +4,7 @@
 import jax.numpy as jnp
 from jax import lax
 from jax.experimental import pallas as pl
+from jax.experimental.pallas import tpu as pltpu
 from jax.sharding import PartitionSpec as P
 
 D = 1024
@@ -47,40 +48,37 @@
     return lax.all_to_all(spread, "mp", 1, 1).reshape(rows, n_mp * cols)
 
 
-def window_attention(query_ref, bias_ref, *refs, n_heads, n_win):
-    kv_refs, out_ref = refs[:n_win], refs[n_win]
+def window_attention(slot_ref, query_ref, *refs, n_heads, n_win, n_nb):
+    kv_refs, out_ref, gathered = refs[:n_win], refs[n_win], refs[n_win + 1]
     width = n_heads * HD
-    win_rows = kv_refs[0].shape[0]
-    bias = bias_ref[0]
+    per_win = kv_refs[0].shape[0] // PN
+    patch = pl.program_id(0)
+    for k in range(n_nb):
+        slot = slot_ref[patch, k]
+        block = slot // per_win
+        local = slot % per_win
+        for w in range(n_win):
+            @pl.when(block == w)
+            def _():
+                gathered[k * PN:(k + 1) * PN, :] = kv_refs[w][pl.ds(pl.multiple_of(local * PN, PN), PN), :]
     lane = lax.broadcasted_iota(jnp.int32, (PN, 2 * HD), 1)
     for pair in range(n_heads // 2):
         cols = slice(pair * 2 * HD, (pair + 1) * 2 * HD)
+        v_cols = slice(width + pair * 2 * HD, width + (pair + 1) * 2 * HD)
         q_pair = query_ref[:, cols]
+        keys = gathered[:, cols]
+        vals = gathered[:, v_cols]
         mixed = []
         for half in range(2):
             keep = (lane >= half * HD) & (lane < (half + 1) * HD)
             q_head = jnp.where(keep, q_pair, jnp.zeros_like(q_pair))
-            scores = []
-            for w in range(n_win):
-                s = lax.dot_general(
-                    q_head, kv_refs[w][:, cols], (((1,), (1,)), ((), ())),
-                    preferred_element_type=jnp.float32,
-                )
-                scores.append(s * (1.0 / HD**0.5) + bias[:, w * win_rows:(w + 1) * win_rows])
-            top = scores[0].max(axis=1, keepdims=True)
-            for s in scores[1:]:
-                top = jnp.maximum(top, s.max(axis=1, keepdims=True))
-            exps = [jnp.exp(s - top) for s in scores]
-            total = exps[0].sum(axis=1, keepdims=True)
-            for e in exps[1:]:
-                total = total + e.sum(axis=1, keepdims=True)
-            acc = None
-            for w in range(n_win):
-                probs = (exps[w] / total).astype(jnp.bfloat16)
-                v_cols = slice(width + pair * 2 * HD, width + (pair + 1) * 2 * HD)
-                term = jnp.dot(probs, kv_refs[w][:, v_cols], preferred_element_type=jnp.float32)
-                acc = term if acc is None else acc + term
-            mixed.append(acc)
+            s = lax.dot_general(
+                q_head, keys, (((1,), (1,)), ((), ())), preferred_element_type=jnp.float32
+            ) * (1.0 / HD**0.5)
+            e = jnp.exp(s - s.max(axis=1, keepdims=True))
+            inv = 1.0 / e.sum(axis=1, keepdims=True)
+            probs = (e * inv).astype(jnp.bfloat16)
+            mixed.append(jnp.dot(probs, vals, preferred_element_type=jnp.float32))
         out = jnp.where(lane < HD, mixed[0], mixed[1])
         out_ref[:, cols] = out.astype(out_ref.dtype)
 
@@ -106,23 +104,19 @@
     owner_dev = listed // patches_here
     offset_dev = jnp.mod(owner_dev - device + n_dev // 2, n_dev) - n_dev // 2
     slot_index = (offset_dev + REACH) * patches_here + jnp.mod(listed, patches_here)
-    slots = jnp.arange(n_win * patches_here, dtype=jnp.int32)
-    chosen = jnp.any(slot_index[:, :, None] == slots[None, None, :], axis=1)
-    bias = jnp.where(chosen, 0.0, -jnp.inf).astype(jnp.float32)
-    bias = jnp.repeat(bias, PN, axis=1).reshape(patches_here, 1, n_win * patches_here * PN)
     kv_list = [window[offset] for offset in range(-REACH, REACH + 1)]
-    kv_spec = pl.BlockSpec((row_count, 2 * width), lambda p: (0, 0))
+    kv_spec = pl.BlockSpec((row_count, 2 * width), lambda p, slots: (0, 0))
     attended = pl.pallas_call(
-        functools.partial(window_attention, n_heads=heads_here, n_win=n_win),
-        grid=(patches_here,),
-        in_specs=[
-            pl.BlockSpec((PN, width), lambda p: (p, 0)),
-            pl.BlockSpec((1, 1, n_win * row_count), lambda p: (p, 0, 0)),
-        ]
-        + [kv_spec] * n_win,
-        out_specs=pl.BlockSpec((PN, width), lambda p: (p, 0)),
+        functools.partial(window_attention, n_heads=heads_here, n_win=n_win, n_nb=K_NB),
+        grid_spec=pltpu.PrefetchScalarGridSpec(
+            num_scalar_prefetch=1,
+            grid=(patches_here,),
+            in_specs=[pl.BlockSpec((PN, width), lambda p, slots: (p, 0))] + [kv_spec] * n_win,
+            out_specs=pl.BlockSpec((PN, width), lambda p, slots: (p, 0)),
+            scratch_shapes=[pltpu.VMEM((K_NB * PN, 2 * width), jnp.bfloat16)],
+        ),
         out_shape=jax.ShapeDtypeStruct((row_count, width), jnp.bfloat16),
-    )(queries, bias, *kv_list)
+    )(slot_index.astype(jnp.int32), queries, *kv_list)
     n_mp = lax.axis_size("mp")
     partial_value = jnp.dot(attended, w_out, preferred_element_type=jnp.float32)
     col_share = scatter_sum(partial_value.astype(jnp.bfloat16), n_mp)

time: 114 us -> 111 us (0.974)
  Pallas kernels: 15.5 us -> 12.4 us
    pallas_call x1, Pallas kernels: 15.5 us -> 12.4 us  [per_device(): pl.pallas_call(functools.partial(window_attention, n_heads=heads_here, n_...]
where the time goes in v5:
time: 111 us
  starting transfers between devices  30.8 us (28%)
  blocking collectives  26.6 us (24%)
  waiting for transfers between devices  25 us (23%)
  Pallas kernels  12.4 us (11%)
  local copies, waits for them, and re-layouts  7.24 us (7%)
  matrix products  5.36 us (5%)
  other arithmetic  3.1 us (3%)
    ppermute x4, starting transfers between devices, from_behind(): lax.ppermute(array, axis, [(i, (i + by) % length) for i in range(length)])  21.3 us
    all_to_all x1, blocking collectives, gather_cols(): return lax.all_to_all(spread, 'mp', 1, 1).reshape(rows, n_mp * cols)  13.3 us
    all_to_all x1, blocking collectives, scatter_sum(): got = lax.all_to_all(parts.reshape(rows, n_mp, cols // n_mp), 'mp', 1, 1)  13.3 us
    pallas_call x1, Pallas kernels, per_device(): pl.pallas_call(functools.partial(window_attention, n_heads=heads_here, n_...  12.4 us
    ppermute x4, waiting for transfers between devices, from_behind(): lax.ppermute(array, axis, [(i, (i + by) % length) for i in range(length)])  11.5 us
    all_to_all x1, waiting for transfers between devices, scatter_sum(): got = lax.all_to_all(parts.reshape(rows, n_mp, cols // n_mp), 'mp', 1, 1)  10.3 us
    all_to_all x1, starting transfers between devices, scatter_sum(): got = lax.all_to_all(parts.reshape(rows, n_mp, cols // n_mp), 'mp', 1, 1)  4.82 us
    all_to_all x1, starting transfers between devices, gather_sum(): lax.all_to_all(jnp.broadcast_to(vector[None], (n_mp,) + vector.shape), 'm...  4.68 us
  transfers between devices with their start and end apart: 6, of which 5 were waited for; matrix products, arithmetic and copies ran while one was open for 3% of the time, Pallas kernels for 0%

profile of v5, /device:TPU:2, one launch (start us, length us, event | category | flops | bytes accessed | tf_op | source)
XLA Modules:
  0.0 110.7 jit_solution(13409212813447234831)
XLA Ops:
  0.0 0.0 copy-start
  0.0 0.0 copy-start.2
  0.0 0.0 copy-start.6
  0.0 1.6 %slice_bitcast_fusion.2 = (bf16[1024,256]{1,0:T(8,128)(2,1)S(1)}, bf16[1024,256]{1,0:T(8,128)(2,1)S(1)}, bf16[1024,256]{1,0:T(8,128)(2,1)S(1)}) fusion(bf16[3,1024,256]{2,1,0:T(8,128)(2,1)} %param.10), kind=kLoop, calls=%fused_computation.38 | loop fusion | bytes 3145728 | tf_op jit(solution)/shard_map/squeeze | solution.py:93
  1.6 0.2 copy-done.2
  1.8 0.3 fusion
  2.1 0.0 copy-done.6
  2.1 1.0 fusion.9
  3.2 0.0 copy-start.1
  3.2 3.5 %collective-permute-start = (bf16[512,512]{1,0:T(8,128)(2,1)S(1)}, bf16[512,512]{1,0:T(8,128)(2,1)S(1)}, u32[]{:S(2)}, u32[]{:S(2)}) collective-permute-start(bf16[512,512]{1,0:T(8,128)(2,1)S(1)} %slice.73.refs_2_), channel_id=1, source_target_pairs={{0,8},{4,12},{8,16},{12,20},{16,24},{20,28},{24,32},{28,36},{32,40... | collective-permute-start | bytes 1572872 | tf_op jit(solution)/shard_map/ppermute | solution.py:19
  6.7 1.9 %collective-permute-start.1 = (bf16[512,512]{1,0:T(8,128)(2,1)S(1)}, bf16[512,512]{1,0:T(8,128)(2,1)S(1)}, u32[]{:S(2)}, u32[]{:S(2)}) collective-permute-start(bf16[512,512]{1,0:T(8,128)(2,1)S(1)} %slice.73.refs_2_), channel_id=1, source_target_pairs={{0,4},{4,8},{8,12},{12,16},{16,20},{20,24},{24,28},{28,32},{32,36}... | collective-permute-start | bytes 1572872 | tf_op jit(solution)/shard_map/ppermute | solution.py:19
  8.6 11.7 %collective-permute-start.2 = (bf16[512,512]{1,0:T(8,128)(2,1)S(1)}, bf16[512,512]{1,0:T(8,128)(2,1)}, u32[]{:S(2)}, u32[]{:S(2)}) collective-permute-start(bf16[512,512]{1,0:T(8,128)(2,1)S(1)} %slice.73.refs_2_), channel_id=1, source_target_pairs={{0,508},{4,0},{8,4},{12,8},{16,12},{20,16},{24,20},{28,24},{32,28}... | collective-permute-start | bytes 1572872 | tf_op jit(solution)/shard_map/ppermute | solution.py:19
  20.3 4.2 %collective-permute-start.3 = (bf16[512,512]{1,0:T(8,128)(2,1)S(1)}, bf16[512,512]{1,0:T(8,128)(2,1)}, u32[]{:S(2)}, u32[]{:S(2)}) collective-permute-start(bf16[512,512]{1,0:T(8,128)(2,1)S(1)} %slice.73.refs_2_), channel_id=1, source_target_pairs={{0,504},{4,508},{8,0},{12,4},{16,8},{20,12},{24,16},{28,20},{32,24... | collective-permute-start | bytes 1572872 | tf_op jit(solution)/shard_map/ppermute | solution.py:19
  24.6 0.7 slice.72.query_ref
  25.3 0.8 constant_dynamic-slice_fusion
  26.0 0.1 copy.19
  26.1 0.6 fusion.34.slot_ref
  26.7 0.0 copy-start.3
  26.7 3.1 %collective-permute-done.refs_0_ = bf16[512,512]{1,0:T(8,128)(2,1)S(1)} collective-permute-done((bf16[512,512]{1,0:T(8,128)(2,1)S(1)}, bf16[512,512]{1,0:T(8,128)(2,1)S(1)}, u32[]{:S(2)}, u32[]{:S(2)}) %collective-permute-start) | collective-permute-done | bytes 524320 | tf_op jit(solution)/shard_map/ppermute | solution.py:19
  29.8 0.0 copy-start.4
  29.8 4.8 %collective-permute-done.1.refs_1_ = bf16[512,512]{1,0:T(8,128)(2,1)S(1)} collective-permute-done((bf16[512,512]{1,0:T(8,128)(2,1)S(1)}, bf16[512,512]{1,0:T(8,128)(2,1)S(1)}, u32[]{:S(2)}, u32[]{:S(2)}) %collective-permute-start.1) | collective-permute-done | bytes 524320 | tf_op jit(solution)/shard_map/ppermute | solution.py:19
  34.6 0.0 copy-start.5
  34.6 0.0 collective-permute-done.2.refs_3_
  34.6 3.7 %collective-permute-done.3.refs_4_ = bf16[512,512]{1,0:T(8,128)(2,1)} collective-permute-done((bf16[512,512]{1,0:T(8,128)(2,1)S(1)}, bf16[512,512]{1,0:T(8,128)(2,1)}, u32[]{:S(2)}, u32[]{:S(2)}) %collective-permute-start.3) | collective-permute-done | bytes 524320 | tf_op jit(solution)/shard_map/ppermute | solution.py:19
  38.3 0.0 copy-done.1
  38.3 0.0 copy-done.4
  38.3 0.0 copy-done.5
  38.3 12.4 %shard_map.82 = bf16[512,256]{1,0:T(8,128)(2,1)} custom-call(s32[4,8]{1,0:T(4,128)} %fusion.34.slot_ref, bf16[512,256]{1,0:T(8,128)(2,1)} %slice.72.query_ref, bf16[512,512]{1,0:T(8,128)(2,1)} %copy-done.4, bf16[512,512]{1,0:T(8,128)(2,1)} %copy-done.5, bf16[512,512]{1,0:T(8,128)(2,1)} %copy-done.1, bf16[512,512]{1,0:T(8,128)(2,1)} %collective-permute-done.2.refs_3_, ...), custom_call_target="tpu_custom_call" | custom-call | tf_op jit(solution)/shard_map/pallas_call | solution.py:109
  50.7 0.0 copy-done.3
  50.7 1.4 %convolution_convert_fusion = bf16[512,1024]{1,0:T(8,128)(2,1)S(1)} fusion(bf16[512,256]{1,0:T(8,128)(2,1)} %shard_map.82, bf16[256,1024]{1,0:T(8,128)(2,1)S(1)} %copy-done.3), kind=kOutput, calls=%fused_computation.12 | convolution fusion | flops 268959744 | bytes 1835008 | tf_op jit(solution)/shard_map/dot_general | solution.py:121
  52.1 1.0 copy.25
  53.1 4.8 %all-to-all-start = ((bf16[512,4,256]{2,0,1:T(8,128)(2,1)}), bf16[512,4,256]{2,0,1:T(8,128)(2,1)S(1)}, u32[]{:S(2)}, u32[]{:S(2)}) async-start(bf16[512,4,256]{2,0,1:T(8,128)(2,1)} %bitcast.29), calls=%async_computation | async-start | bytes 2097152 | tf_op jit(solution)/shard_map/all_to_all | solution.py:30
  57.9 10.3 %all-to-all-done = bf16[512,4,256]{2,0,1:T(8,128)(2,1)S(1)} async-done(((bf16[512,4,256]{2,0,1:T(8,128)(2,1)}), bf16[512,4,256]{2,0,1:T(8,128)(2,1)S(1)}, u32[]{:S(2)}, u32[]{:S(2)}) %all-to-all-start) | async-done | bytes 1048608 | tf_op jit(solution)/shard_map/all_to_all | solution.py:30
  68.3 1.2 %multiply_reduce_fusion = (f32[512]{0:T(512)S(1)}, f32[512,256]{1,0:T(8,128)S(1)}) fusion(bf16[512,4,256]{2,0,1:T(8,128)(2,1)S(1)} %all-to-all-done, bf16[512,1024]{1,0:T(8,128)(2,1)} %param.8, s32[]{:T(128)S(6)} %select_n.23), kind=kLoop, calls=%fused_computation.35 | loop fusion | flops 1441280 | bytes 1837060 | tf_op jit(solution)/shard_map/reduce_sum | solution.py:129
  69.5 0.6 broadcast_in_dim.4
  70.1 4.7 %all-to-all-start.1 = ((f32[4,1,512]{2,1,0:T(1,128)}), f32[4,1,512]{2,1,0:T(1,128)S(1)}, u32[]{:S(2)}, u32[]{:S(2)}) async-start(f32[4,1,512]{2,1,0:T(1,128)} %broadcast_in_dim.4), calls=%async_computation.1 | async-start | bytes 16384 | tf_op jit(solution)/shard_map/all_to_all | solution.py:38
  74.8 0.8 dynamic_slice.11
  75.5 3.1 %all-to-all-done.1 = f32[4,1,512]{2,1,0:T(1,128)S(1)} async-done(((f32[4,1,512]{2,1,0:T(1,128)}), f32[4,1,512]{2,1,0:T(1,128)S(1)}, u32[]{:S(2)}, u32[]{:S(2)}) %all-to-all-start.1) | async-done | bytes 8224 | tf_op jit(solution)/shard_map/all_to_all | solution.py:38
  78.7 0.1 multiply_convert_fusion
  78.8 0.1 broadcast_in_dim.5
  78.9 13.3 %all_to_all.21 = bf16[512,4,256]{2,0,1:T(8,128)(2,1)S(1)} all-to-all(bf16[512,4,256]{2,0,1:T(8,128)(2,1)S(1)} %broadcast_in_dim.5), channel_id=1, replica_groups=mesh['patch'=128,'mp'=4] {'mp'}, dimensions={1} | all-to-all | bytes 2097152 | tf_op jit(solution)/shard_map/all_to_all | solution.py:48
  92.2 1.3 %copy.17 = bf16[512,4,256]{0,2,1:T(8,128)(2,1)} copy(bf16[512,4,256]{2,0,1:T(8,128)(2,1)S(1)} %all_to_all.21) | data formatting | bytes 2097152 | tf_op jit(solution)/shard_map/all_to_all | solution.py:48
  93.5 0.0 copy-done
  93.5 2.9 %convolution_convert_fusion.1 = bf16[512,1024]{1,0:T(8,128)(2,1)S(1)} fusion(bf16[512,1024]{1,0:T(8,128)(2,1)S(1)} %copy-done, bf16[512,1024]{0,1:T(8,128)(2,1)} %bitcast.31, bf16[1024,512]{1,0:T(8,128)(2,1)} %param.13), kind=kOutput, calls=%fused_computation.13 | convolution fusion | flops 1076625408 | bytes 4194304 | tf_op jit(solution)/shard_map/dot_general | solution.py:136
  96.4 0.1 copy.24
  96.5 13.3 %all_to_all.22 = bf16[512,4,256]{2,0,1:T(8,128)(2,1)S(1)} all-to-all(bf16[512,4,256]{2,0,1:T(8,128)(2,1)S(1)} %bitcast.30), channel_id=1, replica_groups=mesh['patch'=128,'mp'=4] {'mp'}, dimensions={1} | all-to-all | bytes 2097152 | tf_op jit(solution)/shard_map/all_to_all | solution.py:30
  109.8 0.8 fusion.24
  (3 shorter events, 0.1 us)
Async XLA Ops:
  0.0 93.5 %copy-start = (bf16[512,1024]{1,0:T(8,128)(2,1)S(1)}, bf16[512,1024]{1,0:T(8,128)(2,1)}, u32[]{:S(2)}) copy-start(bf16[512,1024]{1,0:T(8,128)(2,1)} %param.14) | copy-start | bytes 3145732
  0.0 1.8 %copy-start.2 = (bf16[512,1024]{1,0:T(8,128)(2,1)S(1)}, bf16[512,1024]{1,0:T(8,128)(2,1)}, u32[]{:S(2)}) copy-start(bf16[512,1024]{1,0:T(8,128)(2,1)} %param.8) | copy-start | bytes 3145732
  0.0 2.1 %copy-start.6 = (f32[1024]{0:T(1024)S(1)}, f32[1024]{0:T(1024)}, u32[]{:S(2)}) copy-start(f32[1024]{0:T(1024)} %param.9) | copy-start | bytes 12292
  3.2 35.1 %copy-start.1 = (bf16[512,512]{1,0:T(8,128)(2,1)}, bf16[512,512]{1,0:T(8,128)(2,1)S(1)}, u32[]{:S(2)}) copy-start(bf16[512,512]{1,0:T(8,128)(2,1)S(1)} %slice.73.refs_2_) | copy-start | bytes 1572868
  3.2 26.6 %collective-permute-start = (bf16[512,512]{1,0:T(8,128)(2,1)S(1)}, bf16[512,512]{1,0:T(8,128)(2,1)S(1)}, u32[]{:S(2)}, u32[]{:S(2)}) collective-permute-start(bf16[512,512]{1,0:T(8,128)(2,1)S(1)} %slice.73.refs_2_), channel_id=1, source_target_pairs={{0,8},{4,12},{8,16},{12,20},{16,24},{20,28},{24,32},{28,36},{32,40... | collective-permute-start | bytes 1572872 | tf_op jit(solution)/shard_map/ppermute | solution.py:19
  6.7 27.9 %collective-permute-start.1 = (bf16[512,512]{1,0:T(8,128)(2,1)S(1)}, bf16[512,512]{1,0:T(8,128)(2,1)S(1)}, u32[]{:S(2)}, u32[]{:S(2)}) collective-permute-start(bf16[512,512]{1,0:T(8,128)(2,1)S(1)} %slice.73.refs_2_), channel_id=1, source_target_pairs={{0,4},{4,8},{8,12},{12,16},{16,20},{20,24},{24,28},{28,32},{32,36}... | collective-permute-start | bytes 1572872 | tf_op jit(solution)/shard_map/ppermute | solution.py:19
  8.6 26.0 %collective-permute-start.2 = (bf16[512,512]{1,0:T(8,128)(2,1)S(1)}, bf16[512,512]{1,0:T(8,128)(2,1)}, u32[]{:S(2)}, u32[]{:S(2)}) collective-permute-start(bf16[512,512]{1,0:T(8,128)(2,1)S(1)} %slice.73.refs_2_), channel_id=1, source_target_pairs={{0,508},{4,0},{8,4},{12,8},{16,12},{20,16},{24,20},{28,24},{32,28}... | collective-permute-start | bytes 1572872 | tf_op jit(solution)/shard_map/ppermute | solution.py:19
  20.3 17.9 %collective-permute-start.3 = (bf16[512,512]{1,0:T(8,128)(2,1)S(1)}, bf16[512,512]{1,0:T(8,128)(2,1)}, u32[]{:S(2)}, u32[]{:S(2)}) collective-permute-start(bf16[512,512]{1,0:T(8,128)(2,1)S(1)} %slice.73.refs_2_), channel_id=1, source_target_pairs={{0,504},{4,508},{8,0},{12,4},{16,8},{20,12},{24,16},{28,20},{32,24... | collective-permute-start | bytes 1572872 | tf_op jit(solution)/shard_map/ppermute | solution.py:19
  26.7 24.0 %copy-start.3 = (bf16[256,1024]{1,0:T(8,128)(2,1)S(1)}, bf16[256,1024]{1,0:T(8,128)(2,1)}, u32[]{:S(2)}) copy-start(bf16[256,1024]{1,0:T(8,128)(2,1)} %param.11) | copy-start | bytes 1572868
  29.8 8.5 %copy-start.4 = (bf16[512,512]{1,0:T(8,128)(2,1)}, bf16[512,512]{1,0:T(8,128)(2,1)S(1)}, u32[]{:S(2)}) copy-start(bf16[512,512]{1,0:T(8,128)(2,1)S(1)} %collective-permute-done.refs_0_) | copy-start | bytes 1572868
  34.6 3.7 %copy-start.5 = (bf16[512,512]{1,0:T(8,128)(2,1)}, bf16[512,512]{1,0:T(8,128)(2,1)S(1)}, u32[]{:S(2)}) copy-start(bf16[512,512]{1,0:T(8,128)(2,1)S(1)} %collective-permute-done.1.refs_1_) | copy-start | bytes 1572868
  53.1 15.2 %all-to-all-start = ((bf16[512,4,256]{2,0,1:T(8,128)(2,1)}), bf16[512,4,256]{2,0,1:T(8,128)(2,1)S(1)}, u32[]{:S(2)}, u32[]{:S(2)}) async-start(bf16[512,4,256]{2,0,1:T(8,128)(2,1)} %bitcast.29), calls=%async_computation | async-start | bytes 2097152 | tf_op jit(solution)/shard_map/all_to_all | solution.py:30
  70.1 8.5 %all-to-all-start.1 = ((f32[4,1,512]{2,1,0:T(1,128)}), f32[4,1,512]{2,1,0:T(1,128)S(1)}, u32[]{:S(2)}, u32[]{:S(2)}) async-start(f32[4,1,512]{2,1,0:T(1,128)} %broadcast_in_dim.4), calls=%async_computation.1 | async-start | bytes 16384 | tf_op jit(solution)/shard_map/all_to_all | solution.py:38

commit v6 on v5

--- a/solution.py
+++ b/solution.py
@@ -12,6 +12,7 @@
 PN = 128
 K_NB = 8
 REACH = 2
+N_CHUNK = 2
 
 
 def from_behind(array, axis, by):
@@ -105,27 +106,38 @@
     offset_dev = jnp.mod(owner_dev - device + n_dev // 2, n_dev) - n_dev // 2
     slot_index = (offset_dev + REACH) * patches_here + jnp.mod(listed, patches_here)
     kv_list = [window[offset] for offset in range(-REACH, REACH + 1)]
-    kv_spec = pl.BlockSpec((row_count, 2 * width), lambda p, slots: (0, 0))
-    attended = pl.pallas_call(
-        functools.partial(window_attention, n_heads=heads_here, n_win=n_win, n_nb=K_NB),
-        grid_spec=pltpu.PrefetchScalarGridSpec(
-            num_scalar_prefetch=1,
-            grid=(patches_here,),
-            in_specs=[pl.BlockSpec((PN, width), lambda p, slots: (p, 0))] + [kv_spec] * n_win,
-            out_specs=pl.BlockSpec((PN, width), lambda p, slots: (p, 0)),
-            scratch_shapes=[pltpu.VMEM((K_NB * PN, 2 * width), jnp.bfloat16)],
-        ),
-        out_shape=jax.ShapeDtypeStruct((row_count, width), jnp.bfloat16),
-    )(slot_index.astype(jnp.int32), queries, *kv_list)
     n_mp = lax.axis_size("mp")
+    col_width = D // n_mp
+    col_begin = lax.axis_index("mp") * col_width
+    gain_cols = lax.dynamic_slice_in_dim(gain_mlp, col_begin, col_width, 0)
+    feature_cols = lax.dynamic_slice_in_dim(features, col_begin, col_width, 1)
+    chunk_patches = patches_here // N_CHUNK
+    chunk_rows = chunk_patches * PN
+    outs = []
+    for chunk in range(N_CHUNK):
+        first = chunk * chunk_patches
+        kv_spec = pl.BlockSpec((row_count, 2 * width), lambda p, slots: (0, 0))
+        attended = pl.pallas_call(
+            functools.partial(window_attention, n_heads=heads_here, n_win=n_win, n_nb=K_NB),
+            grid_spec=pltpu.PrefetchScalarGridSpec(
+                num_scalar_prefetch=1,
+                grid=(chunk_patches,),
+                in_specs=[pl.BlockSpec((PN, width), lambda p, slots, f=first: (p + f, 0))]
+                + [kv_spec] * n_win,
+                out_specs=pl.BlockSpec((PN, width), lambda p, slots: (p, 0)),
+                scratch_shapes=[pltpu.VMEM((K_NB * PN, 2 * width), jnp.bfloat16)],
+            ),
+            out_shape=jax.ShapeDtypeStruct((chunk_rows, width), jnp.bfloat16),
+        )(slot_index[first:first + chunk_patches].astype(jnp.int32), queries, *kv_list)
+        rows = slice(chunk * chunk_rows, (chunk + 1) * chunk_rows)
+        outs.append(mlp_part(attended, feature_cols[rows], gain_cols, w_out, w_up, w_down, n_mp))
+    return jnp.concatenate(outs, axis=0)
+
+
+def mlp_part(attended, feature_cols, gain_cols, w_out, w_up, w_down, n_mp):
     partial_value = jnp.dot(attended, w_out, preferred_element_type=jnp.float32)
     col_share = scatter_sum(partial_value.astype(jnp.bfloat16), n_mp)
-    col_width = col_share.shape[1]
-    col_begin = lax.axis_index("mp") * col_width
-    residual_cols = (
-        lax.dynamic_slice_in_dim(features, col_begin, col_width, 1).astype(jnp.float32) + col_share
-    )
-    gain_cols = lax.dynamic_slice_in_dim(gain_mlp, col_begin, col_width, 0)
+    residual_cols = feature_cols.astype(jnp.float32) + col_share
     square_sum = gather_sum(jnp.sum(residual_cols * residual_cols, axis=1), n_mp)
     inverse_rms = lax.rsqrt(square_sum / D + 1e-05)
     normed_cols = (residual_cols * inverse_rms[:, None] * gain_cols).astype(jnp.bfloat16)

time: 111 us -> 148 us (1.33)
  starting transfers between devices: 30.8 us -> 54.4 us
  waiting for transfers between devices: 25 us -> 44.4 us
  blocking collectives: 26.6 us -> 10.5 us
  local copies, waits for them, and re-layouts: 7.24 us -> 10.5 us
  Pallas kernels: 12.4 us -> 15.4 us
  matrix products: 5.36 us -> 7.72 us
    all_to_all x1 -> x4, starting transfers between devices: 4.82 us -> 19.4 us  [scatter_sum(): got = lax.all_to_all(parts.reshape(rows, n_mp, cols // n_mp), 'mp', 1, 1)]
    all_to_all x1 -> x0, blocking collectives: 13.3 us -> none  [scatter_sum(): got = lax.all_to_all(parts.reshape(rows, n_mp, cols // n_mp), 'mp', 1, 1)]
    all_to_all x1 -> x4, waiting for transfers between devices: 10.3 us -> 18.8 us  [scatter_sum(): got = lax.all_to_all(parts.reshape(rows, n_mp, cols // n_mp), 'mp', 1, 1)]
    all_to_all x0 -> x1, starting transfers between devices: none -> 4.89 us  [gather_cols(): return lax.all_to_all(spread, 'mp', 1, 1).reshape(rows, n_mp * cols)]
    all_to_all x1 -> x2, starting transfers between devices: 4.68 us -> 9.35 us  [gather_sum(): lax.all_to_all(jnp.broadcast_to(vector[None], (n_mp,) + vector.shape), 'm...]
    all_to_all x1 -> x2, waiting for transfers between devices: 3.1 us -> 6.91 us  [gather_sum(): lax.all_to_all(jnp.broadcast_to(vector[None], (n_mp,) + vector.shape), 'm...]
    ppermute x4, waiting for transfers between devices: 11.5 us -> 15.3 us  [from_behind(): lax.ppermute(array, axis, [(i, (i + by) % length) for i in range(length)])]
    all_to_all x0 -> x1, waiting for transfers between devices: none -> 3.44 us  [gather_cols(): return lax.all_to_all(spread, 'mp', 1, 1).reshape(rows, n_mp * cols)]
  transfers between devices with their start and end apart: 6 -> 11, of which waited for: 5 -> 10; matrix products, arithmetic and copies ran while one was open for 3% -> 8% of each run, Pallas kernels for 0% -> 5%
where the time goes in v6:
time: 148 us; the launch traced here: 147 us
  starting transfers between devices  54.4 us (37%)
  waiting for transfers between devices  44.4 us (30%)
  Pallas kernels  15.4 us (10%)
  local copies, waits for them, and re-layouts  10.5 us (7%)
  blocking collectives  10.5 us (7%)
  matrix products  7.72 us (5%)
  other arithmetic  3.89 us (3%)
    ppermute x4, starting transfers between devices, from_behind(): lax.ppermute(array, axis, [(i, (i + by) % length) for i in range(length)])  20.8 us
    all_to_all x4, starting transfers between devices, scatter_sum(): got = lax.all_to_all(parts.reshape(rows, n_mp, cols // n_mp), 'mp', 1, 1)  19.4 us
    all_to_all x4, waiting for transfers between devices, scatter_sum(): got = lax.all_to_all(parts.reshape(rows, n_mp, cols // n_mp), 'mp', 1, 1)  18.8 us
    pallas_call x2, Pallas kernels, per_device(): pl.pallas_call(functools.partial(window_attention, n_heads=heads_here, n_...  15.4 us
    ppermute x4, waiting for transfers between devices, from_behind(): lax.ppermute(array, axis, [(i, (i + by) % length) for i in range(length)])  15.3 us
    all_to_all x1, blocking collectives, gather_cols(): return lax.all_to_all(spread, 'mp', 1, 1).reshape(rows, n_mp * cols)  10.5 us
    all_to_all x2, starting transfers between devices, gather_sum(): lax.all_to_all(jnp.broadcast_to(vector[None], (n_mp,) + vector.shape), 'm...  9.35 us
    all_to_all x2, waiting for transfers between devices, gather_sum(): lax.all_to_all(jnp.broadcast_to(vector[None], (n_mp,) + vector.shape), 'm...  6.91 us
  transfers between devices with their start and end apart: 11, of which 10 were waited for; matrix products, arithmetic and copies ran while one was open for 8% of the time, Pallas kernels for 5%

profile of v6, /device:TPU:2, one launch (start us, length us, event | category | flops | bytes accessed | tf_op | source)
XLA Modules:
  0.0 147.0 jit_solution(11299351778373344351)
XLA Ops:
  0.0 1.6 %fusion = f32[512]{0:T(512)S(1)} fusion(bf16[512,1024]{1,0:T(8,128)(2,1)} %param.8), kind=kLoop, calls=%fused_computation.2 | loop fusion | flops 1572352 | bytes 1050624 | tf_op jit(solution)/shard_map/reduce_sum | solution.py:25
  1.6 1.5 %slice_bitcast_fusion.2 = (bf16[1024,256]{1,0:T(8,128)(2,1)S(1)}, bf16[1024,256]{1,0:T(8,128)(2,1)S(1)}, bf16[1024,256]{1,0:T(8,128)(2,1)S(1)}) fusion(bf16[3,1024,256]{2,1,0:T(8,128)(2,1)} %param.10), kind=kLoop, calls=%fused_computation.42 | loop fusion | bytes 3145728 | tf_op jit(solution)/shard_map/squeeze | solution.py:94
  3.2 0.1 copy-done.5
  3.3 1.0 fusion.9
  4.4 13.9 %collective-permute-start.3 = (bf16[512,512]{1,0:T(8,128)(2,1)S(1)}, bf16[512,512]{1,0:T(8,128)(2,1)S(1)}, u32[]{:S(2)}, u32[]{:S(2)}) collective-permute-start(bf16[512,512]{1,0:T(8,128)(2,1)S(1)} %slice.141.refs_2_), channel_id=1, source_target_pairs={{0,504},{4,508},{8,0},{12,4},{16,8},{20,12},{24,16},{28,20},{32,24... | collective-permute-start | bytes 1572872 | tf_op jit(solution)/shard_map/ppermute | solution.py:20
  18.3 1.9 %collective-permute-start.2 = (bf16[512,512]{1,0:T(8,128)(2,1)S(1)}, bf16[512,512]{1,0:T(8,128)(2,1)S(1)}, u32[]{:S(2)}, u32[]{:S(2)}) collective-permute-start(bf16[512,512]{1,0:T(8,128)(2,1)S(1)} %slice.141.refs_2_), channel_id=1, source_target_pairs={{0,508},{4,0},{8,4},{12,8},{16,12},{20,16},{24,20},{28,24},{32,28}... | collective-permute-start | bytes 1572872 | tf_op jit(solution)/shard_map/ppermute | solution.py:20
  20.2 2.4 %collective-permute-start.1 = (bf16[512,512]{1,0:T(8,128)(2,1)S(1)}, bf16[512,512]{1,0:T(8,128)(2,1)}, u32[]{:S(2)}, u32[]{:S(2)}) collective-permute-start(bf16[512,512]{1,0:T(8,128)(2,1)S(1)} %slice.141.refs_2_), channel_id=1, source_target_pairs={{0,4},{4,8},{8,12},{12,16},{16,20},{20,24},{24,28},{28,32},{32,36}... | collective-permute-start | bytes 1572872 | tf_op jit(solution)/shard_map/ppermute | solution.py:20
  22.6 2.6 %collective-permute-start = (bf16[512,512]{1,0:T(8,128)(2,1)S(1)}, bf16[512,512]{1,0:T(8,128)(2,1)}, u32[]{:S(2)}, u32[]{:S(2)}) collective-permute-start(bf16[512,512]{1,0:T(8,128)(2,1)S(1)} %slice.141.refs_2_), channel_id=1, source_target_pairs={{0,8},{4,12},{8,16},{12,20},{16,24},{20,28},{24,32},{28,36},{32,40... | collective-permute-start | bytes 1572872 | tf_op jit(solution)/shard_map/ppermute | solution.py:20
  25.2 0.7 slice.140.query_ref
  25.9 0.8 constant_dynamic-slice_fusion
  26.9 0.6 fusion.61
  27.5 2.0 %collective-permute-done.3.refs_4_ = bf16[512,512]{1,0:T(8,128)(2,1)S(1)} collective-permute-done((bf16[512,512]{1,0:T(8,128)(2,1)S(1)}, bf16[512,512]{1,0:T(8,128)(2,1)S(1)}, u32[]{:S(2)}, u32[]{:S(2)}) %collective-permute-start.3) | collective-permute-done | bytes 524320 | tf_op jit(solution)/shard_map/ppermute | solution.py:20
  29.4 5.6 %collective-permute-done.2.refs_3_ = bf16[512,512]{1,0:T(8,128)(2,1)S(1)} collective-permute-done((bf16[512,512]{1,0:T(8,128)(2,1)S(1)}, bf16[512,512]{1,0:T(8,128)(2,1)S(1)}, u32[]{:S(2)}, u32[]{:S(2)}) %collective-permute-start.2) | collective-permute-done | bytes 524320 | tf_op jit(solution)/shard_map/ppermute | solution.py:20
  35.0 1.7 %collective-permute-done.1.refs_1_ = bf16[512,512]{1,0:T(8,128)(2,1)} collective-permute-done((bf16[512,512]{1,0:T(8,128)(2,1)S(1)}, bf16[512,512]{1,0:T(8,128)(2,1)}, u32[]{:S(2)}, u32[]{:S(2)}) %collective-permute-start.1) | collective-permute-done | bytes 524320 | tf_op jit(solution)/shard_map/ppermute | solution.py:20
  36.7 6.0 %collective-permute-done.refs_0_ = bf16[512,512]{1,0:T(8,128)(2,1)} collective-permute-done((bf16[512,512]{1,0:T(8,128)(2,1)S(1)}, bf16[512,512]{1,0:T(8,128)(2,1)}, u32[]{:S(2)}, u32[]{:S(2)}) %collective-permute-start) | collective-permute-done | bytes 524320 | tf_op jit(solution)/shard_map/ppermute | solution.py:20
  42.7 7.7 %shard_map.82 = bf16[256,256]{1,0:T(8,128)(2,1)} custom-call(s32[2,8]{1,0:T(2,128)} %get-tuple-element.14.slot_ref, bf16[512,256]{1,0:T(8,128)(2,1)} %slice.140.query_ref, bf16[512,512]{1,0:T(8,128)(2,1)} %collective-permute-done.refs_0_, bf16[512,512]{1,0:T(8,128)(2,1)} %collective-permute-done.1.refs_1_, bf16[512,512]{1,0:T(8,128)(2,1)} %copy-done.1, ...), custom_call_target="tpu_custom_call" | custom-call | tf_op jit(solution)/shard_map/pallas_call | solution.py:120
  50.4 1.2 convolution_convert_fusion.3
  51.7 0.8 copy.38
  52.5 4.8 %all-to-all-start = ((bf16[256,4,256]{2,0,1:T(8,128)(2,1)}), bf16[256,4,256]{2,0,1:T(8,128)(2,1)S(1)}, u32[]{:S(2)}, u32[]{:S(2)}) async-start(bf16[256,4,256]{2,0,1:T(8,128)(2,1)} %bitcast.49), calls=%async_computation | async-start | bytes 1048576 | tf_op jit(solution)/shard_map/all_to_all | solution.py:31
  57.3 7.7 %shard_map.83 = bf16[256,256]{1,0:T(8,128)(2,1)} custom-call(s32[2,8]{1,0:T(2,128)} %get-tuple-element.15.slot_ref, bf16[512,256]{1,0:T(8,128)(2,1)} %slice.140.query_ref, bf16[512,512]{1,0:T(8,128)(2,1)} %collective-permute-done.refs_0_, bf16[512,512]{1,0:T(8,128)(2,1)} %collective-permute-done.1.refs_1_, bf16[512,512]{1,0:T(8,128)(2,1)} %copy-done.1, ...), custom_call_target="tpu_custom_call" | custom-call | tf_op jit(solution)/shard_map/pallas_call | solution.py:120
  65.0 1.2 convolution_convert_fusion.1
  66.2 0.8 copy.36
  67.1 4.8 %all-to-all-start.4 = ((bf16[256,4,256]{2,0,1:T(8,128)(2,1)}), bf16[256,4,256]{2,0,1:T(8,128)(2,1)S(1)}, u32[]{:S(2)}, u32[]{:S(2)}) async-start(bf16[256,4,256]{2,0,1:T(8,128)(2,1)} %bitcast.47), calls=%async_computation.4 | async-start | bytes 1048576 | tf_op jit(solution)/shard_map/all_to_all | solution.py:31
  71.9 8.8 %all-to-all-done.4 = bf16[256,4,256]{2,0,1:T(8,128)(2,1)S(1)} async-done(((bf16[256,4,256]{2,0,1:T(8,128)(2,1)}), bf16[256,4,256]{2,0,1:T(8,128)(2,1)S(1)}, u32[]{:S(2)}, u32[]{:S(2)}) %all-to-all-start.4) | async-done | bytes 524320 | tf_op jit(solution)/shard_map/all_to_all | solution.py:31
  80.7 1.2 multiply_reduce_fusion.1
  81.9 0.6 broadcast_in_dim.10
  82.5 4.7 %all-to-all-start.5 = ((f32[4,1,256]{2,1,0:T(1,128)}), f32[4,1,256]{2,1,0:T(1,128)S(1)}, u32[]{:S(2)}, u32[]{:S(2)}) async-start(f32[4,1,256]{2,1,0:T(1,128)} %broadcast_in_dim.10), calls=%async_computation.5 | async-start | bytes 8192 | tf_op jit(solution)/shard_map/all_to_all | solution.py:39
  87.2 0.8 dynamic_slice.11
  87.9 3.1 %all-to-all-done.5 = f32[4,1,256]{2,1,0:T(1,128)S(1)} async-done(((f32[4,1,256]{2,1,0:T(1,128)}), f32[4,1,256]{2,1,0:T(1,128)S(1)}, u32[]{:S(2)}, u32[]{:S(2)}) %all-to-all-start.5) | async-done | bytes 4128 | tf_op jit(solution)/shard_map/all_to_all | solution.py:39
  91.0 0.6 broadcast_in_dim.8
  91.6 4.7 %all-to-all-start.1 = ((f32[4,1,256]{2,1,0:T(1,128)}), f32[4,1,256]{2,1,0:T(1,128)S(1)}, u32[]{:S(2)}, u32[]{:S(2)}) async-start(f32[4,1,256]{2,1,0:T(1,128)} %broadcast_in_dim.8), calls=%async_computation.1 | async-start | bytes 8192 | tf_op jit(solution)/shard_map/all_to_all | solution.py:39
  96.3 3.8 %all-to-all-done.1 = f32[4,1,256]{2,1,0:T(1,128)S(1)} async-done(((f32[4,1,256]{2,1,0:T(1,128)}), f32[4,1,256]{2,1,0:T(1,128)S(1)}, u32[]{:S(2)}, u32[]{:S(2)}) %all-to-all-start.1) | async-done | bytes 4128 | tf_op jit(solution)/shard_map/all_to_all | solution.py:39
  100.1 0.1 multiply_convert_fusion.1
  100.3 10.5 %all_to_all.42 = bf16[256,4,256]{2,0,1:T(8,128)(2,1)S(1)} all-to-all(bf16[256,4,256]{2,0,1:T(8,128)(2,1)S(1)} %broadcast_in_dim.9), channel_id=1, replica_groups=mesh['patch'=128,'mp'=4] {'mp'}, dimensions={1} | all-to-all | bytes 1048576 | tf_op jit(solution)/shard_map/all_to_all | solution.py:49
  110.8 0.8 broadcast_in_dim.11
  111.6 4.9 %all-to-all-start.6 = ((bf16[256,4,256]{2,0,1:T(8,128)(2,1)}), bf16[256,4,256]{2,0,1:T(8,128)(2,1)S(1)}, u32[]{:S(2)}, u32[]{:S(2)}) async-start(bf16[256,4,256]{2,0,1:T(8,128)(2,1)} %broadcast_in_dim.11), calls=%async_computation.6 | async-start | bytes 1048576 | tf_op jit(solution)/shard_map/all_to_all | solution.py:49
  116.5 0.2 copy.21
  116.7 2.1 %convolution_convert_fusion.2 = bf16[256,1024]{1,0:T(8,128)(2,1)S(1)} fusion(bf16[512,1024]{1,0:T(8,128)(2,1)S(1)} %copy-done, bf16[256,1024]{0,1:T(8,128)(2,1)S(1)} %bitcast.52, bf16[1024,512]{1,0:T(8,128)(2,1)} %param.13), kind=kOutput, calls=%fused_computation.14 | convolution fusion | flops 538312704 | bytes 3145728 | tf_op jit(solution)/shard_map/dot_general | solution.py:148
  118.9 0.8 copy.37
  119.7 3.4 %all-to-all-done.6 = bf16[256,4,256]{2,0,1:T(8,128)(2,1)S(1)} async-done(((bf16[256,4,256]{2,0,1:T(8,128)(2,1)}), bf16[256,4,256]{2,0,1:T(8,128)(2,1)S(1)}, u32[]{:S(2)}, u32[]{:S(2)}) %all-to-all-start.6) | async-done | bytes 524320 | tf_op jit(solution)/shard_map/all_to_all | solution.py:49
  123.1 4.9 %all-to-all-start.3 = ((bf16[256,4,256]{2,0,1:T(8,128)(2,1)}), bf16[256,4,256]{2,0,1:T(8,128)(2,1)S(1)}, u32[]{:S(2)}, u32[]{:S(2)}) async-start(bf16[256,4,256]{2,0,1:T(8,128)(2,1)} %bitcast.48), calls=%async_computation.3 | async-start | bytes 1048576 | tf_op jit(solution)/shard_map/all_to_all | solution.py:31
  128.0 0.2 copy.24
  128.3 2.1 %convolution_convert_fusion = bf16[256,1024]{1,0:T(8,128)(2,1)S(1)} fusion(bf16[512,1024]{1,0:T(8,128)(2,1)S(1)} %copy-done, bf16[256,1024]{0,1:T(8,128)(2,1)S(1)} %bitcast.54, bf16[1024,512]{1,0:T(8,128)(2,1)} %param.13), kind=kOutput, calls=%fused_computation.12 | convolution fusion | flops 538312704 | bytes 3145728 | tf_op jit(solution)/shard_map/dot_general | solution.py:148
  130.4 0.8 copy.35
  131.2 3.4 %all-to-all-done.3 = bf16[256,4,256]{2,0,1:T(8,128)(2,1)S(1)} async-done(((bf16[256,4,256]{2,0,1:T(8,128)(2,1)}), bf16[256,4,256]{2,0,1:T(8,128)(2,1)S(1)}, u32[]{:S(2)}, u32[]{:S(2)}) %all-to-all-start.3) | async-done | bytes 524320 | tf_op jit(solution)/shard_map/all_to_all | solution.py:31
  134.7 4.9 %all-to-all-start.7 = ((bf16[256,4,256]{2,0,1:T(8,128)(2,1)}), bf16[256,4,256]{2,0,1:T(8,128)(2,1)S(1)}, u32[]{:S(2)}, u32[]{:S(2)}) async-start(bf16[256,4,256]{2,0,1:T(8,128)(2,1)} %bitcast.46), calls=%async_computation.7 | async-start | bytes 1048576 | tf_op jit(solution)/shard_map/all_to_all | solution.py:31
  139.6 6.6 %all-to-all-done.7 = bf16[256,4,256]{2,0,1:T(8,128)(2,1)S(1)} async-done(((bf16[256,4,256]{2,0,1:T(8,128)(2,1)}), bf16[256,4,256]{2,0,1:T(8,128)(2,1)S(1)}, u32[]{:S(2)}, u32[]{:S(2)}) %all-to-all-start.7) | async-done | bytes 524320 | tf_op jit(solution)/shard_map/all_to_all | solution.py:31
  146.3 0.7 pad_maximum_fusion
  (23 shorter events, 0.4 us)
Async XLA Ops:
  0.0 116.7 %copy-start = (bf16[512,1024]{1,0:T(8,128)(2,1)S(1)}, bf16[512,1024]{1,0:T(8,128)(2,1)}, u32[]{:S(2)}) copy-start(bf16[512,1024]{1,0:T(8,128)(2,1)} %param.14) | copy-start | bytes 3145732
  1.6 1.7 %copy-start.5 = (bf16[512,1024]{1,0:T(8,128)(2,1)S(1)}, bf16[512,1024]{1,0:T(8,128)(2,1)}, u32[]{:S(2)}) copy-start(bf16[512,1024]{1,0:T(8,128)(2,1)} %param.8) | copy-start | bytes 3145732
  1.6 1.7 %copy-start.6 = (f32[1024]{0:T(1024)S(1)}, f32[1024]{0:T(1024)}, u32[]{:S(2)}) copy-start(f32[1024]{0:T(1024)} %param.9) | copy-start | bytes 12292
  4.4 38.3 %copy-start.1 = (bf16[512,512]{1,0:T(8,128)(2,1)}, bf16[512,512]{1,0:T(8,128)(2,1)S(1)}, u32[]{:S(2)}) copy-start(bf16[512,512]{1,0:T(8,128)(2,1)S(1)} %slice.141.refs_2_) | copy-start | bytes 1572868
  4.4 25.0 %collective-permute-start.3 = (bf16[512,512]{1,0:T(8,128)(2,1)S(1)}, bf16[512,512]{1,0:T(8,128)(2,1)S(1)}, u32[]{:S(2)}, u32[]{:S(2)}) collective-permute-start(bf16[512,512]{1,0:T(8,128)(2,1)S(1)} %slice.141.refs_2_), channel_id=1, source_target_pairs={{0,504},{4,508},{8,0},{12,4},{16,8},{20,12},{24,16},{28,20},{32,24... | collective-permute-start | bytes 1572872 | tf_op jit(solution)/shard_map/ppermute | solution.py:20
  18.3 16.8 %collective-permute-start.2 = (bf16[512,512]{1,0:T(8,128)(2,1)S(1)}, bf16[512,512]{1,0:T(8,128)(2,1)S(1)}, u32[]{:S(2)}, u32[]{:S(2)}) collective-permute-start(bf16[512,512]{1,0:T(8,128)(2,1)S(1)} %slice.141.refs_2_), channel_id=1, source_target_pairs={{0,508},{4,0},{8,4},{12,8},{16,12},{20,16},{24,20},{28,24},{32,28}... | collective-permute-start | bytes 1572872 | tf_op jit(solution)/shard_map/ppermute | solution.py:20
  20.2 16.5 %collective-permute-start.1 = (bf16[512,512]{1,0:T(8,128)(2,1)S(1)}, bf16[512,512]{1,0:T(8,128)(2,1)}, u32[]{:S(2)}, u32[]{:S(2)}) collective-permute-start(bf16[512,512]{1,0:T(8,128)(2,1)S(1)} %slice.141.refs_2_), channel_id=1, source_target_pairs={{0,4},{4,8},{8,12},{12,16},{16,20},{20,24},{24,28},{28,32},{32,36}... | collective-permute-start | bytes 1572872 | tf_op jit(solution)/shard_map/ppermute | solution.py:20
  22.6 20.1 %collective-permute-start = (bf16[512,512]{1,0:T(8,128)(2,1)S(1)}, bf16[512,512]{1,0:T(8,128)(2,1)}, u32[]{:S(2)}, u32[]{:S(2)}) collective-permute-start(bf16[512,512]{1,0:T(8,128)(2,1)S(1)} %slice.141.refs_2_), channel_id=1, source_target_pairs={{0,8},{4,12},{8,16},{12,20},{16,24},{20,28},{24,32},{28,36},{32,40... | collective-permute-start | bytes 1572872 | tf_op jit(solution)/shard_map/ppermute | solution.py:20
  25.9 24.5 %copy-start.2 = (bf16[256,1024]{1,0:T(8,128)(2,1)S(1)}, bf16[256,1024]{1,0:T(8,128)(2,1)}, u32[]{:S(2)}) copy-start(bf16[256,1024]{1,0:T(8,128)(2,1)} %param.11) | copy-start | bytes 1572868
  29.4 13.3 %copy-start.3 = (bf16[512,512]{1,0:T(8,128)(2,1)}, bf16[512,512]{1,0:T(8,128)(2,1)S(1)}, u32[]{:S(2)}) copy-start(bf16[512,512]{1,0:T(8,128)(2,1)S(1)} %collective-permute-done.3.refs_4_) | copy-start | bytes 1572868
  35.0 7.7 %copy-start.4 = (bf16[512,512]{1,0:T(8,128)(2,1)}, bf16[512,512]{1,0:T(8,128)(2,1)S(1)}, u32[]{:S(2)}) copy-start(bf16[512,512]{1,0:T(8,128)(2,1)S(1)} %collective-permute-done.2.refs_3_) | copy-start | bytes 1572868
  52.5 14.6 %all-to-all-start = ((bf16[256,4,256]{2,0,1:T(8,128)(2,1)}), bf16[256,4,256]{2,0,1:T(8,128)(2,1)S(1)}, u32[]{:S(2)}, u32[]{:S(2)}) async-start(bf16[256,4,256]{2,0,1:T(8,128)(2,1)} %bitcast.49), calls=%async_computation | async-start | bytes 1048576 | tf_op jit(solution)/shard_map/all_to_all | solution.py:31
  67.1 13.6 %all-to-all-start.4 = ((bf16[256,4,256]{2,0,1:T(8,128)(2,1)}), bf16[256,4,256]{2,0,1:T(8,128)(2,1)S(1)}, u32[]{:S(2)}, u32[]{:S(2)}) async-start(bf16[256,4,256]{2,0,1:T(8,128)(2,1)} %bitcast.47), calls=%async_computation.4 | async-start | bytes 1048576 | tf_op jit(solution)/shard_map/all_to_all | solution.py:31
  82.5 8.5 %all-to-all-start.5 = ((f32[4,1,256]{2,1,0:T(1,128)}), f32[4,1,256]{2,1,0:T(1,128)S(1)}, u32[]{:S(2)}, u32[]{:S(2)}) async-start(f32[4,1,256]{2,1,0:T(1,128)} %broadcast_in_dim.10), calls=%async_computation.5 | async-start | bytes 8192 | tf_op jit(solution)/shard_map/all_to_all | solution.py:39
  91.6 8.5 %all-to-all-start.1 = ((f32[4,1,256]{2,1,0:T(1,128)}), f32[4,1,256]{2,1,0:T(1,128)S(1)}, u32[]{:S(2)}, u32[]{:S(2)}) async-start(f32[4,1,256]{2,1,0:T(1,128)} %broadcast_in_dim.8), calls=%async_computation.1 | async-start | bytes 8192 | tf_op jit(solution)/shard_map/all_to_all | solution.py:39
  111.6 11.5 %all-to-all-start.6 = ((bf16[256,4,256]{2,0,1:T(8,128)(2,1)}), bf16[256,4,256]{2,0,1:T(8,128)(2,1)S(1)}, u32[]{:S(2)}, u32[]{:S(2)}) async-start(bf16[256,4,256]{2,0,1:T(8,128)(2,1)} %broadcast_in_dim.11), calls=%async_computation.6 | async-start | bytes 1048576 | tf_op jit(solution)/shard_map/all_to_all | solution.py:49
  123.1 11.5 %all-to-all-start.3 = ((bf16[256,4,256]{2,0,1:T(8,128)(2,1)}), bf16[256,4,256]{2,0,1:T(8,128)(2,1)S(1)}, u32[]{:S(2)}, u32[]{:S(2)}) async-start(bf16[256,4,256]{2,0,1:T(8,128)(2,1)} %bitcast.48), calls=%async_computation.3 | async-start | bytes 1048576 | tf_op jit(solution)/shard_map/all_to_all | solution.py:31
  134.7 11.5 %all-to-all-start.7 = ((bf16[256,4,256]{2,0,1:T(8,128)(2,1)}), bf16[256,4,256]{2,0,1:T(8,128)(2,1)S(1)}, u32[]{:S(2)}, u32[]{:S(2)}) async-start(bf16[256,4,256]{2,0,1:T(8,128)(2,1)} %bitcast.46), calls=%async_computation.7 | async-start | bytes 1048576 | tf_op jit(solution)/shard_map/all_to_all | solution.py:31

commit v7 on v5

--- a/solution.py
+++ b/solution.py
@@ -25,12 +25,11 @@
     return (rows32 * lax.rsqrt(mean_sq + 1e-05) * gain).astype(jnp.bfloat16)
 
 
-def scatter_sum(parts, n_mp):
-    rows, cols = parts.shape
-    got = lax.all_to_all(parts.reshape(rows, n_mp, cols // n_mp), "mp", 1, 1)
-    total = got[:, 0].astype(jnp.float32)
-    for which in range(1, n_mp):
-        total = total + got[:, which].astype(jnp.float32)
+def scatter_sum(parts):
+    got = lax.all_to_all(parts, "mp", 0, 0)
+    total = got[0].astype(jnp.float32)
+    for which in range(1, got.shape[0]):
+        total = total + got[which].astype(jnp.float32)
     return total
 
 
@@ -42,10 +41,15 @@
     return total
 
 
-def gather_cols(block, n_mp):
-    rows, cols = block.shape
-    spread = jnp.broadcast_to(block[:, None], (rows, n_mp, cols))
-    return lax.all_to_all(spread, "mp", 1, 1).reshape(rows, n_mp * cols)
+def gather_blocks(block, n_mp):
+    return lax.all_to_all(jnp.broadcast_to(block[None], (n_mp,) + block.shape), "mp", 0, 0)
+
+
+def split_dot(left, weight, n_mp):
+    return jnp.einsum(
+        "rk,kjc->jrc", left, weight.reshape(weight.shape[0], n_mp, -1),
+        preferred_element_type=jnp.float32,
+    ).astype(jnp.bfloat16)
 
 
 def window_attention(slot_ref, query_ref, *refs, n_heads, n_win, n_nb):
@@ -118,8 +122,7 @@
         out_shape=jax.ShapeDtypeStruct((row_count, width), jnp.bfloat16),
     )(slot_index.astype(jnp.int32), queries, *kv_list)
     n_mp = lax.axis_size("mp")
-    partial_value = jnp.dot(attended, w_out, preferred_element_type=jnp.float32)
-    col_share = scatter_sum(partial_value.astype(jnp.bfloat16), n_mp)
+    col_share = scatter_sum(split_dot(attended, w_out, n_mp))
     col_width = col_share.shape[1]
     col_begin = lax.axis_index("mp") * col_width
     residual_cols = (
@@ -129,12 +132,13 @@
     square_sum = gather_sum(jnp.sum(residual_cols * residual_cols, axis=1), n_mp)
     inverse_rms = lax.rsqrt(square_sum / D + 1e-05)
     normed_cols = (residual_cols * inverse_rms[:, None] * gain_cols).astype(jnp.bfloat16)
-    normed2 = gather_cols(normed_cols, n_mp)
-    hidden = jax.nn.gelu(
-        jnp.dot(normed2, w_up, preferred_element_type=jnp.float32), approximate=True
-    ).astype(jnp.bfloat16)
-    down_term = jnp.dot(hidden, w_down, preferred_element_type=jnp.float32)
-    down_cols = scatter_sum(down_term.astype(jnp.bfloat16), n_mp)
+    normed2 = gather_blocks(normed_cols, n_mp)
+    up = jnp.einsum(
+        "jrc,jch->rh", normed2, w_up.reshape(n_mp, col_width, -1),
+        preferred_element_type=jnp.float32,
+    )
+    hidden = jax.nn.gelu(up, approximate=True).astype(jnp.bfloat16)
+    down_cols = scatter_sum(split_dot(hidden, w_down, n_mp))
     return (residual_cols + down_cols).astype(jnp.bfloat16)
 
 

time: 111 us -> 112 us (level)
  local copies, waits for them, and re-layouts: 7.24 us -> 4.83 us
  matrix products: 5.36 us -> 6.97 us
    dot_general x2, matrix products: 4.33 us -> 5.94 us  [split_dot(): jnp.einsum('rk,kjc->jrc', left, weight.reshape(weight.shape[0], n_mp, -1)...]
    all_to_all x1 -> x0, local copies, waits for them, and re-layouts: 1.3 us -> none  [gather_cols(): return lax.all_to_all(spread, 'mp', 1, 1).reshape(rows, n_mp * cols)]
where the time goes in v7:
time: 112 us; the launch traced here: 111 us
  starting transfers between devices  30.8 us (28%)
  blocking collectives  27.7 us (25%)
  waiting for transfers between devices  25 us (22%)
  Pallas kernels  12.4 us (11%)
  matrix products  6.97 us (6%)
  local copies, waits for them, and re-layouts  4.83 us (4%)
  other arithmetic  3.1 us (3%)
    ppermute x4, starting transfers between devices, from_behind(): lax.ppermute(array, axis, [(i, (i + by) % length) for i in range(length)])  21.3 us
    all_to_all x1, blocking collectives, scatter_sum(): got = lax.all_to_all(parts, 'mp', 0, 0)  14.4 us
    all_to_all x1, blocking collectives, gather_blocks(): lax.all_to_all(jnp.broadcast_to(block[None], (n_mp,) + block.shape), 'mp'...  13.3 us
    pallas_call x1, Pallas kernels, per_device(): pl.pallas_call(functools.partial(window_attention, n_heads=heads_here, n_...  12.4 us
    ppermute x4, waiting for transfers between devices, from_behind(): lax.ppermute(array, axis, [(i, (i + by) % length) for i in range(length)])  11.5 us
    all_to_all x1, waiting for transfers between devices, scatter_sum(): got = lax.all_to_all(parts, 'mp', 0, 0)  10.3 us
    dot_general x2, matrix products, split_dot(): jnp.einsum('rk,kjc->jrc', left, weight.reshape(weight.shape[0], n_mp, -1)...  5.94 us
    all_to_all x1, starting transfers between devices, scatter_sum(): got = lax.all_to_all(parts, 'mp', 0, 0)  4.82 us
  transfers between devices with their start and end apart: 6, of which 5 were waited for; matrix products, arithmetic and copies ran while one was open for 3% of the time, Pallas kernels for 0%

profile of v7, /device:TPU:2, one launch (start us, length us, event | category | flops | bytes accessed | tf_op | source)
XLA Modules:
  0.0 110.9 jit_solution(16838531784607208791)
XLA Ops:
  0.0 0.0 copy-start
  0.0 0.0 copy-start.2
  0.0 0.0 copy-start.6
  0.0 1.6 %slice_bitcast_fusion.2 = (bf16[1024,256]{1,0:T(8,128)(2,1)S(1)}, bf16[1024,256]{1,0:T(8,128)(2,1)S(1)}, bf16[1024,256]{1,0:T(8,128)(2,1)S(1)}) fusion(bf16[3,1024,256]{2,1,0:T(8,128)(2,1)} %param.10), kind=kLoop, calls=%fused_computation.44 | loop fusion | bytes 3145728 | tf_op jit(solution)/shard_map/squeeze | solution.py:97
  1.6 0.2 copy-done.2
  1.8 0.3 fusion
  2.1 0.0 copy-done.6
  2.1 1.0 fusion.9
  3.2 0.0 copy-start.1
  3.2 3.5 %collective-permute-start = (bf16[512,512]{1,0:T(8,128)(2,1)S(1)}, bf16[512,512]{1,0:T(8,128)(2,1)S(1)}, u32[]{:S(2)}, u32[]{:S(2)}) collective-permute-start(bf16[512,512]{1,0:T(8,128)(2,1)S(1)} %slice.73.refs_2_), channel_id=1, source_target_pairs={{0,8},{4,12},{8,16},{12,20},{16,24},{20,28},{24,32},{28,36},{32,40... | collective-permute-start | bytes 1572872 | tf_op jit(solution)/shard_map/ppermute | solution.py:19
  6.7 1.9 %collective-permute-start.1 = (bf16[512,512]{1,0:T(8,128)(2,1)S(1)}, bf16[512,512]{1,0:T(8,128)(2,1)S(1)}, u32[]{:S(2)}, u32[]{:S(2)}) collective-permute-start(bf16[512,512]{1,0:T(8,128)(2,1)S(1)} %slice.73.refs_2_), channel_id=1, source_target_pairs={{0,4},{4,8},{8,12},{12,16},{16,20},{20,24},{24,28},{28,32},{32,36}... | collective-permute-start | bytes 1572872 | tf_op jit(solution)/shard_map/ppermute | solution.py:19
  8.6 11.7 %collective-permute-start.2 = (bf16[512,512]{1,0:T(8,128)(2,1)S(1)}, bf16[512,512]{1,0:T(8,128)(2,1)}, u32[]{:S(2)}, u32[]{:S(2)}) collective-permute-start(bf16[512,512]{1,0:T(8,128)(2,1)S(1)} %slice.73.refs_2_), channel_id=1, source_target_pairs={{0,508},{4,0},{8,4},{12,8},{16,12},{20,16},{24,20},{28,24},{32,28}... | collective-permute-start | bytes 1572872 | tf_op jit(solution)/shard_map/ppermute | solution.py:19
  20.3 4.2 %collective-permute-start.3 = (bf16[512,512]{1,0:T(8,128)(2,1)S(1)}, bf16[512,512]{1,0:T(8,128)(2,1)}, u32[]{:S(2)}, u32[]{:S(2)}) collective-permute-start(bf16[512,512]{1,0:T(8,128)(2,1)S(1)} %slice.73.refs_2_), channel_id=1, source_target_pairs={{0,504},{4,508},{8,0},{12,4},{16,8},{20,12},{24,16},{28,20},{32,24... | collective-permute-start | bytes 1572872 | tf_op jit(solution)/shard_map/ppermute | solution.py:19
  24.6 0.7 slice.72.query_ref
  25.3 0.8 constant_dynamic-slice_fusion
  26.0 0.1 copy.12
  26.1 0.6 fusion.41.slot_ref
  26.7 0.0 copy-start.3
  26.7 3.1 %collective-permute-done.refs_0_ = bf16[512,512]{1,0:T(8,128)(2,1)S(1)} collective-permute-done((bf16[512,512]{1,0:T(8,128)(2,1)S(1)}, bf16[512,512]{1,0:T(8,128)(2,1)S(1)}, u32[]{:S(2)}, u32[]{:S(2)}) %collective-permute-start) | collective-permute-done | bytes 524320 | tf_op jit(solution)/shard_map/ppermute | solution.py:19
  29.8 0.0 copy-start.4
  29.8 4.8 %collective-permute-done.1.refs_1_ = bf16[512,512]{1,0:T(8,128)(2,1)S(1)} collective-permute-done((bf16[512,512]{1,0:T(8,128)(2,1)S(1)}, bf16[512,512]{1,0:T(8,128)(2,1)S(1)}, u32[]{:S(2)}, u32[]{:S(2)}) %collective-permute-start.1) | collective-permute-done | bytes 524320 | tf_op jit(solution)/shard_map/ppermute | solution.py:19
  34.6 0.0 copy-start.5
  34.6 0.0 collective-permute-done.2.refs_3_
  34.6 3.7 %collective-permute-done.3.refs_4_ = bf16[512,512]{1,0:T(8,128)(2,1)} collective-permute-done((bf16[512,512]{1,0:T(8,128)(2,1)S(1)}, bf16[512,512]{1,0:T(8,128)(2,1)}, u32[]{:S(2)}, u32[]{:S(2)}) %collective-permute-start.3) | collective-permute-done | bytes 524320 | tf_op jit(solution)/shard_map/ppermute | solution.py:19
  38.3 0.0 copy-done.1
  38.3 0.0 copy-done.4
  38.3 0.0 copy-done.5
  38.3 12.4 %shard_map.82 = bf16[512,256]{1,0:T(8,128)(2,1)} custom-call(s32[4,8]{1,0:T(4,128)} %fusion.41.slot_ref, bf16[512,256]{1,0:T(8,128)(2,1)} %slice.72.query_ref, bf16[512,512]{1,0:T(8,128)(2,1)} %copy-done.4, bf16[512,512]{1,0:T(8,128)(2,1)} %copy-done.5, bf16[512,512]{1,0:T(8,128)(2,1)} %copy-done.1, bf16[512,512]{1,0:T(8,128)(2,1)} %collective-permute-done.2.refs_3_, ...), custom_call_target="tpu_custom_call" | custom-call | tf_op jit(solution)/shard_map/pallas_call | solution.py:113
  50.7 0.0 copy-done.3
  50.7 2.4 %fusion.12 = bf16[4,512,256]{2,1,0:T(8,128)(2,1)} fusion(bf16[32,4,8,256]{3,2,1,0:T(8,128)(2,1)S(1)} %bitcast.47, bf16[512,256]{1,0:T(8,128)(2,1)} %shard_map.82), kind=kOutput, calls=%fused_computation.15 | convolution fusion | flops 268959744 | bytes 1835008 | tf_op jit(solution)/shard_map/rk,kjc->jrc/dot_general | solution.py:49
  53.1 4.8 %all-to-all-start = ((bf16[4,512,256]{2,1,0:T(8,128)(2,1)}), bf16[4,512,256]{2,1,0:T(8,128)(2,1)S(1)}, u32[]{:S(2)}, u32[]{:S(2)}) async-start(bf16[4,512,256]{2,1,0:T(8,128)(2,1)} %fusion.12), calls=%async_computation | async-start | bytes 2097152 | tf_op jit(solution)/shard_map/all_to_all | solution.py:29
  57.9 10.3 %all-to-all-done = bf16[4,512,256]{2,1,0:T(8,128)(2,1)S(1)} async-done(((bf16[4,512,256]{2,1,0:T(8,128)(2,1)}), bf16[4,512,256]{2,1,0:T(8,128)(2,1)S(1)}, u32[]{:S(2)}, u32[]{:S(2)}) %all-to-all-start) | async-done | bytes 1048608 | tf_op jit(solution)/shard_map/all_to_all | solution.py:29
  68.2 1.2 %multiply_reduce_fusion = (f32[512]{0:T(512)S(1)}, f32[512,256]{1,0:T(8,128)S(1)}) fusion(bf16[4,512,256]{2,1,0:T(8,128)(2,1)S(1)} %all-to-all-done, bf16[512,1024]{1,0:T(8,128)(2,1)} %param.8, s32[]{:T(128)S(6)} %select_n.23), kind=kLoop, calls=%fused_computation.41 | loop fusion | flops 1441280 | bytes 1837060 | tf_op jit(solution)/shard_map/reduce_sum | solution.py:132
  69.4 0.6 broadcast_in_dim.4
  70.0 4.7 %all-to-all-start.1 = ((f32[4,1,512]{2,1,0:T(1,128)}), f32[4,1,512]{2,1,0:T(1,128)S(1)}, u32[]{:S(2)}, u32[]{:S(2)}) async-start(f32[4,1,512]{2,1,0:T(1,128)} %broadcast_in_dim.4), calls=%async_computation.1 | async-start | bytes 16384 | tf_op jit(solution)/shard_map/all_to_all | solution.py:37
  74.7 0.8 dynamic_slice.11
  75.5 3.1 %all-to-all-done.1 = f32[4,1,512]{2,1,0:T(1,128)S(1)} async-done(((f32[4,1,512]{2,1,0:T(1,128)}), f32[4,1,512]{2,1,0:T(1,128)S(1)}, u32[]{:S(2)}, u32[]{:S(2)}) %all-to-all-start.1) | async-done | bytes 8224 | tf_op jit(solution)/shard_map/all_to_all | solution.py:37
  78.6 0.1 multiply_convert_fusion
  78.7 0.1 broadcast_in_dim.5
  78.8 13.3 %all_to_all.21 = bf16[4,512,256]{2,1,0:T(8,128)(2,1)S(1)} all-to-all(bf16[4,512,256]{2,1,0:T(8,128)(2,1)S(1)} %broadcast_in_dim.5), channel_id=1, replica_groups=mesh['patch'=128,'mp'=4] {'mp'}, dimensions={0} | all-to-all | bytes 2097152 | tf_op jit(solution)/shard_map/all_to_all | solution.py:45
  92.1 0.0 copy-done
  92.1 3.6 %fusion.13 = bf16[4,512,256]{2,1,0:T(8,128)(2,1)} fusion(bf16[64,4,8,256]{3,2,1,0:T(8,128)(2,1)} %bitcast.49, bf16[4,512,256]{2,1,0:T(8,128)(2,1)S(1)} %all_to_all.21, bf16[4,256,512]{2,1,0:T(8,128)(2,1)S(1)} %bitcast.46), kind=kOutput, calls=%fused_computation.17 | convolution fusion | flops 1076625408 | bytes 4194304 | tf_op jit(solution)/shard_map/rk,kjc->jrc/dot_general | solution.py:49
  95.7 14.4 %all_to_all.22 = bf16[4,512,256]{2,1,0:T(8,128)(2,1)S(1)} all-to-all(bf16[4,512,256]{2,1,0:T(8,128)(2,1)} %fusion.13), channel_id=1, replica_groups=mesh['patch'=128,'mp'=4] {'mp'}, dimensions={0} | all-to-all | bytes 2097152 | tf_op jit(solution)/shard_map/all_to_all | solution.py:29
  110.1 0.8 fusion.30
  (3 shorter events, 0.1 us)
Async XLA Ops:
  0.0 92.1 %copy-start = (bf16[1024,512]{1,0:T(8,128)(2,1)S(1)}, bf16[1024,512]{1,0:T(8,128)(2,1)}, u32[]{:S(2)}) copy-start(bf16[1024,512]{1,0:T(8,128)(2,1)} %param.13) | copy-start | bytes 3145732
  0.0 1.8 %copy-start.2 = (bf16[512,1024]{1,0:T(8,128)(2,1)S(1)}, bf16[512,1024]{1,0:T(8,128)(2,1)}, u32[]{:S(2)}) copy-start(bf16[512,1024]{1,0:T(8,128)(2,1)} %param.8) | copy-start | bytes 3145732
  0.0 2.1 %copy-start.6 = (f32[1024]{0:T(1024)S(1)}, f32[1024]{0:T(1024)}, u32[]{:S(2)}) copy-start(f32[1024]{0:T(1024)} %param.9) | copy-start | bytes 12292
  3.2 35.1 %copy-start.1 = (bf16[512,512]{1,0:T(8,128)(2,1)}, bf16[512,512]{1,0:T(8,128)(2,1)S(1)}, u32[]{:S(2)}) copy-start(bf16[512,512]{1,0:T(8,128)(2,1)S(1)} %slice.73.refs_2_) | copy-start | bytes 1572868
  3.2 26.6 %collective-permute-start = (bf16[512,512]{1,0:T(8,128)(2,1)S(1)}, bf16[512,512]{1,0:T(8,128)(2,1)S(1)}, u32[]{:S(2)}, u32[]{:S(2)}) collective-permute-start(bf16[512,512]{1,0:T(8,128)(2,1)S(1)} %slice.73.refs_2_), channel_id=1, source_target_pairs={{0,8},{4,12},{8,16},{12,20},{16,24},{20,28},{24,32},{28,36},{32,40... | collective-permute-start | bytes 1572872 | tf_op jit(solution)/shard_map/ppermute | solution.py:19
  6.7 27.9 %collective-permute-start.1 = (bf16[512,512]{1,0:T(8,128)(2,1)S(1)}, bf16[512,512]{1,0:T(8,128)(2,1)S(1)}, u32[]{:S(2)}, u32[]{:S(2)}) collective-permute-start(bf16[512,512]{1,0:T(8,128)(2,1)S(1)} %slice.73.refs_2_), channel_id=1, source_target_pairs={{0,4},{4,8},{8,12},{12,16},{16,20},{20,24},{24,28},{28,32},{32,36}... | collective-permute-start | bytes 1572872 | tf_op jit(solution)/shard_map/ppermute | solution.py:19
  8.6 26.0 %collective-permute-start.2 = (bf16[512,512]{1,0:T(8,128)(2,1)S(1)}, bf16[512,512]{1,0:T(8,128)(2,1)}, u32[]{:S(2)}, u32[]{:S(2)}) collective-permute-start(bf16[512,512]{1,0:T(8,128)(2,1)S(1)} %slice.73.refs_2_), channel_id=1, source_target_pairs={{0,508},{4,0},{8,4},{12,8},{16,12},{20,16},{24,20},{28,24},{32,28}... | collective-permute-start | bytes 1572872 | tf_op jit(solution)/shard_map/ppermute | solution.py:19
  20.3 17.9 %collective-permute-start.3 = (bf16[512,512]{1,0:T(8,128)(2,1)S(1)}, bf16[512,512]{1,0:T(8,128)(2,1)}, u32[]{:S(2)}, u32[]{:S(2)}) collective-permute-start(bf16[512,512]{1,0:T(8,128)(2,1)S(1)} %slice.73.refs_2_), channel_id=1, source_target_pairs={{0,504},{4,508},{8,0},{12,4},{16,8},{20,12},{24,16},{28,20},{32,24... | collective-permute-start | bytes 1572872 | tf_op jit(solution)/shard_map/ppermute | solution.py:19
  26.7 24.0 %copy-start.3 = (bf16[256,1024]{1,0:T(8,128)(2,1)S(1)}, bf16[256,1024]{1,0:T(8,128)(2,1)}, u32[]{:S(2)}) copy-start(bf16[256,1024]{1,0:T(8,128)(2,1)} %param.11) | copy-start | bytes 1572868
  29.8 8.5 %copy-start.4 = (bf16[512,512]{1,0:T(8,128)(2,1)}, bf16[512,512]{1,0:T(8,128)(2,1)S(1)}, u32[]{:S(2)}) copy-start(bf16[512,512]{1,0:T(8,128)(2,1)S(1)} %collective-permute-done.refs_0_) | copy-start | bytes 1572868
  34.6 3.7 %copy-start.5 = (bf16[512,512]{1,0:T(8,128)(2,1)}, bf16[512,512]{1,0:T(8,128)(2,1)S(1)}, u32[]{:S(2)}) copy-start(bf16[512,512]{1,0:T(8,128)(2,1)S(1)} %collective-permute-done.1.refs_1_) | copy-start | bytes 1572868
  53.1 15.1 %all-to-all-start = ((bf16[4,512,256]{2,1,0:T(8,128)(2,1)}), bf16[4,512,256]{2,1,0:T(8,128)(2,1)S(1)}, u32[]{:S(2)}, u32[]{:S(2)}) async-start(bf16[4,512,256]{2,1,0:T(8,128)(2,1)} %fusion.12), calls=%async_computation | async-start | bytes 2097152 | tf_op jit(solution)/shard_map/all_to_all | solution.py:29
  70.0 8.5 %all-to-all-start.1 = ((f32[4,1,512]{2,1,0:T(1,128)}), f32[4,1,512]{2,1,0:T(1,128)S(1)}, u32[]{:S(2)}, u32[]{:S(2)}) async-start(f32[4,1,512]{2,1,0:T(1,128)} %broadcast_in_dim.4), calls=%async_computation.1 | async-start | bytes 16384 | tf_op jit(solution)/shard_map/all_to_all | solution.py:37

commit v8 on v5

--- a/solution.py
+++ b/solution.py
@@ -94,17 +94,22 @@
     qkv = jnp.dot(normed, w_all, preferred_element_type=jnp.float32).astype(jnp.bfloat16)
     queries = qkv[:, :width]
     own_kv = qkv[:, width:]
-    window = {0: own_kv}
-    for offset in range(-REACH, REACH + 1):
-        if offset != 0:
-            window[offset] = from_behind(own_kv, "patch", -offset)
     device = lax.axis_index("patch")
     n_dev = lax.axis_size("patch")
+    core = device % 2
+    from_before = from_behind(own_kv, "patch", 2)
+    from_after = from_behind(own_kv, "patch", -2)
+    partner = lax.ppermute(own_kv, "patch", [(i, i ^ 1) for i in range(n_dev)])
+    relay = jnp.where(core == 0, from_after, from_before)
+    relayed = lax.ppermute(relay, "patch", [(i, i ^ 1) for i in range(n_dev)])
+    kv_list = [from_before, partner, own_kv, relayed, from_after]
     listed = lax.dynamic_slice_in_dim(neighbours, device * patches_here, patches_here, 0)
     owner_dev = listed // patches_here
     offset_dev = jnp.mod(owner_dev - device + n_dev // 2, n_dev) - n_dev // 2
-    slot_index = (offset_dev + REACH) * patches_here + jnp.mod(listed, patches_here)
-    kv_list = [window[offset] for offset in range(-REACH, REACH + 1)]
+    block = offset_dev + REACH
+    swap = (core == 0) & ((offset_dev == 1) | (offset_dev == -1))
+    block = jnp.where(swap, 4 - block, block)
+    slot_index = block * patches_here + jnp.mod(listed, patches_here)
     kv_spec = pl.BlockSpec((row_count, 2 * width), lambda p, slots: (0, 0))
     attended = pl.pallas_call(
         functools.partial(window_attention, n_heads=heads_here, n_win=n_win, n_nb=K_NB),

time: 111 us -> 117 us (1.054)
  blocking collectives: 26.6 us -> 31.4 us
  starting transfers between devices: 30.8 us -> 29.1 us
  waiting for transfers between devices: 25 us -> 26.7 us
    ppermute x4 -> x2, starting transfers between devices: 21.3 us -> 15.8 us  [from_behind(): lax.ppermute(array, axis, [(i, (i + by) % length) for i in range(length)])]
    all_to_all x1, waiting for transfers between devices: 10.3 us -> 14.3 us  [scatter_sum(): got = lax.all_to_all(parts.reshape(rows, n_mp, cols // n_mp), 'mp', 1, 1)]
    ppermute x0 -> x2, starting transfers between devices: none -> 3.83 us  [the longest x1 1.92 us: per_device(): partner = lax.ppermute(own_kv, 'patch', [(i, i ^ 1) for i in range(n_dev)])]
    all_to_all x1, blocking collectives: 13.3 us -> 16.2 us  [gather_cols(): return lax.all_to_all(spread, 'mp', 1, 1).reshape(rows, n_mp * cols)]
    ppermute x4 -> x2, waiting for transfers between devices: 11.5 us -> 9.21 us  [from_behind(): lax.ppermute(array, axis, [(i, (i + by) % length) for i in range(length)])]
    all_to_all x1, blocking collectives: 13.3 us -> 15.2 us  [scatter_sum(): got = lax.all_to_all(parts.reshape(rows, n_mp, cols // n_mp), 'mp', 1, 1)]
  transfers between devices with their start and end apart: 6 -> 6, of which waited for: 5 -> 4; matrix products, arithmetic and copies ran while one was open for 3% -> 3% of each run, Pallas kernels for 0% -> 0%
where the time goes in v8:
time: 117 us; the launch traced here: 116 us
  blocking collectives  31.4 us (27%)
  starting transfers between devices  29.1 us (25%)
  waiting for transfers between devices  26.7 us (23%)
  Pallas kernels  12.6 us (11%)
  local copies, waits for them, and re-layouts  7.24 us (6%)
  matrix products  5.36 us (5%)
  other arithmetic  4.03 us (3%)
    all_to_all x1, blocking collectives, gather_cols(): return lax.all_to_all(spread, 'mp', 1, 1).reshape(rows, n_mp * cols)  16.2 us
    ppermute x2, starting transfers between devices, from_behind(): lax.ppermute(array, axis, [(i, (i + by) % length) for i in range(length)])  15.8 us
    all_to_all x1, blocking collectives, scatter_sum(): got = lax.all_to_all(parts.reshape(rows, n_mp, cols // n_mp), 'mp', 1, 1)  15.2 us
    all_to_all x1, waiting for transfers between devices, scatter_sum(): got = lax.all_to_all(parts.reshape(rows, n_mp, cols // n_mp), 'mp', 1, 1)  14.3 us
    pallas_call x1, Pallas kernels, per_device(): pl.pallas_call(functools.partial(window_attention, n_heads=heads_here, n_...  12.6 us
    ppermute x2, waiting for transfers between devices, from_behind(): lax.ppermute(array, axis, [(i, (i + by) % length) for i in range(length)])  9.21 us
    all_to_all x1, starting transfers between devices, scatter_sum(): got = lax.all_to_all(parts.reshape(rows, n_mp, cols // n_mp), 'mp', 1, 1)  4.82 us
    all_to_all x1, starting transfers between devices, gather_sum(): lax.all_to_all(jnp.broadcast_to(vector[None], (n_mp,) + vector.shape), 'm...  4.68 us
  transfers between devices with their start and end apart: 6, of which 4 were waited for; matrix products, arithmetic and copies ran while one was open for 3% of the time, Pallas kernels for 0%

profile of v8, /device:TPU:2, one launch (start us, length us, event | category | flops | bytes accessed | tf_op | source)
XLA Modules:
  0.0 116.5 jit_solution(17808540549656016318)
XLA Ops:
  0.0 0.0 copy-start
  0.0 0.0 copy-start.4
  0.0 0.0 copy-start.6
  0.0 1.6 %slice_bitcast_fusion.2 = (bf16[1024,256]{1,0:T(8,128)(2,1)S(1)}, bf16[1024,256]{1,0:T(8,128)(2,1)S(1)}, bf16[1024,256]{1,0:T(8,128)(2,1)S(1)}) fusion(bf16[3,1024,256]{2,1,0:T(8,128)(2,1)} %param.10), kind=kLoop, calls=%fused_computation.38 | loop fusion | bytes 3145728 | tf_op jit(solution)/shard_map/squeeze | solution.py:93
  1.6 0.2 copy-done.4
  1.8 0.3 fusion
  2.1 0.0 copy-done.6
  2.1 1.0 fusion.9
  3.2 0.0 copy-start.1
  3.2 3.5 %collective-permute-start = (bf16[512,512]{1,0:T(8,128)(2,1)S(1)}, bf16[512,512]{1,0:T(8,128)(2,1)S(1)}, u32[]{:S(2)}, u32[]{:S(2)}) collective-permute-start(bf16[512,512]{1,0:T(8,128)(2,1)S(1)} %slice.73.refs_2_), channel_id=1, source_target_pairs={{0,8},{4,12},{8,16},{12,20},{16,24},{20,28},{24,32},{28,36},{32,40... | collective-permute-start | bytes 1572872 | tf_op jit(solution)/shard_map/ppermute | solution.py:19
  6.7 12.3 %collective-permute-start.2 = (bf16[512,512]{1,0:T(8,128)(2,1)S(1)}, bf16[512,512]{1,0:T(8,128)(2,1)S(1)}, u32[]{:S(2)}, u32[]{:S(2)}) collective-permute-start(bf16[512,512]{1,0:T(8,128)(2,1)S(1)} %slice.73.refs_2_), channel_id=1, source_target_pairs={{0,504},{4,508},{8,0},{12,4},{16,8},{20,12},{24,16},{28,20},{32,24... | collective-permute-start | bytes 1572872 | tf_op jit(solution)/shard_map/ppermute | solution.py:19
  19.0 1.9 %collective-permute-start.1 = (bf16[512,512]{1,0:T(8,128)(2,1)S(1)}, bf16[512,512]{1,0:T(8,128)(2,1)}, u32[]{:S(2)}, u32[]{:S(2)}) collective-permute-start(bf16[512,512]{1,0:T(8,128)(2,1)S(1)} %slice.73.refs_2_), channel_id=1, source_target_pairs={{0,4},{4,0},{8,12},{12,8},{16,20},{20,16},{24,28},{28,24},{32,36},... | collective-permute-start | bytes 1572872 | tf_op jit(solution)/shard_map/ppermute | solution.py:102
  20.9 8.0 %collective-permute-done.refs_0_ = bf16[512,512]{1,0:T(8,128)(2,1)S(1)} collective-permute-done((bf16[512,512]{1,0:T(8,128)(2,1)S(1)}, bf16[512,512]{1,0:T(8,128)(2,1)S(1)}, u32[]{:S(2)}, u32[]{:S(2)}) %collective-permute-start) | collective-permute-done | bytes 524320 | tf_op jit(solution)/shard_map/ppermute | solution.py:19
  29.0 0.0 copy-start.2
  29.0 1.2 %collective-permute-done.2.refs_4_ = bf16[512,512]{1,0:T(8,128)(2,1)S(1)} collective-permute-done((bf16[512,512]{1,0:T(8,128)(2,1)S(1)}, bf16[512,512]{1,0:T(8,128)(2,1)S(1)}, u32[]{:S(2)}, u32[]{:S(2)}) %collective-permute-start.2) | collective-permute-done | bytes 524320 | tf_op jit(solution)/shard_map/ppermute | solution.py:19
  30.1 0.0 copy-start.3
  30.1 0.9 broadcast_select_fusion
  31.1 1.9 %collective-permute-start.3 = (bf16[512,512]{1,0:T(8,128)(2,1)}, bf16[512,512]{1,0:T(8,128)(2,1)}, u32[]{:S(2)}, u32[]{:S(2)}) collective-permute-start(bf16[512,512]{1,0:T(8,128)(2,1)} %broadcast_select_fusion), channel_id=1, source_target_pairs={{0,4},{4,0},{8,12},{12,8},{16,20},{20,16},{24,28},{28,24},{32,36},... | collective-permute-start | bytes 1572872 | tf_op jit(solution)/shard_map/ppermute | solution.py:104
  33.0 0.7 slice.72.query_ref
  33.7 0.8 constant_dynamic-slice_fusion
  34.5 0.1 copy.19
  34.5 0.6 fusion.33.slot_ref
  35.1 0.0 copy-start.5
  35.2 0.0 collective-permute-done.1.refs_1_
  35.2 0.0 collective-permute-done.3.refs_3_
  35.2 0.0 copy-done.1
  35.2 0.0 copy-done.2
  35.2 0.0 copy-done.3
  35.2 12.6 %shard_map.82 = bf16[512,256]{1,0:T(8,128)(2,1)} custom-call(s32[4,8]{1,0:T(4,128)} %fusion.33.slot_ref, bf16[512,256]{1,0:T(8,128)(2,1)} %slice.72.query_ref, bf16[512,512]{1,0:T(8,128)(2,1)} %copy-done.2, bf16[512,512]{1,0:T(8,128)(2,1)} %collective-permute-done.1.refs_1_, bf16[512,512]{1,0:T(8,128)(2,1)} %copy-done.1, ...), custom_call_target="tpu_custom_call" | custom-call | tf_op jit(solution)/shard_map/pallas_call | solution.py:114
  47.8 0.0 copy-done.5
  47.8 1.4 %convolution_convert_fusion = bf16[512,1024]{1,0:T(8,128)(2,1)S(1)} fusion(bf16[512,256]{1,0:T(8,128)(2,1)} %shard_map.82, bf16[256,1024]{1,0:T(8,128)(2,1)S(1)} %copy-done.5), kind=kOutput, calls=%fused_computation.12 | convolution fusion | flops 268959744 | bytes 1835008 | tf_op jit(solution)/shard_map/dot_general | solution.py:126
  49.2 1.0 copy.25
  50.2 4.8 %all-to-all-start = ((bf16[512,4,256]{2,0,1:T(8,128)(2,1)}), bf16[512,4,256]{2,0,1:T(8,128)(2,1)S(1)}, u32[]{:S(2)}, u32[]{:S(2)}) async-start(bf16[512,4,256]{2,0,1:T(8,128)(2,1)} %bitcast.29), calls=%async_computation | async-start | bytes 2097152 | tf_op jit(solution)/shard_map/all_to_all | solution.py:30
  55.0 14.3 %all-to-all-done = bf16[512,4,256]{2,0,1:T(8,128)(2,1)S(1)} async-done(((bf16[512,4,256]{2,0,1:T(8,128)(2,1)}), bf16[512,4,256]{2,0,1:T(8,128)(2,1)S(1)}, u32[]{:S(2)}, u32[]{:S(2)}) %all-to-all-start) | async-done | bytes 1048608 | tf_op jit(solution)/shard_map/all_to_all | solution.py:30
  69.3 1.2 %multiply_reduce_fusion = (f32[512]{0:T(512)S(1)}, f32[512,256]{1,0:T(8,128)S(1)}) fusion(bf16[512,4,256]{2,0,1:T(8,128)(2,1)S(1)} %all-to-all-done, bf16[512,1024]{1,0:T(8,128)(2,1)} %param.8, s32[]{:T(128)S(6)} %select_n.40), kind=kLoop, calls=%fused_computation.35 | loop fusion | flops 1441280 | bytes 1837060 | tf_op jit(solution)/shard_map/reduce_sum | solution.py:134
  70.5 0.6 broadcast_in_dim.4
  71.1 4.7 %all-to-all-start.1 = ((f32[4,1,512]{2,1,0:T(1,128)}), f32[4,1,512]{2,1,0:T(1,128)S(1)}, u32[]{:S(2)}, u32[]{:S(2)}) async-start(f32[4,1,512]{2,1,0:T(1,128)} %broadcast_in_dim.4), calls=%async_computation.1 | async-start | bytes 16384 | tf_op jit(solution)/shard_map/all_to_all | solution.py:38
  75.8 0.8 dynamic_slice.11
  76.6 3.1 %all-to-all-done.1 = f32[4,1,512]{2,1,0:T(1,128)S(1)} async-done(((f32[4,1,512]{2,1,0:T(1,128)}), f32[4,1,512]{2,1,0:T(1,128)S(1)}, u32[]{:S(2)}, u32[]{:S(2)}) %all-to-all-start.1) | async-done | bytes 8224 | tf_op jit(solution)/shard_map/all_to_all | solution.py:38
  79.7 0.1 multiply_convert_fusion
  79.8 0.1 broadcast_in_dim.5
  79.9 16.2 %all_to_all.21 = bf16[512,4,256]{2,0,1:T(8,128)(2,1)S(1)} all-to-all(bf16[512,4,256]{2,0,1:T(8,128)(2,1)S(1)} %broadcast_in_dim.5), channel_id=1, replica_groups=mesh['patch'=128,'mp'=4] {'mp'}, dimensions={1} | all-to-all | bytes 2097152 | tf_op jit(solution)/shard_map/all_to_all | solution.py:48
  96.1 1.3 %copy.17 = bf16[512,4,256]{0,2,1:T(8,128)(2,1)} copy(bf16[512,4,256]{2,0,1:T(8,128)(2,1)S(1)} %all_to_all.21) | data formatting | bytes 2097152 | tf_op jit(solution)/shard_map/all_to_all | solution.py:48
  97.4 0.0 copy-done
  97.4 2.9 %convolution_convert_fusion.1 = bf16[512,1024]{1,0:T(8,128)(2,1)S(1)} fusion(bf16[512,1024]{1,0:T(8,128)(2,1)S(1)} %copy-done, bf16[512,1024]{0,1:T(8,128)(2,1)} %bitcast.31, bf16[1024,512]{1,0:T(8,128)(2,1)} %param.13), kind=kOutput, calls=%fused_computation.13 | convolution fusion | flops 1076625408 | bytes 4194304 | tf_op jit(solution)/shard_map/dot_general | solution.py:141
  100.3 0.1 copy.24
  100.4 15.2 %all_to_all.22 = bf16[512,4,256]{2,0,1:T(8,128)(2,1)S(1)} all-to-all(bf16[512,4,256]{2,0,1:T(8,128)(2,1)S(1)} %bitcast.30), channel_id=1, replica_groups=mesh['patch'=128,'mp'=4] {'mp'}, dimensions={1} | all-to-all | bytes 2097152 | tf_op jit(solution)/shard_map/all_to_all | solution.py:30
  115.6 0.8 fusion.24
  (3 shorter events, 0.1 us)
Async XLA Ops:
  0.0 97.4 %copy-start = (bf16[512,1024]{1,0:T(8,128)(2,1)S(1)}, bf16[512,1024]{1,0:T(8,128)(2,1)}, u32[]{:S(2)}) copy-start(bf16[512,1024]{1,0:T(8,128)(2,1)} %param.14) | copy-start | bytes 3145732
  0.0 1.8 %copy-start.4 = (bf16[512,1024]{1,0:T(8,128)(2,1)S(1)}, bf16[512,1024]{1,0:T(8,128)(2,1)}, u32[]{:S(2)}) copy-start(bf16[512,1024]{1,0:T(8,128)(2,1)} %param.8) | copy-start | bytes 3145732
  0.0 2.1 %copy-start.6 = (f32[1024]{0:T(1024)S(1)}, f32[1024]{0:T(1024)}, u32[]{:S(2)}) copy-start(f32[1024]{0:T(1024)} %param.9) | copy-start | bytes 12292
  3.2 32.0 %copy-start.1 = (bf16[512,512]{1,0:T(8,128)(2,1)}, bf16[512,512]{1,0:T(8,128)(2,1)S(1)}, u32[]{:S(2)}) copy-start(bf16[512,512]{1,0:T(8,128)(2,1)S(1)} %slice.73.refs_2_) | copy-start | bytes 1572868
  3.2 25.8 %collective-permute-start = (bf16[512,512]{1,0:T(8,128)(2,1)S(1)}, bf16[512,512]{1,0:T(8,128)(2,1)S(1)}, u32[]{:S(2)}, u32[]{:S(2)}) collective-permute-start(bf16[512,512]{1,0:T(8,128)(2,1)S(1)} %slice.73.refs_2_), channel_id=1, source_target_pairs={{0,8},{4,12},{8,16},{12,20},{16,24},{20,28},{24,32},{28,36},{32,40... | collective-permute-start | bytes 1572872 | tf_op jit(solution)/shard_map/ppermute | solution.py:19
  6.7 23.5 %collective-permute-start.2 = (bf16[512,512]{1,0:T(8,128)(2,1)S(1)}, bf16[512,512]{1,0:T(8,128)(2,1)S(1)}, u32[]{:S(2)}, u32[]{:S(2)}) collective-permute-start(bf16[512,512]{1,0:T(8,128)(2,1)S(1)} %slice.73.refs_2_), channel_id=1, source_target_pairs={{0,504},{4,508},{8,0},{12,4},{16,8},{20,12},{24,16},{28,20},{32,24... | collective-permute-start | bytes 1572872 | tf_op jit(solution)/shard_map/ppermute | solution.py:19
  19.0 16.2 %collective-permute-start.1 = (bf16[512,512]{1,0:T(8,128)(2,1)S(1)}, bf16[512,512]{1,0:T(8,128)(2,1)}, u32[]{:S(2)}, u32[]{:S(2)}) collective-permute-start(bf16[512,512]{1,0:T(8,128)(2,1)S(1)} %slice.73.refs_2_), channel_id=1, source_target_pairs={{0,4},{4,0},{8,12},{12,8},{16,20},{20,16},{24,28},{28,24},{32,36},... | collective-permute-start | bytes 1572872 | tf_op jit(solution)/shard_map/ppermute | solution.py:102
  29.0 6.3 %copy-start.2 = (bf16[512,512]{1,0:T(8,128)(2,1)}, bf16[512,512]{1,0:T(8,128)(2,1)S(1)}, u32[]{:S(2)}) copy-start(bf16[512,512]{1,0:T(8,128)(2,1)S(1)} %collective-permute-done.refs_0_) | copy-start | bytes 1572868
  30.1 5.1 %copy-start.3 = (bf16[512,512]{1,0:T(8,128)(2,1)}, bf16[512,512]{1,0:T(8,128)(2,1)S(1)}, u32[]{:S(2)}) copy-start(bf16[512,512]{1,0:T(8,128)(2,1)S(1)} %collective-permute-done.2.refs_4_) | copy-start | bytes 1572868
  31.1 4.1 %collective-permute-start.3 = (bf16[512,512]{1,0:T(8,128)(2,1)}, bf16[512,512]{1,0:T(8,128)(2,1)}, u32[]{:S(2)}, u32[]{:S(2)}) collective-permute-start(bf16[512,512]{1,0:T(8,128)(2,1)} %broadcast_select_fusion), channel_id=1, source_target_pairs={{0,4},{4,0},{8,12},{12,8},{16,20},{20,16},{24,28},{28,24},{32,36},... | collective-permute-start | bytes 1572872 | tf_op jit(solution)/shard_map/ppermute | solution.py:104
  35.1 12.6 %copy-start.5 = (bf16[256,1024]{1,0:T(8,128)(2,1)S(1)}, bf16[256,1024]{1,0:T(8,128)(2,1)}, u32[]{:S(2)}) copy-start(bf16[256,1024]{1,0:T(8,128)(2,1)} %param.11) | copy-start | bytes 1572868
  50.2 19.1 %all-to-all-start = ((bf16[512,4,256]{2,0,1:T(8,128)(2,1)}), bf16[512,4,256]{2,0,1:T(8,128)(2,1)S(1)}, u32[]{:S(2)}, u32[]{:S(2)}) async-start(bf16[512,4,256]{2,0,1:T(8,128)(2,1)} %bitcast.29), calls=%async_computation | async-start | bytes 2097152 | tf_op jit(solution)/shard_map/all_to_all | solution.py:30
  71.1 8.5 %all-to-all-start.1 = ((f32[4,1,512]{2,1,0:T(1,128)}), f32[4,1,512]{2,1,0:T(1,128)S(1)}, u32[]{:S(2)}, u32[]{:S(2)}) async-start(f32[4,1,512]{2,1,0:T(1,128)} %broadcast_in_dim.4), calls=%async_computation.1 | async-start | bytes 16384 | tf_op jit(solution)/shard_map/all_to_all | solution.py:38

commit v9 on v5

--- a/solution.py
+++ b/solution.py
@@ -31,14 +31,6 @@
     total = got[:, 0].astype(jnp.float32)
     for which in range(1, n_mp):
         total = total + got[:, which].astype(jnp.float32)
-    return total
-
-
-def gather_sum(vector, n_mp):
-    got = lax.all_to_all(jnp.broadcast_to(vector[None], (n_mp,) + vector.shape), "mp", 0, 0)
-    total = got[0]
-    for which in range(1, n_mp):
-        total = total + got[which]
     return total
 
 
@@ -125,11 +117,10 @@
     residual_cols = (
         lax.dynamic_slice_in_dim(features, col_begin, col_width, 1).astype(jnp.float32) + col_share
     )
-    gain_cols = lax.dynamic_slice_in_dim(gain_mlp, col_begin, col_width, 0)
-    square_sum = gather_sum(jnp.sum(residual_cols * residual_cols, axis=1), n_mp)
+    rows_full = gather_cols(residual_cols.astype(jnp.bfloat16), n_mp).astype(jnp.float32)
+    square_sum = jnp.sum(rows_full * rows_full, axis=1, keepdims=True)
     inverse_rms = lax.rsqrt(square_sum / D + 1e-05)
-    normed_cols = (residual_cols * inverse_rms[:, None] * gain_cols).astype(jnp.bfloat16)
-    normed2 = gather_cols(normed_cols, n_mp)
+    normed2 = (rows_full * inverse_rms * gain_mlp).astype(jnp.bfloat16)
     hidden = jax.nn.gelu(
         jnp.dot(normed2, w_up, preferred_element_type=jnp.float32), approximate=True
     ).astype(jnp.bfloat16)

time: 111 us -> 126 us (1.14)
  the two profiles are of different devices: /device:TPU:2 before, /device:TPU:1 now
where the time goes in v9:
time: 126 us
  blocking collectives  35.9 us (28%)
  waiting for transfers between devices  31.8 us (25%)
  starting transfers between devices  25.9 us (21%)
  Pallas kernels  12.4 us (10%)
  local copies, waits for them, and re-layouts  7.2 us (6%)
  matrix products  6.39 us (5%)
  other arithmetic  5.88 us (5%)
    ppermute x4, starting transfers between devices, from_behind(): lax.ppermute(array, axis, [(i, (i + by) % length) for i in range(length)])  21.9 us
    all_to_all x1, blocking collectives, gather_cols(): return lax.all_to_all(spread, 'mp', 1, 1).reshape(rows, n_mp * cols)  18.7 us
    ppermute x4, waiting for transfers between devices, from_behind(): lax.ppermute(array, axis, [(i, (i + by) % length) for i in range(length)])  17.7 us
    all_to_all x1, blocking collectives, scatter_sum(): got = lax.all_to_all(parts.reshape(rows, n_mp, cols // n_mp), 'mp', 1, 1)  17.2 us
    all_to_all x1, waiting for transfers between devices, scatter_sum(): got = lax.all_to_all(parts.reshape(rows, n_mp, cols // n_mp), 'mp', 1, 1)  14.2 us
    pallas_call x1, Pallas kernels, per_device(): pl.pallas_call(functools.partial(window_attention, n_heads=heads_here, n_...  12.4 us
    all_to_all x1, starting transfers between devices, scatter_sum(): got = lax.all_to_all(parts.reshape(rows, n_mp, cols // n_mp), 'mp', 1, 1)  4.02 us
    dot_general x1, matrix products, per_device(): down_term = jnp.dot(hidden, w_down, preferred_element_type=jnp.float32)  3.97 us
  transfers between devices with their start and end apart: 5, of which 5 were waited for; matrix products, arithmetic and copies ran while one was open for 2% of the time, Pallas kernels for 0%

profile of v9, /device:TPU:1, one launch (start us, length us, event | category | flops | bytes accessed | tf_op | source)
XLA Modules:
  0.0 125.6 jit_solution(15504554476775593865)
XLA Ops:
  0.0 0.0 copy-start
  0.0 1.6 %fusion = f32[512]{0:T(512)S(1)} fusion(bf16[512,1024]{1,0:T(8,128)(2,1)} %param.8), kind=kLoop, calls=%fused_computation.2 | loop fusion | flops 1572352 | bytes 1050624 | tf_op jit(solution)/shard_map/reduce_sum | solution.py:24
  1.6 0.0 copy-start.1
  1.6 0.0 copy-start.5
  1.6 1.5 %slice_bitcast_fusion.2 = (bf16[1024,256]{1,0:T(8,128)(2,1)S(1)}, bf16[1024,256]{1,0:T(8,128)(2,1)S(1)}, bf16[1024,256]{1,0:T(8,128)(2,1)S(1)}) fusion(bf16[3,1024,256]{2,1,0:T(8,128)(2,1)} %param.10), kind=kLoop, calls=%fused_computation.40 | loop fusion | bytes 3145728 | tf_op jit(solution)/shard_map/squeeze | solution.py:85
  3.2 0.1 copy-done.1
  3.3 0.0 copy-done.5
  3.3 1.0 fusion.11
  4.4 0.0 copy-start.2
  4.4 14.4 %collective-permute-start.3 = (bf16[512,512]{1,0:T(8,128)(2,1)S(1)}, bf16[512,512]{1,0:T(8,128)(2,1)}, u32[]{:S(2)}, u32[]{:S(2)}) collective-permute-start(bf16[512,512]{1,0:T(8,128)(2,1)S(1)} %slice.53.refs_2_), channel_id=1, source_target_pairs={{0,504},{4,508},{8,0},{12,4},{16,8},{20,12},{24,16},{28,20},{32,24... | collective-permute-start | bytes 1572872 | tf_op jit(solution)/shard_map/ppermute | solution.py:19
  18.8 2.9 %collective-permute-start.2 = (bf16[512,512]{1,0:T(8,128)(2,1)S(1)}, bf16[512,512]{1,0:T(8,128)(2,1)}, u32[]{:S(2)}, u32[]{:S(2)}) collective-permute-start(bf16[512,512]{1,0:T(8,128)(2,1)S(1)} %slice.53.refs_2_), channel_id=1, source_target_pairs={{0,508},{4,0},{8,4},{12,8},{16,12},{20,16},{24,20},{28,24},{32,28}... | collective-permute-start | bytes 1572872 | tf_op jit(solution)/shard_map/ppermute | solution.py:19
  21.7 2.7 %collective-permute-start.1 = (bf16[512,512]{1,0:T(8,128)(2,1)S(1)}, bf16[512,512]{1,0:T(8,128)(2,1)}, u32[]{:S(2)}, u32[]{:S(2)}) collective-permute-start(bf16[512,512]{1,0:T(8,128)(2,1)S(1)} %slice.53.refs_2_), channel_id=1, source_target_pairs={{0,4},{4,8},{8,12},{12,16},{16,20},{20,24},{24,28},{28,32},{32,36}... | collective-permute-start | bytes 1572872 | tf_op jit(solution)/shard_map/ppermute | solution.py:19
  24.4 1.9 %collective-permute-start = (bf16[512,512]{1,0:T(8,128)(2,1)S(1)}, bf16[512,512]{1,0:T(8,128)(2,1)}, u32[]{:S(2)}, u32[]{:S(2)}) collective-permute-start(bf16[512,512]{1,0:T(8,128)(2,1)S(1)} %slice.53.refs_2_), channel_id=1, source_target_pairs={{0,8},{4,12},{8,16},{12,20},{16,24},{20,28},{24,32},{28,36},{32,40... | collective-permute-start | bytes 1572872 | tf_op jit(solution)/shard_map/ppermute | solution.py:19
  26.3 0.7 slice.52.query_ref
  27.0 0.8 constant_dynamic-slice_fusion
  27.8 0.1 copy.19
  27.9 0.6 fusion.36.slot_ref
  28.5 0.0 copy-start.3
  28.5 0.9 collective-permute-done.3.refs_4_
  29.4 0.3 collective-permute-done.2.refs_3_
  29.7 3.9 %collective-permute-done.1.refs_1_ = bf16[512,512]{1,0:T(8,128)(2,1)} collective-permute-done((bf16[512,512]{1,0:T(8,128)(2,1)S(1)}, bf16[512,512]{1,0:T(8,128)(2,1)}, u32[]{:S(2)}, u32[]{:S(2)}) %collective-permute-start.1) | collective-permute-done | bytes 524320 | tf_op jit(solution)/shard_map/ppermute | solution.py:19
  33.6 12.6 %collective-permute-done.refs_0_ = bf16[512,512]{1,0:T(8,128)(2,1)} collective-permute-done((bf16[512,512]{1,0:T(8,128)(2,1)S(1)}, bf16[512,512]{1,0:T(8,128)(2,1)}, u32[]{:S(2)}, u32[]{:S(2)}) %collective-permute-start) | collective-permute-done | bytes 524320 | tf_op jit(solution)/shard_map/ppermute | solution.py:19
  46.2 0.0 copy-done.2
  46.2 12.4 %shard_map.82 = bf16[512,256]{1,0:T(8,128)(2,1)} custom-call(s32[4,8]{1,0:T(4,128)} %fusion.36.slot_ref, bf16[512,256]{1,0:T(8,128)(2,1)} %slice.52.query_ref, bf16[512,512]{1,0:T(8,128)(2,1)} %collective-permute-done.refs_0_, bf16[512,512]{1,0:T(8,128)(2,1)} %collective-permute-done.1.refs_1_, bf16[512,512]{1,0:T(8,128)(2,1)} %copy-done.2, ...), custom_call_target="tpu_custom_call" | custom-call | tf_op jit(solution)/shard_map/pallas_call | solution.py:101
  58.6 0.0 copy-done.3
  58.6 1.4 %convolution_convert_fusion = bf16[512,1024]{1,0:T(8,128)(2,1)S(1)} fusion(bf16[512,256]{1,0:T(8,128)(2,1)} %shard_map.82, bf16[256,1024]{1,0:T(8,128)(2,1)S(1)} %copy-done.3), kind=kOutput, calls=%fused_computation.16 | convolution fusion | flops 268959744 | bytes 1835008 | tf_op jit(solution)/shard_map/dot_general | solution.py:113
  60.0 1.0 copy.25
  61.0 4.0 %all-to-all-start = ((bf16[512,4,256]{2,0,1:T(8,128)(2,1)}), bf16[512,4,256]{2,0,1:T(8,128)(2,1)S(1)}, u32[]{:S(2)}, u32[]{:S(2)}) async-start(bf16[512,4,256]{2,0,1:T(8,128)(2,1)} %bitcast.34), calls=%async_computation | async-start | bytes 2097152 | tf_op jit(solution)/shard_map/all_to_all | solution.py:30
  65.0 14.2 %all-to-all-done = bf16[512,4,256]{2,0,1:T(8,128)(2,1)S(1)} async-done(((bf16[512,4,256]{2,0,1:T(8,128)(2,1)}), bf16[512,4,256]{2,0,1:T(8,128)(2,1)S(1)}, u32[]{:S(2)}, u32[]{:S(2)}) %all-to-all-start) | async-done | bytes 1048608 | tf_op jit(solution)/shard_map/all_to_all | solution.py:30
  79.2 0.2 fusion.43
  79.4 0.1 broadcast_in_dim.2
  79.4 18.7 %all_to_all.15 = bf16[512,4,256]{2,0,1:T(8,128)(2,1)} all-to-all(bf16[512,4,256]{2,0,1:T(8,128)(2,1)S(1)} %broadcast_in_dim.2), channel_id=1, replica_groups=mesh['patch'=128,'mp'=4] {'mp'}, dimensions={1} | all-to-all | bytes 2097152 | tf_op jit(solution)/shard_map/all_to_all | solution.py:40
  98.1 0.0 copy-start.4
  98.1 1.5 %copy.17 = bf16[512,4,256]{0,2,1:T(8,128)(2,1)S(1)} copy(bf16[512,4,256]{2,0,1:T(8,128)(2,1)} %all_to_all.15) | data formatting | bytes 2097152 | tf_op jit(solution)/shard_map/all_to_all | solution.py:40
  99.6 0.3 multiply_reduce_fusion
  99.9 0.0 copy-done.4
  99.9 1.3 %fusion.4 = bf16[512,1024]{0,1:T(8,128)(2,1)} fusion(f32[1024]{0:T(1024)S(1)} %copy-done.4, f32[512]{0:T(512)S(1)} %add_rsqrt_fusion, bf16[512,4,256]{0,2,1:T(8,128)(2,1)S(1)} %copy.17), kind=kLoop, calls=%fused_computation.7 | loop fusion | flops 2097152 | bytes 2103296 | tf_op jit(solution)/shard_map/convert_element_type | solution.py:123
  101.2 0.0 copy-done
  101.2 4.0 %convolution_convert_fusion.1 = bf16[512,1024]{1,0:T(8,128)(2,1)} fusion(bf16[512,1024]{1,0:T(8,128)(2,1)S(1)} %copy-done, bf16[512,1024]{0,1:T(8,128)(2,1)} %fusion.4, bf16[1024,512]{1,0:T(8,128)(2,1)} %param.13), kind=kOutput, calls=%fused_computation.17 | convolution fusion | flops 1076625408 | bytes 4194304 | tf_op jit(solution)/shard_map/dot_general | solution.py:127
  105.2 1.3 %copy.24 = bf16[64,4,8,256]{3,2,0,1:T(8,128)(2,1)S(1)} copy(bf16[64,4,8,256]{3,2,1,0:T(8,128)(2,1)} %bitcast.37) | data formatting | bytes 2097152 | tf_op jit(solution)/shard_map/reshape | solution.py:30
  106.5 17.2 %all_to_all.16 = bf16[512,4,256]{2,0,1:T(8,128)(2,1)S(1)} all-to-all(bf16[512,4,256]{2,0,1:T(8,128)(2,1)S(1)} %bitcast.36), channel_id=1, replica_groups=mesh['patch'=128,'mp'=4] {'mp'}, dimensions={1} | all-to-all | bytes 2097152 | tf_op jit(solution)/shard_map/all_to_all | solution.py:30
  123.7 2.0 %fusion.26 = bf16[512,256]{1,0:T(8,128)(2,1)} fusion(bf16[512,4,256]{2,0,1:T(8,128)(2,1)S(1)} %all_to_all.16, bf16[512,4,256]{2,0,1:T(8,128)(2,1)S(1)} %all-to-all-done, bf16[512,1024]{1,0:T(8,128)(2,1)} %param.8, s32[]{:T(128)S(6)} %select_n.22), kind=kLoop, calls=%fused_computation.32 | loop fusion | flops 2359296 | bytes 2621444 | tf_op jit(solution)/shard_map/convert_element_type | solution.py:129
  (3 shorter events, 0.1 us)
Async XLA Ops:
  0.0 101.2 %copy-start = (bf16[512,1024]{1,0:T(8,128)(2,1)S(1)}, bf16[512,1024]{1,0:T(8,128)(2,1)}, u32[]{:S(2)}) copy-start(bf16[512,1024]{1,0:T(8,128)(2,1)} %param.14) | copy-start | bytes 3145732
  1.6 1.7 %copy-start.1 = (bf16[512,1024]{1,0:T(8,128)(2,1)S(1)}, bf16[512,1024]{1,0:T(8,128)(2,1)}, u32[]{:S(2)}) copy-start(bf16[512,1024]{1,0:T(8,128)(2,1)} %param.8) | copy-start | bytes 3145732
  1.6 1.7 %copy-start.5 = (f32[1024]{0:T(1024)S(1)}, f32[1024]{0:T(1024)}, u32[]{:S(2)}) copy-start(f32[1024]{0:T(1024)} %param.9) | copy-start | bytes 12292
  4.4 41.8 %copy-start.2 = (bf16[512,512]{1,0:T(8,128)(2,1)}, bf16[512,512]{1,0:T(8,128)(2,1)S(1)}, u32[]{:S(2)}) copy-start(bf16[512,512]{1,0:T(8,128)(2,1)S(1)} %slice.53.refs_2_) | copy-start | bytes 1572868
  4.4 25.0 %collective-permute-start.3 = (bf16[512,512]{1,0:T(8,128)(2,1)S(1)}, bf16[512,512]{1,0:T(8,128)(2,1)}, u32[]{:S(2)}, u32[]{:S(2)}) collective-permute-start(bf16[512,512]{1,0:T(8,128)(2,1)S(1)} %slice.53.refs_2_), channel_id=1, source_target_pairs={{0,504},{4,508},{8,0},{12,4},{16,8},{20,12},{24,16},{28,20},{32,24... | collective-permute-start | bytes 1572872 | tf_op jit(solution)/shard_map/ppermute | solution.py:19
  18.8 10.9 %collective-permute-start.2 = (bf16[512,512]{1,0:T(8,128)(2,1)S(1)}, bf16[512,512]{1,0:T(8,128)(2,1)}, u32[]{:S(2)}, u32[]{:S(2)}) collective-permute-start(bf16[512,512]{1,0:T(8,128)(2,1)S(1)} %slice.53.refs_2_), channel_id=1, source_target_pairs={{0,508},{4,0},{8,4},{12,8},{16,12},{20,16},{24,20},{28,24},{32,28}... | collective-permute-start | bytes 1572872 | tf_op jit(solution)/shard_map/ppermute | solution.py:19
  21.7 11.9 %collective-permute-start.1 = (bf16[512,512]{1,0:T(8,128)(2,1)S(1)}, bf16[512,512]{1,0:T(8,128)(2,1)}, u32[]{:S(2)}, u32[]{:S(2)}) collective-permute-start(bf16[512,512]{1,0:T(8,128)(2,1)S(1)} %slice.53.refs_2_), channel_id=1, source_target_pairs={{0,4},{4,8},{8,12},{12,16},{16,20},{20,24},{24,28},{28,32},{32,36}... | collective-permute-start | bytes 1572872 | tf_op jit(solution)/shard_map/ppermute | solution.py:19
  24.4 21.8 %collective-permute-start = (bf16[512,512]{1,0:T(8,128)(2,1)S(1)}, bf16[512,512]{1,0:T(8,128)(2,1)}, u32[]{:S(2)}, u32[]{:S(2)}) collective-permute-start(bf16[512,512]{1,0:T(8,128)(2,1)S(1)} %slice.53.refs_2_), channel_id=1, source_target_pairs={{0,8},{4,12},{8,16},{12,20},{16,24},{20,28},{24,32},{28,36},{32,40... | collective-permute-start | bytes 1572872 | tf_op jit(solution)/shard_map/ppermute | solution.py:19
  28.5 30.1 %copy-start.3 = (bf16[256,1024]{1,0:T(8,128)(2,1)S(1)}, bf16[256,1024]{1,0:T(8,128)(2,1)}, u32[]{:S(2)}) copy-start(bf16[256,1024]{1,0:T(8,128)(2,1)} %param.11) | copy-start | bytes 1572868
  61.0 18.2 %all-to-all-start = ((bf16[512,4,256]{2,0,1:T(8,128)(2,1)}), bf16[512,4,256]{2,0,1:T(8,128)(2,1)S(1)}, u32[]{:S(2)}, u32[]{:S(2)}) async-start(bf16[512,4,256]{2,0,1:T(8,128)(2,1)} %bitcast.34), calls=%async_computation | async-start | bytes 2097152 | tf_op jit(solution)/shard_map/all_to_all | solution.py:30
  98.1 1.8 %copy-start.4 = (f32[1024]{0:T(1024)S(1)}, f32[1024]{0:T(1024)}, u32[]{:S(2)}) copy-start(f32[1024]{0:T(1024)} %param.12) | copy-start | bytes 12292

commit v10 on v5

--- a/solution.py
+++ b/solution.py
@@ -50,8 +50,7 @@
 
 def window_attention(slot_ref, query_ref, *refs, n_heads, n_win, n_nb):
     kv_refs, out_ref, gathered = refs[:n_win], refs[n_win], refs[n_win + 1]
-    width = n_heads * HD
-    per_win = kv_refs[0].shape[0] // PN
+    per_win = kv_refs[0].shape[1] // PN
     patch = pl.program_id(0)
     for k in range(n_nb):
         slot = slot_ref[patch, k]
@@ -60,21 +59,21 @@
         for w in range(n_win):
             @pl.when(block == w)
             def _():
-                gathered[k * PN:(k + 1) * PN, :] = kv_refs[w][pl.ds(pl.multiple_of(local * PN, PN), PN), :]
+                start = pl.multiple_of(local * PN, PN)
+                gathered[:, k * PN:(k + 1) * PN, :] = kv_refs[w][:, pl.ds(start, PN), :]
     lane = lax.broadcasted_iota(jnp.int32, (PN, 2 * HD), 1)
     for pair in range(n_heads // 2):
         cols = slice(pair * 2 * HD, (pair + 1) * 2 * HD)
-        v_cols = slice(width + pair * 2 * HD, width + (pair + 1) * 2 * HD)
-        q_pair = query_ref[:, cols]
-        keys = gathered[:, cols]
-        vals = gathered[:, v_cols]
+        q_pair = query_ref[:, cols] * jnp.asarray(1.0 / HD**0.5, query_ref.dtype)
+        keys = gathered[0, :, cols]
+        vals = gathered[1, :, cols]
         mixed = []
         for half in range(2):
             keep = (lane >= half * HD) & (lane < (half + 1) * HD)
             q_head = jnp.where(keep, q_pair, jnp.zeros_like(q_pair))
             s = lax.dot_general(
                 q_head, keys, (((1,), (1,)), ((), ())), preferred_element_type=jnp.float32
-            ) * (1.0 / HD**0.5)
+            )
             e = jnp.exp(s - s.max(axis=1, keepdims=True))
             inv = 1.0 / e.sum(axis=1, keepdims=True)
             probs = (e * inv).astype(jnp.bfloat16)
@@ -90,10 +89,11 @@
     heads_here = width // HD
     n_win = 2 * REACH + 1
     normed = normalize(features, gain_attn)
-    w_all = jnp.concatenate([w_qkv[0], w_qkv[1], w_qkv[2]], axis=1)
-    qkv = jnp.dot(normed, w_all, preferred_element_type=jnp.float32).astype(jnp.bfloat16)
-    queries = qkv[:, :width]
-    own_kv = qkv[:, width:]
+    qkv = jnp.einsum(
+        "rk,tkc->trc", normed, w_qkv, preferred_element_type=jnp.float32
+    ).astype(jnp.bfloat16)
+    queries = qkv[0]
+    own_kv = qkv[1:]
     window = {0: own_kv}
     for offset in range(-REACH, REACH + 1):
         if offset != 0:
@@ -105,7 +105,7 @@
     offset_dev = jnp.mod(owner_dev - device + n_dev // 2, n_dev) - n_dev // 2
     slot_index = (offset_dev + REACH) * patches_here + jnp.mod(listed, patches_here)
     kv_list = [window[offset] for offset in range(-REACH, REACH + 1)]
-    kv_spec = pl.BlockSpec((row_count, 2 * width), lambda p, slots: (0, 0))
+    kv_spec = pl.BlockSpec((2, row_count, width), lambda p, slots: (0, 0, 0))
     attended = pl.pallas_call(
         functools.partial(window_attention, n_heads=heads_here, n_win=n_win, n_nb=K_NB),
         grid_spec=pltpu.PrefetchScalarGridSpec(
@@ -113,7 +113,7 @@
             grid=(patches_here,),
             in_specs=[pl.BlockSpec((PN, width), lambda p, slots: (p, 0))] + [kv_spec] * n_win,
             out_specs=pl.BlockSpec((PN, width), lambda p, slots: (p, 0)),
-            scratch_shapes=[pltpu.VMEM((K_NB * PN, 2 * width), jnp.bfloat16)],
+            scratch_shapes=[pltpu.VMEM((2, K_NB * PN, width), jnp.bfloat16)],
         ),
         out_shape=jax.ShapeDtypeStruct((row_count, width), jnp.bfloat16),
     )(slot_index.astype(jnp.int32), queries, *kv_list)

time: 111 us -> 112 us (level)
  local copies, waits for them, and re-layouts: 7.24 us -> 5.56 us
  matrix products: 5.36 us -> 6.9 us
  other arithmetic: 3.1 us -> 4.44 us
    reduce_sum x1, other arithmetic: 0.28 us -> 1.62 us  [normalize(): mean_sq = jnp.mean(rows32 * rows32, axis=-1, keepdims=True)]
    dot_general x1, matrix products: 1.04 us -> 2.26 us  [per_device(): jnp.einsum('rk,tkc->trc', normed, w_qkv, preferred_element_type=jnp.float32)]
where the time goes in v10:
time: 112 us
  starting transfers between devices  30.8 us (28%)
  blocking collectives  26.6 us (24%)
  waiting for transfers between devices  24.9 us (22%)
  Pallas kernels  12.2 us (11%)
  matrix products  6.9 us (6%)
  local copies, waits for them, and re-layouts  5.56 us (5%)
  other arithmetic  4.44 us (4%)
    ppermute x4, starting transfers between devices, from_behind(): lax.ppermute(array, axis, [(i, (i + by) % length) for i in range(length)])  21.3 us
    all_to_all x1, blocking collectives, scatter_sum(): got = lax.all_to_all(parts.reshape(rows, n_mp, cols // n_mp), 'mp', 1, 1)  13.3 us
    all_to_all x1, blocking collectives, gather_cols(): return lax.all_to_all(spread, 'mp', 1, 1).reshape(rows, n_mp * cols)  13.3 us
    pallas_call x1, Pallas kernels, per_device(): pl.pallas_call(functools.partial(window_attention, n_heads=heads_here, n_...  12.2 us
    ppermute x4, waiting for transfers between devices, from_behind(): lax.ppermute(array, axis, [(i, (i + by) % length) for i in range(length)])  11.5 us
    all_to_all x1, waiting for transfers between devices, scatter_sum(): got = lax.all_to_all(parts.reshape(rows, n_mp, cols // n_mp), 'mp', 1, 1)  10.3 us
    all_to_all x1, starting transfers between devices, scatter_sum(): got = lax.all_to_all(parts.reshape(rows, n_mp, cols // n_mp), 'mp', 1, 1)  4.83 us
    all_to_all x1, starting transfers between devices, gather_sum(): lax.all_to_all(jnp.broadcast_to(vector[None], (n_mp,) + vector.shape), 'm...  4.68 us
  transfers between devices with their start and end apart: 6, of which 5 were waited for; matrix products, arithmetic and copies ran while one was open for 3% of the time, Pallas kernels for 0%

profile of v10, /device:TPU:2, one launch (start us, length us, event | category | flops | bytes accessed | tf_op | source)
XLA Modules:
  0.0 111.6 jit_solution(11074314222642104087)
XLA Ops:
  0.0 0.0 copy-start
  0.0 1.6 %fusion = f32[512]{0:T(512)S(1)} fusion(bf16[512,1024]{1,0:T(8,128)(2,1)} %param.8), kind=kLoop, calls=%fused_computation.2 | loop fusion | flops 1572352 | bytes 1050624 | tf_op jit(solution)/shard_map/reduce_sum | solution.py:24
  1.6 0.1 copy-done
  1.7 2.3 %fusion.3 = bf16[3,512,256]{2,1,0:T(8,128)(2,1)S(1)} fusion(bf16[3,1024,256]{2,1,0:T(8,128)(2,1)S(1)} %copy-done, bf16[512,1024]{1,0:T(8,128)(2,1)} %param.8, f32[1024]{0:T(1024)} %param.9, f32[512]{0:T(512)S(1)} %add_rsqrt_fusion.1), kind=kOutput, calls=%fused_computation.9 | convolution fusion | flops 807796736 | bytes 3414016 | tf_op jit(solution)/shard_map/rk,tkc->trc/dot_general | solution.py:92
  4.0 0.0 copy-start.1
  4.0 3.5 %collective-permute-start = (bf16[2,512,256]{2,1,0:T(8,128)(2,1)S(1)}, bf16[2,512,256]{2,1,0:T(8,128)(2,1)S(1)}, u32[]{:S(2)}, u32[]{:S(2)}) collective-permute-start(bf16[2,512,256]{2,1,0:T(8,128)(2,1)S(1)} %slice.61.refs_2_), channel_id=1, source_target_pairs={{0,8},{4,12},{8,16},{12,20},{16,24},{20,28},{24,32},{28,36},{32,40... | collective-permute-start | bytes 1572872 | tf_op jit(solution)/shard_map/ppermute | solution.py:19
  7.5 1.9 %collective-permute-start.1 = (bf16[2,512,256]{2,1,0:T(8,128)(2,1)S(1)}, bf16[2,512,256]{2,1,0:T(8,128)(2,1)}, u32[]{:S(2)}, u32[]{:S(2)}) collective-permute-start(bf16[2,512,256]{2,1,0:T(8,128)(2,1)S(1)} %slice.61.refs_2_), channel_id=1, source_target_pairs={{0,4},{4,8},{8,12},{12,16},{16,20},{20,24},{24,28},{28,32},{32,36}... | collective-permute-start | bytes 1572872 | tf_op jit(solution)/shard_map/ppermute | solution.py:19
  9.5 11.7 %collective-permute-start.2 = (bf16[2,512,256]{2,1,0:T(8,128)(2,1)S(1)}, bf16[2,512,256]{2,1,0:T(8,128)(2,1)}, u32[]{:S(2)}, u32[]{:S(2)}) collective-permute-start(bf16[2,512,256]{2,1,0:T(8,128)(2,1)S(1)} %slice.61.refs_2_), channel_id=1, source_target_pairs={{0,508},{4,0},{8,4},{12,8},{16,12},{20,16},{24,20},{28,24},{32,28}... | collective-permute-start | bytes 1572872 | tf_op jit(solution)/shard_map/ppermute | solution.py:19
  21.2 4.2 %collective-permute-start.3 = (bf16[2,512,256]{2,1,0:T(8,128)(2,1)S(1)}, bf16[2,512,256]{2,1,0:T(8,128)(2,1)}, u32[]{:S(2)}, u32[]{:S(2)}) collective-permute-start(bf16[2,512,256]{2,1,0:T(8,128)(2,1)S(1)} %slice.61.refs_2_), channel_id=1, source_target_pairs={{0,504},{4,508},{8,0},{12,4},{16,8},{20,12},{24,16},{28,20},{32,24... | collective-permute-start | bytes 1572872 | tf_op jit(solution)/shard_map/ppermute | solution.py:19
  25.4 0.8 constant_dynamic-slice_fusion
  26.2 0.1 copy.19
  26.3 0.6 fusion.27.slot_ref
  26.9 0.7 slice_bitcast_fusion.query_ref
  27.6 0.0 copy-start.2
  27.6 3.1 %collective-permute-done.refs_0_ = bf16[2,512,256]{2,1,0:T(8,128)(2,1)S(1)} collective-permute-done((bf16[2,512,256]{2,1,0:T(8,128)(2,1)S(1)}, bf16[2,512,256]{2,1,0:T(8,128)(2,1)S(1)}, u32[]{:S(2)}, u32[]{:S(2)}) %collective-permute-start) | collective-permute-done | bytes 524320 | tf_op jit(solution)/shard_map/ppermute | solution.py:19
  30.7 0.0 copy-start.3
  30.7 4.9 %collective-permute-done.1.refs_1_ = bf16[2,512,256]{2,1,0:T(8,128)(2,1)} collective-permute-done((bf16[2,512,256]{2,1,0:T(8,128)(2,1)S(1)}, bf16[2,512,256]{2,1,0:T(8,128)(2,1)}, u32[]{:S(2)}, u32[]{:S(2)}) %collective-permute-start.1) | collective-permute-done | bytes 524320 | tf_op jit(solution)/shard_map/ppermute | solution.py:19
  35.5 0.0 collective-permute-done.2.refs_3_
  35.5 3.6 %collective-permute-done.3.refs_4_ = bf16[2,512,256]{2,1,0:T(8,128)(2,1)} collective-permute-done((bf16[2,512,256]{2,1,0:T(8,128)(2,1)S(1)}, bf16[2,512,256]{2,1,0:T(8,128)(2,1)}, u32[]{:S(2)}, u32[]{:S(2)}) %collective-permute-start.3) | collective-permute-done | bytes 524320 | tf_op jit(solution)/shard_map/ppermute | solution.py:19
  39.1 0.0 copy-done.1
  39.1 0.0 copy-done.3
  39.1 12.2 %shard_map.82 = bf16[512,256]{1,0:T(8,128)(2,1)} custom-call(s32[4,8]{1,0:T(4,128)} %fusion.27.slot_ref, bf16[512,256]{1,0:T(8,128)(2,1)} %slice_bitcast_fusion.query_ref, bf16[2,512,256]{2,1,0:T(8,128)(2,1)} %copy-done.3, bf16[2,512,256]{2,1,0:T(8,128)(2,1)} %collective-permute-done.1.refs_1_, bf16[2,512,256]{2,1,0:T(8,128)(2,1)} %copy-done.1, ...), custom_call_target="tpu_custom_call" | custom-call | tf_op jit(solution)/shard_map/pallas_call | solution.py:109
  51.3 0.0 copy-done.2
  51.3 1.4 %convolution_convert_fusion = bf16[512,1024]{1,0:T(8,128)(2,1)S(1)} fusion(bf16[512,256]{1,0:T(8,128)(2,1)} %shard_map.82, bf16[256,1024]{1,0:T(8,128)(2,1)S(1)} %copy-done.2), kind=kOutput, calls=%fused_computation.6 | convolution fusion | flops 268959744 | bytes 1835008 | tf_op jit(solution)/shard_map/dot_general | solution.py:121
  52.7 1.0 copy.25
  53.8 4.8 %all-to-all-start = ((bf16[512,4,256]{2,0,1:T(8,128)(2,1)}), bf16[512,4,256]{2,0,1:T(8,128)(2,1)S(1)}, u32[]{:S(2)}, u32[]{:S(2)}) async-start(bf16[512,4,256]{2,0,1:T(8,128)(2,1)} %bitcast.31), calls=%async_computation | async-start | bytes 2097152 | tf_op jit(solution)/shard_map/all_to_all | solution.py:30
  58.6 10.3 %all-to-all-done = bf16[512,4,256]{2,0,1:T(8,128)(2,1)S(1)} async-done(((bf16[512,4,256]{2,0,1:T(8,128)(2,1)}), bf16[512,4,256]{2,0,1:T(8,128)(2,1)S(1)}, u32[]{:S(2)}, u32[]{:S(2)}) %all-to-all-start) | async-done | bytes 1048608 | tf_op jit(solution)/shard_map/all_to_all | solution.py:30
  68.9 1.2 %multiply_reduce_fusion = (f32[512]{0:T(512)S(1)}, f32[512,256]{1,0:T(8,128)S(1)}) fusion(bf16[512,4,256]{2,0,1:T(8,128)(2,1)S(1)} %all-to-all-done, bf16[512,1024]{1,0:T(8,128)(2,1)} %param.8, s32[]{:T(128)S(6)} %select_n.23), kind=kLoop, calls=%fused_computation.31 | loop fusion | flops 1441280 | bytes 1837060 | tf_op jit(solution)/shard_map/reduce_sum | solution.py:129
  70.1 0.6 broadcast_in_dim.4
  70.7 4.7 %all-to-all-start.1 = ((f32[4,1,512]{2,1,0:T(1,128)}), f32[4,1,512]{2,1,0:T(1,128)S(1)}, u32[]{:S(2)}, u32[]{:S(2)}) async-start(f32[4,1,512]{2,1,0:T(1,128)} %broadcast_in_dim.4), calls=%async_computation.1 | async-start | bytes 16384 | tf_op jit(solution)/shard_map/all_to_all | solution.py:38
  75.4 0.8 dynamic_slice.11
  76.2 3.1 %all-to-all-done.1 = f32[4,1,512]{2,1,0:T(1,128)S(1)} async-done(((f32[4,1,512]{2,1,0:T(1,128)}), f32[4,1,512]{2,1,0:T(1,128)S(1)}, u32[]{:S(2)}, u32[]{:S(2)}) %all-to-all-start.1) | async-done | bytes 8224 | tf_op jit(solution)/shard_map/all_to_all | solution.py:38
  79.3 0.1 multiply_convert_fusion
  79.4 0.1 broadcast_in_dim.5
  79.5 13.3 %all_to_all.21 = bf16[512,4,256]{2,0,1:T(8,128)(2,1)S(1)} all-to-all(bf16[512,4,256]{2,0,1:T(8,128)(2,1)S(1)} %broadcast_in_dim.5), channel_id=1, replica_groups=mesh['patch'=128,'mp'=4] {'mp'}, dimensions={1} | all-to-all | bytes 2097152 | tf_op jit(solution)/shard_map/all_to_all | solution.py:48
  92.8 1.3 %copy.17 = bf16[512,4,256]{0,2,1:T(8,128)(2,1)} copy(bf16[512,4,256]{2,0,1:T(8,128)(2,1)S(1)} %all_to_all.21) | data formatting | bytes 2097152 | tf_op jit(solution)/shard_map/all_to_all | solution.py:48
  94.1 3.3 %convolution_convert_fusion.1 = bf16[512,1024]{1,0:T(8,128)(2,1)S(1)} fusion(bf16[512,1024]{1,0:T(8,128)(2,1)} %param.14, bf16[512,1024]{0,1:T(8,128)(2,1)} %bitcast.33, bf16[1024,512]{1,0:T(8,128)(2,1)} %param.13), kind=kOutput, calls=%fused_computation.7 | convolution fusion | flops 1076625408 | bytes 4194304 | tf_op jit(solution)/shard_map/dot_general | solution.py:136
  97.4 0.1 copy.24
  97.5 13.3 %all_to_all.22 = bf16[512,4,256]{2,0,1:T(8,128)(2,1)S(1)} all-to-all(bf16[512,4,256]{2,0,1:T(8,128)(2,1)S(1)} %bitcast.32), channel_id=1, replica_groups=mesh['patch'=128,'mp'=4] {'mp'}, dimensions={1} | all-to-all | bytes 2097152 | tf_op jit(solution)/shard_map/all_to_all | solution.py:30
  110.8 0.8 fusion.17
  (3 shorter events, 0.1 us)
Async XLA Ops:
  0.0 1.7 %copy-start = (bf16[3,1024,256]{2,1,0:T(8,128)(2,1)S(1)}, bf16[3,1024,256]{2,1,0:T(8,128)(2,1)}, u32[]{:S(2)}) copy-start(bf16[3,1024,256]{2,1,0:T(8,128)(2,1)} %param.10) | copy-start | bytes 4718596
  4.0 35.1 %copy-start.1 = (bf16[2,512,256]{2,1,0:T(8,128)(2,1)}, bf16[2,512,256]{2,1,0:T(8,128)(2,1)S(1)}, u32[]{:S(2)}) copy-start(bf16[2,512,256]{2,1,0:T(8,128)(2,1)S(1)} %slice.61.refs_2_) | copy-start | bytes 1572868
  4.0 26.6 %collective-permute-start = (bf16[2,512,256]{2,1,0:T(8,128)(2,1)S(1)}, bf16[2,512,256]{2,1,0:T(8,128)(2,1)S(1)}, u32[]{:S(2)}, u32[]{:S(2)}) collective-permute-start(bf16[2,512,256]{2,1,0:T(8,128)(2,1)S(1)} %slice.61.refs_2_), channel_id=1, source_target_pairs={{0,8},{4,12},{8,16},{12,20},{16,24},{20,28},{24,32},{28,36},{32,40... | collective-permute-start | bytes 1572872 | tf_op jit(solution)/shard_map/ppermute | solution.py:19
  7.5 28.0 %collective-permute-start.1 = (bf16[2,512,256]{2,1,0:T(8,128)(2,1)S(1)}, bf16[2,512,256]{2,1,0:T(8,128)(2,1)}, u32[]{:S(2)}, u32[]{:S(2)}) collective-permute-start(bf16[2,512,256]{2,1,0:T(8,128)(2,1)S(1)} %slice.61.refs_2_), channel_id=1, source_target_pairs={{0,4},{4,8},{8,12},{12,16},{16,20},{20,24},{24,28},{28,32},{32,36}... | collective-permute-start | bytes 1572872 | tf_op jit(solution)/shard_map/ppermute | solution.py:19
  9.5 26.1 %collective-permute-start.2 = (bf16[2,512,256]{2,1,0:T(8,128)(2,1)S(1)}, bf16[2,512,256]{2,1,0:T(8,128)(2,1)}, u32[]{:S(2)}, u32[]{:S(2)}) collective-permute-start(bf16[2,512,256]{2,1,0:T(8,128)(2,1)S(1)} %slice.61.refs_2_), channel_id=1, source_target_pairs={{0,508},{4,0},{8,4},{12,8},{16,12},{20,16},{24,20},{28,24},{32,28}... | collective-permute-start | bytes 1572872 | tf_op jit(solution)/shard_map/ppermute | solution.py:19
  21.2 17.9 %collective-permute-start.3 = (bf16[2,512,256]{2,1,0:T(8,128)(2,1)S(1)}, bf16[2,512,256]{2,1,0:T(8,128)(2,1)}, u32[]{:S(2)}, u32[]{:S(2)}) collective-permute-start(bf16[2,512,256]{2,1,0:T(8,128)(2,1)S(1)} %slice.61.refs_2_), channel_id=1, source_target_pairs={{0,504},{4,508},{8,0},{12,4},{16,8},{20,12},{24,16},{28,20},{32,24... | collective-permute-start | bytes 1572872 | tf_op jit(solution)/shard_map/ppermute | solution.py:19
  27.6 23.7 %copy-start.2 = (bf16[256,1024]{1,0:T(8,128)(2,1)S(1)}, bf16[256,1024]{1,0:T(8,128)(2,1)}, u32[]{:S(2)}) copy-start(bf16[256,1024]{1,0:T(8,128)(2,1)} %param.11) | copy-start | bytes 1572868
  30.7 8.5 %copy-start.3 = (bf16[2,512,256]{2,1,0:T(8,128)(2,1)}, bf16[2,512,256]{2,1,0:T(8,128)(2,1)S(1)}, u32[]{:S(2)}) copy-start(bf16[2,512,256]{2,1,0:T(8,128)(2,1)S(1)} %collective-permute-done.refs_0_) | copy-start | bytes 1572868
  53.8 15.1 %all-to-all-start = ((bf16[512,4,256]{2,0,1:T(8,128)(2,1)}), bf16[512,4,256]{2,0,1:T(8,128)(2,1)S(1)}, u32[]{:S(2)}, u32[]{:S(2)}) async-start(bf16[512,4,256]{2,0,1:T(8,128)(2,1)} %bitcast.31), calls=%async_computation | async-start | bytes 2097152 | tf_op jit(solution)/shard_map/all_to_all | solution.py:30
  70.7 8.5 %all-to-all-start.1 = ((f32[4,1,512]{2,1,0:T(1,128)}), f32[4,1,512]{2,1,0:T(1,128)S(1)}, u32[]{:S(2)}, u32[]{:S(2)}) async-start(f32[4,1,512]{2,1,0:T(1,128)} %broadcast_in_dim.4), calls=%async_computation.1 | async-start | bytes 16384 | tf_op jit(solution)/shard_map/all_to_all | solution.py:38

commit v11 on v5

--- a/solution.py
+++ b/solution.py
@@ -25,13 +25,17 @@
     return (rows32 * lax.rsqrt(mean_sq + 1e-05) * gain).astype(jnp.bfloat16)
 
 
-def scatter_sum(parts, n_mp):
+def scatter_sum(parts):
+    got = lax.all_to_all(parts, "mp", 0, 0)
+    total = got[0].astype(jnp.float32)
+    for which in range(1, got.shape[0]):
+        total = total + got[which].astype(jnp.float32)
+    return total
+
+
+def scatter_cols(parts, n_mp):
     rows, cols = parts.shape
-    got = lax.all_to_all(parts.reshape(rows, n_mp, cols // n_mp), "mp", 1, 1)
-    total = got[:, 0].astype(jnp.float32)
-    for which in range(1, n_mp):
-        total = total + got[:, which].astype(jnp.float32)
-    return total
+    return scatter_sum(parts.reshape(rows, n_mp, cols // n_mp).transpose(1, 0, 2))
 
 
 def gather_sum(vector, n_mp):
@@ -49,7 +53,8 @@
 
 
 def window_attention(slot_ref, query_ref, *refs, n_heads, n_win, n_nb):
-    kv_refs, out_ref, gathered = refs[:n_win], refs[n_win], refs[n_win + 1]
+    kv_refs, w_ref, out_ref = refs[:n_win], refs[n_win], refs[n_win + 1]
+    mixed_ref, gathered = refs[n_win + 2], refs[n_win + 3]
     width = n_heads * HD
     per_win = kv_refs[0].shape[0] // PN
     patch = pl.program_id(0)
@@ -80,7 +85,11 @@
             probs = (e * inv).astype(jnp.bfloat16)
             mixed.append(jnp.dot(probs, vals, preferred_element_type=jnp.float32))
         out = jnp.where(lane < HD, mixed[0], mixed[1])
-        out_ref[:, cols] = out.astype(out_ref.dtype)
+        mixed_ref[:, cols] = out.astype(mixed_ref.dtype)
+    projected = jnp.dot(mixed_ref[...], w_ref[...], preferred_element_type=jnp.float32)
+    chunk = out_ref.shape[2]
+    for j in range(out_ref.shape[0]):
+        out_ref[j] = projected[:, j * chunk:(j + 1) * chunk].astype(out_ref.dtype)
 
 
 def per_device(features, gain_attn, w_qkv, w_out, gain_mlp, w_up, w_down, neighbours):
@@ -105,21 +114,25 @@
     offset_dev = jnp.mod(owner_dev - device + n_dev // 2, n_dev) - n_dev // 2
     slot_index = (offset_dev + REACH) * patches_here + jnp.mod(listed, patches_here)
     kv_list = [window[offset] for offset in range(-REACH, REACH + 1)]
+    n_mp = lax.axis_size("mp")
     kv_spec = pl.BlockSpec((row_count, 2 * width), lambda p, slots: (0, 0))
-    attended = pl.pallas_call(
+    partial_value = pl.pallas_call(
         functools.partial(window_attention, n_heads=heads_here, n_win=n_win, n_nb=K_NB),
         grid_spec=pltpu.PrefetchScalarGridSpec(
             num_scalar_prefetch=1,
             grid=(patches_here,),
-            in_specs=[pl.BlockSpec((PN, width), lambda p, slots: (p, 0))] + [kv_spec] * n_win,
-            out_specs=pl.BlockSpec((PN, width), lambda p, slots: (p, 0)),
-            scratch_shapes=[pltpu.VMEM((K_NB * PN, 2 * width), jnp.bfloat16)],
+            in_specs=[pl.BlockSpec((PN, width), lambda p, slots: (p, 0))]
+            + [kv_spec] * n_win
+            + [pl.BlockSpec((width, D), lambda p, slots: (0, 0))],
+            out_specs=pl.BlockSpec((n_mp, PN, D // n_mp), lambda p, slots: (0, p, 0)),
+            scratch_shapes=[
+                pltpu.VMEM((PN, width), jnp.bfloat16),
+                pltpu.VMEM((K_NB * PN, 2 * width), jnp.bfloat16),
+            ],
         ),
-        out_shape=jax.ShapeDtypeStruct((row_count, width), jnp.bfloat16),
-    )(slot_index.astype(jnp.int32), queries, *kv_list)
-    n_mp = lax.axis_size("mp")
-    partial_value = jnp.dot(attended, w_out, preferred_element_type=jnp.float32)
-    col_share = scatter_sum(partial_value.astype(jnp.bfloat16), n_mp)
+        out_shape=jax.ShapeDtypeStruct((n_mp, row_count, D // n_mp), jnp.bfloat16),
+    )(slot_index.astype(jnp.int32), queries, *kv_list, w_out)
+    col_share = scatter_sum(partial_value)
     col_width = col_share.shape[1]
     col_begin = lax.axis_index("mp") * col_width
     residual_cols = (
@@ -134,7 +147,7 @@
         jnp.dot(normed2, w_up, preferred_element_type=jnp.float32), approximate=True
     ).astype(jnp.bfloat16)
     down_term = jnp.dot(hidden, w_down, preferred_element_type=jnp.float32)
-    down_cols = scatter_sum(down_term.astype(jnp.bfloat16), n_mp)
+    down_cols = scatter_cols(down_term.astype(jnp.bfloat16), n_mp)
     return (residual_cols + down_cols).astype(jnp.bfloat16)
 
 

time: 111 us -> 115 us (1.036)
  local copies, waits for them, and re-layouts: 7.24 us -> 8.92 us
    convert_element_type x0 -> x1, local copies, waits for them, and re-layouts: none -> 1.49 us  [per_device(): down_cols = scatter_cols(down_term.astype(jnp.bfloat16), n_mp)]
    dot_general x1 -> x0, matrix products: 1.39 us -> none  [per_device(): partial_value = jnp.dot(attended, w_out, preferred_element_type=jnp.float32)]
where the time goes in v11:
time: 115 us; the launch traced here: 114 us
  starting transfers between devices  30.8 us (27%)
  blocking collectives  27.7 us (24%)
  waiting for transfers between devices  25 us (22%)
  Pallas kernels  13.4 us (12%)
  local copies, waits for them, and re-layouts  8.92 us (8%)
  matrix products  4.98 us (4%)
  other arithmetic  3.1 us (3%)
    ppermute x4, starting transfers between devices, from_behind(): lax.ppermute(array, axis, [(i, (i + by) % length) for i in range(length)])  21.3 us
    all_to_all x1, blocking collectives, scatter_sum(): got = lax.all_to_all(parts, 'mp', 0, 0)  14.4 us
    pallas_call x1, Pallas kernels, per_device(): pl.pallas_call(functools.partial(window_attention, n_heads=heads_here, n_...  13.4 us
    all_to_all x1, blocking collectives, gather_cols(): return lax.all_to_all(spread, 'mp', 1, 1).reshape(rows, n_mp * cols)  13.3 us
    ppermute x4, waiting for transfers between devices, from_behind(): lax.ppermute(array, axis, [(i, (i + by) % length) for i in range(length)])  11.5 us
    all_to_all x1, waiting for transfers between devices, scatter_sum(): got = lax.all_to_all(parts, 'mp', 0, 0)  10.3 us
    all_to_all x1, starting transfers between devices, scatter_sum(): got = lax.all_to_all(parts, 'mp', 0, 0)  4.82 us
    all_to_all x1, starting transfers between devices, gather_sum(): lax.all_to_all(jnp.broadcast_to(vector[None], (n_mp,) + vector.shape), 'm...  4.68 us
  transfers between devices with their start and end apart: 6, of which 5 were waited for; matrix products, arithmetic and copies ran while one was open for 3% of the time, Pallas kernels for 0%

profile of v11, /device:TPU:2, one launch (start us, length us, event | category | flops | bytes accessed | tf_op | source)
XLA Modules:
  0.0 114.0 jit_solution(2876296281932308099)
XLA Ops:
  0.0 0.0 copy-start
  0.0 0.0 copy-start.2
  0.0 0.0 copy-start.6
  0.0 1.6 %slice_bitcast_fusion.2 = (bf16[1024,256]{1,0:T(8,128)(2,1)S(1)}, bf16[1024,256]{1,0:T(8,128)(2,1)S(1)}, bf16[1024,256]{1,0:T(8,128)(2,1)S(1)}) fusion(bf16[3,1024,256]{2,1,0:T(8,128)(2,1)} %param.10), kind=kLoop, calls=%fused_computation.35 | loop fusion | bytes 3145728 | tf_op jit(solution)/shard_map/squeeze | solution.py:102
  1.6 0.2 copy-done.2
  1.8 0.3 fusion
  2.1 0.0 copy-done.6
  2.1 1.0 fusion.9
  3.2 0.0 copy-start.1
  3.2 3.5 %collective-permute-start = (bf16[512,512]{1,0:T(8,128)(2,1)S(1)}, bf16[512,512]{1,0:T(8,128)(2,1)S(1)}, u32[]{:S(2)}, u32[]{:S(2)}) collective-permute-start(bf16[512,512]{1,0:T(8,128)(2,1)S(1)} %slice.73.refs_2_), channel_id=1, source_target_pairs={{0,8},{4,12},{8,16},{12,20},{16,24},{20,28},{24,32},{28,36},{32,40... | collective-permute-start | bytes 1572872 | tf_op jit(solution)/shard_map/ppermute | solution.py:19
  6.7 1.9 %collective-permute-start.1 = (bf16[512,512]{1,0:T(8,128)(2,1)S(1)}, bf16[512,512]{1,0:T(8,128)(2,1)S(1)}, u32[]{:S(2)}, u32[]{:S(2)}) collective-permute-start(bf16[512,512]{1,0:T(8,128)(2,1)S(1)} %slice.73.refs_2_), channel_id=1, source_target_pairs={{0,4},{4,8},{8,12},{12,16},{16,20},{20,24},{24,28},{28,32},{32,36}... | collective-permute-start | bytes 1572872 | tf_op jit(solution)/shard_map/ppermute | solution.py:19
  8.6 11.7 %collective-permute-start.2 = (bf16[512,512]{1,0:T(8,128)(2,1)S(1)}, bf16[512,512]{1,0:T(8,128)(2,1)S(1)}, u32[]{:S(2)}, u32[]{:S(2)}) collective-permute-start(bf16[512,512]{1,0:T(8,128)(2,1)S(1)} %slice.73.refs_2_), channel_id=1, source_target_pairs={{0,508},{4,0},{8,4},{12,8},{16,12},{20,16},{24,20},{28,24},{32,28}... | collective-permute-start | bytes 1572872 | tf_op jit(solution)/shard_map/ppermute | solution.py:19
  20.3 4.2 %collective-permute-start.3 = (bf16[512,512]{1,0:T(8,128)(2,1)S(1)}, bf16[512,512]{1,0:T(8,128)(2,1)}, u32[]{:S(2)}, u32[]{:S(2)}) collective-permute-start(bf16[512,512]{1,0:T(8,128)(2,1)S(1)} %slice.73.refs_2_), channel_id=1, source_target_pairs={{0,504},{4,508},{8,0},{12,4},{16,8},{20,12},{24,16},{28,20},{32,24... | collective-permute-start | bytes 1572872 | tf_op jit(solution)/shard_map/ppermute | solution.py:19
  24.6 0.7 slice.72.query_ref
  25.3 0.8 constant_dynamic-slice_fusion
  26.0 0.1 copy.20
  26.1 0.6 fusion.34.slot_ref
  26.7 3.1 %collective-permute-done.refs_0_ = bf16[512,512]{1,0:T(8,128)(2,1)S(1)} collective-permute-done((bf16[512,512]{1,0:T(8,128)(2,1)S(1)}, bf16[512,512]{1,0:T(8,128)(2,1)S(1)}, u32[]{:S(2)}, u32[]{:S(2)}) %collective-permute-start) | collective-permute-done | bytes 524320 | tf_op jit(solution)/shard_map/ppermute | solution.py:19
  29.8 0.0 copy-start.3
  29.8 4.8 %collective-permute-done.1.refs_1_ = bf16[512,512]{1,0:T(8,128)(2,1)S(1)} collective-permute-done((bf16[512,512]{1,0:T(8,128)(2,1)S(1)}, bf16[512,512]{1,0:T(8,128)(2,1)S(1)}, u32[]{:S(2)}, u32[]{:S(2)}) %collective-permute-start.1) | collective-permute-done | bytes 524320 | tf_op jit(solution)/shard_map/ppermute | solution.py:19
  34.6 0.0 copy-start.4
  34.6 0.0 collective-permute-done.2.refs_3_
  34.6 0.0 copy-start.5
  34.6 3.7 %collective-permute-done.3.refs_4_ = bf16[512,512]{1,0:T(8,128)(2,1)} collective-permute-done((bf16[512,512]{1,0:T(8,128)(2,1)S(1)}, bf16[512,512]{1,0:T(8,128)(2,1)}, u32[]{:S(2)}, u32[]{:S(2)}) %collective-permute-start.3) | collective-permute-done | bytes 524320 | tf_op jit(solution)/shard_map/ppermute | solution.py:19
  38.3 0.0 copy-done.1
  38.3 0.0 copy-done.3
  38.3 0.0 copy-done.4
  38.3 0.0 copy-done.5
  38.3 13.4 %shard_map.82 = bf16[4,512,256]{2,1,0:T(8,128)(2,1)} custom-call(s32[4,8]{1,0:T(4,128)} %fusion.34.slot_ref, bf16[512,256]{1,0:T(8,128)(2,1)} %slice.72.query_ref, bf16[512,512]{1,0:T(8,128)(2,1)} %copy-done.3, bf16[512,512]{1,0:T(8,128)(2,1)} %copy-done.4, bf16[512,512]{1,0:T(8,128)(2,1)} %copy-done.1, bf16[512,512]{1,0:T(8,128)(2,1)} %copy-done.5, ...), custom_call_target="tpu_custom_call" | custom-call | tf_op jit(solution)/shard_map/pallas_call | solution.py:119
  51.7 4.8 %all-to-all-start = ((bf16[4,512,256]{2,1,0:T(8,128)(2,1)}), bf16[4,512,256]{2,1,0:T(8,128)(2,1)S(1)}, u32[]{:S(2)}, u32[]{:S(2)}) async-start(bf16[4,512,256]{2,1,0:T(8,128)(2,1)} %shard_map.82), calls=%async_computation | async-start | bytes 2097152 | tf_op jit(solution)/shard_map/all_to_all | solution.py:29
  56.5 10.3 %all-to-all-done = bf16[4,512,256]{2,1,0:T(8,128)(2,1)S(1)} async-done(((bf16[4,512,256]{2,1,0:T(8,128)(2,1)}), bf16[4,512,256]{2,1,0:T(8,128)(2,1)S(1)}, u32[]{:S(2)}, u32[]{:S(2)}) %all-to-all-start) | async-done | bytes 1048608 | tf_op jit(solution)/shard_map/all_to_all | solution.py:29
  66.9 1.2 %multiply_reduce_fusion = (f32[512]{0:T(512)S(1)}, f32[512,256]{1,0:T(8,128)S(1)}) fusion(bf16[4,512,256]{2,1,0:T(8,128)(2,1)S(1)} %all-to-all-done, bf16[512,1024]{1,0:T(8,128)(2,1)} %param.8, s32[]{:T(128)S(6)} %select_n.23), kind=kLoop, calls=%fused_computation.32 | loop fusion | flops 1441280 | bytes 1837060 | tf_op jit(solution)/shard_map/reduce_sum | solution.py:142
  68.1 0.6 broadcast_in_dim.4
  68.7 4.7 %all-to-all-start.1 = ((f32[4,1,512]{2,1,0:T(1,128)}), f32[4,1,512]{2,1,0:T(1,128)S(1)}, u32[]{:S(2)}, u32[]{:S(2)}) async-start(f32[4,1,512]{2,1,0:T(1,128)} %broadcast_in_dim.4), calls=%async_computation.1 | async-start | bytes 16384 | tf_op jit(solution)/shard_map/all_to_all | solution.py:42
  73.4 0.8 dynamic_slice.11
  74.1 3.1 %all-to-all-done.1 = f32[4,1,512]{2,1,0:T(1,128)S(1)} async-done(((f32[4,1,512]{2,1,0:T(1,128)}), f32[4,1,512]{2,1,0:T(1,128)S(1)}, u32[]{:S(2)}, u32[]{:S(2)}) %all-to-all-start.1) | async-done | bytes 8224 | tf_op jit(solution)/shard_map/all_to_all | solution.py:42
  77.2 0.1 multiply_convert_fusion
  77.4 0.1 broadcast_in_dim.5
  77.5 13.3 %all_to_all.21 = bf16[512,4,256]{2,0,1:T(8,128)(2,1)S(1)} all-to-all(bf16[512,4,256]{2,0,1:T(8,128)(2,1)S(1)} %broadcast_in_dim.5), channel_id=1, replica_groups=mesh['patch'=128,'mp'=4] {'mp'}, dimensions={1} | all-to-all | bytes 2097152 | tf_op jit(solution)/shard_map/all_to_all | solution.py:52
  90.8 1.3 %copy.17 = bf16[512,4,256]{0,2,1:T(8,128)(2,1)} copy(bf16[512,4,256]{2,0,1:T(8,128)(2,1)S(1)} %all_to_all.21) | data formatting | bytes 2097152 | tf_op jit(solution)/shard_map/all_to_all | solution.py:52
  92.1 0.0 copy-done
  92.1 3.9 %convolution_convert_fusion = bf16[512,1024]{1,0:T(8,128)(2,1)} fusion(bf16[512,1024]{1,0:T(8,128)(2,1)S(1)} %copy-done, bf16[512,1024]{0,1:T(8,128)(2,1)} %bitcast.22, bf16[1024,512]{1,0:T(8,128)(2,1)} %param.13), kind=kOutput, calls=%fused_computation.12 | convolution fusion | flops 1076625408 | bytes 4194304 | tf_op jit(solution)/shard_map/dot_general | solution.py:149
  96.0 1.5 %copy.18 = bf16[512,1024]{0,1:T(8,128)(2,1)S(1)} copy(bf16[512,1024]{1,0:T(8,128)(2,1)} %convolution_convert_fusion) | data formatting | bytes 2097152 | tf_op jit(solution)/shard_map/convert_element_type | solution.py:150
  97.5 1.3 %copy.19 = bf16[512,4,256]{2,0,1:T(8,128)(2,1)} copy(bf16[512,4,256]{0,2,1:T(8,128)(2,1)S(1)} %bitcast.20) | data formatting | bytes 2097152 | tf_op jit(solution)/shard_map/reshape | solution.py:38
  98.8 14.4 %all_to_all.22 = bf16[4,512,256]{2,1,0:T(8,128)(2,1)S(1)} all-to-all(bf16[4,512,256]{2,1,0:T(8,128)(2,1)} %bitcast.21), channel_id=1, replica_groups=mesh['patch'=128,'mp'=4] {'mp'}, dimensions={0} | all-to-all | bytes 2097152 | tf_op jit(solution)/shard_map/all_to_all | solution.py:29
  113.2 0.8 fusion.24
  (3 shorter events, 0.1 us)
Async XLA Ops:
  0.0 92.1 %copy-start = (bf16[512,1024]{1,0:T(8,128)(2,1)S(1)}, bf16[512,1024]{1,0:T(8,128)(2,1)}, u32[]{:S(2)}) copy-start(bf16[512,1024]{1,0:T(8,128)(2,1)} %param.14) | copy-start | bytes 3145732
  0.0 1.8 %copy-start.2 = (bf16[512,1024]{1,0:T(8,128)(2,1)S(1)}, bf16[512,1024]{1,0:T(8,128)(2,1)}, u32[]{:S(2)}) copy-start(bf16[512,1024]{1,0:T(8,128)(2,1)} %param.8) | copy-start | bytes 3145732
  0.0 2.1 %copy-start.6 = (f32[1024]{0:T(1024)S(1)}, f32[1024]{0:T(1024)}, u32[]{:S(2)}) copy-start(f32[1024]{0:T(1024)} %param.9) | copy-start | bytes 12292
  3.2 35.1 %copy-start.1 = (bf16[512,512]{1,0:T(8,128)(2,1)}, bf16[512,512]{1,0:T(8,128)(2,1)S(1)}, u32[]{:S(2)}) copy-start(bf16[512,512]{1,0:T(8,128)(2,1)S(1)} %slice.73.refs_2_) | copy-start | bytes 1572868
  3.2 26.6 %collective-permute-start = (bf16[512,512]{1,0:T(8,128)(2,1)S(1)}, bf16[512,512]{1,0:T(8,128)(2,1)S(1)}, u32[]{:S(2)}, u32[]{:S(2)}) collective-permute-start(bf16[512,512]{1,0:T(8,128)(2,1)S(1)} %slice.73.refs_2_), channel_id=1, source_target_pairs={{0,8},{4,12},{8,16},{12,20},{16,24},{20,28},{24,32},{28,36},{32,40... | collective-permute-start | bytes 1572872 | tf_op jit(solution)/shard_map/ppermute | solution.py:19
  6.7 27.9 %collective-permute-start.1 = (bf16[512,512]{1,0:T(8,128)(2,1)S(1)}, bf16[512,512]{1,0:T(8,128)(2,1)S(1)}, u32[]{:S(2)}, u32[]{:S(2)}) collective-permute-start(bf16[512,512]{1,0:T(8,128)(2,1)S(1)} %slice.73.refs_2_), channel_id=1, source_target_pairs={{0,4},{4,8},{8,12},{12,16},{16,20},{20,24},{24,28},{28,32},{32,36}... | collective-permute-start | bytes 1572872 | tf_op jit(solution)/shard_map/ppermute | solution.py:19
  8.6 26.0 %collective-permute-start.2 = (bf16[512,512]{1,0:T(8,128)(2,1)S(1)}, bf16[512,512]{1,0:T(8,128)(2,1)S(1)}, u32[]{:S(2)}, u32[]{:S(2)}) collective-permute-start(bf16[512,512]{1,0:T(8,128)(2,1)S(1)} %slice.73.refs_2_), channel_id=1, source_target_pairs={{0,508},{4,0},{8,4},{12,8},{16,12},{20,16},{24,20},{28,24},{32,28}... | collective-permute-start | bytes 1572872 | tf_op jit(solution)/shard_map/ppermute | solution.py:19
  20.3 17.9 %collective-permute-start.3 = (bf16[512,512]{1,0:T(8,128)(2,1)S(1)}, bf16[512,512]{1,0:T(8,128)(2,1)}, u32[]{:S(2)}, u32[]{:S(2)}) collective-permute-start(bf16[512,512]{1,0:T(8,128)(2,1)S(1)} %slice.73.refs_2_), channel_id=1, source_target_pairs={{0,504},{4,508},{8,0},{12,4},{16,8},{20,12},{24,16},{28,20},{32,24... | collective-permute-start | bytes 1572872 | tf_op jit(solution)/shard_map/ppermute | solution.py:19
  29.8 8.5 %copy-start.3 = (bf16[512,512]{1,0:T(8,128)(2,1)}, bf16[512,512]{1,0:T(8,128)(2,1)S(1)}, u32[]{:S(2)}) copy-start(bf16[512,512]{1,0:T(8,128)(2,1)S(1)} %collective-permute-done.refs_0_) | copy-start | bytes 1572868
  34.6 3.7 %copy-start.4 = (bf16[512,512]{1,0:T(8,128)(2,1)}, bf16[512,512]{1,0:T(8,128)(2,1)S(1)}, u32[]{:S(2)}) copy-start(bf16[512,512]{1,0:T(8,128)(2,1)S(1)} %collective-permute-done.1.refs_1_) | copy-start | bytes 1572868
  34.6 3.7 %copy-start.5 = (bf16[512,512]{1,0:T(8,128)(2,1)}, bf16[512,512]{1,0:T(8,128)(2,1)S(1)}, u32[]{:S(2)}) copy-start(bf16[512,512]{1,0:T(8,128)(2,1)S(1)} %collective-permute-done.2.refs_3_) | copy-start | bytes 1572868
  51.7 15.2 %all-to-all-start = ((bf16[4,512,256]{2,1,0:T(8,128)(2,1)}), bf16[4,512,256]{2,1,0:T(8,128)(2,1)S(1)}, u32[]{:S(2)}, u32[]{:S(2)}) async-start(bf16[4,512,256]{2,1,0:T(8,128)(2,1)} %shard_map.82), calls=%async_computation | async-start | bytes 2097152 | tf_op jit(solution)/shard_map/all_to_all | solution.py:29
  68.7 8.5 %all-to-all-start.1 = ((f32[4,1,512]{2,1,0:T(1,128)}), f32[4,1,512]{2,1,0:T(1,128)S(1)}, u32[]{:S(2)}, u32[]{:S(2)}) async-start(f32[4,1,512]{2,1,0:T(1,128)} %broadcast_in_dim.4), calls=%async_computation.1 | async-start | bytes 16384 | tf_op jit(solution)/shard_map/all_to_all | solution.py:42

commit v12 on v11

--- a/solution.py
+++ b/solution.py
@@ -35,7 +35,11 @@
 
 def scatter_cols(parts, n_mp):
     rows, cols = parts.shape
-    return scatter_sum(parts.reshape(rows, n_mp, cols // n_mp).transpose(1, 0, 2))
+    got = lax.all_to_all(parts.reshape(rows, n_mp, cols // n_mp), "mp", 1, 1)
+    total = got[:, 0].astype(jnp.float32)
+    for which in range(1, n_mp):
+        total = total + got[:, which].astype(jnp.float32)
+    return total
 
 
 def gather_sum(vector, n_mp):

time: 115 us -> 115 us (level)
  no operation moved by 1% of the time
where the time goes in v12:
time: 115 us; the launch traced here: 114 us
  starting transfers between devices  30.8 us (27%)
  blocking collectives  27.7 us (24%)
  waiting for transfers between devices  25 us (22%)
  Pallas kernels  13.4 us (12%)
  local copies, waits for them, and re-layouts  8.92 us (8%)
  matrix products  4.98 us (4%)
  other arithmetic  3.1 us (3%)
    ppermute x4, starting transfers between devices, from_behind(): lax.ppermute(array, axis, [(i, (i + by) % length) for i in range(length)])  21.3 us
    all_to_all x1, blocking collectives, scatter_cols(): got = lax.all_to_all(parts.reshape(rows, n_mp, cols // n_mp), 'mp', 1, 1)  14.4 us
    pallas_call x1, Pallas kernels, per_device(): pl.pallas_call(functools.partial(window_attention, n_heads=heads_here, n_...  13.4 us
    all_to_all x1, blocking collectives, gather_cols(): return lax.all_to_all(spread, 'mp', 1, 1).reshape(rows, n_mp * cols)  13.3 us
    ppermute x4, waiting for transfers between devices, from_behind(): lax.ppermute(array, axis, [(i, (i + by) % length) for i in range(length)])  11.5 us
    all_to_all x1, waiting for transfers between devices, scatter_sum(): got = lax.all_to_all(parts, 'mp', 0, 0)  10.3 us
    all_to_all x1, starting transfers between devices, scatter_sum(): got = lax.all_to_all(parts, 'mp', 0, 0)  4.82 us
    all_to_all x1, starting transfers between devices, gather_sum(): lax.all_to_all(jnp.broadcast_to(vector[None], (n_mp,) + vector.shape), 'm...  4.68 us
  transfers between devices with their start and end apart: 6, of which 5 were waited for; matrix products, arithmetic and copies ran while one was open for 3% of the time, Pallas kernels for 0%

profile of v12, /device:TPU:2, one launch (start us, length us, event | category | flops | bytes accessed | tf_op | source)
XLA Modules:
  0.0 114.0 jit_solution(2876296281932308099)
XLA Ops:
  0.0 0.0 copy-start
  0.0 0.0 copy-start.2
  0.0 0.0 copy-start.6
  0.0 1.6 %slice_bitcast_fusion.2 = (bf16[1024,256]{1,0:T(8,128)(2,1)S(1)}, bf16[1024,256]{1,0:T(8,128)(2,1)S(1)}, bf16[1024,256]{1,0:T(8,128)(2,1)S(1)}) fusion(bf16[3,1024,256]{2,1,0:T(8,128)(2,1)} %param.10), kind=kLoop, calls=%fused_computation.35 | loop fusion | bytes 3145728 | tf_op jit(solution)/shard_map/squeeze | solution.py:106
  1.6 0.2 copy-done.2
  1.8 0.3 fusion
  2.1 0.0 copy-done.6
  2.1 1.0 fusion.9
  3.2 0.0 copy-start.1
  3.2 3.5 %collective-permute-start = (bf16[512,512]{1,0:T(8,128)(2,1)S(1)}, bf16[512,512]{1,0:T(8,128)(2,1)S(1)}, u32[]{:S(2)}, u32[]{:S(2)}) collective-permute-start(bf16[512,512]{1,0:T(8,128)(2,1)S(1)} %slice.73.refs_2_), channel_id=1, source_target_pairs={{0,8},{4,12},{8,16},{12,20},{16,24},{20,28},{24,32},{28,36},{32,40... | collective-permute-start | bytes 1572872 | tf_op jit(solution)/shard_map/ppermute | solution.py:19
  6.7 1.9 %collective-permute-start.1 = (bf16[512,512]{1,0:T(8,128)(2,1)S(1)}, bf16[512,512]{1,0:T(8,128)(2,1)S(1)}, u32[]{:S(2)}, u32[]{:S(2)}) collective-permute-start(bf16[512,512]{1,0:T(8,128)(2,1)S(1)} %slice.73.refs_2_), channel_id=1, source_target_pairs={{0,4},{4,8},{8,12},{12,16},{16,20},{20,24},{24,28},{28,32},{32,36}... | collective-permute-start | bytes 1572872 | tf_op jit(solution)/shard_map/ppermute | solution.py:19
  8.6 11.7 %collective-permute-start.2 = (bf16[512,512]{1,0:T(8,128)(2,1)S(1)}, bf16[512,512]{1,0:T(8,128)(2,1)S(1)}, u32[]{:S(2)}, u32[]{:S(2)}) collective-permute-start(bf16[512,512]{1,0:T(8,128)(2,1)S(1)} %slice.73.refs_2_), channel_id=1, source_target_pairs={{0,508},{4,0},{8,4},{12,8},{16,12},{20,16},{24,20},{28,24},{32,28}... | collective-permute-start | bytes 1572872 | tf_op jit(solution)/shard_map/ppermute | solution.py:19
  20.3 4.2 %collective-permute-start.3 = (bf16[512,512]{1,0:T(8,128)(2,1)S(1)}, bf16[512,512]{1,0:T(8,128)(2,1)}, u32[]{:S(2)}, u32[]{:S(2)}) collective-permute-start(bf16[512,512]{1,0:T(8,128)(2,1)S(1)} %slice.73.refs_2_), channel_id=1, source_target_pairs={{0,504},{4,508},{8,0},{12,4},{16,8},{20,12},{24,16},{28,20},{32,24... | collective-permute-start | bytes 1572872 | tf_op jit(solution)/shard_map/ppermute | solution.py:19
  24.6 0.7 slice.72.query_ref
  25.3 0.8 constant_dynamic-slice_fusion
  26.0 0.1 copy.20
  26.1 0.6 fusion.34.slot_ref
  26.7 3.1 %collective-permute-done.refs_0_ = bf16[512,512]{1,0:T(8,128)(2,1)S(1)} collective-permute-done((bf16[512,512]{1,0:T(8,128)(2,1)S(1)}, bf16[512,512]{1,0:T(8,128)(2,1)S(1)}, u32[]{:S(2)}, u32[]{:S(2)}) %collective-permute-start) | collective-permute-done | bytes 524320 | tf_op jit(solution)/shard_map/ppermute | solution.py:19
  29.8 0.0 copy-start.3
  29.8 4.8 %collective-permute-done.1.refs_1_ = bf16[512,512]{1,0:T(8,128)(2,1)S(1)} collective-permute-done((bf16[512,512]{1,0:T(8,128)(2,1)S(1)}, bf16[512,512]{1,0:T(8,128)(2,1)S(1)}, u32[]{:S(2)}, u32[]{:S(2)}) %collective-permute-start.1) | collective-permute-done | bytes 524320 | tf_op jit(solution)/shard_map/ppermute | solution.py:19
  34.6 0.0 copy-start.4
  34.6 0.0 collective-permute-done.2.refs_3_
  34.6 0.0 copy-start.5
  34.6 3.7 %collective-permute-done.3.refs_4_ = bf16[512,512]{1,0:T(8,128)(2,1)} collective-permute-done((bf16[512,512]{1,0:T(8,128)(2,1)S(1)}, bf16[512,512]{1,0:T(8,128)(2,1)}, u32[]{:S(2)}, u32[]{:S(2)}) %collective-permute-start.3) | collective-permute-done | bytes 524320 | tf_op jit(solution)/shard_map/ppermute | solution.py:19
  38.3 0.0 copy-done.1
  38.3 0.0 copy-done.3
  38.3 0.0 copy-done.4
  38.3 0.0 copy-done.5
  38.3 13.4 %shard_map.82 = bf16[4,512,256]{2,1,0:T(8,128)(2,1)} custom-call(s32[4,8]{1,0:T(4,128)} %fusion.34.slot_ref, bf16[512,256]{1,0:T(8,128)(2,1)} %slice.72.query_ref, bf16[512,512]{1,0:T(8,128)(2,1)} %copy-done.3, bf16[512,512]{1,0:T(8,128)(2,1)} %copy-done.4, bf16[512,512]{1,0:T(8,128)(2,1)} %copy-done.1, bf16[512,512]{1,0:T(8,128)(2,1)} %copy-done.5, ...), custom_call_target="tpu_custom_call" | custom-call | tf_op jit(solution)/shard_map/pallas_call | solution.py:123
  51.7 4.8 %all-to-all-start = ((bf16[4,512,256]{2,1,0:T(8,128)(2,1)}), bf16[4,512,256]{2,1,0:T(8,128)(2,1)S(1)}, u32[]{:S(2)}, u32[]{:S(2)}) async-start(bf16[4,512,256]{2,1,0:T(8,128)(2,1)} %shard_map.82), calls=%async_computation | async-start | bytes 2097152 | tf_op jit(solution)/shard_map/all_to_all | solution.py:29
  56.5 10.3 %all-to-all-done = bf16[4,512,256]{2,1,0:T(8,128)(2,1)S(1)} async-done(((bf16[4,512,256]{2,1,0:T(8,128)(2,1)}), bf16[4,512,256]{2,1,0:T(8,128)(2,1)S(1)}, u32[]{:S(2)}, u32[]{:S(2)}) %all-to-all-start) | async-done | bytes 1048608 | tf_op jit(solution)/shard_map/all_to_all | solution.py:29
  66.8 1.2 %multiply_reduce_fusion = (f32[512]{0:T(512)S(1)}, f32[512,256]{1,0:T(8,128)S(1)}) fusion(bf16[4,512,256]{2,1,0:T(8,128)(2,1)S(1)} %all-to-all-done, bf16[512,1024]{1,0:T(8,128)(2,1)} %param.8, s32[]{:T(128)S(6)} %select_n.23), kind=kLoop, calls=%fused_computation.32 | loop fusion | flops 1441280 | bytes 1837060 | tf_op jit(solution)/shard_map/reduce_sum | solution.py:146
  68.1 0.6 broadcast_in_dim.4
  68.7 4.7 %all-to-all-start.1 = ((f32[4,1,512]{2,1,0:T(1,128)}), f32[4,1,512]{2,1,0:T(1,128)S(1)}, u32[]{:S(2)}, u32[]{:S(2)}) async-start(f32[4,1,512]{2,1,0:T(1,128)} %broadcast_in_dim.4), calls=%async_computation.1 | async-start | bytes 16384 | tf_op jit(solution)/shard_map/all_to_all | solution.py:46
  73.3 0.8 dynamic_slice.11
  74.1 3.1 %all-to-all-done.1 = f32[4,1,512]{2,1,0:T(1,128)S(1)} async-done(((f32[4,1,512]{2,1,0:T(1,128)}), f32[4,1,512]{2,1,0:T(1,128)S(1)}, u32[]{:S(2)}, u32[]{:S(2)}) %all-to-all-start.1) | async-done | bytes 8224 | tf_op jit(solution)/shard_map/all_to_all | solution.py:46
  77.2 0.1 multiply_convert_fusion
  77.4 0.1 broadcast_in_dim.5
  77.4 13.3 %all_to_all.21 = bf16[512,4,256]{2,0,1:T(8,128)(2,1)S(1)} all-to-all(bf16[512,4,256]{2,0,1:T(8,128)(2,1)S(1)} %broadcast_in_dim.5), channel_id=1, replica_groups=mesh['patch'=128,'mp'=4] {'mp'}, dimensions={1} | all-to-all | bytes 2097152 | tf_op jit(solution)/shard_map/all_to_all | solution.py:56
  90.8 1.3 %copy.17 = bf16[512,4,256]{0,2,1:T(8,128)(2,1)} copy(bf16[512,4,256]{2,0,1:T(8,128)(2,1)S(1)} %all_to_all.21) | data formatting | bytes 2097152 | tf_op jit(solution)/shard_map/all_to_all | solution.py:56
  92.1 0.0 copy-done
  92.1 3.9 %convolution_convert_fusion = bf16[512,1024]{1,0:T(8,128)(2,1)} fusion(bf16[512,1024]{1,0:T(8,128)(2,1)S(1)} %copy-done, bf16[512,1024]{0,1:T(8,128)(2,1)} %bitcast.20, bf16[1024,512]{1,0:T(8,128)(2,1)} %param.13), kind=kOutput, calls=%fused_computation.12 | convolution fusion | flops 1076625408 | bytes 4194304 | tf_op jit(solution)/shard_map/dot_general | solution.py:153
  96.0 1.5 %copy.18 = bf16[512,1024]{0,1:T(8,128)(2,1)S(1)} copy(bf16[512,1024]{1,0:T(8,128)(2,1)} %convolution_convert_fusion) | data formatting | bytes 2097152 | tf_op jit(solution)/shard_map/convert_element_type | solution.py:154
  97.5 1.3 %copy.19 = bf16[512,4,256]{2,0,1:T(8,128)(2,1)} copy(bf16[512,4,256]{0,2,1:T(8,128)(2,1)S(1)} %bitcast.19) | data formatting | bytes 2097152 | tf_op jit(solution)/shard_map/reshape | solution.py:38
  98.8 14.4 %all_to_all.22 = bf16[512,4,256]{2,0,1:T(8,128)(2,1)S(1)} all-to-all(bf16[512,4,256]{2,0,1:T(8,128)(2,1)} %copy.19), channel_id=1, replica_groups=mesh['patch'=128,'mp'=4] {'mp'}, dimensions={1} | all-to-all | bytes 2097152 | tf_op jit(solution)/shard_map/all_to_all | solution.py:38
  113.2 0.8 fusion.24
  (3 shorter events, 0.1 us)
Async XLA Ops:
  0.0 92.1 %copy-start = (bf16[512,1024]{1,0:T(8,128)(2,1)S(1)}, bf16[512,1024]{1,0:T(8,128)(2,1)}, u32[]{:S(2)}) copy-start(bf16[512,1024]{1,0:T(8,128)(2,1)} %param.14) | copy-start | bytes 3145732
  0.0 1.8 %copy-start.2 = (bf16[512,1024]{1,0:T(8,128)(2,1)S(1)}, bf16[512,1024]{1,0:T(8,128)(2,1)}, u32[]{:S(2)}) copy-start(bf16[512,1024]{1,0:T(8,128)(2,1)} %param.8) | copy-start | bytes 3145732
  0.0 2.1 %copy-start.6 = (f32[1024]{0:T(1024)S(1)}, f32[1024]{0:T(1024)}, u32[]{:S(2)}) copy-start(f32[1024]{0:T(1024)} %param.9) | copy-start | bytes 12292
  3.2 35.1 %copy-start.1 = (bf16[512,512]{1,0:T(8,128)(2,1)}, bf16[512,512]{1,0:T(8,128)(2,1)S(1)}, u32[]{:S(2)}) copy-start(bf16[512,512]{1,0:T(8,128)(2,1)S(1)} %slice.73.refs_2_) | copy-start | bytes 1572868
  3.2 26.6 %collective-permute-start = (bf16[512,512]{1,0:T(8,128)(2,1)S(1)}, bf16[512,512]{1,0:T(8,128)(2,1)S(1)}, u32[]{:S(2)}, u32[]{:S(2)}) collective-permute-start(bf16[512,512]{1,0:T(8,128)(2,1)S(1)} %slice.73.refs_2_), channel_id=1, source_target_pairs={{0,8},{4,12},{8,16},{12,20},{16,24},{20,28},{24,32},{28,36},{32,40... | collective-permute-start | bytes 1572872 | tf_op jit(solution)/shard_map/ppermute | solution.py:19
  6.7 27.9 %collective-permute-start.1 = (bf16[512,512]{1,0:T(8,128)(2,1)S(1)}, bf16[512,512]{1,0:T(8,128)(2,1)S(1)}, u32[]{:S(2)}, u32[]{:S(2)}) collective-permute-start(bf16[512,512]{1,0:T(8,128)(2,1)S(1)} %slice.73.refs_2_), channel_id=1, source_target_pairs={{0,4},{4,8},{8,12},{12,16},{16,20},{20,24},{24,28},{28,32},{32,36}... | collective-permute-start | bytes 1572872 | tf_op jit(solution)/shard_map/ppermute | solution.py:19
  8.6 26.0 %collective-permute-start.2 = (bf16[512,512]{1,0:T(8,128)(2,1)S(1)}, bf16[512,512]{1,0:T(8,128)(2,1)S(1)}, u32[]{:S(2)}, u32[]{:S(2)}) collective-permute-start(bf16[512,512]{1,0:T(8,128)(2,1)S(1)} %slice.73.refs_2_), channel_id=1, source_target_pairs={{0,508},{4,0},{8,4},{12,8},{16,12},{20,16},{24,20},{28,24},{32,28}... | collective-permute-start | bytes 1572872 | tf_op jit(solution)/shard_map/ppermute | solution.py:19
  20.3 17.9 %collective-permute-start.3 = (bf16[512,512]{1,0:T(8,128)(2,1)S(1)}, bf16[512,512]{1,0:T(8,128)(2,1)}, u32[]{:S(2)}, u32[]{:S(2)}) collective-permute-start(bf16[512,512]{1,0:T(8,128)(2,1)S(1)} %slice.73.refs_2_), channel_id=1, source_target_pairs={{0,504},{4,508},{8,0},{12,4},{16,8},{20,12},{24,16},{28,20},{32,24... | collective-permute-start | bytes 1572872 | tf_op jit(solution)/shard_map/ppermute | solution.py:19
  29.8 8.5 %copy-start.3 = (bf16[512,512]{1,0:T(8,128)(2,1)}, bf16[512,512]{1,0:T(8,128)(2,1)S(1)}, u32[]{:S(2)}) copy-start(bf16[512,512]{1,0:T(8,128)(2,1)S(1)} %collective-permute-done.refs_0_) | copy-start | bytes 1572868
  34.6 3.7 %copy-start.4 = (bf16[512,512]{1,0:T(8,128)(2,1)}, bf16[512,512]{1,0:T(8,128)(2,1)S(1)}, u32[]{:S(2)}) copy-start(bf16[512,512]{1,0:T(8,128)(2,1)S(1)} %collective-permute-done.1.refs_1_) | copy-start | bytes 1572868
  34.6 3.7 %copy-start.5 = (bf16[512,512]{1,0:T(8,128)(2,1)}, bf16[512,512]{1,0:T(8,128)(2,1)S(1)}, u32[]{:S(2)}) copy-start(bf16[512,512]{1,0:T(8,128)(2,1)S(1)} %collective-permute-done.2.refs_3_) | copy-start | bytes 1572868
  51.7 15.1 %all-to-all-start = ((bf16[4,512,256]{2,1,0:T(8,128)(2,1)}), bf16[4,512,256]{2,1,0:T(8,128)(2,1)S(1)}, u32[]{:S(2)}, u32[]{:S(2)}) async-start(bf16[4,512,256]{2,1,0:T(8,128)(2,1)} %shard_map.82), calls=%async_computation | async-start | bytes 2097152 | tf_op jit(solution)/shard_map/all_to_all | solution.py:29
  68.7 8.5 %all-to-all-start.1 = ((f32[4,1,512]{2,1,0:T(1,128)}), f32[4,1,512]{2,1,0:T(1,128)S(1)}, u32[]{:S(2)}, u32[]{:S(2)}) async-start(f32[4,1,512]{2,1,0:T(1,128)} %broadcast_in_dim.4), calls=%async_computation.1 | async-start | bytes 16384 | tf_op jit(solution)/shard_map/all_to_all | solution.py:46

commit v13 on v5

--- a/solution.py
+++ b/solution.py
@@ -52,35 +52,37 @@
     kv_refs, out_ref, gathered = refs[:n_win], refs[n_win], refs[n_win + 1]
     width = n_heads * HD
     per_win = kv_refs[0].shape[0] // PN
-    patch = pl.program_id(0)
-    for k in range(n_nb):
-        slot = slot_ref[patch, k]
-        block = slot // per_win
-        local = slot % per_win
-        for w in range(n_win):
-            @pl.when(block == w)
-            def _():
-                gathered[k * PN:(k + 1) * PN, :] = kv_refs[w][pl.ds(pl.multiple_of(local * PN, PN), PN), :]
     lane = lax.broadcasted_iota(jnp.int32, (PN, 2 * HD), 1)
-    for pair in range(n_heads // 2):
-        cols = slice(pair * 2 * HD, (pair + 1) * 2 * HD)
-        v_cols = slice(width + pair * 2 * HD, width + (pair + 1) * 2 * HD)
-        q_pair = query_ref[:, cols]
-        keys = gathered[:, cols]
-        vals = gathered[:, v_cols]
-        mixed = []
-        for half in range(2):
-            keep = (lane >= half * HD) & (lane < (half + 1) * HD)
-            q_head = jnp.where(keep, q_pair, jnp.zeros_like(q_pair))
-            s = lax.dot_general(
-                q_head, keys, (((1,), (1,)), ((), ())), preferred_element_type=jnp.float32
-            ) * (1.0 / HD**0.5)
-            e = jnp.exp(s - s.max(axis=1, keepdims=True))
-            inv = 1.0 / e.sum(axis=1, keepdims=True)
-            probs = (e * inv).astype(jnp.bfloat16)
-            mixed.append(jnp.dot(probs, vals, preferred_element_type=jnp.float32))
-        out = jnp.where(lane < HD, mixed[0], mixed[1])
-        out_ref[:, cols] = out.astype(out_ref.dtype)
+    for patch in range(query_ref.shape[0] // PN):
+        rows = slice(patch * PN, (patch + 1) * PN)
+        for k in range(n_nb):
+            slot = slot_ref[patch, k]
+            block = slot // per_win
+            local = slot % per_win
+            for w in range(n_win):
+                @pl.when(block == w)
+                def _():
+                    start = pl.multiple_of(local * PN, PN)
+                    gathered[k * PN:(k + 1) * PN, :] = kv_refs[w][pl.ds(start, PN), :]
+        for pair in range(n_heads // 2):
+            cols = slice(pair * 2 * HD, (pair + 1) * 2 * HD)
+            v_cols = slice(width + pair * 2 * HD, width + (pair + 1) * 2 * HD)
+            q_pair = query_ref[rows, cols]
+            keys = gathered[:, cols]
+            vals = gathered[:, v_cols]
+            mixed = []
+            for half in range(2):
+                keep = (lane >= half * HD) & (lane < (half + 1) * HD)
+                q_head = jnp.where(keep, q_pair, jnp.zeros_like(q_pair))
+                s = lax.dot_general(
+                    q_head, keys, (((1,), (1,)), ((), ())), preferred_element_type=jnp.float32
+                ) * (1.0 / HD**0.5)
+                e = jnp.exp(s - s.max(axis=1, keepdims=True))
+                inv = 1.0 / e.sum(axis=1, keepdims=True)
+                probs = (e * inv).astype(jnp.bfloat16)
+                mixed.append(jnp.dot(probs, vals, preferred_element_type=jnp.float32))
+            out = jnp.where(lane < HD, mixed[0], mixed[1])
+            out_ref[rows, cols] = out.astype(out_ref.dtype)
 
 
 def per_device(features, gain_attn, w_qkv, w_out, gain_mlp, w_up, w_down, neighbours):
@@ -110,9 +112,9 @@
         functools.partial(window_attention, n_heads=heads_here, n_win=n_win, n_nb=K_NB),
         grid_spec=pltpu.PrefetchScalarGridSpec(
             num_scalar_prefetch=1,
-            grid=(patches_here,),
-            in_specs=[pl.BlockSpec((PN, width), lambda p, slots: (p, 0))] + [kv_spec] * n_win,
-            out_specs=pl.BlockSpec((PN, width), lambda p, slots: (p, 0)),
+            grid=(1,),
+            in_specs=[pl.BlockSpec((row_count, width), lambda p, slots: (0, 0))] + [kv_spec] * n_win,
+            out_specs=pl.BlockSpec((row_count, width), lambda p, slots: (0, 0)),
             scratch_shapes=[pltpu.VMEM((K_NB * PN, 2 * width), jnp.bfloat16)],
         ),
         out_shape=jax.ShapeDtypeStruct((row_count, width), jnp.bfloat16),

time: 111 us -> 111 us (level)
  no operation moved by 1% of the time
where the time goes in v13:
time: 111 us
  starting transfers between devices  30.8 us (28%)
  blocking collectives  26.6 us (24%)
  waiting for transfers between devices  25 us (23%)
  Pallas kernels  12.4 us (11%)
  local copies, waits for them, and re-layouts  7.24 us (7%)
  matrix products  5.36 us (5%)
  other arithmetic  3.1 us (3%)
    ppermute x4, starting transfers between devices, from_behind(): lax.ppermute(array, axis, [(i, (i + by) % length) for i in range(length)])  21.3 us
    all_to_all x1, blocking collectives, scatter_sum(): got = lax.all_to_all(parts.reshape(rows, n_mp, cols // n_mp), 'mp', 1, 1)  13.3 us
    all_to_all x1, blocking collectives, gather_cols(): return lax.all_to_all(spread, 'mp', 1, 1).reshape(rows, n_mp * cols)  13.3 us
    pallas_call x1, Pallas kernels, per_device(): pl.pallas_call(functools.partial(window_attention, n_heads=heads_here, n_...  12.4 us
    ppermute x4, waiting for transfers between devices, from_behind(): lax.ppermute(array, axis, [(i, (i + by) % length) for i in range(length)])  11.5 us
    all_to_all x1, waiting for transfers between devices, scatter_sum(): got = lax.all_to_all(parts.reshape(rows, n_mp, cols // n_mp), 'mp', 1, 1)  10.3 us
    all_to_all x1, starting transfers between devices, scatter_sum(): got = lax.all_to_all(parts.reshape(rows, n_mp, cols // n_mp), 'mp', 1, 1)  4.82 us
    all_to_all x1, starting transfers between devices, gather_sum(): lax.all_to_all(jnp.broadcast_to(vector[None], (n_mp,) + vector.shape), 'm...  4.68 us
  transfers between devices with their start and end apart: 6, of which 5 were waited for; matrix products, arithmetic and copies ran while one was open for 3% of the time, Pallas kernels for 0%

profile of v13, /device:TPU:2, one launch (start us, length us, event | category | flops | bytes accessed | tf_op | source)
XLA Modules:
  0.0 110.6 jit_solution(12374785992858257444)
XLA Ops:
  0.0 0.0 copy-start
  0.0 0.0 copy-start.2
  0.0 0.0 copy-start.6
  0.0 1.6 %slice_bitcast_fusion.2 = (bf16[1024,256]{1,0:T(8,128)(2,1)S(1)}, bf16[1024,256]{1,0:T(8,128)(2,1)S(1)}, bf16[1024,256]{1,0:T(8,128)(2,1)S(1)}) fusion(bf16[3,1024,256]{2,1,0:T(8,128)(2,1)} %param.10), kind=kLoop, calls=%fused_computation.38 | loop fusion | bytes 3145728 | tf_op jit(solution)/shard_map/squeeze | solution.py:95
  1.6 0.2 copy-done.2
  1.8 0.3 fusion
  2.1 0.0 copy-done.6
  2.1 1.0 fusion.9
  3.2 0.0 copy-start.1
  3.2 3.5 %collective-permute-start = (bf16[512,512]{1,0:T(8,128)(2,1)S(1)}, bf16[512,512]{1,0:T(8,128)(2,1)S(1)}, u32[]{:S(2)}, u32[]{:S(2)}) collective-permute-start(bf16[512,512]{1,0:T(8,128)(2,1)S(1)} %slice.73.refs_2_), channel_id=1, source_target_pairs={{0,8},{4,12},{8,16},{12,20},{16,24},{20,28},{24,32},{28,36},{32,40... | collective-permute-start | bytes 1572872 | tf_op jit(solution)/shard_map/ppermute | solution.py:19
  6.7 1.9 %collective-permute-start.1 = (bf16[512,512]{1,0:T(8,128)(2,1)S(1)}, bf16[512,512]{1,0:T(8,128)(2,1)S(1)}, u32[]{:S(2)}, u32[]{:S(2)}) collective-permute-start(bf16[512,512]{1,0:T(8,128)(2,1)S(1)} %slice.73.refs_2_), channel_id=1, source_target_pairs={{0,4},{4,8},{8,12},{12,16},{16,20},{20,24},{24,28},{28,32},{32,36}... | collective-permute-start | bytes 1572872 | tf_op jit(solution)/shard_map/ppermute | solution.py:19
  8.6 11.7 %collective-permute-start.2 = (bf16[512,512]{1,0:T(8,128)(2,1)S(1)}, bf16[512,512]{1,0:T(8,128)(2,1)}, u32[]{:S(2)}, u32[]{:S(2)}) collective-permute-start(bf16[512,512]{1,0:T(8,128)(2,1)S(1)} %slice.73.refs_2_), channel_id=1, source_target_pairs={{0,508},{4,0},{8,4},{12,8},{16,12},{20,16},{24,20},{28,24},{32,28}... | collective-permute-start | bytes 1572872 | tf_op jit(solution)/shard_map/ppermute | solution.py:19
  20.3 4.2 %collective-permute-start.3 = (bf16[512,512]{1,0:T(8,128)(2,1)S(1)}, bf16[512,512]{1,0:T(8,128)(2,1)}, u32[]{:S(2)}, u32[]{:S(2)}) collective-permute-start(bf16[512,512]{1,0:T(8,128)(2,1)S(1)} %slice.73.refs_2_), channel_id=1, source_target_pairs={{0,504},{4,508},{8,0},{12,4},{16,8},{20,12},{24,16},{28,20},{32,24... | collective-permute-start | bytes 1572872 | tf_op jit(solution)/shard_map/ppermute | solution.py:19
  24.6 0.7 slice.72.query_ref
  25.3 0.8 constant_dynamic-slice_fusion
  26.0 0.1 copy.19
  26.1 0.6 fusion.34.slot_ref
  26.7 0.0 copy-start.3
  26.7 3.1 %collective-permute-done.refs_0_ = bf16[512,512]{1,0:T(8,128)(2,1)S(1)} collective-permute-done((bf16[512,512]{1,0:T(8,128)(2,1)S(1)}, bf16[512,512]{1,0:T(8,128)(2,1)S(1)}, u32[]{:S(2)}, u32[]{:S(2)}) %collective-permute-start) | collective-permute-done | bytes 524320 | tf_op jit(solution)/shard_map/ppermute | solution.py:19
  29.8 0.0 copy-start.4
  29.8 4.8 %collective-permute-done.1.refs_1_ = bf16[512,512]{1,0:T(8,128)(2,1)S(1)} collective-permute-done((bf16[512,512]{1,0:T(8,128)(2,1)S(1)}, bf16[512,512]{1,0:T(8,128)(2,1)S(1)}, u32[]{:S(2)}, u32[]{:S(2)}) %collective-permute-start.1) | collective-permute-done | bytes 524320 | tf_op jit(solution)/shard_map/ppermute | solution.py:19
  34.6 0.0 copy-start.5
  34.6 0.0 collective-permute-done.2.refs_3_
  34.6 3.7 %collective-permute-done.3.refs_4_ = bf16[512,512]{1,0:T(8,128)(2,1)} collective-permute-done((bf16[512,512]{1,0:T(8,128)(2,1)S(1)}, bf16[512,512]{1,0:T(8,128)(2,1)}, u32[]{:S(2)}, u32[]{:S(2)}) %collective-permute-start.3) | collective-permute-done | bytes 524320 | tf_op jit(solution)/shard_map/ppermute | solution.py:19
  38.3 0.0 copy-done.1
  38.3 0.0 copy-done.4
  38.3 0.0 copy-done.5
  38.3 12.4 %shard_map.82 = bf16[512,256]{1,0:T(8,128)(2,1)} custom-call(s32[4,8]{1,0:T(4,128)} %fusion.34.slot_ref, bf16[512,256]{1,0:T(8,128)(2,1)} %slice.72.query_ref, bf16[512,512]{1,0:T(8,128)(2,1)} %copy-done.4, bf16[512,512]{1,0:T(8,128)(2,1)} %copy-done.5, bf16[512,512]{1,0:T(8,128)(2,1)} %copy-done.1, bf16[512,512]{1,0:T(8,128)(2,1)} %collective-permute-done.2.refs_3_, ...), custom_call_target="tpu_custom_call" | custom-call | tf_op jit(solution)/shard_map/pallas_call | solution.py:111
  50.7 0.0 copy-done.3
  50.7 1.4 %convolution_convert_fusion = bf16[512,1024]{1,0:T(8,128)(2,1)S(1)} fusion(bf16[512,256]{1,0:T(8,128)(2,1)} %shard_map.82, bf16[256,1024]{1,0:T(8,128)(2,1)S(1)} %copy-done.3), kind=kOutput, calls=%fused_computation.12 | convolution fusion | flops 268959744 | bytes 1835008 | tf_op jit(solution)/shard_map/dot_general | solution.py:123
  52.1 1.0 copy.25
  53.1 4.8 %all-to-all-start = ((bf16[512,4,256]{2,0,1:T(8,128)(2,1)}), bf16[512,4,256]{2,0,1:T(8,128)(2,1)S(1)}, u32[]{:S(2)}, u32[]{:S(2)}) async-start(bf16[512,4,256]{2,0,1:T(8,128)(2,1)} %bitcast.29), calls=%async_computation | async-start | bytes 2097152 | tf_op jit(solution)/shard_map/all_to_all | solution.py:30
  57.9 10.3 %all-to-all-done = bf16[512,4,256]{2,0,1:T(8,128)(2,1)S(1)} async-done(((bf16[512,4,256]{2,0,1:T(8,128)(2,1)}), bf16[512,4,256]{2,0,1:T(8,128)(2,1)S(1)}, u32[]{:S(2)}, u32[]{:S(2)}) %all-to-all-start) | async-done | bytes 1048608 | tf_op jit(solution)/shard_map/all_to_all | solution.py:30
  68.2 1.2 %multiply_reduce_fusion = (f32[512]{0:T(512)S(1)}, f32[512,256]{1,0:T(8,128)S(1)}) fusion(bf16[512,4,256]{2,0,1:T(8,128)(2,1)S(1)} %all-to-all-done, bf16[512,1024]{1,0:T(8,128)(2,1)} %param.8, s32[]{:T(128)S(6)} %select_n.23), kind=kLoop, calls=%fused_computation.35 | loop fusion | flops 1441280 | bytes 1837060 | tf_op jit(solution)/shard_map/reduce_sum | solution.py:131
  69.5 0.6 broadcast_in_dim.4
  70.1 4.7 %all-to-all-start.1 = ((f32[4,1,512]{2,1,0:T(1,128)}), f32[4,1,512]{2,1,0:T(1,128)S(1)}, u32[]{:S(2)}, u32[]{:S(2)}) async-start(f32[4,1,512]{2,1,0:T(1,128)} %broadcast_in_dim.4), calls=%async_computation.1 | async-start | bytes 16384 | tf_op jit(solution)/shard_map/all_to_all | solution.py:38
  74.7 0.8 dynamic_slice.11
  75.5 3.1 %all-to-all-done.1 = f32[4,1,512]{2,1,0:T(1,128)S(1)} async-done(((f32[4,1,512]{2,1,0:T(1,128)}), f32[4,1,512]{2,1,0:T(1,128)S(1)}, u32[]{:S(2)}, u32[]{:S(2)}) %all-to-all-start.1) | async-done | bytes 8224 | tf_op jit(solution)/shard_map/all_to_all | solution.py:38
  78.6 0.1 multiply_convert_fusion
  78.8 0.1 broadcast_in_dim.5
  78.8 13.3 %all_to_all.21 = bf16[512,4,256]{2,0,1:T(8,128)(2,1)S(1)} all-to-all(bf16[512,4,256]{2,0,1:T(8,128)(2,1)S(1)} %broadcast_in_dim.5), channel_id=1, replica_groups=mesh['patch'=128,'mp'=4] {'mp'}, dimensions={1} | all-to-all | bytes 2097152 | tf_op jit(solution)/shard_map/all_to_all | solution.py:48
  92.2 1.3 %copy.17 = bf16[512,4,256]{0,2,1:T(8,128)(2,1)} copy(bf16[512,4,256]{2,0,1:T(8,128)(2,1)S(1)} %all_to_all.21) | data formatting | bytes 2097152 | tf_op jit(solution)/shard_map/all_to_all | solution.py:48
  93.5 0.0 copy-done
  93.5 2.9 %convolution_convert_fusion.1 = bf16[512,1024]{1,0:T(8,128)(2,1)S(1)} fusion(bf16[512,1024]{1,0:T(8,128)(2,1)S(1)} %copy-done, bf16[512,1024]{0,1:T(8,128)(2,1)} %bitcast.31, bf16[1024,512]{1,0:T(8,128)(2,1)} %param.13), kind=kOutput, calls=%fused_computation.13 | convolution fusion | flops 1076625408 | bytes 4194304 | tf_op jit(solution)/shard_map/dot_general | solution.py:138
  96.4 0.1 copy.24
  96.5 13.3 %all_to_all.22 = bf16[512,4,256]{2,0,1:T(8,128)(2,1)S(1)} all-to-all(bf16[512,4,256]{2,0,1:T(8,128)(2,1)S(1)} %bitcast.30), channel_id=1, replica_groups=mesh['patch'=128,'mp'=4] {'mp'}, dimensions={1} | all-to-all | bytes 2097152 | tf_op jit(solution)/shard_map/all_to_all | solution.py:30
  109.8 0.8 fusion.24
  (3 shorter events, 0.1 us)
Async XLA Ops:
  0.0 93.5 %copy-start = (bf16[512,1024]{1,0:T(8,128)(2,1)S(1)}, bf16[512,1024]{1,0:T(8,128)(2,1)}, u32[]{:S(2)}) copy-start(bf16[512,1024]{1,0:T(8,128)(2,1)} %param.14) | copy-start | bytes 3145732
  0.0 1.8 %copy-start.2 = (bf16[512,1024]{1,0:T(8,128)(2,1)S(1)}, bf16[512,1024]{1,0:T(8,128)(2,1)}, u32[]{:S(2)}) copy-start(bf16[512,1024]{1,0:T(8,128)(2,1)} %param.8) | copy-start | bytes 3145732
  0.0 2.1 %copy-start.6 = (f32[1024]{0:T(1024)S(1)}, f32[1024]{0:T(1024)}, u32[]{:S(2)}) copy-start(f32[1024]{0:T(1024)} %param.9) | copy-start | bytes 12292
  3.2 35.1 %copy-start.1 = (bf16[512,512]{1,0:T(8,128)(2,1)}, bf16[512,512]{1,0:T(8,128)(2,1)S(1)}, u32[]{:S(2)}) copy-start(bf16[512,512]{1,0:T(8,128)(2,1)S(1)} %slice.73.refs_2_) | copy-start | bytes 1572868
  3.2 26.6 %collective-permute-start = (bf16[512,512]{1,0:T(8,128)(2,1)S(1)}, bf16[512,512]{1,0:T(8,128)(2,1)S(1)}, u32[]{:S(2)}, u32[]{:S(2)}) collective-permute-start(bf16[512,512]{1,0:T(8,128)(2,1)S(1)} %slice.73.refs_2_), channel_id=1, source_target_pairs={{0,8},{4,12},{8,16},{12,20},{16,24},{20,28},{24,32},{28,36},{32,40... | collective-permute-start | bytes 1572872 | tf_op jit(solution)/shard_map/ppermute | solution.py:19
  6.7 27.9 %collective-permute-start.1 = (bf16[512,512]{1,0:T(8,128)(2,1)S(1)}, bf16[512,512]{1,0:T(8,128)(2,1)S(1)}, u32[]{:S(2)}, u32[]{:S(2)}) collective-permute-start(bf16[512,512]{1,0:T(8,128)(2,1)S(1)} %slice.73.refs_2_), channel_id=1, source_target_pairs={{0,4},{4,8},{8,12},{12,16},{16,20},{20,24},{24,28},{28,32},{32,36}... | collective-permute-start | bytes 1572872 | tf_op jit(solution)/shard_map/ppermute | solution.py:19
  8.6 26.0 %collective-permute-start.2 = (bf16[512,512]{1,0:T(8,128)(2,1)S(1)}, bf16[512,512]{1,0:T(8,128)(2,1)}, u32[]{:S(2)}, u32[]{:S(2)}) collective-permute-start(bf16[512,512]{1,0:T(8,128)(2,1)S(1)} %slice.73.refs_2_), channel_id=1, source_target_pairs={{0,508},{4,0},{8,4},{12,8},{16,12},{20,16},{24,20},{28,24},{32,28}... | collective-permute-start | bytes 1572872 | tf_op jit(solution)/shard_map/ppermute | solution.py:19
  20.3 17.9 %collective-permute-start.3 = (bf16[512,512]{1,0:T(8,128)(2,1)S(1)}, bf16[512,512]{1,0:T(8,128)(2,1)}, u32[]{:S(2)}, u32[]{:S(2)}) collective-permute-start(bf16[512,512]{1,0:T(8,128)(2,1)S(1)} %slice.73.refs_2_), channel_id=1, source_target_pairs={{0,504},{4,508},{8,0},{12,4},{16,8},{20,12},{24,16},{28,20},{32,24... | collective-permute-start | bytes 1572872 | tf_op jit(solution)/shard_map/ppermute | solution.py:19
  26.7 23.9 %copy-start.3 = (bf16[256,1024]{1,0:T(8,128)(2,1)S(1)}, bf16[256,1024]{1,0:T(8,128)(2,1)}, u32[]{:S(2)}) copy-start(bf16[256,1024]{1,0:T(8,128)(2,1)} %param.11) | copy-start | bytes 1572868
  29.8 8.5 %copy-start.4 = (bf16[512,512]{1,0:T(8,128)(2,1)}, bf16[512,512]{1,0:T(8,128)(2,1)S(1)}, u32[]{:S(2)}) copy-start(bf16[512,512]{1,0:T(8,128)(2,1)S(1)} %collective-permute-done.refs_0_) | copy-start | bytes 1572868
  34.6 3.7 %copy-start.5 = (bf16[512,512]{1,0:T(8,128)(2,1)}, bf16[512,512]{1,0:T(8,128)(2,1)S(1)}, u32[]{:S(2)}) copy-start(bf16[512,512]{1,0:T(8,128)(2,1)S(1)} %collective-permute-done.1.refs_1_) | copy-start | bytes 1572868
  53.1 15.1 %all-to-all-start = ((bf16[512,4,256]{2,0,1:T(8,128)(2,1)}), bf16[512,4,256]{2,0,1:T(8,128)(2,1)S(1)}, u32[]{:S(2)}, u32[]{:S(2)}) async-start(bf16[512,4,256]{2,0,1:T(8,128)(2,1)} %bitcast.29), calls=%async_computation | async-start | bytes 2097152 | tf_op jit(solution)/shard_map/all_to_all | solution.py:30
  70.1 8.5 %all-to-all-start.1 = ((f32[4,1,512]{2,1,0:T(1,128)}), f32[4,1,512]{2,1,0:T(1,128)S(1)}, u32[]{:S(2)}, u32[]{:S(2)}) async-start(f32[4,1,512]{2,1,0:T(1,128)} %broadcast_in_dim.4), calls=%async_computation.1 | async-start | bytes 16384 | tf_op jit(solution)/shard_map/all_to_all | solution.py:38

commit v14 on v5

--- a/solution.py
+++ b/solution.py
@@ -90,10 +90,12 @@
     heads_here = width // HD
     n_win = 2 * REACH + 1
     normed = normalize(features, gain_attn)
-    w_all = jnp.concatenate([w_qkv[0], w_qkv[1], w_qkv[2]], axis=1)
-    qkv = jnp.dot(normed, w_all, preferred_element_type=jnp.float32).astype(jnp.bfloat16)
-    queries = qkv[:, :width]
-    own_kv = qkv[:, width:]
+    projected = [
+        jnp.dot(normed, w_qkv[which], preferred_element_type=jnp.float32).astype(jnp.bfloat16)
+        for which in range(3)
+    ]
+    queries = projected[0]
+    own_kv = jnp.concatenate(projected[1:], axis=1)
     window = {0: own_kv}
     for offset in range(-REACH, REACH + 1):
         if offset != 0:

time: 111 us -> 113 us (1.018)
  matrix products: 5.36 us -> 10 us
  local copies, waits for them, and re-layouts: 7.24 us -> 4.71 us
  waiting for transfers between devices: 25 us -> 23.4 us
  other arithmetic: 3.1 us -> 4.44 us
    dot_general x1 -> x3, matrix products: 1.04 us -> 5.72 us  [per_device(): jnp.dot(normed, w_qkv[which], preferred_element_type=jnp.float32)]
    squeeze x1 -> x0, local copies, waits for them, and re-layouts: 1.61 us -> none  [per_device(): w_all = jnp.concatenate([w_qkv[0], w_qkv[1], w_qkv[2]], axis=1)]
    ppermute x4, waiting for transfers between devices: 11.5 us -> 10 us  [from_behind(): lax.ppermute(array, axis, [(i, (i + by) % length) for i in range(length)])]
    reduce_sum x1, other arithmetic: 0.28 us -> 1.59 us  [normalize(): mean_sq = jnp.mean(rows32 * rows32, axis=-1, keepdims=True)]
  transfers between devices with their start and end apart: 6 -> 6, of which waited for: 5 -> 5; matrix products, arithmetic and copies ran while one was open for 3% -> 4% of each run, Pallas kernels for 0% -> 0%
where the time goes in v14:
time: 113 us
  starting transfers between devices  30.8 us (27%)
  blocking collectives  26.6 us (24%)
  waiting for transfers between devices  23.4 us (21%)
  Pallas kernels  12.4 us (11%)
  matrix products  10 us (9%)
  local copies, waits for them, and re-layouts  4.71 us (4%)
  other arithmetic  4.44 us (4%)
    ppermute x4, starting transfers between devices, from_behind(): lax.ppermute(array, axis, [(i, (i + by) % length) for i in range(length)])  21.3 us
    all_to_all x1, blocking collectives, scatter_sum(): got = lax.all_to_all(parts.reshape(rows, n_mp, cols // n_mp), 'mp', 1, 1)  13.3 us
    all_to_all x1, blocking collectives, gather_cols(): return lax.all_to_all(spread, 'mp', 1, 1).reshape(rows, n_mp * cols)  13.3 us
    pallas_call x1, Pallas kernels, per_device(): pl.pallas_call(functools.partial(window_attention, n_heads=heads_here, n_...  12.4 us
    all_to_all x1, waiting for transfers between devices, scatter_sum(): got = lax.all_to_all(parts.reshape(rows, n_mp, cols // n_mp), 'mp', 1, 1)  10.3 us
    ppermute x4, waiting for transfers between devices, from_behind(): lax.ppermute(array, axis, [(i, (i + by) % length) for i in range(length)])  10 us
    dot_general x3, matrix products, per_device(): jnp.dot(normed, w_qkv[which], preferred_element_type=jnp.float32)  5.72 us
    all_to_all x1, starting transfers between devices, scatter_sum(): got = lax.all_to_all(parts.reshape(rows, n_mp, cols // n_mp), 'mp', 1, 1)  4.82 us
  transfers between devices with their start and end apart: 6, of which 5 were waited for; matrix products, arithmetic and copies ran while one was open for 4% of the time, Pallas kernels for 0%

profile of v14, /device:TPU:2, one launch (start us, length us, event | category | flops | bytes accessed | tf_op | source)
XLA Modules:
  0.0 112.7 jit_solution(15273714765435156237)
XLA Ops:
  0.0 0.0 copy-start
  0.0 1.6 %fusion = f32[512]{0:T(512)S(1)} fusion(bf16[512,1024]{1,0:T(8,128)(2,1)} %param.8), kind=kLoop, calls=%fused_computation.2 | loop fusion | flops 1572352 | bytes 1050624 | tf_op jit(solution)/shard_map/reduce_sum | solution.py:24
  1.6 0.0 copy-start.2
  1.6 0.0 copy-start.5
  1.6 1.9 %convolution_convert_fusion.2 = bf16[512,256]{1,0:T(8,128)(2,1)S(1)} fusion(bf16[3,1024,256]{2,1,0:T(8,128)(2,1)} %param.10, bf16[512,1024]{1,0:T(8,128)(2,1)} %param.8, f32[1024]{0:T(1024)} %param.9, f32[512]{0:T(512)S(1)} %add_rsqrt_fusion.1), kind=kOutput, calls=%fused_computation.8 | convolution fusion | flops 270663680 | bytes 1841152 | tf_op jit(solution)/shard_map/dot_general | solution.py:94
  3.6 0.0 copy-done.2
  3.6 0.0 copy-done.5
  3.6 1.5 %convolution_convert_fusion.3 = bf16[512,256]{1,0:T(8,128)(2,1)S(1)} fusion(bf16[3,1024,256]{2,1,0:T(8,128)(2,1)} %param.10, bf16[512,1024]{1,0:T(8,128)(2,1)S(1)} %copy-done.2, f32[1024]{0:T(1024)S(1)} %copy-done.5, f32[512]{0:T(512)S(1)} %add_rsqrt_fusion.1), kind=kOutput, calls=%fused_computation.9 | convolution fusion | flops 270663680 | bytes 1841152 | tf_op jit(solution)/shard_map/dot_general | solution.py:94
  5.2 0.0 copy-start.1
  5.2 3.5 %collective-permute-start = (bf16[512,512]{1,0:T(8,128)(2,1)S(1)}, bf16[512,512]{1,0:T(8,128)(2,1)S(1)}, u32[]{:S(2)}, u32[]{:S(2)}) collective-permute-start(bf16[512,512]{1,0:T(8,128)(2,1)S(1)} %pad_maximum_fusion.refs_2_), channel_id=1, source_target_pairs={{0,8},{4,12},{8,16},{12,20},{16,24},{20,28},{24,32},{28,36},{32,40... | collective-permute-start | bytes 1572872 | tf_op jit(solution)/shard_map/ppermute | solution.py:19
  8.7 1.9 %collective-permute-start.1 = (bf16[512,512]{1,0:T(8,128)(2,1)S(1)}, bf16[512,512]{1,0:T(8,128)(2,1)}, u32[]{:S(2)}, u32[]{:S(2)}) collective-permute-start(bf16[512,512]{1,0:T(8,128)(2,1)S(1)} %pad_maximum_fusion.refs_2_), channel_id=1, source_target_pairs={{0,4},{4,8},{8,12},{12,16},{16,20},{20,24},{24,28},{28,32},{32,36}... | collective-permute-start | bytes 1572872 | tf_op jit(solution)/shard_map/ppermute | solution.py:19
  10.6 11.7 %collective-permute-start.2 = (bf16[512,512]{1,0:T(8,128)(2,1)S(1)}, bf16[512,512]{1,0:T(8,128)(2,1)}, u32[]{:S(2)}, u32[]{:S(2)}) collective-permute-start(bf16[512,512]{1,0:T(8,128)(2,1)S(1)} %pad_maximum_fusion.refs_2_), channel_id=1, source_target_pairs={{0,508},{4,0},{8,4},{12,8},{16,12},{20,16},{24,20},{28,24},{32,28}... | collective-permute-start | bytes 1572872 | tf_op jit(solution)/shard_map/ppermute | solution.py:19
  22.4 4.2 %collective-permute-start.3 = (bf16[512,512]{1,0:T(8,128)(2,1)S(1)}, bf16[512,512]{1,0:T(8,128)(2,1)}, u32[]{:S(2)}, u32[]{:S(2)}) collective-permute-start(bf16[512,512]{1,0:T(8,128)(2,1)S(1)} %pad_maximum_fusion.refs_2_), channel_id=1, source_target_pairs={{0,504},{4,508},{8,0},{12,4},{16,8},{20,12},{24,16},{28,20},{32,24... | collective-permute-start | bytes 1572872 | tf_op jit(solution)/shard_map/ppermute | solution.py:19
  26.6 0.8 constant_dynamic-slice_fusion
  27.3 0.1 copy.27
  27.4 0.6 fusion.28.slot_ref
  28.0 2.2 %convolution_convert_fusion.4.query_ref = bf16[512,256]{1,0:T(8,128)(2,1)} fusion(bf16[3,1024,256]{2,1,0:T(8,128)(2,1)} %param.10, bf16[512,1024]{1,0:T(8,128)(2,1)S(1)} %copy-done.2, f32[1024]{0:T(1024)S(1)} %copy-done.5, f32[512]{0:T(512)S(1)} %add_rsqrt_fusion.1), kind=kOutput, calls=%fused_computation.10 | convolution fusion | flops 270663680 | bytes 1841152 | tf_op jit(solution)/shard_map/dot_general | solution.py:94
  30.3 0.0 copy-done.1
  30.3 0.0 copy-start.3
  30.3 1.6 %collective-permute-done.refs_0_ = bf16[512,512]{1,0:T(8,128)(2,1)S(1)} collective-permute-done((bf16[512,512]{1,0:T(8,128)(2,1)S(1)}, bf16[512,512]{1,0:T(8,128)(2,1)S(1)}, u32[]{:S(2)}, u32[]{:S(2)}) %collective-permute-start) | collective-permute-done | bytes 524320 | tf_op jit(solution)/shard_map/ppermute | solution.py:19
  31.8 0.0 copy-start.4
  31.8 4.9 %collective-permute-done.1.refs_1_ = bf16[512,512]{1,0:T(8,128)(2,1)} collective-permute-done((bf16[512,512]{1,0:T(8,128)(2,1)S(1)}, bf16[512,512]{1,0:T(8,128)(2,1)}, u32[]{:S(2)}, u32[]{:S(2)}) %collective-permute-start.1) | collective-permute-done | bytes 524320 | tf_op jit(solution)/shard_map/ppermute | solution.py:19
  36.7 0.0 collective-permute-done.2.refs_3_
  36.7 3.6 %collective-permute-done.3.refs_4_ = bf16[512,512]{1,0:T(8,128)(2,1)} collective-permute-done((bf16[512,512]{1,0:T(8,128)(2,1)S(1)}, bf16[512,512]{1,0:T(8,128)(2,1)}, u32[]{:S(2)}, u32[]{:S(2)}) %collective-permute-start.3) | collective-permute-done | bytes 524320 | tf_op jit(solution)/shard_map/ppermute | solution.py:19
  40.3 0.0 copy-done.4
  40.3 12.4 %shard_map.82 = bf16[512,256]{1,0:T(8,128)(2,1)} custom-call(s32[4,8]{1,0:T(4,128)} %fusion.28.slot_ref, bf16[512,256]{1,0:T(8,128)(2,1)} %convolution_convert_fusion.4.query_ref, bf16[512,512]{1,0:T(8,128)(2,1)} %copy-done.4, bf16[512,512]{1,0:T(8,128)(2,1)} %collective-permute-done.1.refs_1_, bf16[512,512]{1,0:T(8,128)(2,1)} %copy-done.1, ...), custom_call_target="tpu_custom_call" | custom-call | tf_op jit(solution)/shard_map/pallas_call | solution.py:111
  52.7 0.0 copy-done.3
  52.7 1.4 %convolution_convert_fusion = bf16[512,1024]{1,0:T(8,128)(2,1)S(1)} fusion(bf16[512,256]{1,0:T(8,128)(2,1)} %shard_map.82, bf16[256,1024]{1,0:T(8,128)(2,1)S(1)} %copy-done.3), kind=kOutput, calls=%fused_computation.6 | convolution fusion | flops 268959744 | bytes 1835008 | tf_op jit(solution)/shard_map/dot_general | solution.py:123
  54.1 1.0 copy.33
  55.1 4.8 %all-to-all-start = ((bf16[512,4,256]{2,0,1:T(8,128)(2,1)}), bf16[512,4,256]{2,0,1:T(8,128)(2,1)S(1)}, u32[]{:S(2)}, u32[]{:S(2)}) async-start(bf16[512,4,256]{2,0,1:T(8,128)(2,1)} %bitcast.32), calls=%async_computation | async-start | bytes 2097152 | tf_op jit(solution)/shard_map/all_to_all | solution.py:30
  59.9 10.3 %all-to-all-done = bf16[512,4,256]{2,0,1:T(8,128)(2,1)S(1)} async-done(((bf16[512,4,256]{2,0,1:T(8,128)(2,1)}), bf16[512,4,256]{2,0,1:T(8,128)(2,1)S(1)}, u32[]{:S(2)}, u32[]{:S(2)}) %all-to-all-start) | async-done | bytes 1048608 | tf_op jit(solution)/shard_map/all_to_all | solution.py:30
  70.3 1.2 %multiply_reduce_fusion = (f32[512]{0:T(512)S(1)}, f32[512,256]{1,0:T(8,128)S(1)}) fusion(bf16[512,4,256]{2,0,1:T(8,128)(2,1)S(1)} %all-to-all-done, bf16[512,1024]{1,0:T(8,128)(2,1)} %param.8, s32[]{:T(128)S(6)} %select_n.23), kind=kLoop, calls=%fused_computation.33 | loop fusion | flops 1441280 | bytes 1837060 | tf_op jit(solution)/shard_map/reduce_sum | solution.py:131
  71.5 0.6 broadcast_in_dim.4
  72.1 4.7 %all-to-all-start.1 = ((f32[4,1,512]{2,1,0:T(1,128)}), f32[4,1,512]{2,1,0:T(1,128)S(1)}, u32[]{:S(2)}, u32[]{:S(2)}) async-start(f32[4,1,512]{2,1,0:T(1,128)} %broadcast_in_dim.4), calls=%async_computation.1 | async-start | bytes 16384 | tf_op jit(solution)/shard_map/all_to_all | solution.py:38
  76.8 0.8 dynamic_slice.11
  77.5 3.1 %all-to-all-done.1 = f32[4,1,512]{2,1,0:T(1,128)S(1)} async-done(((f32[4,1,512]{2,1,0:T(1,128)}), f32[4,1,512]{2,1,0:T(1,128)S(1)}, u32[]{:S(2)}, u32[]{:S(2)}) %all-to-all-start.1) | async-done | bytes 8224 | tf_op jit(solution)/shard_map/all_to_all | solution.py:38
  80.6 0.1 multiply_convert_fusion
  80.8 0.1 broadcast_in_dim.5
  80.9 13.3 %all_to_all.21 = bf16[512,4,256]{2,0,1:T(8,128)(2,1)S(1)} all-to-all(bf16[512,4,256]{2,0,1:T(8,128)(2,1)S(1)} %broadcast_in_dim.5), channel_id=1, replica_groups=mesh['patch'=128,'mp'=4] {'mp'}, dimensions={1} | all-to-all | bytes 2097152 | tf_op jit(solution)/shard_map/all_to_all | solution.py:48
  94.2 1.3 %copy.23 = bf16[512,4,256]{0,2,1:T(8,128)(2,1)} copy(bf16[512,4,256]{2,0,1:T(8,128)(2,1)S(1)} %all_to_all.21) | data formatting | bytes 2097152 | tf_op jit(solution)/shard_map/all_to_all | solution.py:48
  95.5 0.0 copy-done
  95.5 2.9 %convolution_convert_fusion.1 = bf16[512,1024]{1,0:T(8,128)(2,1)S(1)} fusion(bf16[512,1024]{1,0:T(8,128)(2,1)S(1)} %copy-done, bf16[512,1024]{0,1:T(8,128)(2,1)} %bitcast.34, bf16[1024,512]{1,0:T(8,128)(2,1)} %param.13), kind=kOutput, calls=%fused_computation.7 | convolution fusion | flops 1076625408 | bytes 4194304 | tf_op jit(solution)/shard_map/dot_general | solution.py:138
  98.4 0.1 copy.32
  98.5 13.3 %all_to_all.22 = bf16[512,4,256]{2,0,1:T(8,128)(2,1)S(1)} all-to-all(bf16[512,4,256]{2,0,1:T(8,128)(2,1)S(1)} %bitcast.33), channel_id=1, replica_groups=mesh['patch'=128,'mp'=4] {'mp'}, dimensions={1} | all-to-all | bytes 2097152 | tf_op jit(solution)/shard_map/all_to_all | solution.py:30
  111.8 0.8 fusion.12
  (3 shorter events, 0.1 us)
Async XLA Ops:
  0.0 95.5 %copy-start = (bf16[512,1024]{1,0:T(8,128)(2,1)S(1)}, bf16[512,1024]{1,0:T(8,128)(2,1)}, u32[]{:S(2)}) copy-start(bf16[512,1024]{1,0:T(8,128)(2,1)} %param.14) | copy-start | bytes 3145732
  1.6 2.0 %copy-start.2 = (bf16[512,1024]{1,0:T(8,128)(2,1)S(1)}, bf16[512,1024]{1,0:T(8,128)(2,1)}, u32[]{:S(2)}) copy-start(bf16[512,1024]{1,0:T(8,128)(2,1)} %param.8) | copy-start | bytes 3145732
  1.6 2.0 %copy-start.5 = (f32[1024]{0:T(1024)S(1)}, f32[1024]{0:T(1024)}, u32[]{:S(2)}) copy-start(f32[1024]{0:T(1024)} %param.9) | copy-start | bytes 12292
  5.2 25.1 %copy-start.1 = (bf16[512,512]{1,0:T(8,128)(2,1)}, bf16[512,512]{1,0:T(8,128)(2,1)S(1)}, u32[]{:S(2)}) copy-start(bf16[512,512]{1,0:T(8,128)(2,1)S(1)} %pad_maximum_fusion.refs_2_) | copy-start | bytes 1572868
  5.2 26.6 %collective-permute-start = (bf16[512,512]{1,0:T(8,128)(2,1)S(1)}, bf16[512,512]{1,0:T(8,128)(2,1)S(1)}, u32[]{:S(2)}, u32[]{:S(2)}) collective-permute-start(bf16[512,512]{1,0:T(8,128)(2,1)S(1)} %pad_maximum_fusion.refs_2_), channel_id=1, source_target_pairs={{0,8},{4,12},{8,16},{12,20},{16,24},{20,28},{24,32},{28,36},{32,40... | collective-permute-start | bytes 1572872 | tf_op jit(solution)/shard_map/ppermute | solution.py:19
  8.7 28.0 %collective-permute-start.1 = (bf16[512,512]{1,0:T(8,128)(2,1)S(1)}, bf16[512,512]{1,0:T(8,128)(2,1)}, u32[]{:S(2)}, u32[]{:S(2)}) collective-permute-start(bf16[512,512]{1,0:T(8,128)(2,1)S(1)} %pad_maximum_fusion.refs_2_), channel_id=1, source_target_pairs={{0,4},{4,8},{8,12},{12,16},{16,20},{20,24},{24,28},{28,32},{32,36}... | collective-permute-start | bytes 1572872 | tf_op jit(solution)/shard_map/ppermute | solution.py:19
  10.6 26.1 %collective-permute-start.2 = (bf16[512,512]{1,0:T(8,128)(2,1)S(1)}, bf16[512,512]{1,0:T(8,128)(2,1)}, u32[]{:S(2)}, u32[]{:S(2)}) collective-permute-start(bf16[512,512]{1,0:T(8,128)(2,1)S(1)} %pad_maximum_fusion.refs_2_), channel_id=1, source_target_pairs={{0,508},{4,0},{8,4},{12,8},{16,12},{20,16},{24,20},{28,24},{32,28}... | collective-permute-start | bytes 1572872 | tf_op jit(solution)/shard_map/ppermute | solution.py:19
  22.4 17.9 %collective-permute-start.3 = (bf16[512,512]{1,0:T(8,128)(2,1)S(1)}, bf16[512,512]{1,0:T(8,128)(2,1)}, u32[]{:S(2)}, u32[]{:S(2)}) collective-permute-start(bf16[512,512]{1,0:T(8,128)(2,1)S(1)} %pad_maximum_fusion.refs_2_), channel_id=1, source_target_pairs={{0,504},{4,508},{8,0},{12,4},{16,8},{20,12},{24,16},{28,20},{32,24... | collective-permute-start | bytes 1572872 | tf_op jit(solution)/shard_map/ppermute | solution.py:19
  30.3 22.4 %copy-start.3 = (bf16[256,1024]{1,0:T(8,128)(2,1)S(1)}, bf16[256,1024]{1,0:T(8,128)(2,1)}, u32[]{:S(2)}) copy-start(bf16[256,1024]{1,0:T(8,128)(2,1)} %param.11) | copy-start | bytes 1572868
  31.8 8.5 %copy-start.4 = (bf16[512,512]{1,0:T(8,128)(2,1)}, bf16[512,512]{1,0:T(8,128)(2,1)S(1)}, u32[]{:S(2)}) copy-start(bf16[512,512]{1,0:T(8,128)(2,1)S(1)} %collective-permute-done.refs_0_) | copy-start | bytes 1572868
  55.1 15.1 %all-to-all-start = ((bf16[512,4,256]{2,0,1:T(8,128)(2,1)}), bf16[512,4,256]{2,0,1:T(8,128)(2,1)S(1)}, u32[]{:S(2)}, u32[]{:S(2)}) async-start(bf16[512,4,256]{2,0,1:T(8,128)(2,1)} %bitcast.32), calls=%async_computation | async-start | bytes 2097152 | tf_op jit(solution)/shard_map/all_to_all | solution.py:30
  72.1 8.5 %all-to-all-start.1 = ((f32[4,1,512]{2,1,0:T(1,128)}), f32[4,1,512]{2,1,0:T(1,128)S(1)}, u32[]{:S(2)}, u32[]{:S(2)}) async-start(f32[4,1,512]{2,1,0:T(1,128)} %broadcast_in_dim.4), calls=%async_computation.1 | async-start | bytes 16384 | tf_op jit(solution)/shard_map/all_to_all | solution.py:38

commit v15 on v10

--- a/solution.py
+++ b/solution.py
@@ -48,6 +48,11 @@
     return lax.all_to_all(spread, "mp", 1, 1).reshape(rows, n_mp * cols)
 
 
+def project_qkv(x_ref, inv_ref, gain_ref, w_ref, out_ref):
+    normed = (x_ref[...].astype(jnp.float32) * inv_ref[...] * gain_ref[...]).astype(jnp.bfloat16)
+    out_ref[0] = jnp.dot(normed, w_ref[0], preferred_element_type=jnp.float32).astype(out_ref.dtype)
+
+
 def window_attention(slot_ref, query_ref, *refs, n_heads, n_win, n_nb):
     kv_refs, out_ref, gathered = refs[:n_win], refs[n_win], refs[n_win + 1]
     per_win = kv_refs[0].shape[1] // PN
@@ -88,10 +93,20 @@
     width = w_qkv.shape[2]
     heads_here = width // HD
     n_win = 2 * REACH + 1
-    normed = normalize(features, gain_attn)
-    qkv = jnp.einsum(
-        "rk,tkc->trc", normed, w_qkv, preferred_element_type=jnp.float32
-    ).astype(jnp.bfloat16)
+    rows32 = features.astype(jnp.float32)
+    inverse = lax.rsqrt(jnp.mean(rows32 * rows32, axis=-1, keepdims=True) + 1e-05)
+    qkv = pl.pallas_call(
+        project_qkv,
+        grid=(3,),
+        in_specs=[
+            pl.BlockSpec((row_count, D), lambda t: (0, 0)),
+            pl.BlockSpec((row_count, 1), lambda t: (0, 0)),
+            pl.BlockSpec((1, D), lambda t: (0, 0)),
+            pl.BlockSpec((1, D, width), lambda t: (t, 0, 0)),
+        ],
+        out_specs=pl.BlockSpec((1, row_count, width), lambda t: (t, 0, 0)),
+        out_shape=jax.ShapeDtypeStruct((3, row_count, width), jnp.bfloat16),
+    )(features, inverse, gain_attn.reshape(1, D), w_qkv)
     queries = qkv[0]
     own_kv = qkv[1:]
     window = {0: own_kv}

time: 112 us -> 116 us (1.036)
  Pallas kernels: 12.2 us -> 16.5 us
  local copies, waits for them, and re-layouts: 5.56 us -> 8.34 us
  matrix products: 6.9 us -> 4.33 us
    pallas_call x0 -> x1, Pallas kernels: none -> 4.28 us  [per_device(): pl.pallas_call(project_qkv, grid=(3,), in_specs=[pl.BlockSpec((row_count,...]
    dot_general x1 -> x0, matrix products: 2.26 us -> none  [per_device(): jnp.einsum('rk,tkc->trc', normed, w_qkv, preferred_element_type=jnp.float32)]
where the time goes in v15:
time: 116 us; the launch traced here: 115 us
  starting transfers between devices  30.8 us (27%)
  blocking collectives  26.6 us (23%)
  waiting for transfers between devices  24 us (21%)
  Pallas kernels  16.5 us (14%)
  local copies, waits for them, and re-layouts  8.34 us (7%)
  other arithmetic  4.37 us (4%)
  matrix products  4.33 us (4%)
    ppermute x4, starting transfers between devices, from_behind(): lax.ppermute(array, axis, [(i, (i + by) % length) for i in range(length)])  21.3 us
    all_to_all x1, blocking collectives, scatter_sum(): got = lax.all_to_all(parts.reshape(rows, n_mp, cols // n_mp), 'mp', 1, 1)  13.3 us
    all_to_all x1, blocking collectives, gather_cols(): return lax.all_to_all(spread, 'mp', 1, 1).reshape(rows, n_mp * cols)  13.3 us
    pallas_call x1, Pallas kernels, per_device(): pl.pallas_call(functools.partial(window_attention, n_heads=heads_here, n_...  12.2 us
    ppermute x4, waiting for transfers between devices, from_behind(): lax.ppermute(array, axis, [(i, (i + by) % length) for i in range(length)])  10.6 us
    all_to_all x1, waiting for transfers between devices, scatter_sum(): got = lax.all_to_all(parts.reshape(rows, n_mp, cols // n_mp), 'mp', 1, 1)  10.3 us
    all_to_all x1, starting transfers between devices, scatter_sum(): got = lax.all_to_all(parts.reshape(rows, n_mp, cols // n_mp), 'mp', 1, 1)  4.83 us
    all_to_all x1, starting transfers between devices, gather_sum(): lax.all_to_all(jnp.broadcast_to(vector[None], (n_mp,) + vector.shape), 'm...  4.68 us
  transfers between devices with their start and end apart: 6, of which 5 were waited for; matrix products, arithmetic and copies ran while one was open for 3% of the time, Pallas kernels for 0%

profile of v15, /device:TPU:2, one launch (start us, length us, event | category | flops | bytes accessed | tf_op | source)
XLA Modules:
  0.0 115.1 jit_solution(91064906990359558)
XLA Ops:
  0.0 0.0 copy-start
  0.0 1.6 %multiply_reduce_fusion = f32[512]{0:T(512)S(1)} fusion(bf16[512,1024]{1,0:T(8,128)(2,1)} %x_ref.1), kind=kLoop, calls=%fused_computation | loop fusion | flops 1572352 | bytes 1050624 | tf_op jit(solution)/shard_map/reduce_sum | solution.py:97
  1.6 0.9 copy.21.inv_ref
  2.5 4.3 %shard_map.82 = bf16[3,512,256]{2,1,0:T(8,128)(2,1)} custom-call(bf16[512,1024]{1,0:T(8,128)(2,1)} %x_ref.1, f32[512,1]{1,0:T(8,128)} %copy.21.inv_ref, f32[1,1024]{1,0:T(1,128)} %bitcast.33, bf16[3,1024,256]{2,1,0:T(8,128)(2,1)} %w_ref.1), custom_call_target="tpu_custom_call" | custom-call | tf_op jit(solution)/shard_map/pallas_call | solution.py:98
  6.8 1.1 slice.61.refs_2_
  7.8 0.0 copy-start.1
  7.8 3.5 %collective-permute-start = (bf16[2,512,256]{2,1,0:T(8,128)(2,1)S(1)}, bf16[2,512,256]{2,1,0:T(8,128)(2,1)S(1)}, u32[]{:S(2)}, u32[]{:S(2)}) collective-permute-start(bf16[2,512,256]{2,1,0:T(8,128)(2,1)S(1)} %slice.61.refs_2_), channel_id=1, source_target_pairs={{0,8},{4,12},{8,16},{12,20},{16,24},{20,28},{24,32},{28,36},{32,40... | collective-permute-start | bytes 1572872 | tf_op jit(solution)/shard_map/ppermute | solution.py:19
  11.3 1.9 %collective-permute-start.1 = (bf16[2,512,256]{2,1,0:T(8,128)(2,1)S(1)}, bf16[2,512,256]{2,1,0:T(8,128)(2,1)S(1)}, u32[]{:S(2)}, u32[]{:S(2)}) collective-permute-start(bf16[2,512,256]{2,1,0:T(8,128)(2,1)S(1)} %slice.61.refs_2_), channel_id=1, source_target_pairs={{0,4},{4,8},{8,12},{12,16},{16,20},{20,24},{24,28},{28,32},{32,36}... | collective-permute-start | bytes 1572872 | tf_op jit(solution)/shard_map/ppermute | solution.py:19
  13.3 11.7 %collective-permute-start.2 = (bf16[2,512,256]{2,1,0:T(8,128)(2,1)S(1)}, bf16[2,512,256]{2,1,0:T(8,128)(2,1)}, u32[]{:S(2)}, u32[]{:S(2)}) collective-permute-start(bf16[2,512,256]{2,1,0:T(8,128)(2,1)S(1)} %slice.61.refs_2_), channel_id=1, source_target_pairs={{0,508},{4,0},{8,4},{12,8},{16,12},{20,16},{24,20},{28,24},{32,28}... | collective-permute-start | bytes 1572872 | tf_op jit(solution)/shard_map/ppermute | solution.py:19
  25.0 4.2 %collective-permute-start.3 = (bf16[2,512,256]{2,1,0:T(8,128)(2,1)S(1)}, bf16[2,512,256]{2,1,0:T(8,128)(2,1)}, u32[]{:S(2)}, u32[]{:S(2)}) collective-permute-start(bf16[2,512,256]{2,1,0:T(8,128)(2,1)S(1)} %slice.61.refs_2_), channel_id=1, source_target_pairs={{0,504},{4,508},{8,0},{12,4},{16,8},{20,12},{24,16},{28,20},{32,24... | collective-permute-start | bytes 1572872 | tf_op jit(solution)/shard_map/ppermute | solution.py:19
  29.2 0.8 constant_dynamic-slice_fusion
  30.0 0.1 copy.25
  30.1 0.6 fusion.19.slot_ref
  30.6 1.7 %slice_bitcast_fusion.query_ref = bf16[512,256]{1,0:T(8,128)(2,1)} fusion(bf16[3,512,256]{2,1,0:T(8,128)(2,1)} %shard_map.82), kind=kLoop, calls=%fused_computation.23 | loop fusion | bytes 524288 | tf_op jit(solution)/shard_map/squeeze | solution.py:110
  32.3 0.0 copy-start.2
  32.3 2.2 %collective-permute-done.refs_0_ = bf16[2,512,256]{2,1,0:T(8,128)(2,1)S(1)} collective-permute-done((bf16[2,512,256]{2,1,0:T(8,128)(2,1)S(1)}, bf16[2,512,256]{2,1,0:T(8,128)(2,1)S(1)}, u32[]{:S(2)}, u32[]{:S(2)}) %collective-permute-start) | collective-permute-done | bytes 524320 | tf_op jit(solution)/shard_map/ppermute | solution.py:19
  34.5 0.0 copy-start.3
  34.5 4.8 %collective-permute-done.1.refs_1_ = bf16[2,512,256]{2,1,0:T(8,128)(2,1)S(1)} collective-permute-done((bf16[2,512,256]{2,1,0:T(8,128)(2,1)S(1)}, bf16[2,512,256]{2,1,0:T(8,128)(2,1)S(1)}, u32[]{:S(2)}, u32[]{:S(2)}) %collective-permute-start.1) | collective-permute-done | bytes 524320 | tf_op jit(solution)/shard_map/ppermute | solution.py:19
  39.2 0.0 copy-start.4
  39.2 0.0 collective-permute-done.2.refs_3_
  39.2 3.7 %collective-permute-done.3.refs_4_ = bf16[2,512,256]{2,1,0:T(8,128)(2,1)} collective-permute-done((bf16[2,512,256]{2,1,0:T(8,128)(2,1)S(1)}, bf16[2,512,256]{2,1,0:T(8,128)(2,1)}, u32[]{:S(2)}, u32[]{:S(2)}) %collective-permute-start.3) | collective-permute-done | bytes 524320 | tf_op jit(solution)/shard_map/ppermute | solution.py:19
  42.9 0.0 copy-done.1
  42.9 0.0 copy-done.3
  42.9 0.0 copy-done.4
  42.9 12.2 %shard_map.83 = bf16[512,256]{1,0:T(8,128)(2,1)} custom-call(s32[4,8]{1,0:T(4,128)} %fusion.19.slot_ref, bf16[512,256]{1,0:T(8,128)(2,1)} %slice_bitcast_fusion.query_ref, bf16[2,512,256]{2,1,0:T(8,128)(2,1)} %copy-done.3, bf16[2,512,256]{2,1,0:T(8,128)(2,1)} %copy-done.4, bf16[2,512,256]{2,1,0:T(8,128)(2,1)} %copy-done.1, ...), custom_call_target="tpu_custom_call" | custom-call | tf_op jit(solution)/shard_map/pallas_call | solution.py:124
  55.1 0.0 copy-done.2
  55.1 1.4 %convolution_convert_fusion = bf16[512,1024]{1,0:T(8,128)(2,1)S(1)} fusion(bf16[512,256]{1,0:T(8,128)(2,1)} %shard_map.83, bf16[256,1024]{1,0:T(8,128)(2,1)S(1)} %copy-done.2), kind=kOutput, calls=%fused_computation.2 | convolution fusion | flops 268959744 | bytes 1835008 | tf_op jit(solution)/shard_map/dot_general | solution.py:136
  56.5 1.0 copy.31
  57.6 4.8 %all-to-all-start = ((bf16[512,4,256]{2,0,1:T(8,128)(2,1)}), bf16[512,4,256]{2,0,1:T(8,128)(2,1)S(1)}, u32[]{:S(2)}, u32[]{:S(2)}) async-start(bf16[512,4,256]{2,0,1:T(8,128)(2,1)} %bitcast.27), calls=%async_computation | async-start | bytes 2097152 | tf_op jit(solution)/shard_map/all_to_all | solution.py:30
  62.4 10.3 %all-to-all-done = bf16[512,4,256]{2,0,1:T(8,128)(2,1)S(1)} async-done(((bf16[512,4,256]{2,0,1:T(8,128)(2,1)}), bf16[512,4,256]{2,0,1:T(8,128)(2,1)S(1)}, u32[]{:S(2)}, u32[]{:S(2)}) %all-to-all-start) | async-done | bytes 1048608 | tf_op jit(solution)/shard_map/all_to_all | solution.py:30
  72.7 1.2 %multiply_reduce_fusion.1 = (f32[512]{0:T(512)S(1)}, f32[512,256]{1,0:T(8,128)S(1)}) fusion(bf16[512,4,256]{2,0,1:T(8,128)(2,1)S(1)} %all-to-all-done, bf16[512,1024]{1,0:T(8,128)(2,1)} %x_ref.1, s32[]{:T(128)S(6)} %select_n.23), kind=kLoop, calls=%fused_computation.22 | loop fusion | flops 1441280 | bytes 1837060 | tf_op jit(solution)/shard_map/reduce_sum | solution.py:144
  73.9 0.6 broadcast_in_dim.4
  74.5 4.7 %all-to-all-start.1 = ((f32[4,1,512]{2,1,0:T(1,128)}), f32[4,1,512]{2,1,0:T(1,128)S(1)}, u32[]{:S(2)}, u32[]{:S(2)}) async-start(f32[4,1,512]{2,1,0:T(1,128)} %broadcast_in_dim.4), calls=%async_computation.1 | async-start | bytes 16384 | tf_op jit(solution)/shard_map/all_to_all | solution.py:38
  79.2 0.8 dynamic_slice.11
  80.0 3.1 %all-to-all-done.1 = f32[4,1,512]{2,1,0:T(1,128)S(1)} async-done(((f32[4,1,512]{2,1,0:T(1,128)}), f32[4,1,512]{2,1,0:T(1,128)S(1)}, u32[]{:S(2)}, u32[]{:S(2)}) %all-to-all-start.1) | async-done | bytes 8224 | tf_op jit(solution)/shard_map/all_to_all | solution.py:38
  83.1 0.1 multiply_convert_fusion
  83.2 0.1 broadcast_in_dim.5
  83.3 13.3 %all_to_all.21 = bf16[512,4,256]{2,0,1:T(8,128)(2,1)S(1)} all-to-all(bf16[512,4,256]{2,0,1:T(8,128)(2,1)S(1)} %broadcast_in_dim.5), channel_id=1, replica_groups=mesh['patch'=128,'mp'=4] {'mp'}, dimensions={1} | all-to-all | bytes 2097152 | tf_op jit(solution)/shard_map/all_to_all | solution.py:48
  96.6 1.3 %copy.23 = bf16[512,4,256]{0,2,1:T(8,128)(2,1)} copy(bf16[512,4,256]{2,0,1:T(8,128)(2,1)S(1)} %all_to_all.21) | data formatting | bytes 2097152 | tf_op jit(solution)/shard_map/all_to_all | solution.py:48
  98.0 0.0 copy-done
  98.0 2.9 %convolution_convert_fusion.1 = bf16[512,1024]{1,0:T(8,128)(2,1)S(1)} fusion(bf16[512,1024]{1,0:T(8,128)(2,1)S(1)} %copy-done, bf16[512,1024]{0,1:T(8,128)(2,1)} %bitcast.29, bf16[1024,512]{1,0:T(8,128)(2,1)} %param.13), kind=kOutput, calls=%fused_computation.3 | convolution fusion | flops 1076625408 | bytes 4194304 | tf_op jit(solution)/shard_map/dot_general | solution.py:151
  100.9 0.1 copy.30
  101.0 13.3 %all_to_all.22 = bf16[512,4,256]{2,0,1:T(8,128)(2,1)S(1)} all-to-all(bf16[512,4,256]{2,0,1:T(8,128)(2,1)S(1)} %bitcast.28), channel_id=1, replica_groups=mesh['patch'=128,'mp'=4] {'mp'}, dimensions={1} | all-to-all | bytes 2097152 | tf_op jit(solution)/shard_map/all_to_all | solution.py:30
  114.3 0.8 fusion.9
  (2 shorter events, 0.0 us)
Async XLA Ops:
  0.0 98.0 %copy-start = (bf16[512,1024]{1,0:T(8,128)(2,1)S(1)}, bf16[512,1024]{1,0:T(8,128)(2,1)}, u32[]{:S(2)}) copy-start(bf16[512,1024]{1,0:T(8,128)(2,1)} %param.14) | copy-start | bytes 3145732
  7.8 35.1 %copy-start.1 = (bf16[2,512,256]{2,1,0:T(8,128)(2,1)}, bf16[2,512,256]{2,1,0:T(8,128)(2,1)S(1)}, u32[]{:S(2)}) copy-start(bf16[2,512,256]{2,1,0:T(8,128)(2,1)S(1)} %slice.61.refs_2_) | copy-start | bytes 1572868
  7.8 26.6 %collective-permute-start = (bf16[2,512,256]{2,1,0:T(8,128)(2,1)S(1)}, bf16[2,512,256]{2,1,0:T(8,128)(2,1)S(1)}, u32[]{:S(2)}, u32[]{:S(2)}) collective-permute-start(bf16[2,512,256]{2,1,0:T(8,128)(2,1)S(1)} %slice.61.refs_2_), channel_id=1, source_target_pairs={{0,8},{4,12},{8,16},{12,20},{16,24},{20,28},{24,32},{28,36},{32,40... | collective-permute-start | bytes 1572872 | tf_op jit(solution)/shard_map/ppermute | solution.py:19
  11.3 27.9 %collective-permute-start.1 = (bf16[2,512,256]{2,1,0:T(8,128)(2,1)S(1)}, bf16[2,512,256]{2,1,0:T(8,128)(2,1)S(1)}, u32[]{:S(2)}, u32[]{:S(2)}) collective-permute-start(bf16[2,512,256]{2,1,0:T(8,128)(2,1)S(1)} %slice.61.refs_2_), channel_id=1, source_target_pairs={{0,4},{4,8},{8,12},{12,16},{16,20},{20,24},{24,28},{28,32},{32,36}... | collective-permute-start | bytes 1572872 | tf_op jit(solution)/shard_map/ppermute | solution.py:19
  13.3 26.0 %collective-permute-start.2 = (bf16[2,512,256]{2,1,0:T(8,128)(2,1)S(1)}, bf16[2,512,256]{2,1,0:T(8,128)(2,1)}, u32[]{:S(2)}, u32[]{:S(2)}) collective-permute-start(bf16[2,512,256]{2,1,0:T(8,128)(2,1)S(1)} %slice.61.refs_2_), channel_id=1, source_target_pairs={{0,508},{4,0},{8,4},{12,8},{16,12},{20,16},{24,20},{28,24},{32,28}... | collective-permute-start | bytes 1572872 | tf_op jit(solution)/shard_map/ppermute | solution.py:19
  25.0 17.9 %collective-permute-start.3 = (bf16[2,512,256]{2,1,0:T(8,128)(2,1)S(1)}, bf16[2,512,256]{2,1,0:T(8,128)(2,1)}, u32[]{:S(2)}, u32[]{:S(2)}) collective-permute-start(bf16[2,512,256]{2,1,0:T(8,128)(2,1)S(1)} %slice.61.refs_2_), channel_id=1, source_target_pairs={{0,504},{4,508},{8,0},{12,4},{16,8},{20,12},{24,16},{28,20},{32,24... | collective-permute-start | bytes 1572872 | tf_op jit(solution)/shard_map/ppermute | solution.py:19
  32.3 22.8 %copy-start.2 = (bf16[256,1024]{1,0:T(8,128)(2,1)S(1)}, bf16[256,1024]{1,0:T(8,128)(2,1)}, u32[]{:S(2)}) copy-start(bf16[256,1024]{1,0:T(8,128)(2,1)} %param.11) | copy-start | bytes 1572868
  34.5 8.5 %copy-start.3 = (bf16[2,512,256]{2,1,0:T(8,128)(2,1)}, bf16[2,512,256]{2,1,0:T(8,128)(2,1)S(1)}, u32[]{:S(2)}) copy-start(bf16[2,512,256]{2,1,0:T(8,128)(2,1)S(1)} %collective-permute-done.refs_0_) | copy-start | bytes 1572868
  39.2 3.7 %copy-start.4 = (bf16[2,512,256]{2,1,0:T(8,128)(2,1)}, bf16[2,512,256]{2,1,0:T(8,128)(2,1)S(1)}, u32[]{:S(2)}) copy-start(bf16[2,512,256]{2,1,0:T(8,128)(2,1)S(1)} %collective-permute-done.1.refs_1_) | copy-start | bytes 1572868
  57.6 15.1 %all-to-all-start = ((bf16[512,4,256]{2,0,1:T(8,128)(2,1)}), bf16[512,4,256]{2,0,1:T(8,128)(2,1)S(1)}, u32[]{:S(2)}, u32[]{:S(2)}) async-start(bf16[512,4,256]{2,0,1:T(8,128)(2,1)} %bitcast.27), calls=%async_computation | async-start | bytes 2097152 | tf_op jit(solution)/shard_map/all_to_all | solution.py:30
  74.5 8.5 %all-to-all-start.1 = ((f32[4,1,512]{2,1,0:T(1,128)}), f32[4,1,512]{2,1,0:T(1,128)S(1)}, u32[]{:S(2)}, u32[]{:S(2)}) async-start(f32[4,1,512]{2,1,0:T(1,128)} %broadcast_in_dim.4), calls=%async_computation.1 | async-start | bytes 16384 | tf_op jit(solution)/shard_map/all_to_all | solution.py:38

commit v16 on v5

--- a/solution.py
+++ b/solution.py
@@ -90,8 +90,9 @@
     heads_here = width // HD
     n_win = 2 * REACH + 1
     normed = normalize(features, gain_attn)
-    w_all = jnp.concatenate([w_qkv[0], w_qkv[1], w_qkv[2]], axis=1)
-    qkv = jnp.dot(normed, w_all, preferred_element_type=jnp.float32).astype(jnp.bfloat16)
+    qkv = jnp.einsum(
+        "rk,tkc->rtc", normed, w_qkv, preferred_element_type=jnp.float32
+    ).astype(jnp.bfloat16).reshape(row_count, 3 * width)
     queries = qkv[:, :width]
     own_kv = qkv[:, width:]
     window = {0: own_kv}

time: 111 us -> 113 us (1.018)
  matrix products: 5.36 us -> 6.98 us
  other arithmetic: 3.1 us -> 4.45 us
  local copies, waits for them, and re-layouts: 7.24 us -> 5.92 us
    squeeze x1 -> x0, local copies, waits for them, and re-layouts: 1.61 us -> none  [per_device(): w_all = jnp.concatenate([w_qkv[0], w_qkv[1], w_qkv[2]], axis=1)]
    reduce_sum x1, other arithmetic: 0.28 us -> 1.62 us  [normalize(): mean_sq = jnp.mean(rows32 * rows32, axis=-1, keepdims=True)]
    dot_general x1, matrix products: 1.04 us -> 2.34 us  [per_device(): jnp.einsum('rk,tkc->rtc', normed, w_qkv, preferred_element_type=jnp.float32)]
where the time goes in v16:
time: 113 us; the launch traced here: 112 us
  starting transfers between devices  30.8 us (27%)
  blocking collectives  26.6 us (24%)
  waiting for transfers between devices  24.8 us (22%)
  Pallas kernels  12.4 us (11%)
  matrix products  6.98 us (6%)
  local copies, waits for them, and re-layouts  5.92 us (5%)
  other arithmetic  4.45 us (4%)
    ppermute x4, starting transfers between devices, from_behind(): lax.ppermute(array, axis, [(i, (i + by) % length) for i in range(length)])  21.3 us
    all_to_all x1, blocking collectives, gather_cols(): return lax.all_to_all(spread, 'mp', 1, 1).reshape(rows, n_mp * cols)  13.3 us
    all_to_all x1, blocking collectives, scatter_sum(): got = lax.all_to_all(parts.reshape(rows, n_mp, cols // n_mp), 'mp', 1, 1)  13.3 us
    pallas_call x1, Pallas kernels, per_device(): pl.pallas_call(functools.partial(window_attention, n_heads=heads_here, n_...  12.4 us
    ppermute x4, waiting for transfers between devices, from_behind(): lax.ppermute(array, axis, [(i, (i + by) % length) for i in range(length)])  11.4 us
    all_to_all x1, waiting for transfers between devices, scatter_sum(): got = lax.all_to_all(parts.reshape(rows, n_mp, cols // n_mp), 'mp', 1, 1)  10.3 us
    all_to_all x1, starting transfers between devices, scatter_sum(): got = lax.all_to_all(parts.reshape(rows, n_mp, cols // n_mp), 'mp', 1, 1)  4.82 us
    all_to_all x1, starting transfers between devices, gather_sum(): lax.all_to_all(jnp.broadcast_to(vector[None], (n_mp,) + vector.shape), 'm...  4.68 us
  transfers between devices with their start and end apart: 6, of which 5 were waited for; matrix products, arithmetic and copies ran while one was open for 3% of the time, Pallas kernels for 0%

profile of v16, /device:TPU:2, one launch (start us, length us, event | category | flops | bytes accessed | tf_op | source)
XLA Modules:
  0.0 112.2 jit_solution(2131275569618181314)
XLA Ops:
  0.0 0.0 copy-start
  0.0 1.6 %fusion = f32[512]{0:T(512)S(1)} fusion(bf16[512,1024]{1,0:T(8,128)(2,1)} %param.8), kind=kLoop, calls=%fused_computation.2 | loop fusion | flops 1572352 | bytes 1050624 | tf_op jit(solution)/shard_map/reduce_sum | solution.py:24
  1.6 0.1 copy-done
  1.7 2.3 %convolution_convert_fusion.2 = bf16[512,3,256]{0,2,1:T(8,128)(2,1)S(1)} fusion(bf16[3,1024,256]{2,1,0:T(8,128)(2,1)S(1)} %copy-done, bf16[512,1024]{1,0:T(8,128)(2,1)} %param.8, f32[1024]{0:T(1024)} %param.9, f32[512]{0:T(512)S(1)} %add_rsqrt_fusion.1), kind=kOutput, calls=%fused_computation.8 | convolution fusion | flops 807796736 | bytes 3414016 | tf_op jit(solution)/shard_map/rk,tkc->rtc/dot_general | solution.py:93
  4.1 0.2 copy.36.refs_2_
  4.3 0.0 copy-start.1
  4.3 3.5 %collective-permute-start = (bf16[512,512]{1,0:T(8,128)(2,1)S(1)}, bf16[512,512]{1,0:T(8,128)(2,1)}, u32[]{:S(2)}, u32[]{:S(2)}) collective-permute-start(bf16[512,512]{1,0:T(8,128)(2,1)S(1)} %copy.36.refs_2_), channel_id=1, source_target_pairs={{0,8},{4,12},{8,16},{12,20},{16,24},{20,28},{24,32},{28,36},{32,40... | collective-permute-start | bytes 1572872 | tf_op jit(solution)/shard_map/ppermute | solution.py:19
  7.8 1.9 %collective-permute-start.1 = (bf16[512,512]{1,0:T(8,128)(2,1)S(1)}, bf16[512,512]{1,0:T(8,128)(2,1)}, u32[]{:S(2)}, u32[]{:S(2)}) collective-permute-start(bf16[512,512]{1,0:T(8,128)(2,1)S(1)} %copy.36.refs_2_), channel_id=1, source_target_pairs={{0,4},{4,8},{8,12},{12,16},{16,20},{20,24},{24,28},{28,32},{32,36}... | collective-permute-start | bytes 1572872 | tf_op jit(solution)/shard_map/ppermute | solution.py:19
  9.8 11.7 %collective-permute-start.2 = (bf16[512,512]{1,0:T(8,128)(2,1)S(1)}, bf16[512,512]{1,0:T(8,128)(2,1)}, u32[]{:S(2)}, u32[]{:S(2)}) collective-permute-start(bf16[512,512]{1,0:T(8,128)(2,1)S(1)} %copy.36.refs_2_), channel_id=1, source_target_pairs={{0,508},{4,0},{8,4},{12,8},{16,12},{20,16},{24,20},{28,24},{32,28}... | collective-permute-start | bytes 1572872 | tf_op jit(solution)/shard_map/ppermute | solution.py:19
  21.5 4.2 %collective-permute-start.3 = (bf16[512,512]{1,0:T(8,128)(2,1)S(1)}, bf16[512,512]{1,0:T(8,128)(2,1)}, u32[]{:S(2)}, u32[]{:S(2)}) collective-permute-start(bf16[512,512]{1,0:T(8,128)(2,1)S(1)} %copy.36.refs_2_), channel_id=1, source_target_pairs={{0,504},{4,508},{8,0},{12,4},{16,8},{20,12},{24,16},{28,20},{32,24... | collective-permute-start | bytes 1572872 | tf_op jit(solution)/shard_map/ppermute | solution.py:19
  25.7 0.8 constant_dynamic-slice_fusion
  26.5 0.1 copy.34
  26.6 0.8 copy.35.query_ref
  27.4 0.6 fusion.26.slot_ref
  28.0 0.0 copy-start.2
  28.0 3.0 %collective-permute-done.refs_0_ = bf16[512,512]{1,0:T(8,128)(2,1)} collective-permute-done((bf16[512,512]{1,0:T(8,128)(2,1)S(1)}, bf16[512,512]{1,0:T(8,128)(2,1)}, u32[]{:S(2)}, u32[]{:S(2)}) %collective-permute-start) | collective-permute-done | bytes 524320 | tf_op jit(solution)/shard_map/ppermute | solution.py:19
  31.1 4.8 %collective-permute-done.1.refs_1_ = bf16[512,512]{1,0:T(8,128)(2,1)} collective-permute-done((bf16[512,512]{1,0:T(8,128)(2,1)S(1)}, bf16[512,512]{1,0:T(8,128)(2,1)}, u32[]{:S(2)}, u32[]{:S(2)}) %collective-permute-start.1) | collective-permute-done | bytes 524320 | tf_op jit(solution)/shard_map/ppermute | solution.py:19
  35.8 0.0 collective-permute-done.2.refs_3_
  35.8 3.6 %collective-permute-done.3.refs_4_ = bf16[512,512]{1,0:T(8,128)(2,1)} collective-permute-done((bf16[512,512]{1,0:T(8,128)(2,1)S(1)}, bf16[512,512]{1,0:T(8,128)(2,1)}, u32[]{:S(2)}, u32[]{:S(2)}) %collective-permute-start.3) | collective-permute-done | bytes 524320 | tf_op jit(solution)/shard_map/ppermute | solution.py:19
  39.4 0.0 copy-done.1
  39.4 12.4 %shard_map.82 = bf16[512,256]{1,0:T(8,128)(2,1)} custom-call(s32[4,8]{1,0:T(4,128)} %fusion.26.slot_ref, bf16[512,256]{1,0:T(8,128)(2,1)} %copy.35.query_ref, bf16[512,512]{1,0:T(8,128)(2,1)} %collective-permute-done.refs_0_, bf16[512,512]{1,0:T(8,128)(2,1)} %collective-permute-done.1.refs_1_, bf16[512,512]{1,0:T(8,128)(2,1)} %copy-done.1, ...), custom_call_target="tpu_custom_call" | custom-call | tf_op jit(solution)/shard_map/pallas_call | solution.py:110
  51.8 0.0 copy-done.2
  51.8 1.4 %convolution_convert_fusion = bf16[512,1024]{1,0:T(8,128)(2,1)S(1)} fusion(bf16[512,256]{1,0:T(8,128)(2,1)} %shard_map.82, bf16[256,1024]{1,0:T(8,128)(2,1)S(1)} %copy-done.2), kind=kOutput, calls=%fused_computation.6 | convolution fusion | flops 268959744 | bytes 1835008 | tf_op jit(solution)/shard_map/dot_general | solution.py:122
  53.2 1.0 copy.42
  54.3 4.8 %all-to-all-start = ((bf16[512,4,256]{2,0,1:T(8,128)(2,1)}), bf16[512,4,256]{2,0,1:T(8,128)(2,1)S(1)}, u32[]{:S(2)}, u32[]{:S(2)}) async-start(bf16[512,4,256]{2,0,1:T(8,128)(2,1)} %bitcast.28), calls=%async_computation | async-start | bytes 2097152 | tf_op jit(solution)/shard_map/all_to_all | solution.py:30
  59.1 10.3 %all-to-all-done = bf16[512,4,256]{2,0,1:T(8,128)(2,1)S(1)} async-done(((bf16[512,4,256]{2,0,1:T(8,128)(2,1)}), bf16[512,4,256]{2,0,1:T(8,128)(2,1)S(1)}, u32[]{:S(2)}, u32[]{:S(2)}) %all-to-all-start) | async-done | bytes 1048608 | tf_op jit(solution)/shard_map/all_to_all | solution.py:30
  69.4 1.2 %multiply_reduce_fusion = (f32[512]{0:T(512)S(1)}, f32[512,256]{1,0:T(8,128)S(1)}) fusion(bf16[512,4,256]{2,0,1:T(8,128)(2,1)S(1)} %all-to-all-done, bf16[512,1024]{1,0:T(8,128)(2,1)} %param.8, s32[]{:T(128)S(6)} %select_n.23), kind=kLoop, calls=%fused_computation.30 | loop fusion | flops 1441280 | bytes 1837060 | tf_op jit(solution)/shard_map/reduce_sum | solution.py:130
  70.6 0.6 broadcast_in_dim.4
  71.2 4.7 %all-to-all-start.1 = ((f32[4,1,512]{2,1,0:T(1,128)}), f32[4,1,512]{2,1,0:T(1,128)S(1)}, u32[]{:S(2)}, u32[]{:S(2)}) async-start(f32[4,1,512]{2,1,0:T(1,128)} %broadcast_in_dim.4), calls=%async_computation.1 | async-start | bytes 16384 | tf_op jit(solution)/shard_map/all_to_all | solution.py:38
  75.9 0.8 dynamic_slice.11
  76.7 3.1 %all-to-all-done.1 = f32[4,1,512]{2,1,0:T(1,128)S(1)} async-done(((f32[4,1,512]{2,1,0:T(1,128)}), f32[4,1,512]{2,1,0:T(1,128)S(1)}, u32[]{:S(2)}, u32[]{:S(2)}) %all-to-all-start.1) | async-done | bytes 8224 | tf_op jit(solution)/shard_map/all_to_all | solution.py:38
  79.8 0.1 multiply_convert_fusion
  79.9 0.1 broadcast_in_dim.5
  80.0 13.3 %all_to_all.21 = bf16[512,4,256]{2,0,1:T(8,128)(2,1)S(1)} all-to-all(bf16[512,4,256]{2,0,1:T(8,128)(2,1)S(1)} %broadcast_in_dim.5), channel_id=1, replica_groups=mesh['patch'=128,'mp'=4] {'mp'}, dimensions={1} | all-to-all | bytes 2097152 | tf_op jit(solution)/shard_map/all_to_all | solution.py:48
  93.3 1.3 %copy.31 = bf16[512,4,256]{0,2,1:T(8,128)(2,1)} copy(bf16[512,4,256]{2,0,1:T(8,128)(2,1)S(1)} %all_to_all.21) | data formatting | bytes 2097152 | tf_op jit(solution)/shard_map/all_to_all | solution.py:48
  94.6 3.3 %convolution_convert_fusion.1 = bf16[512,1024]{1,0:T(8,128)(2,1)S(1)} fusion(bf16[512,1024]{1,0:T(8,128)(2,1)} %param.14, bf16[512,1024]{0,1:T(8,128)(2,1)} %bitcast.30, bf16[1024,512]{1,0:T(8,128)(2,1)} %param.13), kind=kOutput, calls=%fused_computation.7 | convolution fusion | flops 1076625408 | bytes 4194304 | tf_op jit(solution)/shard_map/dot_general | solution.py:137
  97.9 0.1 copy.41
  98.0 13.3 %all_to_all.22 = bf16[512,4,256]{2,0,1:T(8,128)(2,1)S(1)} all-to-all(bf16[512,4,256]{2,0,1:T(8,128)(2,1)S(1)} %bitcast.29), channel_id=1, replica_groups=mesh['patch'=128,'mp'=4] {'mp'}, dimensions={1} | all-to-all | bytes 2097152 | tf_op jit(solution)/shard_map/all_to_all | solution.py:30
  111.3 0.8 fusion.16
  (4 shorter events, 0.1 us)
Async XLA Ops:
  0.0 1.7 %copy-start = (bf16[3,1024,256]{2,1,0:T(8,128)(2,1)S(1)}, bf16[3,1024,256]{2,1,0:T(8,128)(2,1)}, u32[]{:S(2)}) copy-start(bf16[3,1024,256]{2,1,0:T(8,128)(2,1)} %param.10) | copy-start | bytes 4718596
  4.3 35.1 %copy-start.1 = (bf16[512,512]{1,0:T(8,128)(2,1)}, bf16[512,512]{1,0:T(8,128)(2,1)S(1)}, u32[]{:S(2)}) copy-start(bf16[512,512]{1,0:T(8,128)(2,1)S(1)} %copy.36.refs_2_) | copy-start | bytes 1572868
  4.3 26.7 %collective-permute-start = (bf16[512,512]{1,0:T(8,128)(2,1)S(1)}, bf16[512,512]{1,0:T(8,128)(2,1)}, u32[]{:S(2)}, u32[]{:S(2)}) collective-permute-start(bf16[512,512]{1,0:T(8,128)(2,1)S(1)} %copy.36.refs_2_), channel_id=1, source_target_pairs={{0,8},{4,12},{8,16},{12,20},{16,24},{20,28},{24,32},{28,36},{32,40... | collective-permute-start | bytes 1572872 | tf_op jit(solution)/shard_map/ppermute | solution.py:19
  7.8 28.0 %collective-permute-start.1 = (bf16[512,512]{1,0:T(8,128)(2,1)S(1)}, bf16[512,512]{1,0:T(8,128)(2,1)}, u32[]{:S(2)}, u32[]{:S(2)}) collective-permute-start(bf16[512,512]{1,0:T(8,128)(2,1)S(1)} %copy.36.refs_2_), channel_id=1, source_target_pairs={{0,4},{4,8},{8,12},{12,16},{16,20},{20,24},{24,28},{28,32},{32,36}... | collective-permute-start | bytes 1572872 | tf_op jit(solution)/shard_map/ppermute | solution.py:19
  9.8 26.1 %collective-permute-start.2 = (bf16[512,512]{1,0:T(8,128)(2,1)S(1)}, bf16[512,512]{1,0:T(8,128)(2,1)}, u32[]{:S(2)}, u32[]{:S(2)}) collective-permute-start(bf16[512,512]{1,0:T(8,128)(2,1)S(1)} %copy.36.refs_2_), channel_id=1, source_target_pairs={{0,508},{4,0},{8,4},{12,8},{16,12},{20,16},{24,20},{28,24},{32,28}... | collective-permute-start | bytes 1572872 | tf_op jit(solution)/shard_map/ppermute | solution.py:19
  21.5 17.9 %collective-permute-start.3 = (bf16[512,512]{1,0:T(8,128)(2,1)S(1)}, bf16[512,512]{1,0:T(8,128)(2,1)}, u32[]{:S(2)}, u32[]{:S(2)}) collective-permute-start(bf16[512,512]{1,0:T(8,128)(2,1)S(1)} %copy.36.refs_2_), channel_id=1, source_target_pairs={{0,504},{4,508},{8,0},{12,4},{16,8},{20,12},{24,16},{28,20},{32,24... | collective-permute-start | bytes 1572872 | tf_op jit(solution)/shard_map/ppermute | solution.py:19
  28.0 23.8 %copy-start.2 = (bf16[256,1024]{1,0:T(8,128)(2,1)S(1)}, bf16[256,1024]{1,0:T(8,128)(2,1)}, u32[]{:S(2)}) copy-start(bf16[256,1024]{1,0:T(8,128)(2,1)} %param.11) | copy-start | bytes 1572868
  54.3 15.1 %all-to-all-start = ((bf16[512,4,256]{2,0,1:T(8,128)(2,1)}), bf16[512,4,256]{2,0,1:T(8,128)(2,1)S(1)}, u32[]{:S(2)}, u32[]{:S(2)}) async-start(bf16[512,4,256]{2,0,1:T(8,128)(2,1)} %bitcast.28), calls=%async_computation | async-start | bytes 2097152 | tf_op jit(solution)/shard_map/all_to_all | solution.py:30
  71.2 8.5 %all-to-all-start.1 = ((f32[4,1,512]{2,1,0:T(1,128)}), f32[4,1,512]{2,1,0:T(1,128)S(1)}, u32[]{:S(2)}, u32[]{:S(2)}) async-start(f32[4,1,512]{2,1,0:T(1,128)} %broadcast_in_dim.4), calls=%async_computation.1 | async-start | bytes 16384 | tf_op jit(solution)/shard_map/all_to_all | solution.py:38

commit v17 on v5

--- a/solution.py
+++ b/solution.py
@@ -65,7 +65,7 @@
     for pair in range(n_heads // 2):
         cols = slice(pair * 2 * HD, (pair + 1) * 2 * HD)
         v_cols = slice(width + pair * 2 * HD, width + (pair + 1) * 2 * HD)
-        q_pair = query_ref[:, cols]
+        q_pair = query_ref[:, cols] * jnp.asarray(1.0 / HD**0.5, query_ref.dtype)
         keys = gathered[:, cols]
         vals = gathered[:, v_cols]
         mixed = []
@@ -74,7 +74,7 @@
             q_head = jnp.where(keep, q_pair, jnp.zeros_like(q_pair))
             s = lax.dot_general(
                 q_head, keys, (((1,), (1,)), ((), ())), preferred_element_type=jnp.float32
-            ) * (1.0 / HD**0.5)
+            )
             e = jnp.exp(s - s.max(axis=1, keepdims=True))
             inv = 1.0 / e.sum(axis=1, keepdims=True)
             probs = (e * inv).astype(jnp.bfloat16)

time: 111 us -> 111 us (level)
  no operation moved by 1% of the time
where the time goes in v17:
time: 111 us
  starting transfers between devices  30.8 us (28%)
  blocking collectives  26.6 us (24%)
  waiting for transfers between devices  25 us (23%)
  Pallas kernels  12.4 us (11%)
  local copies, waits for them, and re-layouts  7.24 us (7%)
  matrix products  5.36 us (5%)
  other arithmetic  3.1 us (3%)
    ppermute x4, starting transfers between devices, from_behind(): lax.ppermute(array, axis, [(i, (i + by) % length) for i in range(length)])  21.3 us
    all_to_all x1, blocking collectives, gather_cols(): return lax.all_to_all(spread, 'mp', 1, 1).reshape(rows, n_mp * cols)  13.3 us
    all_to_all x1, blocking collectives, scatter_sum(): got = lax.all_to_all(parts.reshape(rows, n_mp, cols // n_mp), 'mp', 1, 1)  13.3 us
    pallas_call x1, Pallas kernels, per_device(): pl.pallas_call(functools.partial(window_attention, n_heads=heads_here, n_...  12.4 us
    ppermute x4, waiting for transfers between devices, from_behind(): lax.ppermute(array, axis, [(i, (i + by) % length) for i in range(length)])  11.5 us
    all_to_all x1, waiting for transfers between devices, scatter_sum(): got = lax.all_to_all(parts.reshape(rows, n_mp, cols // n_mp), 'mp', 1, 1)  10.3 us
    all_to_all x1, starting transfers between devices, scatter_sum(): got = lax.all_to_all(parts.reshape(rows, n_mp, cols // n_mp), 'mp', 1, 1)  4.82 us
    all_to_all x1, starting transfers between devices, gather_sum(): lax.all_to_all(jnp.broadcast_to(vector[None], (n_mp,) + vector.shape), 'm...  4.68 us
  transfers between devices with their start and end apart: 6, of which 5 were waited for; matrix products, arithmetic and copies ran while one was open for 3% of the time, Pallas kernels for 0%

profile of v17, /device:TPU:2, one launch (start us, length us, event | category | flops | bytes accessed | tf_op | source)
XLA Modules:
  0.0 110.6 jit_solution(10657082719649986282)
XLA Ops:
  0.0 0.0 copy-start
  0.0 0.0 copy-start.2
  0.0 0.0 copy-start.6
  0.0 1.6 %slice_bitcast_fusion.2 = (bf16[1024,256]{1,0:T(8,128)(2,1)S(1)}, bf16[1024,256]{1,0:T(8,128)(2,1)S(1)}, bf16[1024,256]{1,0:T(8,128)(2,1)S(1)}) fusion(bf16[3,1024,256]{2,1,0:T(8,128)(2,1)} %param.10), kind=kLoop, calls=%fused_computation.38 | loop fusion | bytes 3145728 | tf_op jit(solution)/shard_map/squeeze | solution.py:93
  1.6 0.2 copy-done.2
  1.8 0.3 fusion
  2.1 0.0 copy-done.6
  2.1 1.0 fusion.9
  3.2 0.0 copy-start.1
  3.2 3.5 %collective-permute-start = (bf16[512,512]{1,0:T(8,128)(2,1)S(1)}, bf16[512,512]{1,0:T(8,128)(2,1)S(1)}, u32[]{:S(2)}, u32[]{:S(2)}) collective-permute-start(bf16[512,512]{1,0:T(8,128)(2,1)S(1)} %slice.73.refs_2_), channel_id=1, source_target_pairs={{0,8},{4,12},{8,16},{12,20},{16,24},{20,28},{24,32},{28,36},{32,40... | collective-permute-start | bytes 1572872 | tf_op jit(solution)/shard_map/ppermute | solution.py:19
  6.7 1.9 %collective-permute-start.1 = (bf16[512,512]{1,0:T(8,128)(2,1)S(1)}, bf16[512,512]{1,0:T(8,128)(2,1)S(1)}, u32[]{:S(2)}, u32[]{:S(2)}) collective-permute-start(bf16[512,512]{1,0:T(8,128)(2,1)S(1)} %slice.73.refs_2_), channel_id=1, source_target_pairs={{0,4},{4,8},{8,12},{12,16},{16,20},{20,24},{24,28},{28,32},{32,36}... | collective-permute-start | bytes 1572872 | tf_op jit(solution)/shard_map/ppermute | solution.py:19
  8.6 11.7 %collective-permute-start.2 = (bf16[512,512]{1,0:T(8,128)(2,1)S(1)}, bf16[512,512]{1,0:T(8,128)(2,1)}, u32[]{:S(2)}, u32[]{:S(2)}) collective-permute-start(bf16[512,512]{1,0:T(8,128)(2,1)S(1)} %slice.73.refs_2_), channel_id=1, source_target_pairs={{0,508},{4,0},{8,4},{12,8},{16,12},{20,16},{24,20},{28,24},{32,28}... | collective-permute-start | bytes 1572872 | tf_op jit(solution)/shard_map/ppermute | solution.py:19
  20.3 4.2 %collective-permute-start.3 = (bf16[512,512]{1,0:T(8,128)(2,1)S(1)}, bf16[512,512]{1,0:T(8,128)(2,1)}, u32[]{:S(2)}, u32[]{:S(2)}) collective-permute-start(bf16[512,512]{1,0:T(8,128)(2,1)S(1)} %slice.73.refs_2_), channel_id=1, source_target_pairs={{0,504},{4,508},{8,0},{12,4},{16,8},{20,12},{24,16},{28,20},{32,24... | collective-permute-start | bytes 1572872 | tf_op jit(solution)/shard_map/ppermute | solution.py:19
  24.6 0.7 slice.72.query_ref
  25.3 0.8 constant_dynamic-slice_fusion
  26.0 0.1 copy.19
  26.1 0.6 fusion.34.slot_ref
  26.7 0.0 copy-start.3
  26.7 3.1 %collective-permute-done.refs_0_ = bf16[512,512]{1,0:T(8,128)(2,1)S(1)} collective-permute-done((bf16[512,512]{1,0:T(8,128)(2,1)S(1)}, bf16[512,512]{1,0:T(8,128)(2,1)S(1)}, u32[]{:S(2)}, u32[]{:S(2)}) %collective-permute-start) | collective-permute-done | bytes 524320 | tf_op jit(solution)/shard_map/ppermute | solution.py:19
  29.8 0.0 copy-start.4
  29.8 4.8 %collective-permute-done.1.refs_1_ = bf16[512,512]{1,0:T(8,128)(2,1)S(1)} collective-permute-done((bf16[512,512]{1,0:T(8,128)(2,1)S(1)}, bf16[512,512]{1,0:T(8,128)(2,1)S(1)}, u32[]{:S(2)}, u32[]{:S(2)}) %collective-permute-start.1) | collective-permute-done | bytes 524320 | tf_op jit(solution)/shard_map/ppermute | solution.py:19
  34.6 0.0 copy-start.5
  34.6 0.0 collective-permute-done.2.refs_3_
  34.6 3.7 %collective-permute-done.3.refs_4_ = bf16[512,512]{1,0:T(8,128)(2,1)} collective-permute-done((bf16[512,512]{1,0:T(8,128)(2,1)S(1)}, bf16[512,512]{1,0:T(8,128)(2,1)}, u32[]{:S(2)}, u32[]{:S(2)}) %collective-permute-start.3) | collective-permute-done | bytes 524320 | tf_op jit(solution)/shard_map/ppermute | solution.py:19
  38.3 0.0 copy-done.1
  38.3 0.0 copy-done.4
  38.3 0.0 copy-done.5
  38.3 12.4 %shard_map.82 = bf16[512,256]{1,0:T(8,128)(2,1)} custom-call(s32[4,8]{1,0:T(4,128)} %fusion.34.slot_ref, bf16[512,256]{1,0:T(8,128)(2,1)} %slice.72.query_ref, bf16[512,512]{1,0:T(8,128)(2,1)} %copy-done.4, bf16[512,512]{1,0:T(8,128)(2,1)} %copy-done.5, bf16[512,512]{1,0:T(8,128)(2,1)} %copy-done.1, bf16[512,512]{1,0:T(8,128)(2,1)} %collective-permute-done.2.refs_3_, ...), custom_call_target="tpu_custom_call" | custom-call | tf_op jit(solution)/shard_map/pallas_call | solution.py:109
  50.7 0.0 copy-done.3
  50.7 1.4 %convolution_convert_fusion = bf16[512,1024]{1,0:T(8,128)(2,1)S(1)} fusion(bf16[512,256]{1,0:T(8,128)(2,1)} %shard_map.82, bf16[256,1024]{1,0:T(8,128)(2,1)S(1)} %copy-done.3), kind=kOutput, calls=%fused_computation.12 | convolution fusion | flops 268959744 | bytes 1835008 | tf_op jit(solution)/shard_map/dot_general | solution.py:121
  52.1 1.0 copy.25
  53.1 4.8 %all-to-all-start = ((bf16[512,4,256]{2,0,1:T(8,128)(2,1)}), bf16[512,4,256]{2,0,1:T(8,128)(2,1)S(1)}, u32[]{:S(2)}, u32[]{:S(2)}) async-start(bf16[512,4,256]{2,0,1:T(8,128)(2,1)} %bitcast.29), calls=%async_computation | async-start | bytes 2097152 | tf_op jit(solution)/shard_map/all_to_all | solution.py:30
  57.9 10.3 %all-to-all-done = bf16[512,4,256]{2,0,1:T(8,128)(2,1)S(1)} async-done(((bf16[512,4,256]{2,0,1:T(8,128)(2,1)}), bf16[512,4,256]{2,0,1:T(8,128)(2,1)S(1)}, u32[]{:S(2)}, u32[]{:S(2)}) %all-to-all-start) | async-done | bytes 1048608 | tf_op jit(solution)/shard_map/all_to_all | solution.py:30
  68.2 1.2 %multiply_reduce_fusion = (f32[512]{0:T(512)S(1)}, f32[512,256]{1,0:T(8,128)S(1)}) fusion(bf16[512,4,256]{2,0,1:T(8,128)(2,1)S(1)} %all-to-all-done, bf16[512,1024]{1,0:T(8,128)(2,1)} %param.8, s32[]{:T(128)S(6)} %select_n.23), kind=kLoop, calls=%fused_computation.35 | loop fusion | flops 1441280 | bytes 1837060 | tf_op jit(solution)/shard_map/reduce_sum | solution.py:129
  69.4 0.6 broadcast_in_dim.4
  70.1 4.7 %all-to-all-start.1 = ((f32[4,1,512]{2,1,0:T(1,128)}), f32[4,1,512]{2,1,0:T(1,128)S(1)}, u32[]{:S(2)}, u32[]{:S(2)}) async-start(f32[4,1,512]{2,1,0:T(1,128)} %broadcast_in_dim.4), calls=%async_computation.1 | async-start | bytes 16384 | tf_op jit(solution)/shard_map/all_to_all | solution.py:38
  74.7 0.8 dynamic_slice.11
  75.5 3.1 %all-to-all-done.1 = f32[4,1,512]{2,1,0:T(1,128)S(1)} async-done(((f32[4,1,512]{2,1,0:T(1,128)}), f32[4,1,512]{2,1,0:T(1,128)S(1)}, u32[]{:S(2)}, u32[]{:S(2)}) %all-to-all-start.1) | async-done | bytes 8224 | tf_op jit(solution)/shard_map/all_to_all | solution.py:38
  78.6 0.1 multiply_convert_fusion
  78.8 0.1 broadcast_in_dim.5
  78.8 13.3 %all_to_all.21 = bf16[512,4,256]{2,0,1:T(8,128)(2,1)S(1)} all-to-all(bf16[512,4,256]{2,0,1:T(8,128)(2,1)S(1)} %broadcast_in_dim.5), channel_id=1, replica_groups=mesh['patch'=128,'mp'=4] {'mp'}, dimensions={1} | all-to-all | bytes 2097152 | tf_op jit(solution)/shard_map/all_to_all | solution.py:48
  92.2 1.3 %copy.17 = bf16[512,4,256]{0,2,1:T(8,128)(2,1)} copy(bf16[512,4,256]{2,0,1:T(8,128)(2,1)S(1)} %all_to_all.21) | data formatting | bytes 2097152 | tf_op jit(solution)/shard_map/all_to_all | solution.py:48
  93.5 0.0 copy-done
  93.5 2.9 %convolution_convert_fusion.1 = bf16[512,1024]{1,0:T(8,128)(2,1)S(1)} fusion(bf16[512,1024]{1,0:T(8,128)(2,1)S(1)} %copy-done, bf16[512,1024]{0,1:T(8,128)(2,1)} %bitcast.31, bf16[1024,512]{1,0:T(8,128)(2,1)} %param.13), kind=kOutput, calls=%fused_computation.13 | convolution fusion | flops 1076625408 | bytes 4194304 | tf_op jit(solution)/shard_map/dot_general | solution.py:136
  96.4 0.1 copy.24
  96.5 13.3 %all_to_all.22 = bf16[512,4,256]{2,0,1:T(8,128)(2,1)S(1)} all-to-all(bf16[512,4,256]{2,0,1:T(8,128)(2,1)S(1)} %bitcast.30), channel_id=1, replica_groups=mesh['patch'=128,'mp'=4] {'mp'}, dimensions={1} | all-to-all | bytes 2097152 | tf_op jit(solution)/shard_map/all_to_all | solution.py:30
  109.8 0.8 fusion.24
  (3 shorter events, 0.1 us)
Async XLA Ops:
  0.0 93.5 %copy-start = (bf16[512,1024]{1,0:T(8,128)(2,1)S(1)}, bf16[512,1024]{1,0:T(8,128)(2,1)}, u32[]{:S(2)}) copy-start(bf16[512,1024]{1,0:T(8,128)(2,1)} %param.14) | copy-start | bytes 3145732
  0.0 1.8 %copy-start.2 = (bf16[512,1024]{1,0:T(8,128)(2,1)S(1)}, bf16[512,1024]{1,0:T(8,128)(2,1)}, u32[]{:S(2)}) copy-start(bf16[512,1024]{1,0:T(8,128)(2,1)} %param.8) | copy-start | bytes 3145732
  0.0 2.1 %copy-start.6 = (f32[1024]{0:T(1024)S(1)}, f32[1024]{0:T(1024)}, u32[]{:S(2)}) copy-start(f32[1024]{0:T(1024)} %param.9) | copy-start | bytes 12292
  3.2 35.1 %copy-start.1 = (bf16[512,512]{1,0:T(8,128)(2,1)}, bf16[512,512]{1,0:T(8,128)(2,1)S(1)}, u32[]{:S(2)}) copy-start(bf16[512,512]{1,0:T(8,128)(2,1)S(1)} %slice.73.refs_2_) | copy-start | bytes 1572868
  3.2 26.6 %collective-permute-start = (bf16[512,512]{1,0:T(8,128)(2,1)S(1)}, bf16[512,512]{1,0:T(8,128)(2,1)S(1)}, u32[]{:S(2)}, u32[]{:S(2)}) collective-permute-start(bf16[512,512]{1,0:T(8,128)(2,1)S(1)} %slice.73.refs_2_), channel_id=1, source_target_pairs={{0,8},{4,12},{8,16},{12,20},{16,24},{20,28},{24,32},{28,36},{32,40... | collective-permute-start | bytes 1572872 | tf_op jit(solution)/shard_map/ppermute | solution.py:19
  6.7 27.9 %collective-permute-start.1 = (bf16[512,512]{1,0:T(8,128)(2,1)S(1)}, bf16[512,512]{1,0:T(8,128)(2,1)S(1)}, u32[]{:S(2)}, u32[]{:S(2)}) collective-permute-start(bf16[512,512]{1,0:T(8,128)(2,1)S(1)} %slice.73.refs_2_), channel_id=1, source_target_pairs={{0,4},{4,8},{8,12},{12,16},{16,20},{20,24},{24,28},{28,32},{32,36}... | collective-permute-start | bytes 1572872 | tf_op jit(solution)/shard_map/ppermute | solution.py:19
  8.6 26.0 %collective-permute-start.2 = (bf16[512,512]{1,0:T(8,128)(2,1)S(1)}, bf16[512,512]{1,0:T(8,128)(2,1)}, u32[]{:S(2)}, u32[]{:S(2)}) collective-permute-start(bf16[512,512]{1,0:T(8,128)(2,1)S(1)} %slice.73.refs_2_), channel_id=1, source_target_pairs={{0,508},{4,0},{8,4},{12,8},{16,12},{20,16},{24,20},{28,24},{32,28}... | collective-permute-start | bytes 1572872 | tf_op jit(solution)/shard_map/ppermute | solution.py:19
  20.3 17.9 %collective-permute-start.3 = (bf16[512,512]{1,0:T(8,128)(2,1)S(1)}, bf16[512,512]{1,0:T(8,128)(2,1)}, u32[]{:S(2)}, u32[]{:S(2)}) collective-permute-start(bf16[512,512]{1,0:T(8,128)(2,1)S(1)} %slice.73.refs_2_), channel_id=1, source_target_pairs={{0,504},{4,508},{8,0},{12,4},{16,8},{20,12},{24,16},{28,20},{32,24... | collective-permute-start | bytes 1572872 | tf_op jit(solution)/shard_map/ppermute | solution.py:19
  26.7 23.9 %copy-start.3 = (bf16[256,1024]{1,0:T(8,128)(2,1)S(1)}, bf16[256,1024]{1,0:T(8,128)(2,1)}, u32[]{:S(2)}) copy-start(bf16[256,1024]{1,0:T(8,128)(2,1)} %param.11) | copy-start | bytes 1572868
  29.8 8.5 %copy-start.4 = (bf16[512,512]{1,0:T(8,128)(2,1)}, bf16[512,512]{1,0:T(8,128)(2,1)S(1)}, u32[]{:S(2)}) copy-start(bf16[512,512]{1,0:T(8,128)(2,1)S(1)} %collective-permute-done.refs_0_) | copy-start | bytes 1572868
  34.6 3.7 %copy-start.5 = (bf16[512,512]{1,0:T(8,128)(2,1)}, bf16[512,512]{1,0:T(8,128)(2,1)S(1)}, u32[]{:S(2)}) copy-start(bf16[512,512]{1,0:T(8,128)(2,1)S(1)} %collective-permute-done.1.refs_1_) | copy-start | bytes 1572868
  53.1 15.1 %all-to-all-start = ((bf16[512,4,256]{2,0,1:T(8,128)(2,1)}), bf16[512,4,256]{2,0,1:T(8,128)(2,1)S(1)}, u32[]{:S(2)}, u32[]{:S(2)}) async-start(bf16[512,4,256]{2,0,1:T(8,128)(2,1)} %bitcast.29), calls=%async_computation | async-start | bytes 2097152 | tf_op jit(solution)/shard_map/all_to_all | solution.py:30
  70.1 8.5 %all-to-all-start.1 = ((f32[4,1,512]{2,1,0:T(1,128)}), f32[4,1,512]{2,1,0:T(1,128)S(1)}, u32[]{:S(2)}, u32[]{:S(2)}) async-start(f32[4,1,512]{2,1,0:T(1,128)} %broadcast_in_dim.4), calls=%async_computation.1 | async-start | bytes 16384 | tf_op jit(solution)/shard_map/all_to_all | solution.py:38
